TPU v7x, 32 devices: a whole 2x2x4 slice. The times are simulated.
32 devices in a mesh: groups: 2 (over y), ctx: 4 (over z), sub: 2 (over x), head: 2 (over core).
Axes of the slice: x: 2, y: 2, z: 4, core: 2. Of those that a mesh axis runs over, the one named last changes fastest.
Arguments:
- queries: bfloat16 [32, 10240, 128], P(('sub', 'head'), ('groups', 'ctx')), parts along dimension 1, may hold values from -6 to 6
- keys: bfloat16 [32, 10240, 128], P(('sub', 'head'), ('groups', 'ctx')), parts along dimension 1, may hold values from -6 to 6
- values: bfloat16 [32, 10240, 128], P(('sub', 'head'), ('groups', 'ctx')), parts along dimension 1, may hold values from -90 to 90
- out_grad: bfloat16 [32, 10240, 128], P(('sub', 'head'), ('groups', 'ctx')), parts along dimension 1, may hold values from -6 to 6
- norm_gain: float32 [32, 128], P(('sub', 'head')), may hold values from 0.25 to 1.75
- doc_ids: int32 [40], P(('groups', 'ctx')), parts along dimension 0, may hold values from 0 to 3, never falling along the last dimension, each value on 1 to 10 neighbouring positions
Outputs:
- grad_queries: bfloat16 [32, 10240, 128], P(('sub', 'head'), ('groups', 'ctx')), parts along dimension 1
- grad_keys: bfloat16 [32, 10240, 128], P(('sub', 'head'), ('groups', 'ctx')), parts along dimension 1
- grad_values: bfloat16 [32, 10240, 128], P(('sub', 'head'), ('groups', 'ctx')), parts along dimension 1
There are 2 independent parts, one for each index of `groups`. A program takes and returns all parts, laid end to end along the dimension named above; an argument that names none is the same for every part. Nothing has to cross between parts.
Inputs may be any that keep to these rules, and one draw needn't show every extreme that they name: `doc_ids`: never falls; each of its 4 values labels 1 to 10 consecutive blocks, one value exactly 10.
All inputs are finite; a program needn't handle non-finite values.
Results may differ from a plain program's by a relative error of at most 0.0058.
Values sent between devices are 32-bit elements; how exact they have to be, the bound alone decides.
No kernel may reach another device: no remote copies, remote signals or barrier semaphores. Data moves between devices by JAX's collectives and lax.ppermute only.
A program may use at most 128 MiB of HBM per device.

v0:
```python
import jax
import jax.numpy as jnp
from jax import lax
from jax.sharding import PartitionSpec as P


def carried_in(value, axis, combine, identity, reverse):
    peers, index = (lax.axis_size(axis), lax.axis_index(axis))
    everything = jax.tree.map(lambda part: lax.all_gather(part, axis), value)
    start = jax.tree.map(
        lambda part, zero: jnp.broadcast_to(jnp.asarray(zero, part.dtype), part.shape),
        value,
        identity,
    )

    def lap(k, before):
        at = peers - 1 - k if reverse else k
        reached = at > index if reverse else at < index
        new = combine(before, jax.tree.map(lambda part: part[at], everything))
        return jax.tree.map(lambda a, b: jnp.where(reached, a, b), new, before)

    return lax.fori_loop(0, peers, lap, start)


def carry_combine(earlier_part, later_part):
    joined = jnp.where(earlier_part[0] == later_part[0], 1.0, 0.0).astype(jnp.float32)
    return (later_part[0], later_part[1] + joined * earlier_part[1])


def on_device(queries, keys, values, out_grad, norm_gain, doc_ids):
    head_count, tok_count, head_width = queries.shape
    block_count = doc_ids.shape[0]
    block_len = tok_count // block_count
    block_shape = (head_count, block_count, block_len, head_width)
    highest_precision = lax.Precision.HIGHEST
    query_blocks = queries.reshape(block_shape)
    key_blocks = keys.reshape(block_shape)
    value_blocks = values.reshape(block_shape)
    row_ids = lax.broadcasted_iota(jnp.int32, (block_len, block_len), 0)
    col_ids = lax.broadcasted_iota(jnp.int32, (block_len, block_len), 1)
    causal = row_ids >= col_ids
    doc_values = doc_ids.astype(jnp.float32)
    block_pos = jnp.arange(block_count, dtype=jnp.int32)
    same_doc = doc_values[:, None] == doc_values[None, :]
    earlier_mask = (same_doc & (block_pos[None, :] < block_pos[:, None])).astype(jnp.float32)
    later_mask = (same_doc & (block_pos[None, :] > block_pos[:, None])).astype(jnp.float32)
    scores = jnp.einsum(
        "hnid,hnjd->hnij", query_blocks, key_blocks, preferred_element_type=jnp.float32
    )
    block_probs = jnp.where(causal, scores, 0.0).astype(jnp.bfloat16)
    intra_part = jnp.einsum(
        "hnij,hnjd->hnid", block_probs, value_blocks, preferred_element_type=jnp.float32
    )
    key_value_block = jnp.einsum(
        "hnid,hnie->hnde", key_blocks, value_blocks, preferred_element_type=jnp.float32
    )
    local_prefix = jnp.einsum(
        "bc,hcde->hbde", earlier_mask, key_value_block, precision=highest_precision
    )
    last_match = (doc_values == doc_values[-1]).astype(jnp.float32)
    device_kv = jnp.einsum("c,hcde->hde", last_match, key_value_block, precision=highest_precision)
    prior_doc, prior_state = carried_in(
        (doc_values[-1], device_kv),
        "ctx",
        carry_combine,
        (jnp.float32(-1.0), jnp.zeros_like(device_kv)),
        False,
    )
    prior_match = (doc_values == prior_doc).astype(jnp.float32)
    entering = prior_match[None, :, None, None] * prior_state[:, None, :, :]
    preceding_states = (local_prefix + entering).astype(jnp.bfloat16)
    cross_block_part = jnp.einsum(
        "hnid,hnde->hnie", query_blocks, preceding_states, preferred_element_type=jnp.float32
    )
    raw_attn = (intra_part + cross_block_part).reshape(head_count, tok_count, head_width)
    feature_count = head_count * head_width * lax.axis_size(("sub", "head"))
    scaled = norm_gain[:, None, :] * out_grad.astype(jnp.float32)
    square_total = lax.psum(jnp.sum(raw_attn * raw_attn, axis=(0, 2)), ("sub", "head"))
    root_mean = jnp.sqrt(square_total / feature_count + 1e-06)
    normed = raw_attn / root_mean[None, :, None]
    scaled_mean = lax.psum(jnp.sum(scaled * normed, axis=(0, 2)), ("sub", "head")) / feature_count
    d_attn = ((scaled - normed * scaled_mean[None, :, None]) / root_mean[None, :, None]).astype(
        jnp.bfloat16
    )
    output_grad_blocks = d_attn.reshape(block_shape)
    grad_scores = jnp.einsum(
        "hnid,hnjd->hnij", output_grad_blocks, value_blocks, preferred_element_type=jnp.float32
    )
    grad_probs = jnp.where(causal, grad_scores, 0.0).astype(jnp.bfloat16)
    query_gradient = jnp.einsum(
        "hnij,hnjd->hnid", grad_probs, key_blocks, preferred_element_type=jnp.float32
    )
    key_gradient = jnp.einsum(
        "hnij,hnid->hnjd", grad_probs, query_blocks, preferred_element_type=jnp.float32
    )
    value_gradient = jnp.einsum(
        "hnij,hnid->hnjd", block_probs, output_grad_blocks, preferred_element_type=jnp.float32
    )
    query_grad_block = jnp.einsum(
        "hnid,hnie->hnde", query_blocks, output_grad_blocks, preferred_element_type=jnp.float32
    )
    local_suffix = jnp.einsum(
        "bc,hcde->hbde", later_mask, query_grad_block, precision=highest_precision
    )
    first_match = (doc_values == doc_values[0]).astype(jnp.float32)
    device_qd = jnp.einsum(
        "c,hcde->hde", first_match, query_grad_block, precision=highest_precision
    )
    next_doc, next_state = carried_in(
        (doc_values[0], device_qd),
        "ctx",
        carry_combine,
        (jnp.float32(-1.0), jnp.zeros_like(device_qd)),
        True,
    )
    next_match = (doc_values == next_doc).astype(jnp.float32)
    leaving = next_match[None, :, None, None] * next_state[:, None, :, :]
    following_states = (local_suffix + leaving).astype(jnp.bfloat16)
    query_gradient = query_gradient + jnp.einsum(
        "hnie,hnde->hnid", output_grad_blocks, preceding_states, preferred_element_type=jnp.float32
    )
    key_gradient = key_gradient + jnp.einsum(
        "hnie,hnde->hnid", value_blocks, following_states, preferred_element_type=jnp.float32
    )
    value_gradient = value_gradient + jnp.einsum(
        "hnid,hnde->hnie", key_blocks, following_states, preferred_element_type=jnp.float32
    )
    out_shape = (head_count, tok_count, head_width)
    return (
        query_gradient.reshape(out_shape).astype(jnp.bfloat16),
        key_gradient.reshape(out_shape).astype(jnp.bfloat16),
        value_gradient.reshape(out_shape).astype(jnp.bfloat16),
    )


def solution(mesh):
    return jax.shard_map(
        on_device,
        mesh=mesh,
        in_specs=(
            P(("sub", "head"), ("groups", "ctx"), None),
            P(("sub", "head"), ("groups", "ctx"), None),
            P(("sub", "head"), ("groups", "ctx"), None),
            P(("sub", "head"), ("groups", "ctx"), None),
            P(("sub", "head"), None),
            P(("groups", "ctx")),
        ),
        out_specs=(
            P(("sub", "head"), ("groups", "ctx"), None),
            P(("sub", "head"), ("groups", "ctx"), None),
            P(("sub", "head"), ("groups", "ctx"), None),
        ),
        check_vma=False,
    )
```

profile of v0, /device:TPU:0, one launch (start us, length us, event | category | flops | bytes accessed | tf_op | source)
XLA Modules:
  0.0 199.0 jit_solution(3285715845271670284)
XLA Ops:
  7.2 0.8 convert_element_type.51
  8.0 1.2 dynamic-slice
  9.3 3.4 %fusion.30 = f32[8,5,128,128]{3,2,1,0:T(8,128)S(1)} fusion(bf16[8,5,256,128]{3,2,1,0:T(8,128)(2,1)} %bitcast.118, bf16[8,5,256,128]{3,2,1,0:T(8,128)(2,1)} %bitcast.122), kind=kOutput, calls=%fused_computation.55 | convolution fusion | flops 335544320 | bytes 7864320 | tf_op jit(solution)/shard_map/hnid,hnie->hnde/dot_general | solution.py:54
  12.7 1.4 fusion.28
  14.2 4.8 %fusion.4 = f32[1,8,128,128]{3,0,2,1:T(1,128)} fusion(f32[8,5,128,128]{3,2,1,0:T(8,128)S(1)} %fusion.30, f32[]{:T(128)} %bitcast.8, s32[5]{0:T(128)S(1)} %copy-done.15), kind=kOutput, calls=%fused_computation.17 | convolution fusion | flops 7864330 | bytes 3145752 | tf_op jit(solution)/shard_map/c,hcde->hde/dot_general | solution.py:61
  19.1 0.7 slice_dynamic-update-slice_fusion
  19.9 13.7 %all-reduce.2 = (f32[4]{0:T(128)S(1)}, f32[4]{0:T(128)S(1)}) all-reduce(f32[4]{0:T(128)S(1)} %get-tuple-element.341, f32[4]{0:T(128)S(1)} %slice_dynamic-update-slice_fusion), channel_id=1, replica_groups=mesh['groups'=2,'ctx'=4,'sub'=2,'head'=2] {'ctx'}, use_global_device_ids=true, to_apply=%add | all-reduce | flops 8 | bytes 64
  33.6 7.4 %fusion.6 = f32[8,128,128,5]{2,3,1,0:T(8,128)} fusion(f32[8,5,128,128]{3,2,1,0:T(8,128)} %copy-done.1, f32[5]{0:T(128)S(1)} %convert_element_type.51), kind=kOutput, calls=%fused_computation.19 | convolution fusion | flops 39321676 | bytes 5242900 | tf_op jit(solution)/shard_map/bc,hcde->hbde/dot_general | solution.py:57
  41.0 1.5 select_convert_fusion.1
  42.5 2.3 %copy-done.4 = bf16[8,5,256,256]{3,2,1,0:T(8,128)(2,1)} copy-done((bf16[8,5,256,256]{3,2,1,0:T(8,128)(2,1)}, bf16[8,5,256,256]{3,2,1,0:T(8,128)(2,1)S(1)}, u32[]{:S(2)}) %copy-start.4) | copy-done | bytes 5242904
  44.8 3.9 %fusion.29 = f32[8,5,256,128]{3,2,1,0:T(8,128)} fusion(bf16[8,5,256,256]{3,2,1,0:T(8,128)(2,1)S(1)} %select_convert_fusion.1, bf16[8,5,256,128]{3,2,1,0:T(8,128)(2,1)S(1)} %bitcast.123), kind=kOutput, calls=%fused_computation.54 | convolution fusion | flops 671088640 | bytes 13107200 | tf_op jit(solution)/shard_map/hnij,hnjd->hnid/dot_general | solution.py:51
  48.7 19.1 %all-gather.5.cloned.1.call-done = f32[32,128,128]{2,1,0:T(8,128)} async-done(((f32[8,128,128]{2,1,0:T(8,128)}), f32[32,128,128]{2,1,0:T(8,128)}) %all-gather.5.cloned.1.call-update) | async-done | bytes 2097168 | tf_op jit(solution)/shard_map/all_gather | solution.py:9
  67.8 13.5 %while.34 = (s32[]{:T(128)}, f32[]{:T(128)}, f32[8,128,128]{2,1,0:T(8,128)S(1)}, s32[]{:T(128)}, f32[4]{0:T(128)S(1)}, /*index=5*/f32[4,8,128,128]{3,2,1,0:T(8,128)}, s32[]{:T(128)}, f32[]{:T(128)}, f32[]{:T(128)}, s32[]{:T(128)}) while((s32[]{:T(128)}, f32[]{:T(128)}, f32[8,128,128]{2,1,0:T(8,128)S(1)}, s32[]{:T(128)}, ...), condition=%wide.region_1.2_spmd.clone, body=%wide.region_0.1_spmd.clone.sunk | while | flops 524295 | bytes 1573048 | solution.py:22
  69.7 1.5 fusion.62
  71.2 0.6 dynamic_slice.45
  73.1 1.5 fusion.62
  74.6 0.6 dynamic_slice.45
  76.5 1.5 fusion.62
  79.9 1.5 fusion.62
  81.4 3.0 %fusion.9 = bf16[8,5,128,128]{3,2,1,0:T(8,128)(2,1)S(1)} fusion(f32[8,128,128,5]{2,3,1,0:T(8,128)} %fusion.6, f32[8,128,128]{2,1,0:T(8,128)S(1)} %get-tuple-element.269, f32[5]{0:T(128)S(1)} %compare_convert_fusion.1), kind=kLoop, calls=%fused_computation.24 | loop fusion | flops 1966080 | bytes 4456468 | tf_op jit(solution)/shard_map/convert_element_type | solution.py:71
  84.4 0.8 copy-done.5
  85.2 3.2 %multiply_reduce_fusion.1 = (f32[5,256]{1,0:T(8,128)S(1)}, f32[8,5,256,128]{3,2,1,0:T(8,128)}) fusion(f32[8,5,256,128]{3,2,1,0:T(8,128)S(1)} %copy-done.5, bf16[8,5,256,128]{3,2,1,0:T(8,128)(2,1)S(1)} %bitcast.109, bf16[8,5,128,128]{3,2,1,0:T(8,128)(2,1)S(1)} %fusion.9), kind=kOutput, calls=%fused_computation.15 | convolution fusion | flops 339475200 | bytes 14423040 | tf_op jit(solution)/shard_map/hnid,hnde->hnie/dot_general | solution.py:72
  88.4 7.0 %psum.14 = f32[1280]{0:T(1024)S(1)} all-reduce(f32[1280]{0:T(1024)S(1)} %reduce_sum.21), channel_id=1, replica_groups=mesh['groups'=2,'ctx'=4,'sub'=2,'head'=2] {'sub','head'}, use_global_device_ids=true, to_apply=%region_3.4 | all-reduce | flops 1280 | bytes 10240 | tf_op jit(solution)/shard_map/psum | solution.py:78
  95.4 4.3 %multiply_reduce_fusion = f32[1280]{0:T(1024)S(1)} fusion(bf16[8,1280,128]{2,1,0:T(8,128)(2,1)} %param.13, f32[8,128]{1,0:T(8,128)S(1)} %copy-done.14, f32[1280]{0:T(1024)S(1)} %add_sqrt_fusion, f32[8,5,256,128]{3,2,1,0:T(8,128)} %get-tuple-element.344), kind=kLoop, calls=%fused_computation.14 | loop fusion | flops 6552320 | bytes 7878656 | tf_op jit(solution)/shard_map/reduce_sum | solution.py:81
  99.7 6.0 %psum.15 = f32[1280]{0:T(1024)S(1)} all-reduce(f32[1280]{0:T(1024)S(1)} %multiply_reduce_fusion), channel_id=1, replica_groups=mesh['groups'=2,'ctx'=4,'sub'=2,'head'=2] {'sub','head'}, use_global_device_ids=true, to_apply=%region_5.6 | all-reduce | flops 1280 | bytes 10240 | tf_op jit(solution)/shard_map/psum | solution.py:81
  105.7 4.1 %divide_convert_fusion = bf16[8,1280,128]{2,1,0:T(8,128)(2,1)S(1)} fusion(bf16[8,1280,128]{2,1,0:T(8,128)(2,1)} %param.13, f32[1280]{0:T(1024)S(1)} %broadcast_multiply_fusion, f32[1280]{0:T(1024)S(1)} %add_sqrt_fusion, f32[8,128]{1,0:T(8,128)S(1)} %copy-done.14, f32[8,5,256,128]{3,2,1,0:T(8,128)} %get-tuple-element.344), kind=kLoop, calls=%fused_computation.13 | loop fusion | flops 9175040 | bytes 10500096 | tf_op jit(solution)/shard_map/convert_element_type | solution.py:82
  109.9 1.5 copy-done.2
  111.4 2.4 %convolution_bitcast_fusion = f32[8,5,128,128]{2,3,1,0:T(8,128)} fusion(bf16[8,5,256,128]{3,2,1,0:T(8,128)(2,1)S(1)} %bitcast.112, bf16[8,5,256,128]{3,2,1,0:T(8,128)(2,1)S(1)} %bitcast.111), kind=kOutput, calls=%fused_computation.25 | convolution fusion | flops 335544320 | bytes 7864320 | tf_op jit(solution)/shard_map/hnid,hnie->hnde/dot_general | solution.py:99
  113.7 4.8 %copy.42 = f32[8,5,128,128]{3,1,2,0:T(8,128)} copy(f32[8,5,128,128]{2,3,1,0:T(8,128)} %convolution_bitcast_fusion) | data formatting | bytes 5242880 | tf_op jit(solution)/shard_map/hnid,hnie->hnde/dot_general | solution.py:99
  118.5 5.7 %fusion.19 = f32[1,8,128,128]{3,0,2,1:T(1,128)} fusion(f32[8,5,128,128]{3,1,2,0:T(8,128)} %copy.42, f32[]{:T(128)} %bitcast.23, s32[5]{0:T(128)S(1)} %copy-done.15), kind=kOutput, calls=%fused_computation.40 | convolution fusion | flops 7864330 | bytes 3145752 | tf_op jit(solution)/shard_map/c,hcde->hde/dot_general | solution.py:106
  124.3 6.6 %fusion.13 = f32[8,128,128,5]{2,3,1,0:T(8,128)} fusion(f32[8,5,128,128]{3,1,2,0:T(8,128)} %copy.42, f32[5]{0:T(128)S(1)} %convert_element_type.51), kind=kOutput, calls=%fused_computation.35 | convolution fusion | flops 39321676 | bytes 5242900 | tf_op jit(solution)/shard_map/bc,hcde->hbde/dot_general | solution.py:102
  130.8 1.5 select_convert_fusion
  132.6 1.5 fusion.31
  134.1 2.4 %add_convert_fusion = bf16[8,5,256,128]{3,2,1,0:T(8,128)(2,1)} fusion(f32[8,5,256,128]{3,2,1,0:T(8,128)S(1)} %fusion.31, bf16[8,5,256,128]{3,2,1,0:T(8,128)(2,1)S(1)} %bitcast.114, bf16[8,5,128,128]{3,2,1,0:T(8,128)(2,1)S(1)} %copy-done.13), kind=kOutput, calls=%fused_computation.12 | convolution fusion | flops 338165760 | bytes 11796480 | tf_op jit(solution)/shard_map/hnie,hnde->hnid/dot_general | solution.py:119
  136.6 3.9 %fusion.33 = f32[8,5,256,128]{3,2,1,0:T(8,128)} fusion(bf16[8,5,256,256]{3,2,1,0:T(8,128)(2,1)S(1)} %bitcast.117, bf16[8,5,256,128]{3,2,1,0:T(8,128)(2,1)S(1)} %bitcast.115), kind=kOutput, calls=%fused_computation.58 | convolution fusion | flops 671088640 | bytes 13107200 | tf_op jit(solution)/shard_map/hnij,hnid->hnjd/dot_general | solution.py:96
  140.5 3.9 %fusion.32 = f32[8,5,256,128]{3,2,1,0:T(8,128)} fusion(bf16[8,5,256,256]{3,2,1,0:T(8,128)(2,1)S(1)} %select_convert_fusion, bf16[8,5,256,128]{3,2,1,0:T(8,128)(2,1)S(1)} %bitcast.110), kind=kOutput, calls=%fused_computation.57 | convolution fusion | flops 671088640 | bytes 13107200 | tf_op jit(solution)/shard_map/hnij,hnid->hnjd/dot_general | solution.py:93
  144.4 23.7 %all-gather.7.cloned.1.call-done = f32[32,128,128]{2,1,0:T(8,128)} async-done(((f32[8,128,128]{2,1,0:T(8,128)}), f32[32,128,128]{2,1,0:T(8,128)}) %all-gather.7.cloned.1.call-update) | async-done | bytes 2097168 | tf_op jit(solution)/shard_map/all_gather | solution.py:9
  168.1 13.6 %while.35 = (s32[]{:T(128)}, f32[]{:T(128)}, f32[8,128,128]{2,1,0:T(8,128)S(1)}, s32[]{:T(128)}, f32[4]{0:T(128)S(1)}, /*index=5*/f32[4,8,128,128]{3,2,1,0:T(8,1...) while((s32[]{:T(128)}, f32[]{:T(128)}, ...), condition=%wide.region_7.8_spmd.clone, body=%wide.region_6.7_spmd.clone.sunk | while | flops 524299 | bytes 1573110 | solution.py:22
  170.0 1.5 fusion.63
  171.5 0.6 dynamic_slice.47
  173.4 1.5 fusion.63
  174.9 0.6 dynamic_slice.47
  176.8 1.5 fusion.63
  178.3 0.6 dynamic_slice.47
  180.2 1.5 fusion.63
  181.7 3.0 %fusion.8 = bf16[8,5,128,128]{3,2,1,0:T(8,128)(2,1)S(1)} fusion(f32[8,128,128,5]{2,3,1,0:T(8,128)} %fusion.13, f32[8,128,128]{2,1,0:T(8,128)S(1)} %get-tuple-element.271, f32[5]{0:T(128)S(1)} %compare_convert_fusion), kind=kLoop, calls=%fused_computation.22 | loop fusion | flops 1966080 | bytes 4456468 | tf_op jit(solution)/shard_map/convert_element_type | solution.py:118
  184.7 5.1 %fusion.2 = bf16[8,5,256,128]{3,2,1,0:T(8,128)(2,1)} fusion(f32[8,5,256,128]{3,2,1,0:T(8,128)} %fusion.33, bf16[8,5,256,128]{3,2,1,0:T(8,128)(2,1)S(1)} %bitcast.121, bf16[8,5,128,128]{3,2,1,0:T(8,128)(2,1)S(1)} %fusion.8), kind=kOutput, calls=%fused_computation.7 | convolution fusion | flops 338165760 | bytes 11796480 | tf_op jit(solution)/shard_map/hnid,hnde->hnie/dot_general | solution.py:125
  189.9 2.3 %fusion.3 = bf16[8,5,256,128]{3,2,1,0:T(8,128)(2,1)} fusion(f32[8,5,256,128]{3,2,1,0:T(8,128)S(1)} %bitcast.127, bf16[8,5,128,128]{3,2,1,0:T(8,128)(2,1)S(1)} %fusion.8, bf16[8,5,256,128]{3,2,1,0:T(8,128)(2,1)S(1)} %bitcast.125), kind=kOutput, calls=%fused_computation.9 | convolution fusion | flops 338165760 | bytes 11796480 | tf_op jit(solution)/shard_map/hnie,hnde->hnid/dot_general | solution.py:122
  (56 shorter events, 2.4 us)
Async XLA Ops:
  7.2 33.8 %copy-start = (bf16[8,1280,128]{2,1,0:T(8,128)(2,1)S(1)}, bf16[8,1280,128]{2,1,0:T(8,128)(2,1)}, u32[]{:S(2)}) copy-start(bf16[8,1280,128]{2,1,0:T(8,128)(2,1)} %param.10) | copy-start | bytes 7864324
  7.2 60.7 %all-gather.5.cloned.1.call-start = ((), (), s32[]{:S(2)}) async-start(), calls=%async_computation | async-start | bytes 2621440 | tf_op jit(solution)/shard_map/all_gather | solution.py:9
  9.3 4.9 %copy-start.15 = (s32[5]{0:T(128)S(1)}, s32[5]{0:T(128)}, u32[]{:S(2)}) copy-start(s32[5]{0:T(128)} %param.15) | copy-start | bytes 64
  12.7 1.5 copy-start.1
  19.0 149.1 %all-gather.7.cloned.1.call-start = ((), (), s32[]{:S(2)}) async-start(), calls=%async_computation.1 | async-start | bytes 2621440 | tf_op jit(solution)/shard_map/all_gather | solution.py:9
  33.6 7.4 %copy-start.6 = (bf16[8,1280,128]{2,1,0:T(8,128)(2,1)S(1)}, bf16[8,1280,128]{2,1,0:T(8,128)(2,1)}, u32[]{:S(2)}) copy-start(bf16[8,1280,128]{2,1,0:T(8,128)(2,1)} %param.11) | copy-start | bytes 7864324
  41.0 3.9 %copy-start.9 = (bf16[8,1280,128]{2,1,0:T(8,128)(2,1)S(1)}, bf16[8,1280,128]{2,1,0:T(8,128)(2,1)}, u32[]{:S(2)}) copy-start(bf16[8,1280,128]{2,1,0:T(8,128)(2,1)} %param.12) | copy-start | bytes 7864324
  42.5 2.3 %copy-start.4 = (bf16[8,5,256,256]{3,2,1,0:T(8,128)(2,1)}, bf16[8,5,256,256]{3,2,1,0:T(8,128)(2,1)S(1)}, u32[]{:S(2)}) copy-start(bf16[8,5,256,256]{3,2,1,0:T(8,128)(2,1)S(1)} %select_convert_fusion.1) | copy-start | bytes 15728644
  81.4 3.7 %copy-start.5 = (f32[8,5,256,128]{3,2,1,0:T(8,128)S(1)}, f32[8,5,256,128]{3,2,1,0:T(8,128)}, u32[]{:S(2)}) copy-start(f32[8,5,256,128]{3,2,1,0:T(8,128)} %fusion.29) | copy-start | bytes 15728644
  85.2 3.2 %copy-start.12 = (bf16[8,5,128,128]{3,2,1,0:T(8,128)(2,1)}, bf16[8,5,128,128]{3,2,1,0:T(8,128)(2,1)S(1)}, u32[]{:S(2)}) copy-start(bf16[8,5,128,128]{3,2,1,0:T(8,128)(2,1)S(1)} %fusion.9) | copy-start | bytes 3932164
  85.2 10.3 %copy-start.14 = (f32[8,128]{1,0:T(8,128)S(1)}, f32[8,128]{1,0:T(8,128)}, u32[]{:S(2)}) copy-start(f32[8,128]{1,0:T(8,128)} %param.14) | copy-start | bytes 12292
  109.9 1.5 copy-start.2
  124.2 6.6 %copy-start.3 = (bf16[8,1280,128]{2,1,0:T(8,128)(2,1)S(1)}, bf16[8,1280,128]{2,1,0:T(8,128)(2,1)}, u32[]{:S(2)}) copy-start(bf16[8,1280,128]{2,1,0:T(8,128)(2,1)} %copy-done.2) | copy-start | bytes 7864324
  124.2 6.6 %copy-start.10 = (bf16[8,1280,128]{2,1,0:T(8,128)(2,1)S(1)}, bf16[8,1280,128]{2,1,0:T(8,128)(2,1)}, u32[]{:S(2)}) copy-start(bf16[8,1280,128]{2,1,0:T(8,128)(2,1)} %param.12) | copy-start | bytes 7864324
  130.8 1.7 copy-start.7
  130.8 5.7 %slice-start = ((s8[5242880]{0:T(1024)(128)(4,1)}), s8[4194304]{0:T(1024)(128)(4,1)S(1)}, s32[]{:S(2)}) async-start(s8[5242880]{0:T(1024)(128)(4,1)} %bitcast.116), calls=%async_computation.2 | async-start | bytes 8388608
  132.6 1.6 copy-start.13
  132.6 4.0 %slice-start.1 = ((s8[5242880]{0:T(1024)(128)(4,1)}), s8[1048576]{0:T(1024)(128)(4,1)S(1)}, s32[]{:S(2)}) async-start(s8[5242880]{0:T(1024)(128)(4,1)} %bitcast.116), calls=%async_computation.3 | async-start | bytes 2097152
  181.7 3.0 %copy-start.8 = (bf16[8,1280,128]{2,1,0:T(8,128)(2,1)S(1)}, bf16[8,1280,128]{2,1,0:T(8,128)(2,1)}, u32[]{:S(2)}) copy-start(bf16[8,1280,128]{2,1,0:T(8,128)(2,1)} %param.11) | copy-start | bytes 7864324
  181.7 8.1 %slice-start.2 = ((s8[5242880]{0:T(1024)(128)(4,1)}), s8[4194304]{0:T(1024)(128)(4,1)S(1)}, s32[]{:S(2)}) async-start(s8[5242880]{0:T(1024)(128)(4,1)} %bitcast.126), calls=%async_computation.4 | async-start | bytes 8388608
  184.7 5.1 %copy-start.11 = (bf16[8,1280,128]{2,1,0:T(8,128)(2,1)S(1)}, bf16[8,1280,128]{2,1,0:T(8,128)(2,1)}, u32[]{:S(2)}) copy-start(bf16[8,1280,128]{2,1,0:T(8,128)(2,1)} %param.12) | copy-start | bytes 7864324
  184.7 5.1 %slice-start.3 = ((s8[5242880]{0:T(1024)(128)(4,1)}), s8[1048576]{0:T(1024)(128)(4,1)S(1)}, s32[]{:S(2)}) async-start(s8[5242880]{0:T(1024)(128)(4,1)} %bitcast.126), calls=%async_computation.5 | async-start | bytes 2097152
Sparse Core Ops, SparseCore 0:
  19.2 48.6 all-gather.4
  124.3 43.7 all-gather.6
where the time goes:
time: 200 us; the launch traced here: 199 us
  matrix products  59.6 us (30%)
  waiting for transfers between devices  42.9 us (21%)
  other arithmetic  27 us (14%)
  blocking collectives  26.7 us (13%)
  local copies, waits for them, and re-layouts  17.8 us (9%)
  between operations  14.3 us (7%)
  loops' own time  10.6 us (5%)
    all_gather x2, waiting for transfers between devices, carried_in(): everything = jax.tree.map(lambda part: lax.all_gather(part, axis), value)  42.9 us
    unnamed x1, blocking collectives  13.7 us
    select_n x8, other arithmetic, lap(): return jax.tree.map(lambda a, b: jnp.where(reached, a, b), new, before)  11.8 us
    another operation x2, loops' own time, carried_in(): return lax.fori_loop(0, peers, lap, start)  10.6 us
    dot_general x1, matrix products, on_device(): jnp.einsum('bc,hcde->hbde', earlier_mask, key_value_block, precision=high...  7.38 us
    psum x1, blocking collectives, on_device(): lax.psum(jnp.sum(raw_attn * raw_attn, axis=(0, 2)), ('sub', 'head'))  7 us
    unnamed x44, local copies, waits for them, and re-layouts  6.97 us
    dot_general x1, matrix products, on_device(): jnp.einsum('bc,hcde->hbde', later_mask, query_grad_block, precision=highe...  6.56 us
  transfers between devices with their start and end apart: 2, of which 2 were waited for; matrix products, arithmetic and copies ran while one was open for 17% of the time, Pallas kernels for 0%

commit v1 on v0

--- a/solution.py
+++ b/solution.py
@@ -4,27 +4,41 @@
 from jax.sharding import PartitionSpec as P
 
 
-def carried_in(value, axis, combine, identity, reverse):
-    peers, index = (lax.axis_size(axis), lax.axis_index(axis))
-    everything = jax.tree.map(lambda part: lax.all_gather(part, axis), value)
-    start = jax.tree.map(
-        lambda part, zero: jnp.broadcast_to(jnp.asarray(zero, part.dtype), part.shape),
-        value,
-        identity,
-    )
+def segmented_scan(doc, state, axis, reverse):
+    peers = lax.axis_size(axis)
+    index = lax.axis_index(axis)
+    none_doc = jnp.float32(-1.0)
 
-    def lap(k, before):
-        at = peers - 1 - k if reverse else k
-        reached = at > index if reverse else at < index
-        new = combine(before, jax.tree.map(lambda part: part[at], everything))
-        return jax.tree.map(lambda a, b: jnp.where(reached, a, b), new, before)
+    def shift(value, step):
+        if reverse:
+            pairs = [(j, j - step) for j in range(step, peers)]
+        else:
+            pairs = [(j, j + step) for j in range(peers - step)]
+        return lax.ppermute(value, axis, pairs)
 
-    return lax.fori_loop(0, peers, lap, start)
+    def combine(near_doc, near_state, far_doc, far_state):
+        joined = (near_doc == far_doc).astype(jnp.float32)
+        return near_doc, near_state + joined * far_state
 
-
-def carry_combine(earlier_part, later_part):
-    joined = jnp.where(earlier_part[0] == later_part[0], 1.0, 0.0).astype(jnp.float32)
-    return (later_part[0], later_part[1] + joined * earlier_part[1])
+    if peers == 1:
+        return none_doc, jnp.zeros_like(state)
+    got_doc, got_state = shift((doc, state), 1)
+    valid = (index >= 1) if not reverse else (index <= peers - 2)
+    ex_doc = jnp.where(valid, got_doc, none_doc)
+    ex_state = jnp.where(valid, got_state, 0.0)
+    in_doc, in_state = combine(doc, state, ex_doc, ex_state)
+    covered = 1
+    while covered < peers - 1:
+        step = covered + 1
+        got_doc, got_state = shift((in_doc, in_state), step)
+        valid = (index >= step) if not reverse else (index <= peers - 1 - step)
+        got_doc = jnp.where(valid, got_doc, none_doc)
+        got_state = jnp.where(valid, got_state, 0.0)
+        ex_doc, ex_state = combine(ex_doc, ex_state, got_doc, got_state)
+        covered = covered + step
+        if covered < peers - 1:
+            in_doc, in_state = combine(in_doc, in_state, got_doc, got_state)
+    return ex_doc, ex_state
 
 
 def on_device(queries, keys, values, out_grad, norm_gain, doc_ids):
@@ -44,6 +58,12 @@
     same_doc = doc_values[:, None] == doc_values[None, :]
     earlier_mask = (same_doc & (block_pos[None, :] < block_pos[:, None])).astype(jnp.float32)
     later_mask = (same_doc & (block_pos[None, :] > block_pos[:, None])).astype(jnp.float32)
+    key_value_block = jnp.einsum(
+        "hnid,hnie->hnde", key_blocks, value_blocks, preferred_element_type=jnp.float32
+    )
+    last_match = (doc_values == doc_values[-1]).astype(jnp.float32)
+    device_kv = jnp.einsum("c,hcde->hde", last_match, key_value_block, precision=highest_precision)
+    prior_doc, prior_state = segmented_scan(doc_values[-1], device_kv, "ctx", False)
     scores = jnp.einsum(
         "hnid,hnjd->hnij", query_blocks, key_blocks, preferred_element_type=jnp.float32
     )
@@ -51,20 +71,8 @@
     intra_part = jnp.einsum(
         "hnij,hnjd->hnid", block_probs, value_blocks, preferred_element_type=jnp.float32
     )
-    key_value_block = jnp.einsum(
-        "hnid,hnie->hnde", key_blocks, value_blocks, preferred_element_type=jnp.float32
-    )
     local_prefix = jnp.einsum(
         "bc,hcde->hbde", earlier_mask, key_value_block, precision=highest_precision
-    )
-    last_match = (doc_values == doc_values[-1]).astype(jnp.float32)
-    device_kv = jnp.einsum("c,hcde->hde", last_match, key_value_block, precision=highest_precision)
-    prior_doc, prior_state = carried_in(
-        (doc_values[-1], device_kv),
-        "ctx",
-        carry_combine,
-        (jnp.float32(-1.0), jnp.zeros_like(device_kv)),
-        False,
     )
     prior_match = (doc_values == prior_doc).astype(jnp.float32)
     entering = prior_match[None, :, None, None] * prior_state[:, None, :, :]
@@ -75,14 +83,25 @@
     raw_attn = (intra_part + cross_block_part).reshape(head_count, tok_count, head_width)
     feature_count = head_count * head_width * lax.axis_size(("sub", "head"))
     scaled = norm_gain[:, None, :] * out_grad.astype(jnp.float32)
-    square_total = lax.psum(jnp.sum(raw_attn * raw_attn, axis=(0, 2)), ("sub", "head"))
-    root_mean = jnp.sqrt(square_total / feature_count + 1e-06)
-    normed = raw_attn / root_mean[None, :, None]
-    scaled_mean = lax.psum(jnp.sum(scaled * normed, axis=(0, 2)), ("sub", "head")) / feature_count
-    d_attn = ((scaled - normed * scaled_mean[None, :, None]) / root_mean[None, :, None]).astype(
-        jnp.bfloat16
+    local_sums = jnp.stack(
+        [jnp.sum(raw_attn * raw_attn, axis=(0, 2)), jnp.sum(scaled * raw_attn, axis=(0, 2))]
     )
+    total_sums = lax.psum(local_sums, ("sub", "head"))
+    root_mean = jnp.sqrt(total_sums[0] / feature_count + 1e-06)
+    inner_mean = total_sums[1] / feature_count
+    factor = inner_mean / (root_mean * root_mean)
+    d_attn = (
+        (scaled - raw_attn * factor[None, :, None]) / root_mean[None, :, None]
+    ).astype(jnp.bfloat16)
     output_grad_blocks = d_attn.reshape(block_shape)
+    query_grad_block = jnp.einsum(
+        "hnid,hnie->hnde", query_blocks, output_grad_blocks, preferred_element_type=jnp.float32
+    )
+    first_match = (doc_values == doc_values[0]).astype(jnp.float32)
+    device_qd = jnp.einsum(
+        "c,hcde->hde", first_match, query_grad_block, precision=highest_precision
+    )
+    next_doc, next_state = segmented_scan(doc_values[0], device_qd, "ctx", True)
     grad_scores = jnp.einsum(
         "hnid,hnjd->hnij", output_grad_blocks, value_blocks, preferred_element_type=jnp.float32
     )
@@ -96,22 +115,8 @@
     value_gradient = jnp.einsum(
         "hnij,hnid->hnjd", block_probs, output_grad_blocks, preferred_element_type=jnp.float32
     )
-    query_grad_block = jnp.einsum(
-        "hnid,hnie->hnde", query_blocks, output_grad_blocks, preferred_element_type=jnp.float32
-    )
     local_suffix = jnp.einsum(
         "bc,hcde->hbde", later_mask, query_grad_block, precision=highest_precision
-    )
-    first_match = (doc_values == doc_values[0]).astype(jnp.float32)
-    device_qd = jnp.einsum(
-        "c,hcde->hde", first_match, query_grad_block, precision=highest_precision
-    )
-    next_doc, next_state = carried_in(
-        (doc_values[0], device_qd),
-        "ctx",
-        carry_combine,
-        (jnp.float32(-1.0), jnp.zeros_like(device_qd)),
-        True,
     )
     next_match = (doc_values == next_doc).astype(jnp.float32)
     leaving = next_match[None, :, None, None] * next_state[:, None, :, :]

time: 200 us -> 160 us (0.80)
  starting transfers between devices: 0.08 us -> 24.5 us
  blocking collectives: 26.7 us -> 10.3 us
  other arithmetic: 27 us -> 11.4 us
  loops' own time: 10.6 us -> 0 us
  between operations: 14.3 us -> 4.79 us
  local copies, waits for them, and re-layouts: 17.8 us -> 9.19 us
  waiting for transfers between devices: 42.9 us -> 40.7 us
    all_gather x2 -> x0, waiting for transfers between devices: 42.9 us -> none  [carried_in(): everything = jax.tree.map(lambda part: lax.all_gather(part, axis), value)]
    ppermute x0 -> x8, waiting for transfers between devices: none -> 40.7 us  [shift(): return lax.ppermute(value, axis, pairs)]
    ppermute x0 -> x8, starting transfers between devices: none -> 24.5 us  [shift(): return lax.ppermute(value, axis, pairs)]
    unnamed x1 -> x0, blocking collectives: 13.7 us -> none
    select_n x8 -> x0, other arithmetic: 11.8 us -> none  [lap(): return jax.tree.map(lambda a, b: jnp.where(reached, a, b), new, before)]
    another operation x2 -> x0, loops' own time: 10.6 us -> none  [carried_in(): return lax.fori_loop(0, peers, lap, start)]
    dynamic_slice x8 -> x0, local copies, waits for them, and re-layouts: 4.68 us -> none  [lap(): new = combine(before, jax.tree.map(lambda part: part[at], everything))]
    dot_general x1, matrix products: 6.56 us -> 2.22 us  [on_device(): jnp.einsum('bc,hcde->hbde', later_mask, query_grad_block, precision=highe...]
  transfers between devices with their start and end apart: 2 -> 8, of which waited for: 2 -> 3; matrix products, arithmetic and copies ran while one was open for 17% -> 22% of each run, Pallas kernels for 0% -> 0%
where the time goes in v1:
time: 160 us; the launch traced here: 159 us
  matrix products  58.1 us (36%)
  waiting for transfers between devices  40.7 us (25%)
  starting transfers between devices  24.5 us (15%)
  other arithmetic  11.4 us (7%)
  blocking collectives  10.3 us (6%)
  local copies, waits for them, and re-layouts  9.19 us (6%)
  between operations  4.79 us (3%)
    ppermute x8, waiting for transfers between devices, shift(): return lax.ppermute(value, axis, pairs)  40.7 us
    ppermute x8, starting transfers between devices, shift(): return lax.ppermute(value, axis, pairs)  24.5 us
    psum x1, blocking collectives, on_device(): total_sums = lax.psum(local_sums, ('sub', 'head'))  10.3 us
    dot_general x1, matrix products, on_device(): jnp.einsum('hnij,hnid->hnjd', block_probs, output_grad_blocks, preferred_...  7.37 us
    dot_general x1, matrix products, on_device(): jnp.einsum('bc,hcde->hbde', earlier_mask, key_value_block, precision=high...  7.22 us
    dot_general x1, matrix products, on_device(): jnp.einsum('c,hcde->hde', first_match, query_grad_block, precision=highes...  5.18 us
    dot_general x1, matrix products, on_device(): jnp.einsum('c,hcde->hde', last_match, key_value_block, precision=highest_...  4.89 us
    dot_general x1, local copies, waits for them, and re-layouts, on_device(): jnp.einsum('hnid,hnie->hnde', query_blocks, output_grad_blocks, preferred...  4.7 us
  transfers between devices with their start and end apart: 8, of which 3 were waited for; matrix products, arithmetic and copies ran while one was open for 22% of the time, Pallas kernels for 0%

profile of v1, /device:TPU:0, one launch (start us, length us, event | category | flops | bytes accessed | tf_op | source)
XLA Modules:
  0.0 159.0 jit_solution(8993034932632156992)
XLA Ops:
  0.6 0.0 copy-start
  0.6 0.8 convert_element_type.63
  1.5 0.6 fusion.34
  2.0 1.3 collective-permute-start.6
  3.3 1.3 collective-permute-start.4
  4.6 7.6 %collective-permute-start.2 = (f32[]{:T(128)}, f32[]{:T(128)}, u32[]{:S(2)}, u32[]{:S(2)}) collective-permute-start(f32[]{:T(128)} %bitcast.7), channel_id=1, source_target_pairs={{0,8},{4,12},{1,9},{5,13},{2,10},{6,14},{3,11},{7,15},{16,24},{20,... | collective-permute-start | bytes 20 | tf_op jit(solution)/shard_map/ppermute | solution.py:17
  12.2 5.0 %collective-permute-start = (f32[]{:T(128)}, f32[]{:T(128)}, u32[]{:S(2)}, u32[]{:S(2)}) collective-permute-start(f32[]{:T(128)} %bitcast.7), channel_id=1, source_target_pairs={{0,4},{4,8},{8,12},{1,5},{5,9},{9,13},{2,6},{6,10},{10,14},{3,7},{... | collective-permute-start | bytes 20 | tf_op jit(solution)/shard_map/ppermute | solution.py:17
  17.2 3.4 %fusion.36 = f32[8,5,128,128]{3,2,1,0:T(8,128)S(1)} fusion(bf16[8,5,256,128]{3,2,1,0:T(8,128)(2,1)} %bitcast.105, bf16[8,5,256,128]{3,2,1,0:T(8,128)(2,1)} %bitcast.109), kind=kOutput, calls=%fused_computation.62 | convolution fusion | flops 335544320 | bytes 7864320 | tf_op jit(solution)/shard_map/hnid,hnie->hnde/dot_general | solution.py:61
  20.6 0.0 copy-start.2
  20.6 1.5 copy-done.2
  22.1 4.9 %fusion.6 = f32[1,8,128,128]{3,0,2,1:T(1,128)} fusion(f32[8,5,128,128]{3,2,1,0:T(8,128)S(1)} %fusion.36, f32[]{:T(128)} %bitcast.7, s32[5]{0:T(128)S(1)} %copy-done.16), kind=kOutput, calls=%fused_computation.16 | convolution fusion | flops 7864330 | bytes 3145752 | tf_op jit(solution)/shard_map/c,hcde->hde/dot_general | solution.py:65
  27.0 1.4 collective-permute-start.1
  28.5 0.0 copy-start.9
  28.5 3.4 %select_convert_fusion.1 = bf16[8,5,256,256]{3,2,1,0:T(8,128)(2,1)S(1)} fusion(pred[256,256]{1,0:T(8,128)(4,1)S(1)} %iota_compare_fusion, bf16[8,5,256,128]{3,2,1,0:T(8,128)(2,1)S(1)} %bitcast.95, bf16[8,5,256,128]{3,2,1,0:T(8,128)(2,1)} %bitcast.106), kind=kOutput, calls=%fused_computation.1 | convolution fusion | flops 676331520 | bytes 10551296 | tf_op jit(solution)/shard_map/hnid,hnjd->hnij/dot_general | solution.py:67
  31.9 4.0 %fusion.35 = f32[8,5,256,128]{3,2,1,0:T(8,128)} fusion(bf16[8,5,256,256]{3,2,1,0:T(8,128)(2,1)S(1)} %select_convert_fusion.1, bf16[8,5,256,128]{3,2,1,0:T(8,128)(2,1)S(1)} %bitcast.110), kind=kOutput, calls=%fused_computation.61 | convolution fusion | flops 671088640 | bytes 13107200 | tf_op jit(solution)/shard_map/hnij,hnjd->hnid/dot_general | solution.py:71
  37.2 2.1 %collective-permute-done.1 = f32[8,128,128]{2,1,0:T(8,128)S(1)} collective-permute-done((f32[8,128,128]{2,1,0:T(8,128)}, f32[8,128,128]{2,1,0:T(8,128)S(1)}, u32[]{:S(2)}, u32[]{:S(2)}) %collective-permute-start.1) | collective-permute-done | bytes 524320 | tf_op jit(solution)/shard_map/ppermute | solution.py:17
  39.3 1.9 %multiply_add_fusion.3 = f32[8,128,128]{2,1,0:T(8,128)} fusion(f32[8,128,128]{2,1,0:T(8,128)} %bitcast.11, f32[8,128,128]{2,1,0:T(8,128)S(1)} %collective-permute-done.1, f32[]{:T(128)S(6)} %convert_element_type.66, pred[]{:T(512)S(6)} %ge.12), kind=kLoop, calls=%fused_computation.28 | loop fusion | flops 393216 | bytes 1572869 | tf_op jit(solution)/shard_map/add | solution.py:21
  41.2 4.8 %collective-permute-start.3 = (f32[8,128,128]{2,1,0:T(8,128)}, f32[8,128,128]{2,1,0:T(8,128)}, u32[]{:S(2)}, u32[]{:S(2)}) collective-permute-start(f32[8,128,128]{2,1,0:T(8,128)} %multiply_add_fusion.3), channel_id=1, source_target_pairs={{0,8},{4,12},{1,9},{5,13},{2,10},{6,14},{3,11},{7,15},{16,24},{20,... | collective-permute-start | bytes 1572872 | tf_op jit(solution)/shard_map/ppermute | solution.py:17
  46.0 7.2 %fusion.8 = f32[8,128,128,5]{2,3,1,0:T(8,128)} fusion(f32[8,5,128,128]{3,2,1,0:T(8,128)} %copy-done.2, f32[5]{0:T(128)S(1)} %convert_element_type.63), kind=kOutput, calls=%fused_computation.18 | convolution fusion | flops 39321676 | bytes 5242900 | tf_op jit(solution)/shard_map/bc,hcde->hbde/dot_general | solution.py:74
  55.7 0.1 multiply_add_fusion.2
  55.8 3.0 %fusion.11 = bf16[8,5,128,128]{3,2,1,0:T(8,128)(2,1)S(1)} fusion(f32[8,128,128,5]{2,3,1,0:T(8,128)} %fusion.8, f32[8,128,128]{2,1,0:T(8,128)S(1)} %multiply_add_fusion.2, f32[5]{0:T(128)S(1)} %get-tuple-element.6), kind=kLoop, calls=%fused_computation.23 | loop fusion | flops 1966080 | bytes 4456468 | tf_op jit(solution)/shard_map/convert_element_type | solution.py:79
  58.8 0.8 copy-done.7
  59.5 1.2 multiply_reduce_fusion
  60.8 1.1 copy-done.14
  61.9 0.8 fusion.2
  62.6 0.4 copy-done.1
  63.1 10.3 %psum.7 = f32[2,1280]{1,0:T(2,128)S(1)} all-reduce(f32[2,1280]{1,0:T(2,128)S(1)} %pad_maximum_fusion), channel_id=1, replica_groups=mesh['groups'=2,'ctx'=4,'sub'=2,'head'=2] {'sub','head'}, use_global_device_ids=true, to_apply=%region_2.3 | all-reduce | flops 2560 | bytes 20480 | tf_op jit(solution)/shard_map/psum | solution.py:89
  73.5 4.0 %fusion.5 = bf16[8,1280,128]{2,1,0:T(8,128)(2,1)S(1)} fusion(f32[8,5,256,128]{3,2,1,0:T(8,128)} %copy-done.1, bf16[8,1280,128]{2,1,0:T(8,128)(2,1)} %param.9, f32[1280]{0:T(1024)S(1)} %get-tuple-element.4, f32[1280]{0:T(1024)S(1)} %multiply_divide_fusion, f32[8,128]{1,0:T(8,128)S(1)} %copy-done.15), kind=kLoop, calls=%fused_computation.11 | loop fusion | flops 7864320 | bytes 10500096 | tf_op jit(solution)/shard_map/convert_element_type | solution.py:95
  77.5 0.0 copy-start.3
  77.5 7.4 %fusion.39 = f32[8,5,256,128]{3,2,1,0:T(8,128)} fusion(bf16[8,5,256,256]{3,2,1,0:T(8,128)(2,1)} %copy-done.6, bf16[8,5,256,128]{3,2,1,0:T(8,128)(2,1)S(1)} %bitcast.99), kind=kOutput, calls=%fused_computation.65 | convolution fusion | flops 671088640 | bytes 13107200 | tf_op jit(solution)/shard_map/hnij,hnid->hnjd/dot_general | solution.py:115
  84.9 2.4 %convolution_bitcast_fusion = f32[8,5,128,128]{2,3,1,0:T(8,128)} fusion(bf16[8,5,256,128]{3,2,1,0:T(8,128)(2,1)S(1)} %bitcast.100, bf16[8,5,256,128]{3,2,1,0:T(8,128)(2,1)S(1)} %bitcast.98), kind=kOutput, calls=%fused_computation.24 | convolution fusion | flops 335544320 | bytes 7864320 | tf_op jit(solution)/shard_map/hnid,hnie->hnde/dot_general | solution.py:97
  87.3 3.9 %select_convert_fusion = bf16[8,5,256,256]{3,2,1,0:T(8,128)(2,1)} fusion(pred[256,256]{1,0:T(8,128)(4,1)S(1)} %iota_compare_fusion, bf16[8,5,256,128]{3,2,1,0:T(8,128)(2,1)S(1)} %bitcast.101, bf16[8,5,256,128]{3,2,1,0:T(8,128)(2,1)S(1)} %bitcast.111), kind=kOutput, calls=%fused_computation | convolution fusion | flops 676331520 | bytes 10551296 | tf_op jit(solution)/shard_map/hnid,hnjd->hnij/dot_general | solution.py:105
  91.2 4.7 %copy.29 = f32[8,5,128,128]{3,1,2,0:T(8,128)} copy(f32[8,5,128,128]{2,3,1,0:T(8,128)} %convolution_bitcast_fusion) | data formatting | bytes 5242880 | tf_op jit(solution)/shard_map/hnid,hnie->hnde/dot_general | solution.py:97
  95.9 5.2 %fusion.25 = f32[1,8,128,128]{3,0,2,1:T(1,128)S(1)} fusion(f32[8,5,128,128]{3,1,2,0:T(8,128)} %copy.29, f32[]{:T(128)} %bitcast.21, s32[5]{0:T(128)S(1)} %copy-done.16), kind=kOutput, calls=%fused_computation.49 | convolution fusion | flops 7864330 | bytes 3145752 | tf_op jit(solution)/shard_map/c,hcde->hde/dot_general | solution.py:101
  101.1 1.4 collective-permute-start.5
  102.5 4.2 %fusion.38 = f32[8,5,256,128]{3,2,1,0:T(8,128)S(1)} fusion(bf16[8,5,256,256]{3,2,1,0:T(8,128)(2,1)} %select_convert_fusion, bf16[8,5,256,128]{3,2,1,0:T(8,128)(2,1)S(1)} %bitcast.97), kind=kOutput, calls=%fused_computation.64 | convolution fusion | flops 671088640 | bytes 13107200 | tf_op jit(solution)/shard_map/hnij,hnid->hnjd/dot_general | solution.py:112
  106.8 1.5 fusion.37
  108.3 17.3 %collective-permute-done.5 = f32[8,128,128]{2,1,0:T(8,128)S(1)} collective-permute-done((f32[8,128,128]{2,1,0:T(8,128)S(1)}, f32[8,128,128]{2,1,0:T(8,128)S(1)}, u32[]{:S(2)}, u32[]{:S(2)}) %collective-permute-start.5) | collective-permute-done | bytes 524320 | tf_op jit(solution)/shard_map/ppermute | solution.py:17
  125.6 0.1 multiply_add_fusion.1
  125.6 0.0 copy-start.4
  125.6 1.8 %collective-permute-start.7 = (f32[8,128,128]{2,1,0:T(8,128)S(1)}, f32[8,128,128]{2,1,0:T(8,128)S(1)}, u32[]{:S(2)}, u32[]{:S(2)}) collective-permute-start(f32[8,128,128]{2,1,0:T(8,128)S(1)} %multiply_add_fusion.1), channel_id=1, source_target_pairs={{8,0},{12,4},{9,1},{13,5},{10,2},{14,6},{11,3},{15,7},{24,16},{28,... | collective-permute-start | bytes 1572872 | tf_op jit(solution)/shard_map/ppermute | solution.py:17
  127.5 2.2 %fusion.19 = f32[8,128,128,5]{2,3,1,0:T(8,128)S(1)} fusion(f32[8,5,128,128]{3,1,2,0:T(8,128)S(1)} %copy-done.5, f32[5]{0:T(128)S(1)} %convert_element_type.63), kind=kOutput, calls=%fused_computation.44 | convolution fusion | flops 39321676 | bytes 5242900 | tf_op jit(solution)/shard_map/bc,hcde->hbde/dot_general | solution.py:118
  129.7 2.4 %add_convert_fusion = bf16[8,5,256,128]{3,2,1,0:T(8,128)(2,1)} fusion(f32[8,5,256,128]{3,2,1,0:T(8,128)S(1)} %fusion.37, bf16[8,5,256,128]{3,2,1,0:T(8,128)(2,1)S(1)} %bitcast.102, bf16[8,5,128,128]{3,2,1,0:T(8,128)(2,1)S(1)} %copy-done.13), kind=kOutput, calls=%fused_computation.13 | convolution fusion | flops 338165760 | bytes 11796480 | tf_op jit(solution)/shard_map/hnie,hnde->hnid/dot_general | solution.py:124
  132.2 21.3 %collective-permute-done.7 = f32[8,128,128]{2,1,0:T(8,128)S(1)} collective-permute-done((f32[8,128,128]{2,1,0:T(8,128)S(1)}, f32[8,128,128]{2,1,0:T(8,128)S(1)}, u32[]{:S(2)}, u32[]{:S(2)}) %collective-permute-start.7) | collective-permute-done | bytes 524320 | tf_op jit(solution)/shard_map/ppermute | solution.py:17
  153.4 0.1 multiply_add_fusion
  153.5 0.6 fusion.10
  154.2 2.4 %fusion = bf16[8,5,256,128]{3,2,1,0:T(8,128)(2,1)} fusion(f32[8,5,256,128]{3,2,1,0:T(8,128)S(1)} %bitcast.114, bf16[8,5,256,128]{3,2,1,0:T(8,128)(2,1)S(1)} %bitcast.108, bf16[8,5,128,128]{3,2,1,0:T(8,128)(2,1)S(1)} %fusion.10), kind=kOutput, calls=%fused_computation.3 | convolution fusion | flops 338165760 | bytes 11796480 | tf_op jit(solution)/shard_map/hnid,hnde->hnie/dot_general | solution.py:130
  156.6 2.4 %fusion.1 = bf16[8,5,256,128]{3,2,1,0:T(8,128)(2,1)} fusion(f32[8,5,256,128]{3,2,1,0:T(8,128)S(1)} %fusion.38, bf16[8,5,128,128]{3,2,1,0:T(8,128)(2,1)S(1)} %fusion.10, bf16[8,5,256,128]{3,2,1,0:T(8,128)(2,1)S(1)} %bitcast.112), kind=kOutput, calls=%fused_computation.5 | convolution fusion | flops 338165760 | bytes 11796480 | tf_op jit(solution)/shard_map/hnie,hnde->hnid/dot_general | solution.py:127
  (47 shorter events, 0.2 us)
Async XLA Ops:
  0.6 27.8 %copy-start = (bf16[8,1280,128]{2,1,0:T(8,128)(2,1)S(1)}, bf16[8,1280,128]{2,1,0:T(8,128)(2,1)}, u32[]{:S(2)}) copy-start(bf16[8,1280,128]{2,1,0:T(8,128)(2,1)} %param.6) | copy-start | bytes 7864324
  2.0 52.4 %collective-permute-start.6 = (f32[]{:T(128)}, f32[]{:T(128)}, u32[]{:S(2)}, u32[]{:S(2)}) collective-permute-start(f32[]{:T(128)} %bitcast.21), channel_id=1, source_target_pairs={{8,0},{12,4},{9,1},{13,5},{10,2},{14,6},{11,3},{15,7},{24,16},{28,... | collective-permute-start | bytes 20 | tf_op jit(solution)/shard_map/ppermute | solution.py:17
  3.3 49.9 %collective-permute-start.4 = (f32[]{:T(128)}, f32[]{:T(128)}, u32[]{:S(2)}, u32[]{:S(2)}) collective-permute-start(f32[]{:T(128)} %bitcast.21), channel_id=1, source_target_pairs={{4,0},{8,4},{12,8},{5,1},{9,5},{13,9},{6,2},{10,6},{14,10},{7,3},{... | collective-permute-start | bytes 20 | tf_op jit(solution)/shard_map/ppermute | solution.py:17
  4.6 50.5 %collective-permute-start.2 = (f32[]{:T(128)}, f32[]{:T(128)}, u32[]{:S(2)}, u32[]{:S(2)}) collective-permute-start(f32[]{:T(128)} %bitcast.7), channel_id=1, source_target_pairs={{0,8},{4,12},{1,9},{5,13},{2,10},{6,14},{3,11},{7,15},{16,24},{20,... | collective-permute-start | bytes 20 | tf_op jit(solution)/shard_map/ppermute | solution.py:17
  12.2 23.7 %collective-permute-start = (f32[]{:T(128)}, f32[]{:T(128)}, u32[]{:S(2)}, u32[]{:S(2)}) collective-permute-start(f32[]{:T(128)} %bitcast.7), channel_id=1, source_target_pairs={{0,4},{4,8},{8,12},{1,5},{5,9},{9,13},{2,6},{6,10},{10,14},{3,7},{... | collective-permute-start | bytes 20 | tf_op jit(solution)/shard_map/ppermute | solution.py:17
  17.2 4.9 %copy-start.16 = (s32[5]{0:T(128)S(1)}, s32[5]{0:T(128)}, u32[]{:S(2)}) copy-start(s32[5]{0:T(128)} %param.11) | copy-start | bytes 64
  20.6 1.5 copy-start.2
  27.0 12.3 %collective-permute-start.1 = (f32[8,128,128]{2,1,0:T(8,128)}, f32[8,128,128]{2,1,0:T(8,128)S(1)}, u32[]{:S(2)}, u32[]{:S(2)}) collective-permute-start(f32[8,128,128]{2,1,0:T(8,128)} %bitcast.11), channel_id=1, source_target_pairs={{0,4},{4,8},{8,12},{1,5},{5,9},{9,13},{2,6},{6,10},{10,14},{3,7},{... | collective-permute-start | bytes 1572872 | tf_op jit(solution)/shard_map/ppermute | solution.py:17
  28.5 3.4 %copy-start.9 = (bf16[8,1280,128]{2,1,0:T(8,128)(2,1)S(1)}, bf16[8,1280,128]{2,1,0:T(8,128)(2,1)}, u32[]{:S(2)}) copy-start(bf16[8,1280,128]{2,1,0:T(8,128)(2,1)} %param.8) | copy-start | bytes 7864324
  31.9 4.0 %copy-start.6 = (bf16[8,5,256,256]{3,2,1,0:T(8,128)(2,1)}, bf16[8,5,256,256]{3,2,1,0:T(8,128)(2,1)S(1)}, u32[]{:S(2)}) copy-start(bf16[8,5,256,256]{3,2,1,0:T(8,128)(2,1)S(1)} %select_convert_fusion.1) | copy-start | bytes 15728644
  41.2 14.5 %collective-permute-start.3 = (f32[8,128,128]{2,1,0:T(8,128)}, f32[8,128,128]{2,1,0:T(8,128)}, u32[]{:S(2)}, u32[]{:S(2)}) collective-permute-start(f32[8,128,128]{2,1,0:T(8,128)} %multiply_add_fusion.3), channel_id=1, source_target_pairs={{0,8},{4,12},{1,9},{5,13},{2,10},{6,14},{3,11},{7,15},{16,24},{20,... | collective-permute-start | bytes 1572872 | tf_op jit(solution)/shard_map/ppermute | solution.py:17
  55.8 3.7 %copy-start.7 = (f32[8,5,256,128]{3,2,1,0:T(8,128)S(1)}, f32[8,5,256,128]{3,2,1,0:T(8,128)}, u32[]{:S(2)}) copy-start(f32[8,5,256,128]{3,2,1,0:T(8,128)} %fusion.35) | copy-start | bytes 15728644
  59.5 1.2 copy-start.12
  59.5 2.3 %copy-start.14 = (bf16[8,1280,128]{2,1,0:T(8,128)(2,1)S(1)}, bf16[8,1280,128]{2,1,0:T(8,128)(2,1)}, u32[]{:S(2)}) copy-start(bf16[8,1280,128]{2,1,0:T(8,128)(2,1)} %param.9) | copy-start | bytes 7864324
  59.5 2.3 %copy-start.15 = (f32[8,128]{1,0:T(8,128)S(1)}, f32[8,128]{1,0:T(8,128)}, u32[]{:S(2)}) copy-start(f32[8,128]{1,0:T(8,128)} %param.10) | copy-start | bytes 12292
  60.7 2.4 %copy-start.1 = (f32[8,5,256,128]{3,2,1,0:T(8,128)}, f32[8,5,256,128]{3,2,1,0:T(8,128)S(1)}, u32[]{:S(2)}) copy-start(f32[8,5,256,128]{3,2,1,0:T(8,128)S(1)} %get-tuple-element.10) | copy-start | bytes 15728644
  77.5 9.8 %copy-start.3 = (bf16[8,1280,128]{2,1,0:T(8,128)(2,1)}, bf16[8,1280,128]{2,1,0:T(8,128)(2,1)S(1)}, u32[]{:S(2)}) copy-start(bf16[8,1280,128]{2,1,0:T(8,128)(2,1)S(1)} %fusion.5) | copy-start | bytes 7864324
  84.9 2.4 %copy-start.10 = (bf16[8,1280,128]{2,1,0:T(8,128)(2,1)S(1)}, bf16[8,1280,128]{2,1,0:T(8,128)(2,1)}, u32[]{:S(2)}) copy-start(bf16[8,1280,128]{2,1,0:T(8,128)(2,1)} %param.8) | copy-start | bytes 7864324
  95.9 10.9 %slice-start = ((s8[5242880]{0:T(1024)(128)(4,1)}), s8[4194304]{0:T(1024)(128)(4,1)S(1)}, s32[]{:S(2)}) async-start(s8[5242880]{0:T(1024)(128)(4,1)} %bitcast.103), calls=%async_computation | async-start | bytes 8388608
  101.1 5.7 %slice-start.1 = ((s8[5242880]{0:T(1024)(128)(4,1)}), s8[1048576]{0:T(1024)(128)(4,1)S(1)}, s32[]{:S(2)}) async-start(s8[5242880]{0:T(1024)(128)(4,1)} %bitcast.103), calls=%async_computation.1 | async-start | bytes 2097152
  101.1 24.5 %collective-permute-start.5 = (f32[8,128,128]{2,1,0:T(8,128)S(1)}, f32[8,128,128]{2,1,0:T(8,128)S(1)}, u32[]{:S(2)}, u32[]{:S(2)}) collective-permute-start(f32[8,128,128]{2,1,0:T(8,128)S(1)} %bitcast.118), channel_id=1, source_target_pairs={{4,0},{8,4},{12,8},{5,1},{9,5},{13,9},{6,2},{10,6},{14,10},{7,3},{... | collective-permute-start | bytes 1572872 | tf_op jit(solution)/shard_map/ppermute | solution.py:17
  102.5 4.2 %copy-start.8 = (bf16[8,1280,128]{2,1,0:T(8,128)(2,1)S(1)}, bf16[8,1280,128]{2,1,0:T(8,128)(2,1)}, u32[]{:S(2)}) copy-start(bf16[8,1280,128]{2,1,0:T(8,128)(2,1)} %param.7) | copy-start | bytes 7864324
  106.8 20.7 %copy-start.5 = (f32[8,5,128,128]{3,1,2,0:T(8,128)S(1)}, f32[8,5,128,128]{3,1,2,0:T(8,128)}, u32[]{:S(2)}) copy-start(f32[8,5,128,128]{3,1,2,0:T(8,128)} %copy.29) | copy-start | bytes 7864324
  125.6 4.1 %copy-start.4 = (bf16[8,1280,128]{2,1,0:T(8,128)(2,1)S(1)}, bf16[8,1280,128]{2,1,0:T(8,128)(2,1)}, u32[]{:S(2)}) copy-start(bf16[8,1280,128]{2,1,0:T(8,128)(2,1)} %copy-done.3) | copy-start | bytes 7864324
  125.6 4.1 %copy-start.13 = (bf16[8,5,128,128]{3,2,1,0:T(8,128)(2,1)S(1)}, bf16[8,5,128,128]{3,2,1,0:T(8,128)(2,1)}, u32[]{:S(2)}) copy-start(bf16[8,5,128,128]{3,2,1,0:T(8,128)(2,1)} %copy-done.12) | copy-start | bytes 3932164
  125.6 27.8 %collective-permute-start.7 = (f32[8,128,128]{2,1,0:T(8,128)S(1)}, f32[8,128,128]{2,1,0:T(8,128)S(1)}, u32[]{:S(2)}, u32[]{:S(2)}) collective-permute-start(f32[8,128,128]{2,1,0:T(8,128)S(1)} %multiply_add_fusion.1), channel_id=1, source_target_pairs={{8,0},{12,4},{9,1},{13,5},{10,2},{14,6},{11,3},{15,7},{24,16},{28,... | collective-permute-start | bytes 1572872 | tf_op jit(solution)/shard_map/ppermute | solution.py:17
  127.5 26.7 %slice-start.2 = ((s8[5242880]{0:T(1024)(128)(4,1)}), s8[4194304]{0:T(1024)(128)(4,1)S(1)}, s32[]{:S(2)}) async-start(s8[5242880]{0:T(1024)(128)(4,1)} %bitcast.113), calls=%async_computation.2 | async-start | bytes 8388608
  129.7 24.5 %slice-start.3 = ((s8[5242880]{0:T(1024)(128)(4,1)}), s8[1048576]{0:T(1024)(128)(4,1)S(1)}, s32[]{:S(2)}) async-start(s8[5242880]{0:T(1024)(128)(4,1)} %bitcast.113), calls=%async_computation.3 | async-start | bytes 2097152
  154.2 2.4 %copy-start.11 = (bf16[8,1280,128]{2,1,0:T(8,128)(2,1)S(1)}, bf16[8,1280,128]{2,1,0:T(8,128)(2,1)}, u32[]{:S(2)}) copy-start(bf16[8,1280,128]{2,1,0:T(8,128)(2,1)} %param.8) | copy-start | bytes 7864324

commit v2 on v1

v2 whole, which is shorter than its diff:
```python
import functools

import jax
import jax.numpy as jnp
from jax import lax
from jax.experimental import pallas as pl
from jax.sharding import PartitionSpec as P

_ROWS_MINOR = (((1,), (1,)), ((), ()))
_ROWS_MAJOR = (((0,), (0,)), ((), ()))


def segmented_scan(doc, state, axis, reverse):
    peers = lax.axis_size(axis)
    index = lax.axis_index(axis)
    none_doc = jnp.float32(-1.0)
    pad = jnp.broadcast_to(doc, (state.shape[0], 8, state.shape[2])).astype(jnp.float32)

    def shift(value_doc, value_state, step):
        if reverse:
            pairs = [(j, j - step) for j in range(step, peers)]
        else:
            pairs = [(j, j + step) for j in range(peers - step)]
        row = jnp.broadcast_to(value_doc, pad.shape)
        got = lax.ppermute(jnp.concatenate([value_state, row], axis=1), axis, pairs)
        valid = (index <= peers - 1 - step) if reverse else (index >= step)
        got_doc = jnp.where(valid, got[0, state.shape[1], 0], none_doc)
        got_state = jnp.where(valid, got[:, : state.shape[1]], 0.0)
        return got_doc, got_state

    def combine(near_doc, near_state, far_doc, far_state):
        joined = (near_doc == far_doc).astype(jnp.float32)
        return near_doc, near_state + joined * far_state

    if peers == 1:
        return none_doc, jnp.zeros_like(state)
    ex_doc, ex_state = shift(doc, state, 1)
    in_doc, in_state = combine(doc, state, ex_doc, ex_state)
    covered = 1
    while covered < peers - 1:
        step = covered + 1
        got_doc, got_state = shift(in_doc, in_state, step)
        ex_doc, ex_state = combine(ex_doc, ex_state, got_doc, got_state)
        covered = covered + step
        if covered < peers - 1:
            in_doc, in_state = combine(in_doc, in_state, got_doc, got_state)
    return ex_doc, ex_state


def _causal(block_len):
    row_ids = lax.broadcasted_iota(jnp.int32, (block_len, block_len), 0)
    col_ids = lax.broadcasted_iota(jnp.int32, (block_len, block_len), 1)
    return row_ids >= col_ids


def forward_kernel(block_len, q_ref, k_ref, v_ref, o_ref):
    causal = _causal(block_len)
    for n in range(q_ref.shape[1] // block_len):
        rows = pl.ds(n * block_len, block_len)
        q, k, v = q_ref[0, rows, :], k_ref[0, rows, :], v_ref[0, rows, :]
        scores = lax.dot_general(q, k, _ROWS_MINOR, preferred_element_type=jnp.float32)
        probs = jnp.where(causal, scores, 0.0).astype(jnp.bfloat16)
        o_ref[0, rows, :] = jnp.dot(probs, v, preferred_element_type=jnp.float32)


def backward_kernel(block_len, q_ref, k_ref, v_ref, d_ref, s_ref, dq_ref, dk_ref, dv_ref):
    causal = _causal(block_len)
    for n in range(q_ref.shape[1] // block_len):
        rows = pl.ds(n * block_len, block_len)
        q, k, v = q_ref[0, rows, :], k_ref[0, rows, :], v_ref[0, rows, :]
        d = d_ref[0, rows, :]
        scores = lax.dot_general(q, k, _ROWS_MINOR, preferred_element_type=jnp.float32)
        probs = jnp.where(causal, scores, 0.0).astype(jnp.bfloat16)
        grad_scores = lax.dot_general(d, v, _ROWS_MINOR, preferred_element_type=jnp.float32)
        grad_probs = jnp.where(causal, grad_scores, 0.0).astype(jnp.bfloat16)
        dq = jnp.dot(grad_probs, k, preferred_element_type=jnp.float32)
        dq = dq + lax.dot_general(d, s_ref[0, n], _ROWS_MINOR, preferred_element_type=jnp.float32)
        dq_ref[0, rows, :] = dq.astype(dq_ref.dtype)
        dk_ref[0, rows, :] = lax.dot_general(
            grad_probs, q, _ROWS_MAJOR, preferred_element_type=jnp.float32
        )
        dv_ref[0, rows, :] = lax.dot_general(
            probs, d, _ROWS_MAJOR, preferred_element_type=jnp.float32
        )


def per_head_call(kernel, inputs, out_dtypes, flops):
    head_count, tok_count, head_width = inputs[0].shape

    def spec(shape):
        return pl.BlockSpec((1,) + shape[1:], lambda h: (h,) + (0,) * (len(shape) - 1))

    in_bytes = sum(x.size * x.dtype.itemsize for x in inputs)
    out_bytes = sum(head_count * tok_count * head_width * jnp.dtype(t).itemsize for t in out_dtypes)
    return pl.pallas_call(
        kernel,
        grid=(head_count,),
        in_specs=[spec(x.shape) for x in inputs],
        out_specs=[spec(inputs[0].shape) for _ in out_dtypes],
        out_shape=[jax.ShapeDtypeStruct(inputs[0].shape, t) for t in out_dtypes],
        cost_estimate=pl.CostEstimate(
            flops=flops, transcendentals=0, bytes_accessed=in_bytes + out_bytes
        ),
    )(*inputs)


def on_device(queries, keys, values, out_grad, norm_gain, doc_ids):
    head_count, tok_count, head_width = queries.shape
    block_count = doc_ids.shape[0]
    block_len = tok_count // block_count
    block_shape = (head_count, block_count, block_len, head_width)
    highest_precision = lax.Precision.HIGHEST
    query_blocks = queries.reshape(block_shape)
    key_blocks = keys.reshape(block_shape)
    value_blocks = values.reshape(block_shape)
    doc_values = doc_ids.astype(jnp.float32)
    block_pos = jnp.arange(block_count, dtype=jnp.int32)
    same_doc = doc_values[:, None] == doc_values[None, :]
    earlier_mask = (same_doc & (block_pos[None, :] < block_pos[:, None])).astype(jnp.float32)
    later_mask = (same_doc & (block_pos[None, :] > block_pos[:, None])).astype(jnp.float32)
    pair_flops = 2 * head_count * block_count * block_len * block_len * head_width
    key_value_block = jnp.einsum(
        "hnid,hnie->hnde", key_blocks, value_blocks, preferred_element_type=jnp.float32
    )
    last_match = (doc_values == doc_values[-1]).astype(jnp.float32)
    device_kv = jnp.einsum("c,hcde->hde", last_match, key_value_block, precision=highest_precision)
    prior_doc, prior_state = segmented_scan(doc_values[-1], device_kv, "ctx", False)
    (intra_part,) = per_head_call(
        functools.partial(forward_kernel, block_len),
        [queries, keys, values],
        [jnp.float32],
        2 * pair_flops,
    )
    local_prefix = jnp.einsum(
        "bc,hcde->hbde", earlier_mask, key_value_block, precision=highest_precision
    )
    prior_match = (doc_values == prior_doc).astype(jnp.float32)
    entering = prior_match[None, :, None, None] * prior_state[:, None, :, :]
    preceding_states = (local_prefix + entering).astype(jnp.bfloat16)
    cross_block_part = jnp.einsum(
        "hnid,hnde->hnie", query_blocks, preceding_states, preferred_element_type=jnp.float32
    )
    raw_attn = intra_part + cross_block_part.reshape(head_count, tok_count, head_width)
    feature_count = head_count * head_width * lax.axis_size(("sub", "head"))
    scaled = norm_gain[:, None, :] * out_grad.astype(jnp.float32)
    local_sums = jnp.stack(
        [jnp.sum(raw_attn * raw_attn, axis=(0, 2)), jnp.sum(scaled * raw_attn, axis=(0, 2))]
    )
    total_sums = lax.psum(local_sums, ("sub", "head"))
    root_mean = jnp.sqrt(total_sums[0] / feature_count + 1e-06)
    inner_mean = total_sums[1] / feature_count
    factor = inner_mean / (root_mean * root_mean)
    d_attn = (
        (scaled - raw_attn * factor[None, :, None]) / root_mean[None, :, None]
    ).astype(jnp.bfloat16)
    output_grad_blocks = d_attn.reshape(block_shape)
    query_grad_block = jnp.einsum(
        "hnid,hnie->hnde", query_blocks, output_grad_blocks, preferred_element_type=jnp.float32
    )
    first_match = (doc_values == doc_values[0]).astype(jnp.float32)
    device_qd = jnp.einsum(
        "c,hcde->hde", first_match, query_grad_block, precision=highest_precision
    )
    next_doc, next_state = segmented_scan(doc_values[0], device_qd, "ctx", True)
    query_gradient, key_intra, value_intra = per_head_call(
        functools.partial(backward_kernel, block_len),
        [queries, keys, values, d_attn, preceding_states],
        [jnp.bfloat16, jnp.float32, jnp.float32],
        5 * pair_flops,
    )
    local_suffix = jnp.einsum(
        "bc,hcde->hbde", later_mask, query_grad_block, precision=highest_precision
    )
    next_match = (doc_values == next_doc).astype(jnp.float32)
    leaving = next_match[None, :, None, None] * next_state[:, None, :, :]
    following_states = (local_suffix + leaving).astype(jnp.bfloat16)
    key_cross = jnp.einsum(
        "hnie,hnde->hnid", value_blocks, following_states, preferred_element_type=jnp.float32
    )
    value_cross = jnp.einsum(
        "hnid,hnde->hnie", key_blocks, following_states, preferred_element_type=jnp.float32
    )
    out_shape = (head_count, tok_count, head_width)
    return (
        query_gradient,
        (key_intra + key_cross.reshape(out_shape)).astype(jnp.bfloat16),
        (value_intra + value_cross.reshape(out_shape)).astype(jnp.bfloat16),
    )


def solution(mesh):
    return jax.shard_map(
        on_device,
        mesh=mesh,
        in_specs=(
            P(("sub", "head"), ("groups", "ctx"), None),
            P(("sub", "head"), ("groups", "ctx"), None),
            P(("sub", "head"), ("groups", "ctx"), None),
            P(("sub", "head"), ("groups", "ctx"), None),
            P(("sub", "head"), None),
            P(("groups", "ctx")),
        ),
        out_specs=(
            P(("sub", "head"), ("groups", "ctx"), None),
            P(("sub", "head"), ("groups", "ctx"), None),
            P(("sub", "head"), ("groups", "ctx"), None),
        ),
        check_vma=False,
    )
```

time: 160 us -> 192 us (1.20)
  Pallas kernels: 0 us -> 26.9 us
  local copies, waits for them, and re-layouts: 9.19 us -> 31.8 us
  matrix products: 58.1 us -> 36.3 us
  other arithmetic: 11.4 us -> 31.7 us
  starting transfers between devices: 24.5 us -> 14.1 us
  waiting for transfers between devices: 40.7 us -> 35.3 us
    pallas_call x0 -> x2, Pallas kernels: none -> 26.9 us  [per_head_call(): pl.pallas_call(kernel, grid=(head_count,), in_specs=[spec(x.shape) for x...]
    dot_general x7 -> x0, matrix products: 26.8 us -> none  [the longest x1 7.37 us: on_device(): jnp.einsum('hnij,hnid->hnjd', block_probs, output_grad_blocks, preferred_...]
    dot_general x0 -> x3, local copies, waits for them, and re-layouts: none -> 17.7 us  [the longest x1 5.95 us: on_device(): jnp.einsum('hnid,hnde->hnie', query_blocks, preceding_states, preferred_e...]
    convert_element_type x0 -> x2, other arithmetic: none -> 10.6 us  [the longest x1 10.6 us: on_device(): (value_intra + value_cross.reshape(out_shape)).astype(jnp.bfloat16)]
    ppermute x8 -> x4, starting transfers between devices: 24.5 us -> 14.1 us  [shift(): got = lax.ppermute(jnp.concatenate([value_state, row], axis=1), axis, pairs)]
    reduce_sum x1, other arithmetic: 0.78 us -> 6.38 us  [on_device(): jnp.sum(raw_attn * raw_attn, axis=(0, 2))]
    ppermute x8 -> x4, waiting for transfers between devices: 40.7 us -> 35.3 us  [shift(): got = lax.ppermute(jnp.concatenate([value_state, row], axis=1), axis, pairs)]
    dot_general x1, matrix products: 2.22 us -> 6.39 us  [on_device(): jnp.einsum('bc,hcde->hbde', later_mask, query_grad_block, precision=highe...]
  transfers between devices with their start and end apart: 8 -> 4, of which waited for: 3 -> 4; matrix products, arithmetic and copies ran while one was open for 22% -> 6% of each run, Pallas kernels for 0% -> 14%
where the time goes in v2:
time: 192 us; the launch traced here: 191 us
  matrix products  36.3 us (19%)
  waiting for transfers between devices  35.3 us (18%)
  local copies, waits for them, and re-layouts  31.8 us (17%)
  other arithmetic  31.7 us (17%)
  Pallas kernels  26.9 us (14%)
  starting transfers between devices  14.1 us (7%)
  blocking collectives  10.1 us (5%)
  between operations  4.77 us (2%)
    ppermute x4, waiting for transfers between devices, shift(): got = lax.ppermute(jnp.concatenate([value_state, row], axis=1), axis, pairs)  35.3 us
    pallas_call x2, Pallas kernels, per_head_call(): pl.pallas_call(kernel, grid=(head_count,), in_specs=[spec(x.shape) for x...  26.9 us
    ppermute x4, starting transfers between devices, shift(): got = lax.ppermute(jnp.concatenate([value_state, row], axis=1), axis, pairs)  14.1 us
    convert_element_type x1, other arithmetic, on_device(): (value_intra + value_cross.reshape(out_shape)).astype(jnp.bfloat16)  10.6 us
    psum x1, blocking collectives, on_device(): total_sums = lax.psum(local_sums, ('sub', 'head'))  10.1 us
    dot_general x1, matrix products, on_device(): jnp.einsum('bc,hcde->hbde', later_mask, query_grad_block, precision=highe...  6.39 us
    reduce_sum x1, other arithmetic, on_device(): jnp.sum(raw_attn * raw_attn, axis=(0, 2))  6.38 us
    dot_general x1, local copies, waits for them, and re-layouts, on_device(): jnp.einsum('hnid,hnde->hnie', query_blocks, preceding_states, preferred_e...  5.95 us
  transfers between devices with their start and end apart: 4, of which 4 were waited for; matrix products, arithmetic and copies ran while one was open for 6% of the time, Pallas kernels for 14%

profile of v2, /device:TPU:0, one launch (start us, length us, event | category | flops | bytes accessed | tf_op | source)
XLA Modules:
  0.0 191.0 jit_solution(16847093061081609069)
XLA Ops:
  0.6 0.7 convert_element_type.44
  1.3 0.6 fusion.34
  1.9 3.4 %fusion.35 = f32[8,5,128,128]{3,2,1,0:T(8,128)S(1)} fusion(bf16[8,5,256,128]{3,2,1,0:T(8,128)(2,1)} %bitcast.82, bf16[8,5,256,128]{3,2,1,0:T(8,128)(2,1)} %bitcast.84), kind=kOutput, calls=%fused_computation.62 | convolution fusion | flops 335544320 | bytes 7864320 | tf_op jit(solution)/shard_map/hnid,hnie->hnde/dot_general | solution.py:122
  5.3 4.1 %fusion.2 = f32[1,8,128,128]{3,0,2,1:T(1,128)S(1)} fusion(f32[8,5,128,128]{3,2,1,0:T(8,128)S(1)} %fusion.35, f32[]{:T(128)} %bitcast.6, s32[5]{0:T(128)S(1)} %copy-done.6), kind=kOutput, calls=%fused_computation.9 | convolution fusion | flops 7864330 | bytes 3145752 | tf_op jit(solution)/shard_map/c,hcde->hde/dot_general | solution.py:126
  9.4 1.5 concatenate.12
  10.9 5.7 %collective-permute-start = (f32[8,136,128]{2,1,0:T(8,128)}, f32[8,136,128]{2,1,0:T(8,128)}, u32[]{:S(2)}, u32[]{:S(2)}) collective-permute-start(f32[8,136,128]{2,1,0:T(8,128)} %concatenate.12), channel_id=1, source_target_pairs={{0,4},{4,8},{8,12},{1,5},{5,9},{9,13},{2,6},{6,10},{10,14},{3,7},{... | collective-permute-start | bytes 1671176 | tf_op jit(solution)/shard_map/ppermute | solution.py:25
  16.7 10.1 %shard_map.85 = f32[8,1280,128]{2,1,0:T(8,128)} custom-call(bf16[8,1280,128]{2,1,0:T(8,128)(2,1)} %q_ref.3, bf16[8,1280,128]{2,1,0:T(8,128)(2,1)} %k_ref.3, bf16[8,1280,128]{2,1,0:T(8,128)(2,1)} %v_ref.3), custom_call_target="tpu_custom_call" | custom-call | flops 1342177280 | bytes 13107200 | tf_op jit(solution)/shard_map/pallas_call | solution.py:95
  26.8 1.2 collective-permute-done
  28.0 1.2 slice.50
  30.5 1.1 multiply_add_fusion.1
  31.6 0.7 concatenate.13
  32.3 5.6 %collective-permute-start.1 = (f32[8,136,128]{2,1,0:T(8,128)S(1)}, f32[8,136,128]{2,1,0:T(8,128)S(1)}, u32[]{:S(2)}, u32[]{:S(2)}) collective-permute-start(f32[8,136,128]{2,1,0:T(8,128)S(1)} %concatenate.13), channel_id=1, source_target_pairs={{0,8},{4,12},{1,9},{5,13},{2,10},{6,14},{3,11},{7,15},{16,24},{20,... | collective-permute-start | bytes 1671176 | tf_op jit(solution)/shard_map/ppermute | solution.py:25
  38.0 5.5 %fusion.4 = f32[8,128,128,5]{2,3,1,0:T(8,128)} fusion(f32[8,5,128,128]{3,2,1,0:T(8,128)S(1)} %fusion.35, f32[5]{0:T(128)S(1)} %convert_element_type.44), kind=kOutput, calls=%fused_computation.11 | convolution fusion | flops 39321676 | bytes 5242900 | tf_op jit(solution)/shard_map/bc,hcde->hbde/dot_general | solution.py:134
  43.4 5.4 %collective-permute-done.1 = f32[8,136,128]{2,1,0:T(8,128)S(1)} collective-permute-done((f32[8,136,128]{2,1,0:T(8,128)S(1)}, f32[8,136,128]{2,1,0:T(8,128)S(1)}, u32[]{:S(2)}, u32[]{:S(2)}) %collective-permute-start.1) | collective-permute-done | bytes 557088 | tf_op jit(solution)/shard_map/ppermute | solution.py:25
  48.8 0.5 slice.52
  49.9 1.1 fusion.11
  51.1 0.0 copy-start
  51.1 3.0 %fusion.7.s_ref = bf16[8,5,128,128]{3,2,1,0:T(8,128)(2,1)S(1)} fusion(f32[8,128,128,5]{2,3,1,0:T(8,128)} %fusion.4, f32[8,128,128]{2,1,0:T(8,128)S(1)} %fusion.11, f32[5]{0:T(128)S(1)} %compare_convert_fusion.1), kind=kLoop, calls=%fused_computation.16 | loop fusion | flops 1966080 | bytes 4456468 | tf_op jit(solution)/shard_map/convert_element_type | solution.py:139
  54.1 1.1 copy-done.4
  55.1 3.3 %convolution_bitcast_fusion.2 = f32[8,5,256,128]{2,3,1,0:T(8,128)} fusion(bf16[8,5,128,128]{3,2,1,0:T(8,128)(2,1)S(1)} %fusion.7.s_ref, bf16[8,5,256,128]{3,2,1,0:T(8,128)(2,1)S(1)} %bitcast.80), kind=kOutput, calls=%fused_computation.19 | convolution fusion | flops 335544320 | bytes 9175040 | tf_op jit(solution)/shard_map/hnid,hnde->hnie/dot_general | solution.py:140
  58.4 6.0 %copy.24 = f32[8,5,256,128]{3,2,1,0:T(8,128)} copy(f32[8,5,256,128]{2,3,1,0:T(8,128)} %convolution_bitcast_fusion.2) | data formatting | bytes 10485760 | tf_op jit(solution)/shard_map/hnid,hnde->hnie/dot_general | solution.py:140
  64.4 6.4 %multiply_reduce_fusion.1 = (f32[1280]{0:T(1024)S(1)}, f32[1280]{0:T(1024)S(1)}) fusion(f32[8,1280,128]{2,1,0:T(8,128)} %shard_map.85, f32[8,5,256,128]{3,2,1,0:T(8,128)} %copy.24, bf16[8,1280,128]{2,1,0:T(8,128)(2,1)} %param.9, f32[8,128]{1,0:T(8,128)S(1)} %copy-done.5), kind=kLoop, calls=%fused_computation.7 | loop fusion | flops 9172480 | bytes 13121536 | tf_op jit(solution)/shard_map/reduce_sum | solution.py:147
  70.8 10.1 %psum.7 = f32[2,1280]{1,0:T(2,128)S(1)} all-reduce(f32[2,1280]{1,0:T(2,128)S(1)} %pad_maximum_fusion), channel_id=1, replica_groups=mesh['groups'=2,'ctx'=4,'sub'=2,'head'=2] {'sub','head'}, use_global_device_ids=true, to_apply=%region_2.3 | all-reduce | flops 2560 | bytes 20480 | tf_op jit(solution)/shard_map/psum | solution.py:149
  81.0 5.8 %divide_convert_fusion.d_ref = bf16[8,1280,128]{2,1,0:T(8,128)(2,1)S(1)} fusion(bf16[8,1280,128]{2,1,0:T(8,128)(2,1)} %param.9, f32[1280]{0:T(1024)S(1)} %get-tuple-element.12, f32[1280]{0:T(1024)S(1)} %multiply_divide_fusion, f32[8,128]{1,0:T(8,128)S(1)} %copy-done.5, f32[8,1280,128]{2,1,0:T(8,128)} %shard_map.85, f32[8,5,256,128]{3,2,1,0:T(8,128)} %copy.24), kind=kLoop, calls=%fused_computation.5 | loop fusion | flops 9175040 | bytes 15742976 | tf_op jit(solution)/shard_map/convert_element_type | solution.py:155
  86.8 1.5 copy-done.3
  88.2 2.4 %convolution_bitcast_fusion.3 = f32[8,5,128,128]{2,3,1,0:T(8,128)} fusion(bf16[8,5,256,128]{3,2,1,0:T(8,128)(2,1)S(1)} %bitcast.86, bf16[8,5,256,128]{3,2,1,0:T(8,128)(2,1)S(1)} %bitcast.81), kind=kOutput, calls=%fused_computation.20 | convolution fusion | flops 335544320 | bytes 7864320 | tf_op jit(solution)/shard_map/hnid,hnie->hnde/dot_general | solution.py:157
  90.6 4.7 %copy.26 = f32[8,5,128,128]{3,1,2,0:T(8,128)} copy(f32[8,5,128,128]{2,3,1,0:T(8,128)} %convolution_bitcast_fusion.3) | data formatting | bytes 5242880 | tf_op jit(solution)/shard_map/hnid,hnie->hnde/dot_general | solution.py:157
  95.3 4.9 %fusion.25 = f32[1,8,128,128]{3,0,2,1:T(1,128)S(1)} fusion(f32[8,5,128,128]{3,1,2,0:T(8,128)} %copy.26, f32[]{:T(128)} %bitcast.22, s32[5]{0:T(128)S(1)} %copy-done.6), kind=kOutput, calls=%fused_computation.50 | convolution fusion | flops 7864330 | bytes 3145752 | tf_op jit(solution)/shard_map/c,hcde->hde/dot_general | solution.py:161
  100.2 0.7 concatenate.14
  100.9 1.5 collective-permute-start.2
  102.5 26.1 %collective-permute-done.2 = f32[8,136,128]{2,1,0:T(8,128)S(1)} collective-permute-done((f32[8,136,128]{2,1,0:T(8,128)S(1)}, f32[8,136,128]{2,1,0:T(8,128)S(1)}, u32[]{:S(2)}, u32[]{:S(2)}) %collective-permute-start.2) | collective-permute-done | bytes 557088 | tf_op jit(solution)/shard_map/ppermute | solution.py:25
  128.6 0.5 slice.56
  130.4 0.1 multiply_add_fusion
  130.5 0.7 concatenate.15
  131.2 1.3 collective-permute-start.3
  132.5 6.4 %fusion.19 = f32[8,128,128,5]{2,3,1,0:T(8,128)} fusion(f32[8,5,128,128]{3,1,2,0:T(8,128)} %copy.26, f32[5]{0:T(128)S(1)} %convert_element_type.44), kind=kOutput, calls=%fused_computation.45 | convolution fusion | flops 39321676 | bytes 5242900 | tf_op jit(solution)/shard_map/bc,hcde->hbde/dot_general | solution.py:171
  138.9 16.8 %shard_map.86 = (bf16[8,1280,128]{2,1,0:T(8,128)(2,1)}, f32[8,1280,128]{2,1,0:T(8,128)}, f32[8,1280,128]{2,1,0:T(8,128)}) custom-call(bf16[8,1280,128]{2,1,0:T(8,128)(2,1)} %q_ref.3, bf16[8,1280,128]{2,1,0:T(8,128)(2,1)} %k_ref.3, bf16[8,1280,128]{2,1,0:T(8,128)(2,1)} %v_ref.3, bf16[8,1280,128]{2,1,0:T(8,128)(2,1)} %copy-done.3, ...), custom_call_target="tpu_custom_call" | custom-call | flops 3355443200 | bytes 24903680 | tf_op jit(solution)/shard_map/pallas_call | solution.py:95
  155.6 2.5 %collective-permute-done.3 = f32[8,136,128]{2,1,0:T(8,128)S(1)} collective-permute-done((f32[8,136,128]{2,1,0:T(8,128)S(1)}, f32[8,136,128]{2,1,0:T(8,128)S(1)}, u32[]{:S(2)}, u32[]{:S(2)}) %collective-permute-start.3) | collective-permute-done | bytes 557088 | tf_op jit(solution)/shard_map/ppermute | solution.py:25
  158.2 0.5 slice.58
  159.3 0.1 fusion.9
  159.4 0.0 copy-start.1
  159.4 3.0 %fusion.6 = bf16[8,5,128,128]{3,2,1,0:T(8,128)(2,1)S(1)} fusion(f32[8,128,128,5]{2,3,1,0:T(8,128)} %fusion.19, f32[8,128,128]{2,1,0:T(8,128)S(1)} %fusion.9, f32[5]{0:T(128)S(1)} %compare_convert_fusion), kind=kLoop, calls=%fused_computation.14 | loop fusion | flops 1966080 | bytes 4456468 | tf_op jit(solution)/shard_map/convert_element_type | solution.py:176
  162.4 0.0 copy-done.1
  162.4 3.1 %convolution_bitcast_fusion = f32[8,5,256,128]{2,3,1,0:T(8,128)} fusion(bf16[8,5,128,128]{3,2,1,0:T(8,128)(2,1)S(1)} %fusion.6, bf16[8,5,256,128]{3,2,1,0:T(8,128)(2,1)S(1)} %bitcast.83), kind=kOutput, calls=%fused_computation.17 | convolution fusion | flops 335544320 | bytes 9175040 | tf_op jit(solution)/shard_map/hnid,hnde->hnie/dot_general | solution.py:180
  165.6 3.2 %convolution_bitcast_fusion.1 = f32[8,5,256,128]{2,3,1,0:T(8,128)} fusion(bf16[8,5,128,128]{3,2,1,0:T(8,128)(2,1)S(1)} %fusion.6, bf16[8,5,256,128]{3,2,1,0:T(8,128)(2,1)S(1)} %bitcast.85), kind=kOutput, calls=%fused_computation.18 | convolution fusion | flops 335544320 | bytes 9175040 | tf_op jit(solution)/shard_map/hnie,hnde->hnid/dot_general | solution.py:177
  168.7 5.9 %copy.30 = f32[8,5,256,128]{3,2,1,0:T(8,128)} copy(f32[8,5,256,128]{2,3,1,0:T(8,128)} %convolution_bitcast_fusion) | data formatting | bytes 10485760 | tf_op jit(solution)/shard_map/hnid,hnde->hnie/dot_general | solution.py:180
  174.6 5.9 %copy.28 = f32[8,5,256,128]{3,2,1,0:T(8,128)} copy(f32[8,5,256,128]{2,3,1,0:T(8,128)} %convolution_bitcast_fusion.1) | data formatting | bytes 10485760 | tf_op jit(solution)/shard_map/hnie,hnde->hnid/dot_general | solution.py:177
  180.5 10.6 %fusion = (bf16[8,1280,128]{2,1,0:T(8,128)(2,1)}, bf16[8,1280,128]{2,1,0:T(8,128)(2,1)}) fusion(f32[8,1280,128]{2,1,0:T(8,128)} %get-tuple-element.8, f32[8,5,256,128]{3,2,1,0:T(8,128)} %copy.30, f32[8,1280,128]{2,1,0:T(8,128)} %get-tuple-element.7, f32[8,5,256,128]{3,2,1,0:T(8,128)} %copy.28), kind=kLoop, calls=%fused_computation.1 | loop fusion | flops 5242880 | bytes 26214400 | tf_op jit(solution)/shard_map/convert_element_type | solution.py:187
  (16 shorter events, 0.1 us)
Async XLA Ops:
  1.9 3.4 %copy-start.6 = (s32[5]{0:T(128)S(1)}, s32[5]{0:T(128)}, u32[]{:S(2)}) copy-start(s32[5]{0:T(128)} %param.11) | copy-start | bytes 64
  10.9 17.1 %collective-permute-start = (f32[8,136,128]{2,1,0:T(8,128)}, f32[8,136,128]{2,1,0:T(8,128)}, u32[]{:S(2)}, u32[]{:S(2)}) collective-permute-start(f32[8,136,128]{2,1,0:T(8,128)} %concatenate.12), channel_id=1, source_target_pairs={{0,4},{4,8},{8,12},{1,5},{5,9},{9,13},{2,6},{6,10},{10,14},{3,7},{... | collective-permute-start | bytes 1671176 | tf_op jit(solution)/shard_map/ppermute | solution.py:25
  32.3 16.4 %collective-permute-start.1 = (f32[8,136,128]{2,1,0:T(8,128)S(1)}, f32[8,136,128]{2,1,0:T(8,128)S(1)}, u32[]{:S(2)}, u32[]{:S(2)}) collective-permute-start(f32[8,136,128]{2,1,0:T(8,128)S(1)} %concatenate.13), channel_id=1, source_target_pairs={{0,8},{4,12},{1,9},{5,13},{2,10},{6,14},{3,11},{7,15},{16,24},{20,... | collective-permute-start | bytes 1671176 | tf_op jit(solution)/shard_map/ppermute | solution.py:25
  51.1 4.1 %copy-start = (bf16[8,1280,128]{2,1,0:T(8,128)(2,1)S(1)}, bf16[8,1280,128]{2,1,0:T(8,128)(2,1)}, u32[]{:S(2)}) copy-start(bf16[8,1280,128]{2,1,0:T(8,128)(2,1)} %q_ref.3) | copy-start | bytes 7864324
  54.1 1.1 copy-start.4
  58.4 6.0 %copy-start.5 = (f32[8,128]{1,0:T(8,128)S(1)}, f32[8,128]{1,0:T(8,128)}, u32[]{:S(2)}) copy-start(f32[8,128]{1,0:T(8,128)} %param.10) | copy-start | bytes 12292
  86.7 1.5 copy-start.3
  100.9 27.7 %collective-permute-start.2 = (f32[8,136,128]{2,1,0:T(8,128)S(1)}, f32[8,136,128]{2,1,0:T(8,128)S(1)}, u32[]{:S(2)}, u32[]{:S(2)}) collective-permute-start(f32[8,136,128]{2,1,0:T(8,128)S(1)} %concatenate.14), channel_id=1, source_target_pairs={{4,0},{8,4},{12,8},{5,1},{9,5},{13,9},{6,2},{10,6},{14,10},{7,3},{... | collective-permute-start | bytes 1671176 | tf_op jit(solution)/shard_map/ppermute | solution.py:25
  131.2 27.0 %collective-permute-start.3 = (f32[8,136,128]{2,1,0:T(8,128)S(1)}, f32[8,136,128]{2,1,0:T(8,128)S(1)}, u32[]{:S(2)}, u32[]{:S(2)}) collective-permute-start(f32[8,136,128]{2,1,0:T(8,128)S(1)} %concatenate.15), channel_id=1, source_target_pairs={{8,0},{12,4},{9,1},{13,5},{10,2},{14,6},{11,3},{15,7},{24,16},{28,... | collective-permute-start | bytes 1671176 | tf_op jit(solution)/shard_map/ppermute | solution.py:25
  159.4 3.0 %copy-start.1 = (bf16[8,1280,128]{2,1,0:T(8,128)(2,1)S(1)}, bf16[8,1280,128]{2,1,0:T(8,128)(2,1)}, u32[]{:S(2)}) copy-start(bf16[8,1280,128]{2,1,0:T(8,128)(2,1)} %k_ref.3) | copy-start | bytes 7864324
  162.4 3.1 %copy-start.2 = (bf16[8,1280,128]{2,1,0:T(8,128)(2,1)S(1)}, bf16[8,1280,128]{2,1,0:T(8,128)(2,1)}, u32[]{:S(2)}) copy-start(bf16[8,1280,128]{2,1,0:T(8,128)(2,1)} %v_ref.3) | copy-start | bytes 7864324

commit v3 on v2

--- a/solution.py
+++ b/solution.py
@@ -10,7 +10,7 @@
 _ROWS_MAJOR = (((0,), (0,)), ((), ()))
 
 
-def segmented_scan(doc, state, axis, reverse):
+def segmented_scan(doc, state, axis, reverse, cover):
     peers = lax.axis_size(axis)
     index = lax.axis_index(axis)
     none_doc = jnp.float32(-1.0)
@@ -33,8 +33,10 @@
         return near_doc, near_state + joined * far_state
 
     if peers == 1:
-        return none_doc, jnp.zeros_like(state)
-    ex_doc, ex_state = shift(doc, state, 1)
+        return none_doc, jnp.zeros_like(state), cover()
+    got_doc, got_state = shift(doc, state, 1)
+    covered_value = cover()
+    ex_doc, ex_state, covered_value = lax.optimization_barrier((got_doc, got_state, covered_value))
     in_doc, in_state = combine(doc, state, ex_doc, ex_state)
     covered = 1
     while covered < peers - 1:
@@ -44,7 +46,7 @@
         covered = covered + step
         if covered < peers - 1:
             in_doc, in_state = combine(in_doc, in_state, got_doc, got_state)
-    return ex_doc, ex_state
+    return ex_doc, ex_state, covered_value
 
 
 def _causal(block_len):
@@ -82,6 +84,28 @@
         dv_ref[0, rows, :] = lax.dot_general(
             probs, d, _ROWS_MAJOR, preferred_element_type=jnp.float32
         )
+
+
+def forward_finish_kernel(block_len, i_ref, q_ref, s_ref, o_ref):
+    for n in range(q_ref.shape[1] // block_len):
+        rows = pl.ds(n * block_len, block_len)
+        o_ref[0, rows, :] = i_ref[0, rows, :] + jnp.dot(
+            q_ref[0, rows, :], s_ref[0, n], preferred_element_type=jnp.float32
+        )
+
+
+def backward_finish_kernel(block_len, ik_ref, iv_ref, k_ref, v_ref, s_ref, dk_ref, dv_ref):
+    for n in range(k_ref.shape[1] // block_len):
+        rows = pl.ds(n * block_len, block_len)
+        state = s_ref[0, n]
+        dk = ik_ref[0, rows, :] + lax.dot_general(
+            v_ref[0, rows, :], state, _ROWS_MINOR, preferred_element_type=jnp.float32
+        )
+        dv = iv_ref[0, rows, :] + jnp.dot(
+            k_ref[0, rows, :], state, preferred_element_type=jnp.float32
+        )
+        dk_ref[0, rows, :] = dk.astype(dk_ref.dtype)
+        dv_ref[0, rows, :] = dv.astype(dv_ref.dtype)
 
 
 def per_head_call(kernel, inputs, out_dtypes, flops):
@@ -124,12 +148,17 @@
     )
     last_match = (doc_values == doc_values[-1]).astype(jnp.float32)
     device_kv = jnp.einsum("c,hcde->hde", last_match, key_value_block, precision=highest_precision)
-    prior_doc, prior_state = segmented_scan(doc_values[-1], device_kv, "ctx", False)
-    (intra_part,) = per_head_call(
-        functools.partial(forward_kernel, block_len),
-        [queries, keys, values],
-        [jnp.float32],
-        2 * pair_flops,
+    prior_doc, prior_state, intra_part = segmented_scan(
+        doc_values[-1],
+        device_kv,
+        "ctx",
+        False,
+        lambda: per_head_call(
+            functools.partial(forward_kernel, block_len),
+            [queries, keys, values],
+            [jnp.float32],
+            2 * pair_flops,
+        )[0],
     )
     local_prefix = jnp.einsum(
         "bc,hcde->hbde", earlier_mask, key_value_block, precision=highest_precision
@@ -137,10 +166,12 @@
     prior_match = (doc_values == prior_doc).astype(jnp.float32)
     entering = prior_match[None, :, None, None] * prior_state[:, None, :, :]
     preceding_states = (local_prefix + entering).astype(jnp.bfloat16)
-    cross_block_part = jnp.einsum(
-        "hnid,hnde->hnie", query_blocks, preceding_states, preferred_element_type=jnp.float32
-    )
-    raw_attn = intra_part + cross_block_part.reshape(head_count, tok_count, head_width)
+    (raw_attn,) = per_head_call(
+        functools.partial(forward_finish_kernel, block_len),
+        [intra_part, queries, preceding_states],
+        [jnp.float32],
+        pair_flops // 2,
+    )
     feature_count = head_count * head_width * lax.axis_size(("sub", "head"))
     scaled = norm_gain[:, None, :] * out_grad.astype(jnp.float32)
     local_sums = jnp.stack(
@@ -161,12 +192,17 @@
     device_qd = jnp.einsum(
         "c,hcde->hde", first_match, query_grad_block, precision=highest_precision
     )
-    next_doc, next_state = segmented_scan(doc_values[0], device_qd, "ctx", True)
-    query_gradient, key_intra, value_intra = per_head_call(
-        functools.partial(backward_kernel, block_len),
-        [queries, keys, values, d_attn, preceding_states],
-        [jnp.bfloat16, jnp.float32, jnp.float32],
-        5 * pair_flops,
+    next_doc, next_state, (query_gradient, key_intra, value_intra) = segmented_scan(
+        doc_values[0],
+        device_qd,
+        "ctx",
+        True,
+        lambda: per_head_call(
+            functools.partial(backward_kernel, block_len),
+            [queries, keys, values, d_attn, preceding_states],
+            [jnp.bfloat16, jnp.float32, jnp.float32],
+            5 * pair_flops,
+        ),
     )
     local_suffix = jnp.einsum(
         "bc,hcde->hbde", later_mask, query_grad_block, precision=highest_precision
@@ -174,18 +210,13 @@
     next_match = (doc_values == next_doc).astype(jnp.float32)
     leaving = next_match[None, :, None, None] * next_state[:, None, :, :]
     following_states = (local_suffix + leaving).astype(jnp.bfloat16)
-    key_cross = jnp.einsum(
-        "hnie,hnde->hnid", value_blocks, following_states, preferred_element_type=jnp.float32
-    )
-    value_cross = jnp.einsum(
-        "hnid,hnde->hnie", key_blocks, following_states, preferred_element_type=jnp.float32
-    )
-    out_shape = (head_count, tok_count, head_width)
-    return (
-        query_gradient,
-        (key_intra + key_cross.reshape(out_shape)).astype(jnp.bfloat16),
-        (value_intra + value_cross.reshape(out_shape)).astype(jnp.bfloat16),
-    )
+    key_gradient, value_gradient = per_head_call(
+        functools.partial(backward_finish_kernel, block_len),
+        [key_intra, value_intra, keys, values, following_states],
+        [jnp.bfloat16, jnp.bfloat16],
+        pair_flops,
+    )
+    return query_gradient, key_gradient, value_gradient
 
 
 def solution(mesh):

time: 192 us -> 174 us (0.906)
  Pallas kernels: 26.9 us -> 46.2 us
  local copies, waits for them, and re-layouts: 31.8 us -> 12.8 us
  other arithmetic: 31.7 us -> 19.9 us
  matrix products: 36.3 us -> 25 us
  waiting for transfers between devices: 35.3 us -> 39.6 us
    pallas_call x2 -> x4, Pallas kernels: 26.9 us -> 46.2 us  [per_head_call(): pl.pallas_call(kernel, grid=(head_count,), in_specs=[spec(x.shape) for x...]
    dot_general x3 -> x0, local copies, waits for them, and re-layouts: 17.7 us -> none  [the longest x1 5.95 us: on_device(): jnp.einsum('hnid,hnde->hnie', query_blocks, preceding_states, preferred_e...]
    convert_element_type x1 -> x0, other arithmetic: 10.6 us -> none  [on_device(): (value_intra + value_cross.reshape(out_shape)).astype(jnp.bfloat16)]
    dot_general x3 -> x0, matrix products: 9.57 us -> none  [the longest x1 3.27 us: on_device(): jnp.einsum('hnid,hnde->hnie', query_blocks, preceding_states, preferred_e...]
    ppermute x4, waiting for transfers between devices: 35.3 us -> 39.6 us  [shift(): got = lax.ppermute(jnp.concatenate([value_state, row], axis=1), axis, pairs)]
    reduce_sum x1, other arithmetic: 6.38 us -> 3.66 us  [on_device(): jnp.sum(raw_attn * raw_attn, axis=(0, 2))]
    convert_element_type x1, other arithmetic: 5.77 us -> 3.46 us  [on_device(): d_attn = ((scaled - raw_attn * factor[None, :, None]) / root_mean[None, :...]
  transfers between devices with their start and end apart: 4 -> 4, of which waited for: 4 -> 4; matrix products, arithmetic and copies ran while one was open for 6% -> 7% of each run, Pallas kernels for 14% -> 16%
where the time goes in v3:
time: 174 us; the launch traced here: 173 us
  Pallas kernels  46.2 us (27%)
  waiting for transfers between devices  39.6 us (23%)
  matrix products  25 us (14%)
  other arithmetic  19.9 us (11%)
  starting transfers between devices  13.9 us (8%)
  local copies, waits for them, and re-layouts  12.8 us (7%)
  blocking collectives  10.3 us (6%)
  between operations  4.73 us (3%)
    pallas_call x4, Pallas kernels, per_head_call(): pl.pallas_call(kernel, grid=(head_count,), in_specs=[spec(x.shape) for x...  46.2 us
    ppermute x4, waiting for transfers between devices, shift(): got = lax.ppermute(jnp.concatenate([value_state, row], axis=1), axis, pairs)  39.6 us
    ppermute x4, starting transfers between devices, shift(): got = lax.ppermute(jnp.concatenate([value_state, row], axis=1), axis, pairs)  13.9 us
    psum x1, blocking collectives, on_device(): total_sums = lax.psum(local_sums, ('sub', 'head'))  10.3 us
    dot_general x1, matrix products, on_device(): jnp.einsum('bc,hcde->hbde', later_mask, query_grad_block, precision=highe...  6.29 us
    dot_general x1, matrix products, on_device(): jnp.einsum('bc,hcde->hbde', earlier_mask, key_value_block, precision=high...  5.46 us
    dot_general x1, matrix products, on_device(): jnp.einsum('c,hcde->hde', first_match, query_grad_block, precision=highes...  4.86 us
    dot_general x1, matrix products, on_device(): jnp.einsum('c,hcde->hde', last_match, key_value_block, precision=highest_...  4.12 us
  transfers between devices with their start and end apart: 4, of which 4 were waited for; matrix products, arithmetic and copies ran while one was open for 7% of the time, Pallas kernels for 16%

profile of v3, /device:TPU:0, one launch (start us, length us, event | category | flops | bytes accessed | tf_op | source)
XLA Modules:
  0.0 172.6 jit_solution(3855396278887495474)
XLA Ops:
  0.6 0.7 convert_element_type.37
  1.3 0.6 fusion.32
  1.9 3.4 %fusion.33 = f32[8,5,128,128]{3,2,1,0:T(8,128)S(1)} fusion(bf16[8,5,256,128]{3,2,1,0:T(8,128)(2,1)} %bitcast.53, bf16[8,5,256,128]{3,2,1,0:T(8,128)(2,1)} %bitcast.54), kind=kOutput, calls=%fused_computation.54 | convolution fusion | flops 335544320 | bytes 7864320 | tf_op jit(solution)/shard_map/hnid,hnie->hnde/dot_general | solution.py:146
  5.3 0.0 copy-done.6
  5.3 4.1 %fusion = f32[1,8,128,128]{3,0,2,1:T(1,128)S(1)} fusion(f32[8,5,128,128]{3,2,1,0:T(8,128)S(1)} %fusion.33, f32[]{:T(128)} %bitcast.3, s32[5]{0:T(128)S(1)} %copy-done.6), kind=kOutput, calls=%fused_computation.4 | convolution fusion | flops 7864330 | bytes 3145752 | tf_op jit(solution)/shard_map/c,hcde->hde/dot_general | solution.py:150
  9.4 1.5 concatenate.12
  10.9 5.8 %collective-permute-start = (f32[8,136,128]{2,1,0:T(8,128)}, f32[8,136,128]{2,1,0:T(8,128)}, u32[]{:S(2)}, u32[]{:S(2)}) collective-permute-start(f32[8,136,128]{2,1,0:T(8,128)} %concatenate.12), channel_id=1, source_target_pairs={{0,4},{4,8},{8,12},{1,5},{5,9},{9,13},{2,6},{6,10},{10,14},{3,7},{... | collective-permute-start | bytes 1671176 | tf_op jit(solution)/shard_map/ppermute | solution.py:25
  16.7 10.2 %shard_map.85.i_ref = f32[8,1280,128]{2,1,0:T(8,128)} custom-call(bf16[8,1280,128]{2,1,0:T(8,128)(2,1)} %q_ref.5, bf16[8,1280,128]{2,1,0:T(8,128)(2,1)} %k_ref.5, bf16[8,1280,128]{2,1,0:T(8,128)(2,1)} %v_ref.5), custom_call_target="tpu_custom_call" | custom-call | flops 1342177280 | bytes 13107200 | tf_op jit(solution)/shard_map/pallas_call | solution.py:119
  26.8 1.2 collective-permute-done
  28.0 1.2 slice.50
  29.9 1.9 %slice_select_fusion.3 = f32[8,128,128]{2,1,0:T(8,128)} fusion(f32[8,136,128]{2,1,0:T(8,128)} %collective-permute-done, pred[]{:T(512)S(6)} %ge.6), kind=kLoop, calls=%fused_computation.20 | loop fusion | flops 131072 | bytes 1048577 | tf_op jit(solution)/shard_map/jit(_where)/select_n | solution.py:28
  32.4 1.1 multiply_add_fusion.1
  33.5 0.7 concatenate.13
  34.2 0.0 copy-start.3
  34.2 5.6 %collective-permute-start.1 = (f32[8,136,128]{2,1,0:T(8,128)S(1)}, f32[8,136,128]{2,1,0:T(8,128)S(1)}, u32[]{:S(2)}, u32[]{:S(2)}) collective-permute-start(f32[8,136,128]{2,1,0:T(8,128)S(1)} %concatenate.13), channel_id=1, source_target_pairs={{0,8},{4,12},{1,9},{5,13},{2,10},{6,14},{3,11},{7,15},{16,24},{20,... | collective-permute-start | bytes 1671176 | tf_op jit(solution)/shard_map/ppermute | solution.py:25
  39.8 5.5 %fusion.2 = f32[8,128,128,5]{2,3,1,0:T(8,128)} fusion(f32[8,5,128,128]{3,2,1,0:T(8,128)S(1)} %fusion.33, f32[5]{0:T(128)S(1)} %convert_element_type.37), kind=kOutput, calls=%fused_computation.6 | convolution fusion | flops 39321676 | bytes 5242900 | tf_op jit(solution)/shard_map/bc,hcde->hbde/dot_general | solution.py:163
  45.3 5.5 %collective-permute-done.1 = f32[8,136,128]{2,1,0:T(8,128)S(1)} collective-permute-done((f32[8,136,128]{2,1,0:T(8,128)S(1)}, f32[8,136,128]{2,1,0:T(8,128)S(1)}, u32[]{:S(2)}, u32[]{:S(2)}) %collective-permute-start.1) | collective-permute-done | bytes 557088 | tf_op jit(solution)/shard_map/ppermute | solution.py:25
  50.8 0.8 copy-done.4
  51.6 0.5 slice.52
  52.8 0.0 copy-done.3
  52.8 1.1 fusion.9
  53.9 3.9 %fusion.5.s_ref = bf16[8,5,128,128]{3,2,1,0:T(8,128)(2,1)} fusion(f32[8,128,128,5]{2,3,1,0:T(8,128)} %fusion.2, f32[8,128,128]{2,1,0:T(8,128)S(1)} %fusion.9, f32[5]{0:T(128)S(1)} %compare_convert_fusion.1), kind=kLoop, calls=%fused_computation.11 | loop fusion | flops 1966080 | bytes 4456468 | tf_op jit(solution)/shard_map/convert_element_type | solution.py:168
  57.8 8.8 %shard_map.86 = f32[8,1280,128]{2,1,0:T(8,128)} custom-call(f32[8,1280,128]{2,1,0:T(8,128)} %shard_map.85.i_ref, bf16[8,1280,128]{2,1,0:T(8,128)(2,1)} %q_ref.5, bf16[8,5,128,128]{3,2,1,0:T(8,128)(2,1)} %fusion.5.s_ref), custom_call_target="tpu_custom_call" | custom-call | flops 335544320 | bytes 14417920 | tf_op jit(solution)/shard_map/pallas_call | solution.py:119
  66.6 0.0 copy-done.1
  66.6 0.0 copy-done.5
  66.6 3.7 %multiply_reduce_fusion.1 = (f32[1280]{0:T(1024)S(1)}, f32[1280]{0:T(1024)S(1)}) fusion(f32[8,1280,128]{2,1,0:T(8,128)} %shard_map.86, bf16[8,1280,128]{2,1,0:T(8,128)(2,1)S(1)} %copy-done.1, f32[8,128]{1,0:T(8,128)S(1)} %copy-done.5), kind=kLoop, calls=%fused_computation.2 | loop fusion | flops 7861760 | bytes 7878656 | tf_op jit(solution)/shard_map/reduce_sum | solution.py:178
  70.3 10.3 %psum.7 = f32[2,1280]{1,0:T(2,128)S(1)} all-reduce(f32[2,1280]{1,0:T(2,128)S(1)} %pad_maximum_fusion), channel_id=1, replica_groups=mesh['groups'=2,'ctx'=4,'sub'=2,'head'=2] {'sub','head'}, use_global_device_ids=true, to_apply=%region_2.3 | all-reduce | flops 2560 | bytes 20480 | tf_op jit(solution)/shard_map/psum | solution.py:180
  80.7 0.0 copy-start
  80.7 3.5 %divide_convert_fusion.d_ref = bf16[8,1280,128]{2,1,0:T(8,128)(2,1)S(1)} fusion(f32[8,1280,128]{2,1,0:T(8,128)} %shard_map.86, bf16[8,1280,128]{2,1,0:T(8,128)(2,1)S(1)} %copy-done.1, f32[1280]{0:T(1024)S(1)} %get-tuple-element.32, f32[1280]{0:T(1024)S(1)} %multiply_divide_fusion, f32[8,128]{1,0:T(8,128)S(1)} %copy-done.5), kind=kLoop, calls=%fused_computation | loop fusion | flops 7864320 | bytes 10500096 | tf_op jit(solution)/shard_map/convert_element_type | solution.py:186
  84.1 0.0 copy-start.2
  84.2 1.5 copy-done.2
  85.6 0.9 convolution_bitcast_fusion
  86.5 3.7 %copy.13 = f32[8,5,128,128]{3,1,2,0:T(8,128)} copy(f32[8,5,128,128]{2,3,1,0:T(8,128)S(1)} %convolution_bitcast_fusion) | data formatting | bytes 5242880 | tf_op jit(solution)/shard_map/hnid,hnie->hnde/dot_general | solution.py:188
  90.3 4.9 %fusion.24 = f32[1,8,128,128]{3,0,2,1:T(1,128)S(1)} fusion(f32[8,5,128,128]{3,1,2,0:T(8,128)} %copy.13, f32[]{:T(128)} %bitcast.17, s32[5]{0:T(128)S(1)} %copy-done.6), kind=kOutput, calls=%fused_computation.43 | convolution fusion | flops 7864330 | bytes 3145752 | tf_op jit(solution)/shard_map/c,hcde->hde/dot_general | solution.py:192
  95.1 0.7 concatenate.14
  95.8 1.3 collective-permute-start.2
  97.1 16.8 %shard_map.87 = (bf16[8,1280,128]{2,1,0:T(8,128)(2,1)}, f32[8,1280,128]{2,1,0:T(8,128)}, f32[8,1280,128]{2,1,0:T(8,128)}) custom-call(bf16[8,1280,128]{2,1,0:T(8,128)(2,1)} %q_ref.5, bf16[8,1280,128]{2,1,0:T(8,128)(2,1)} %k_ref.5, bf16[8,1280,128]{2,1,0:T(8,128)(2,1)} %v_ref.5, bf16[8,1280,128]{2,1,0:T(8,128)(2,1)} %copy-done.2, ...), custom_call_target="tpu_custom_call" | custom-call | flops 3355443200 | bytes 24903680 | tf_op jit(solution)/shard_map/pallas_call | solution.py:119
  113.9 9.3 %collective-permute-done.2 = f32[8,136,128]{2,1,0:T(8,128)S(1)} collective-permute-done((f32[8,136,128]{2,1,0:T(8,128)S(1)}, f32[8,136,128]{2,1,0:T(8,128)S(1)}, u32[]{:S(2)}, u32[]{:S(2)}) %collective-permute-start.2) | collective-permute-done | bytes 557088 | tf_op jit(solution)/shard_map/ppermute | solution.py:25
  123.2 0.5 slice.56
  125.0 0.1 multiply_add_fusion
  125.1 0.7 concatenate.15
  125.7 1.3 collective-permute-start.3
  127.0 6.3 %fusion.17 = f32[8,128,128,5]{2,3,1,0:T(8,128)} fusion(f32[8,5,128,128]{3,1,2,0:T(8,128)} %copy.13, f32[5]{0:T(128)S(1)} %convert_element_type.37), kind=kOutput, calls=%fused_computation.37 | convolution fusion | flops 39321676 | bytes 5242900 | tf_op jit(solution)/shard_map/bc,hcde->hbde/dot_general | solution.py:207
  133.3 23.6 %collective-permute-done.3 = f32[8,136,128]{2,1,0:T(8,128)S(1)} collective-permute-done((f32[8,136,128]{2,1,0:T(8,128)S(1)}, f32[8,136,128]{2,1,0:T(8,128)S(1)}, u32[]{:S(2)}, u32[]{:S(2)}) %collective-permute-start.3) | collective-permute-done | bytes 557088 | tf_op jit(solution)/shard_map/ppermute | solution.py:25
  156.9 0.5 slice.58
  158.1 0.1 fusion.7
  158.2 3.9 %fusion.4.s_ref = bf16[8,5,128,128]{3,2,1,0:T(8,128)(2,1)} fusion(f32[8,128,128,5]{2,3,1,0:T(8,128)} %fusion.17, f32[8,128,128]{2,1,0:T(8,128)S(1)} %fusion.7, f32[5]{0:T(128)S(1)} %compare_convert_fusion), kind=kLoop, calls=%fused_computation.9 | loop fusion | flops 1966080 | bytes 4456468 | tf_op jit(solution)/shard_map/convert_element_type | solution.py:212
  162.1 10.5 %shard_map.88 = (bf16[8,1280,128]{2,1,0:T(8,128)(2,1)}, bf16[8,1280,128]{2,1,0:T(8,128)(2,1)}) custom-call(f32[8,1280,128]{2,1,0:T(8,128)} %get-tuple-element.23.ik_ref, f32[8,1280,128]{2,1,0:T(8,128)} %get-tuple-element.24.iv_ref, bf16[8,1280,128]{2,1,0:T(8,128)(2,1)} %k_ref.5, bf16[8,1280,128]{2,1,0:T(8,128)(2,1)} %v_ref.5, ...), custom_call_target="tpu_custom_call" | custom-call | flops 671088640 | bytes 22282240 | tf_op jit(solution)/shard_map/pallas_call | solution.py:119
  (13 shorter events, 0.1 us)
Async XLA Ops:
  1.9 3.4 %copy-start.6 = (s32[5]{0:T(128)S(1)}, s32[5]{0:T(128)}, u32[]{:S(2)}) copy-start(s32[5]{0:T(128)} %param.11) | copy-start | bytes 64
  10.9 17.1 %collective-permute-start = (f32[8,136,128]{2,1,0:T(8,128)}, f32[8,136,128]{2,1,0:T(8,128)}, u32[]{:S(2)}, u32[]{:S(2)}) collective-permute-start(f32[8,136,128]{2,1,0:T(8,128)} %concatenate.12), channel_id=1, source_target_pairs={{0,4},{4,8},{8,12},{1,5},{5,9},{9,13},{2,6},{6,10},{10,14},{3,7},{... | collective-permute-start | bytes 1671176 | tf_op jit(solution)/shard_map/ppermute | solution.py:25
  34.2 18.6 %copy-start.3 = (f32[8,128,128]{2,1,0:T(8,128)S(1)}, f32[8,128,128]{2,1,0:T(8,128)}, u32[]{:S(2)}) copy-start(f32[8,128,128]{2,1,0:T(8,128)} %slice_select_fusion.3) | copy-start | bytes 1572868
  34.2 16.6 %collective-permute-start.1 = (f32[8,136,128]{2,1,0:T(8,128)S(1)}, f32[8,136,128]{2,1,0:T(8,128)S(1)}, u32[]{:S(2)}, u32[]{:S(2)}) collective-permute-start(f32[8,136,128]{2,1,0:T(8,128)S(1)} %concatenate.13), channel_id=1, source_target_pairs={{0,8},{4,12},{1,9},{5,13},{2,10},{6,14},{3,11},{7,15},{16,24},{20,... | collective-permute-start | bytes 1671176 | tf_op jit(solution)/shard_map/ppermute | solution.py:25
  50.8 0.8 copy-start.4
  57.8 8.8 %copy-start.1 = (bf16[8,1280,128]{2,1,0:T(8,128)(2,1)S(1)}, bf16[8,1280,128]{2,1,0:T(8,128)(2,1)}, u32[]{:S(2)}) copy-start(bf16[8,1280,128]{2,1,0:T(8,128)(2,1)} %param.9) | copy-start | bytes 7864324
  57.8 8.8 %copy-start.5 = (f32[8,128]{1,0:T(8,128)S(1)}, f32[8,128]{1,0:T(8,128)}, u32[]{:S(2)}) copy-start(f32[8,128]{1,0:T(8,128)} %param.10) | copy-start | bytes 12292
  80.7 5.0 %copy-start = (bf16[8,1280,128]{2,1,0:T(8,128)(2,1)S(1)}, bf16[8,1280,128]{2,1,0:T(8,128)(2,1)}, u32[]{:S(2)}) copy-start(bf16[8,1280,128]{2,1,0:T(8,128)(2,1)} %q_ref.5) | copy-start | bytes 7864324
  84.1 1.5 copy-start.2
  95.8 27.4 %collective-permute-start.2 = (f32[8,136,128]{2,1,0:T(8,128)S(1)}, f32[8,136,128]{2,1,0:T(8,128)S(1)}, u32[]{:S(2)}, u32[]{:S(2)}) collective-permute-start(f32[8,136,128]{2,1,0:T(8,128)S(1)} %concatenate.14), channel_id=1, source_target_pairs={{4,0},{8,4},{12,8},{5,1},{9,5},{13,9},{6,2},{10,6},{14,10},{7,3},{... | collective-permute-start | bytes 1671176 | tf_op jit(solution)/shard_map/ppermute | solution.py:25
  125.7 31.2 %collective-permute-start.3 = (f32[8,136,128]{2,1,0:T(8,128)S(1)}, f32[8,136,128]{2,1,0:T(8,128)S(1)}, u32[]{:S(2)}, u32[]{:S(2)}) collective-permute-start(f32[8,136,128]{2,1,0:T(8,128)S(1)} %concatenate.15), channel_id=1, source_target_pairs={{8,0},{12,4},{9,1},{13,5},{10,2},{14,6},{11,3},{15,7},{24,16},{28,... | collective-permute-start | bytes 1671176 | tf_op jit(solution)/shard_map/ppermute | solution.py:25

commit v4 on v3

v4 whole, which is shorter than its diff:
```python
import functools
import math

import jax
import jax.numpy as jnp
from jax import lax
from jax.experimental import pallas as pl
from jax.sharding import PartitionSpec as P

_ROWS_MINOR = (((1,), (1,)), ((), ()))
_ROWS_MAJOR = (((0,), (0,)), ((), ()))


def segmented_scan(doc, state, axis, reverse, cover):
    peers = lax.axis_size(axis)
    index = lax.axis_index(axis)
    none_doc = jnp.float32(-1.0)
    pad = jnp.broadcast_to(doc, (state.shape[0], 8, state.shape[2])).astype(jnp.float32)

    def shift(value_doc, value_state, step):
        if reverse:
            pairs = [(j, j - step) for j in range(step, peers)]
        else:
            pairs = [(j, j + step) for j in range(peers - step)]
        row = jnp.broadcast_to(value_doc, pad.shape)
        got = lax.ppermute(jnp.concatenate([value_state, row], axis=1), axis, pairs)
        valid = (index <= peers - 1 - step) if reverse else (index >= step)
        got_doc = jnp.where(valid, got[0, state.shape[1], 0], none_doc)
        got_state = jnp.where(valid, got[:, : state.shape[1]], 0.0)
        return got_doc, got_state

    def combine(near_doc, near_state, far_doc, far_state):
        joined = (near_doc == far_doc).astype(jnp.float32)
        return near_doc, near_state + joined * far_state

    if peers == 1:
        return none_doc, jnp.zeros_like(state), cover()
    got_doc, got_state = shift(doc, state, 1)
    covered_value = cover()
    ex_doc, ex_state, covered_value = lax.optimization_barrier((got_doc, got_state, covered_value))
    in_doc, in_state = combine(doc, state, ex_doc, ex_state)
    covered = 1
    while covered < peers - 1:
        step = covered + 1
        got_doc, got_state = shift(in_doc, in_state, step)
        ex_doc, ex_state = combine(ex_doc, ex_state, got_doc, got_state)
        covered = covered + step
        if covered < peers - 1:
            in_doc, in_state = combine(in_doc, in_state, got_doc, got_state)
    return ex_doc, ex_state, covered_value


def _causal(block_len):
    row_ids = lax.broadcasted_iota(jnp.int32, (block_len, block_len), 0)
    col_ids = lax.broadcasted_iota(jnp.int32, (block_len, block_len), 1)
    return row_ids >= col_ids


def _raw_block(causal, q, k, v, state):
    scores = lax.dot_general(q, k, _ROWS_MINOR, preferred_element_type=jnp.float32)
    probs = jnp.where(causal, scores, 0.0).astype(jnp.bfloat16)
    raw = jnp.dot(probs, v, preferred_element_type=jnp.float32)
    return raw + jnp.dot(q, state, preferred_element_type=jnp.float32)


def forward_kernel(block_len, q_ref, k_ref, v_ref, g_ref, n_ref, s_ref, o_ref):
    causal = _causal(block_len)

    @pl.when(pl.program_id(0) == 0)
    def _():
        o_ref[...] = jnp.zeros_like(o_ref)

    for n in range(q_ref.shape[1] // block_len):
        rows = pl.ds(n * block_len, block_len)
        q, k, v = q_ref[0, rows, :], k_ref[0, rows, :], v_ref[0, rows, :]
        raw = _raw_block(causal, q, k, v, s_ref[0, n])
        scaled = n_ref[0] * g_ref[0, rows, :].astype(jnp.float32)
        o_ref[rows, 0:1] += jnp.sum(raw * raw, axis=1, keepdims=True)
        o_ref[rows, 1:2] += jnp.sum(scaled * raw, axis=1, keepdims=True)


def grad_kernel(block_len, q_ref, k_ref, v_ref, g_ref, n_ref, s_ref, c_ref, d_ref, qd_ref):
    causal = _causal(block_len)
    for n in range(q_ref.shape[1] // block_len):
        rows = pl.ds(n * block_len, block_len)
        q, k, v = q_ref[0, rows, :], k_ref[0, rows, :], v_ref[0, rows, :]
        raw = _raw_block(causal, q, k, v, s_ref[0, n])
        scaled = n_ref[0] * g_ref[0, rows, :].astype(jnp.float32)
        root_mean = c_ref[rows, 0:1]
        factor = c_ref[rows, 1:2]
        d = ((scaled - raw * factor) / root_mean).astype(jnp.bfloat16)
        d_ref[0, rows, :] = d
        qd_ref[0, n] = lax.dot_general(q, d, _ROWS_MAJOR, preferred_element_type=jnp.float32)


def query_grad_kernel(block_len, k_ref, v_ref, d_ref, s_ref, dq_ref):
    causal = _causal(block_len)
    for n in range(k_ref.shape[1] // block_len):
        rows = pl.ds(n * block_len, block_len)
        k, v, d = k_ref[0, rows, :], v_ref[0, rows, :], d_ref[0, rows, :]
        grad_scores = lax.dot_general(d, v, _ROWS_MINOR, preferred_element_type=jnp.float32)
        grad_probs = jnp.where(causal, grad_scores, 0.0).astype(jnp.bfloat16)
        dq = jnp.dot(grad_probs, k, preferred_element_type=jnp.float32)
        dq = dq + lax.dot_general(d, s_ref[0, n], _ROWS_MINOR, preferred_element_type=jnp.float32)
        dq_ref[0, rows, :] = dq.astype(dq_ref.dtype)


def key_value_grad_kernel(block_len, q_ref, k_ref, v_ref, d_ref, s_ref, dk_ref, dv_ref):
    causal = _causal(block_len)
    for n in range(q_ref.shape[1] // block_len):
        rows = pl.ds(n * block_len, block_len)
        q, k, v = q_ref[0, rows, :], k_ref[0, rows, :], v_ref[0, rows, :]
        d = d_ref[0, rows, :]
        state = s_ref[0, n]
        scores = lax.dot_general(q, k, _ROWS_MINOR, preferred_element_type=jnp.float32)
        probs = jnp.where(causal, scores, 0.0).astype(jnp.bfloat16)
        grad_scores = lax.dot_general(d, v, _ROWS_MINOR, preferred_element_type=jnp.float32)
        grad_probs = jnp.where(causal, grad_scores, 0.0).astype(jnp.bfloat16)
        dk = lax.dot_general(grad_probs, q, _ROWS_MAJOR, preferred_element_type=jnp.float32)
        dk = dk + lax.dot_general(v, state, _ROWS_MINOR, preferred_element_type=jnp.float32)
        dv = lax.dot_general(probs, d, _ROWS_MAJOR, preferred_element_type=jnp.float32)
        dv = dv + jnp.dot(k, state, preferred_element_type=jnp.float32)
        dk_ref[0, rows, :] = dk.astype(dk_ref.dtype)
        dv_ref[0, rows, :] = dv.astype(dv_ref.dtype)


def per_head_call(kernel, inputs, outputs, flops):
    def spec(shape, per_head):
        if per_head:
            return pl.BlockSpec((1,) + shape[1:], lambda h: (h,) + (0,) * (len(shape) - 1))
        return pl.BlockSpec(shape, lambda h: (0,) * len(shape))

    head_count = inputs[0][0].shape[0]
    in_bytes = sum(x.size * x.dtype.itemsize for x, _ in inputs)
    out_bytes = sum(math.prod(o.shape) * o.dtype.itemsize for o, _ in outputs)
    return pl.pallas_call(
        kernel,
        grid=(head_count,),
        in_specs=[spec(x.shape, h) for x, h in inputs],
        out_specs=[spec(o.shape, h) for o, h in outputs],
        out_shape=[o for o, _ in outputs],
        cost_estimate=pl.CostEstimate(
            flops=flops, transcendentals=0, bytes_accessed=in_bytes + out_bytes
        ),
    )(*[x for x, _ in inputs])


def on_device(queries, keys, values, out_grad, norm_gain, doc_ids):
    head_count, tok_count, head_width = queries.shape
    block_count = doc_ids.shape[0]
    block_len = tok_count // block_count
    block_shape = (head_count, block_count, block_len, head_width)
    highest_precision = lax.Precision.HIGHEST
    key_blocks = keys.reshape(block_shape)
    value_blocks = values.reshape(block_shape)
    gain = norm_gain.reshape(head_count, 1, head_width)
    doc_values = doc_ids.astype(jnp.float32)
    block_pos = jnp.arange(block_count, dtype=jnp.int32)
    same_doc = doc_values[:, None] == doc_values[None, :]
    earlier_mask = (same_doc & (block_pos[None, :] < block_pos[:, None])).astype(jnp.float32)
    later_mask = (same_doc & (block_pos[None, :] > block_pos[:, None])).astype(jnp.float32)
    pair_flops = 2 * head_count * block_count * block_len * block_len * head_width
    full = jax.ShapeDtypeStruct(queries.shape, jnp.bfloat16)
    state_shape = (head_count, block_count, head_width, head_width)
    key_value_block = jnp.einsum(
        "hnid,hnie->hnde", key_blocks, value_blocks, preferred_element_type=jnp.float32
    )
    last_match = (doc_values == doc_values[-1]).astype(jnp.float32)
    device_kv = jnp.einsum("c,hcde->hde", last_match, key_value_block, precision=highest_precision)
    local_prefix = jnp.einsum(
        "bc,hcde->hbde", earlier_mask, key_value_block, precision=highest_precision
    )
    prior_doc, prior_state, _ = segmented_scan(
        doc_values[-1], device_kv, "ctx", False, lambda: jnp.float32(0.0)
    )
    prior_match = (doc_values == prior_doc).astype(jnp.float32)
    entering = prior_match[None, :, None, None] * prior_state[:, None, :, :]
    preceding_states = (local_prefix + entering).astype(jnp.bfloat16)
    (local_sums,) = per_head_call(
        functools.partial(forward_kernel, block_len),
        [(queries, True), (keys, True), (values, True), (out_grad, True), (gain, True),
         (preceding_states, True)],
        [(jax.ShapeDtypeStruct((tok_count, 2), jnp.float32), False)],
        5 * pair_flops // 2,
    )
    feature_count = head_count * head_width * lax.axis_size(("sub", "head"))
    total_sums = lax.psum(local_sums, ("sub", "head"))
    root_mean = jnp.sqrt(total_sums[:, 0] / feature_count + 1e-06)
    inner_mean = total_sums[:, 1] / feature_count
    factor = inner_mean / (root_mean * root_mean)
    coefs = jnp.stack([root_mean, factor], axis=1)
    d_attn, query_grad_block = per_head_call(
        functools.partial(grad_kernel, block_len),
        [(queries, True), (keys, True), (values, True), (out_grad, True), (gain, True),
         (preceding_states, True), (coefs, False)],
        [(full, True), (jax.ShapeDtypeStruct(state_shape, jnp.float32), True)],
        3 * pair_flops,
    )
    first_match = (doc_values == doc_values[0]).astype(jnp.float32)
    device_qd = jnp.einsum(
        "c,hcde->hde", first_match, query_grad_block, precision=highest_precision
    )
    next_doc, next_state, (query_gradient,) = segmented_scan(
        doc_values[0],
        device_qd,
        "ctx",
        True,
        lambda: per_head_call(
            functools.partial(query_grad_kernel, block_len),
            [(keys, True), (values, True), (d_attn, True), (preceding_states, True)],
            [(full, True)],
            5 * pair_flops // 2,
        ),
    )
    local_suffix = jnp.einsum(
        "bc,hcde->hbde", later_mask, query_grad_block, precision=highest_precision
    )
    next_match = (doc_values == next_doc).astype(jnp.float32)
    leaving = next_match[None, :, None, None] * next_state[:, None, :, :]
    following_states = (local_suffix + leaving).astype(jnp.bfloat16)
    key_gradient, value_gradient = per_head_call(
        functools.partial(key_value_grad_kernel, block_len),
        [(queries, True), (keys, True), (values, True), (d_attn, True),
         (following_states, True)],
        [(full, True), (full, True)],
        5 * pair_flops,
    )
    return query_gradient, key_gradient, value_gradient


def solution(mesh):
    return jax.shard_map(
        on_device,
        mesh=mesh,
        in_specs=(
            P(("sub", "head"), ("groups", "ctx"), None),
            P(("sub", "head"), ("groups", "ctx"), None),
            P(("sub", "head"), ("groups", "ctx"), None),
            P(("sub", "head"), ("groups", "ctx"), None),
            P(("sub", "head"), None),
            P(("groups", "ctx")),
        ),
        out_specs=(
            P(("sub", "head"), ("groups", "ctx"), None),
            P(("sub", "head"), ("groups", "ctx"), None),
            P(("sub", "head"), ("groups", "ctx"), None),
        ),
        check_vma=False,
    )
```

time: 174 us -> 200 us (1.15)
  waiting for transfers between devices: 39.6 us -> 55.6 us
  Pallas kernels: 46.2 us -> 55.1 us
  blocking collectives: 10.3 us -> 18 us
  local copies, waits for them, and re-layouts: 12.8 us -> 9.71 us
    ppermute x4, waiting for transfers between devices: 39.6 us -> 55.6 us  [shift(): got = lax.ppermute(jnp.concatenate([value_state, row], axis=1), axis, pairs)]
    pallas_call x4, Pallas kernels: 46.2 us -> 55.1 us  [per_head_call(): pl.pallas_call(kernel, grid=(head_count,), in_specs=[spec(x.shape, h) for...]
    psum x1, blocking collectives: 10.3 us -> 18 us  [on_device(): total_sums = lax.psum(local_sums, ('sub', 'head'))]
    dot_general x1 -> x0, local copies, waits for them, and re-layouts: 3.71 us -> none  [on_device(): jnp.einsum('hnid,hnie->hnde', query_blocks, output_grad_blocks, preferred...]
    reduce_sum x1 -> x0, other arithmetic: 3.66 us -> none  [on_device(): jnp.sum(raw_attn * raw_attn, axis=(0, 2))]
    convert_element_type x1 -> x0, other arithmetic: 3.46 us -> none  [on_device(): d_attn = ((scaled - raw_attn * factor[None, :, None]) / root_mean[None, :...]
    add x4, other arithmetic: 2.33 us -> 4.42 us  [combine(): return (near_doc, near_state + joined * far_state)]
  transfers between devices with their start and end apart: 4 -> 4, of which waited for: 4 -> 4; matrix products, arithmetic and copies ran while one was open for 7% -> 5% of each run, Pallas kernels for 16% -> 5%
where the time goes in v4:
time: 200 us; the launch traced here: 199 us
  waiting for transfers between devices  55.6 us (28%)
  Pallas kernels  55.1 us (28%)
  matrix products  24 us (12%)
  other arithmetic  18 us (9%)
  blocking collectives  18 us (9%)
  starting transfers between devices  14.2 us (7%)
  local copies, waits for them, and re-layouts  9.71 us (5%)
  between operations  4.51 us (2%)
    ppermute x4, waiting for transfers between devices, shift(): got = lax.ppermute(jnp.concatenate([value_state, row], axis=1), axis, pairs)  55.6 us
    pallas_call x4, Pallas kernels, per_head_call(): pl.pallas_call(kernel, grid=(head_count,), in_specs=[spec(x.shape, h) for...  55.1 us
    psum x1, blocking collectives, on_device(): total_sums = lax.psum(local_sums, ('sub', 'head'))  18 us
    ppermute x4, starting transfers between devices, shift(): got = lax.ppermute(jnp.concatenate([value_state, row], axis=1), axis, pairs)  14.2 us
    dot_general x1, matrix products, on_device(): jnp.einsum('c,hcde->hde', first_match, query_grad_block, precision=highes...  5.68 us
    dot_general x1, matrix products, on_device(): jnp.einsum('bc,hcde->hbde', earlier_mask, key_value_block, precision=high...  5.41 us
    dot_general x1, matrix products, on_device(): jnp.einsum('bc,hcde->hbde', later_mask, query_grad_block, precision=highe...  5.41 us
    add x4, other arithmetic, combine(): return (near_doc, near_state + joined * far_state)  4.42 us
  transfers between devices with their start and end apart: 4, of which 4 were waited for; matrix products, arithmetic and copies ran while one was open for 5% of the time, Pallas kernels for 5%

profile of v4, /device:TPU:0, one launch (start us, length us, event | category | flops | bytes accessed | tf_op | source)
XLA Modules:
  0.0 199.3 jit_solution(18238817809437989965)
XLA Ops:
  0.6 0.7 convert_element_type.31
  1.3 0.6 fusion.33
  1.9 0.0 copy-start.5
  1.9 3.4 %fusion.34 = f32[8,5,128,128]{3,2,1,0:T(8,128)S(1)} fusion(bf16[8,5,256,128]{3,2,1,0:T(8,128)(2,1)} %bitcast.45, bf16[8,5,256,128]{3,2,1,0:T(8,128)(2,1)} %bitcast.46), kind=kOutput, calls=%fused_computation.49 | convolution fusion | flops 335544320 | bytes 7864320 | tf_op jit(solution)/shard_map/hnid,hnie->hnde/dot_general | solution.py:165
  5.3 0.0 copy-done.5
  5.3 4.1 %fusion.4 = f32[1,8,128,128]{3,0,2,1:T(1,128)S(1)} fusion(f32[8,5,128,128]{3,2,1,0:T(8,128)S(1)} %fusion.34, f32[]{:T(128)} %bitcast.7, s32[5]{0:T(128)S(1)} %copy-done.5), kind=kOutput, calls=%fused_computation.4 | convolution fusion | flops 7864330 | bytes 3145752 | tf_op jit(solution)/shard_map/c,hcde->hde/dot_general | solution.py:169
  9.4 1.5 concatenate.12
  10.9 5.7 %collective-permute-start = (f32[8,136,128]{2,1,0:T(8,128)}, f32[8,136,128]{2,1,0:T(8,128)}, u32[]{:S(2)}, u32[]{:S(2)}) collective-permute-start(f32[8,136,128]{2,1,0:T(8,128)} %concatenate.12), channel_id=1, source_target_pairs={{0,4},{4,8},{8,12},{1,5},{5,9},{9,13},{2,6},{6,10},{10,14},{3,7},{... | collective-permute-start | bytes 1671176 | tf_op jit(solution)/shard_map/ppermute | solution.py:26
  16.7 11.4 %collective-permute-done = f32[8,136,128]{2,1,0:T(8,128)} collective-permute-done((f32[8,136,128]{2,1,0:T(8,128)}, f32[8,136,128]{2,1,0:T(8,128)}, u32[]{:S(2)}, u32[]{:S(2)}) %collective-permute-start) | collective-permute-done | bytes 557088 | tf_op jit(solution)/shard_map/ppermute | solution.py:26
  28.0 1.2 slice.50
  29.9 1.9 slice_select_fusion.3
  32.4 1.1 multiply_add_fusion.1
  33.5 0.7 concatenate.13
  34.2 0.0 copy-start.2
  34.2 5.6 %collective-permute-start.1 = (f32[8,136,128]{2,1,0:T(8,128)S(1)}, f32[8,136,128]{2,1,0:T(8,128)S(1)}, u32[]{:S(2)}, u32[]{:S(2)}) collective-permute-start(f32[8,136,128]{2,1,0:T(8,128)S(1)} %concatenate.13), channel_id=1, source_target_pairs={{0,8},{4,12},{1,9},{5,13},{2,10},{6,14},{3,11},{7,15},{16,24},{20,... | collective-permute-start | bytes 1671176 | tf_op jit(solution)/shard_map/ppermute | solution.py:26
  39.8 5.4 %fusion.6 = f32[8,128,128,5]{2,3,1,0:T(8,128)} fusion(f32[8,5,128,128]{3,2,1,0:T(8,128)S(1)} %fusion.34, f32[5]{0:T(128)S(1)} %convert_element_type.31), kind=kOutput, calls=%fused_computation.6 | convolution fusion | flops 39321676 | bytes 5242900 | tf_op jit(solution)/shard_map/bc,hcde->hbde/dot_general | solution.py:170
  45.2 5.6 %collective-permute-done.1 = f32[8,136,128]{2,1,0:T(8,128)S(1)} collective-permute-done((f32[8,136,128]{2,1,0:T(8,128)S(1)}, f32[8,136,128]{2,1,0:T(8,128)S(1)}, u32[]{:S(2)}, u32[]{:S(2)}) %collective-permute-start.1) | collective-permute-done | bytes 557088 | tf_op jit(solution)/shard_map/ppermute | solution.py:26
  50.8 0.0 copy-start.4
  50.8 0.8 copy-done.4
  51.6 0.5 slice.52
  52.8 0.0 copy-done.2
  52.8 1.1 fusion.16
  53.9 3.9 %fusion.9.s_ref = bf16[8,5,128,128]{3,2,1,0:T(8,128)(2,1)} fusion(f32[8,128,128,5]{2,3,1,0:T(8,128)} %fusion.6, f32[8,128,128]{2,1,0:T(8,128)S(1)} %fusion.16, f32[5]{0:T(128)S(1)} %compare_convert_fusion.1), kind=kLoop, calls=%fused_computation.11 | loop fusion | flops 1966080 | bytes 4456468 | tf_op jit(solution)/shard_map/convert_element_type | solution.py:178
  57.8 11.4 %shard_map.85 = f32[1280,2]{1,0:T(8,128)} custom-call(bf16[8,1280,128]{2,1,0:T(8,128)(2,1)} %q_ref.5, bf16[8,1280,128]{2,1,0:T(8,128)(2,1)} %k_ref.7, bf16[8,1280,128]{2,1,0:T(8,128)(2,1)} %v_ref.7, bf16[8,1280,128]{2,1,0:T(8,128)(2,1)} %g_ref.3, f32[8,1,128]{2,1,0:T(1,128)} %bitcast.51, bf16[8,5,128,128]{3,2,1,0:T(8,128)(2,1)} %fusion.9.s_ref), custom_call_target="tpu_custom_call" | custom-call | flops 1677721600 | bytes 11810816 | tf_op jit(solution)/shard_map/pallas_call | solution.py:136
  69.2 18.0 %psum.7 = f32[1280,2]{1,0:T(8,128)S(1)} all-reduce(f32[1280,2]{1,0:T(8,128)} %shard_map.85), channel_id=1, replica_groups=mesh['groups'=2,'ctx'=4,'sub'=2,'head'=2] {'sub','head'}, use_global_device_ids=true, to_apply=%region_0.1 | all-reduce | flops 2560 | bytes 20480 | tf_op jit(solution)/shard_map/psum | solution.py:187
  87.1 0.3 fusion.12
  87.5 1.1 pad_maximum_fusion.c_ref
  88.5 17.1 %shard_map.86 = (bf16[8,1280,128]{2,1,0:T(8,128)(2,1)}, f32[8,5,128,128]{3,2,1,0:T(8,128)}) custom-call(bf16[8,1280,128]{2,1,0:T(8,128)(2,1)} %q_ref.5, bf16[8,1280,128]{2,1,0:T(8,128)(2,1)} %k_ref.7, bf16[8,1280,128]{2,1,0:T(8,128)(2,1)} %v_ref.7, bf16[8,1280,128]{2,1,0:T(8,128)(2,1)} %g_ref.3, f32[8,1,128]{2,1,0:T(1,128)} %bitcast.52, ...), custom_call_target="tpu_custom_call" | custom-call | flops 2013265920 | bytes 17053696 | tf_op jit(solution)/shard_map/pallas_call | solution.py:136
  105.7 5.7 %fusion = f32[1,8,128,128]{3,0,2,1:T(1,128)S(1)} fusion(f32[8,5,128,128]{3,2,1,0:T(8,128)} %get-tuple-element.14, f32[]{:T(128)} %bitcast.15, s32[5]{0:T(128)S(1)} %copy-done.5), kind=kOutput, calls=%fused_computation | convolution fusion | flops 7864330 | bytes 3145752 | tf_op jit(solution)/shard_map/c,hcde->hde/dot_general | solution.py:200
  111.4 1.4 concatenate.14
  112.7 1.3 collective-permute-start.2
  114.0 10.3 %shard_map.87 = bf16[8,1280,128]{2,1,0:T(8,128)(2,1)} custom-call(bf16[8,1280,128]{2,1,0:T(8,128)(2,1)} %k_ref.7, bf16[8,1280,128]{2,1,0:T(8,128)(2,1)} %v_ref.7, bf16[8,1280,128]{2,1,0:T(8,128)(2,1)} %get-tuple-element.15.d_ref, bf16[8,5,128,128]{3,2,1,0:T(8,128)(2,1)} %fusion.9.s_ref), custom_call_target="tpu_custom_call" | custom-call | flops 1677721600 | bytes 11796480 | tf_op jit(solution)/shard_map/pallas_call | solution.py:136
  124.3 17.2 %collective-permute-done.2 = f32[8,136,128]{2,1,0:T(8,128)} collective-permute-done((f32[8,136,128]{2,1,0:T(8,128)}, f32[8,136,128]{2,1,0:T(8,128)}, u32[]{:S(2)}, u32[]{:S(2)}) %collective-permute-start.2) | collective-permute-done | bytes 557088 | tf_op jit(solution)/shard_map/ppermute | solution.py:26
  141.5 1.2 slice.56
  143.3 1.9 slice_select_fusion.1
  145.8 1.1 multiply_add_fusion
  146.9 0.6 concatenate.15
  147.5 0.0 copy-start.1
  147.5 1.6 collective-permute-start.3
  149.1 0.0 copy-done
  149.1 5.4 %fusion.2 = f32[8,128,128,5]{2,3,1,0:T(8,128)} fusion(f32[8,5,128,128]{3,2,1,0:T(8,128)S(1)} %copy-done, f32[5]{0:T(128)S(1)} %convert_element_type.31), kind=kOutput, calls=%fused_computation.2 | convolution fusion | flops 39321676 | bytes 5242900 | tf_op jit(solution)/shard_map/bc,hcde->hbde/dot_general | solution.py:215
  154.5 21.5 %collective-permute-done.3 = f32[8,136,128]{2,1,0:T(8,128)S(1)} collective-permute-done((f32[8,136,128]{2,1,0:T(8,128)S(1)}, f32[8,136,128]{2,1,0:T(8,128)S(1)}, u32[]{:S(2)}, u32[]{:S(2)}) %collective-permute-start.3) | collective-permute-done | bytes 557088 | tf_op jit(solution)/shard_map/ppermute | solution.py:26
  176.1 0.8 copy-done.3
  176.9 0.5 slice.58
  177.9 0.0 copy-done.1
  177.9 1.1 fusion.14
  179.0 3.9 %fusion.8.s_ref = bf16[8,5,128,128]{3,2,1,0:T(8,128)(2,1)} fusion(f32[8,128,128,5]{2,3,1,0:T(8,128)} %fusion.2, f32[8,128,128]{2,1,0:T(8,128)S(1)} %fusion.14, f32[5]{0:T(128)S(1)} %compare_convert_fusion), kind=kLoop, calls=%fused_computation.9 | loop fusion | flops 1966080 | bytes 4456468 | tf_op jit(solution)/shard_map/convert_element_type | solution.py:220
  182.9 16.3 %shard_map.88 = (bf16[8,1280,128]{2,1,0:T(8,128)(2,1)}, bf16[8,1280,128]{2,1,0:T(8,128)(2,1)}) custom-call(bf16[8,1280,128]{2,1,0:T(8,128)(2,1)} %q_ref.5, bf16[8,1280,128]{2,1,0:T(8,128)(2,1)} %k_ref.7, bf16[8,1280,128]{2,1,0:T(8,128)(2,1)} %v_ref.7, bf16[8,1280,128]{2,1,0:T(8,128)(2,1)} %get-tuple-element.15.d_ref, bf16[8,5,128,128]{3,2,1,0:T(8,128)(2,1)} %fusion.8.s_ref), custom_call_target="tpu_custom_call" | custom-call | flops 3355443200 | bytes 17039360 | tf_op jit(solution)/shard_map/pallas_call | solution.py:136
  (4 shorter events, 0.0 us)
Async XLA Ops:
  1.9 3.4 %copy-start.5 = (s32[5]{0:T(128)S(1)}, s32[5]{0:T(128)}, u32[]{:S(2)}) copy-start(s32[5]{0:T(128)} %param.11) | copy-start | bytes 64
  10.9 17.1 %collective-permute-start = (f32[8,136,128]{2,1,0:T(8,128)}, f32[8,136,128]{2,1,0:T(8,128)}, u32[]{:S(2)}, u32[]{:S(2)}) collective-permute-start(f32[8,136,128]{2,1,0:T(8,128)} %concatenate.12), channel_id=1, source_target_pairs={{0,4},{4,8},{8,12},{1,5},{5,9},{9,13},{2,6},{6,10},{10,14},{3,7},{... | collective-permute-start | bytes 1671176 | tf_op jit(solution)/shard_map/ppermute | solution.py:26
  34.2 18.6 %copy-start.2 = (f32[8,128,128]{2,1,0:T(8,128)S(1)}, f32[8,128,128]{2,1,0:T(8,128)}, u32[]{:S(2)}) copy-start(f32[8,128,128]{2,1,0:T(8,128)} %slice_select_fusion.3) | copy-start | bytes 1572868
  34.2 16.6 %collective-permute-start.1 = (f32[8,136,128]{2,1,0:T(8,128)S(1)}, f32[8,136,128]{2,1,0:T(8,128)S(1)}, u32[]{:S(2)}, u32[]{:S(2)}) collective-permute-start(f32[8,136,128]{2,1,0:T(8,128)S(1)} %concatenate.13), channel_id=1, source_target_pairs={{0,8},{4,12},{1,9},{5,13},{2,10},{6,14},{3,11},{7,15},{16,24},{20,... | collective-permute-start | bytes 1671176 | tf_op jit(solution)/shard_map/ppermute | solution.py:26
  50.8 0.8 copy-start.4
  112.7 28.7 %collective-permute-start.2 = (f32[8,136,128]{2,1,0:T(8,128)}, f32[8,136,128]{2,1,0:T(8,128)}, u32[]{:S(2)}, u32[]{:S(2)}) collective-permute-start(f32[8,136,128]{2,1,0:T(8,128)} %concatenate.14), channel_id=1, source_target_pairs={{4,0},{8,4},{12,8},{5,1},{9,5},{13,9},{6,2},{10,6},{14,10},{7,3},{... | collective-permute-start | bytes 1671176 | tf_op jit(solution)/shard_map/ppermute | solution.py:26
  124.3 24.8 %copy-start = (f32[8,5,128,128]{3,2,1,0:T(8,128)S(1)}, f32[8,5,128,128]{3,2,1,0:T(8,128)}, u32[]{:S(2)}) copy-start(f32[8,5,128,128]{3,2,1,0:T(8,128)} %get-tuple-element.14) | copy-start | bytes 7864324
  147.5 30.4 %copy-start.1 = (f32[8,128,128]{2,1,0:T(8,128)S(1)}, f32[8,128,128]{2,1,0:T(8,128)}, u32[]{:S(2)}) copy-start(f32[8,128,128]{2,1,0:T(8,128)} %slice_select_fusion.1) | copy-start | bytes 1572868
  147.5 28.6 %collective-permute-start.3 = (f32[8,136,128]{2,1,0:T(8,128)S(1)}, f32[8,136,128]{2,1,0:T(8,128)S(1)}, u32[]{:S(2)}, u32[]{:S(2)}) collective-permute-start(f32[8,136,128]{2,1,0:T(8,128)S(1)} %concatenate.15), channel_id=1, source_target_pairs={{8,0},{12,4},{9,1},{13,5},{10,2},{14,6},{11,3},{15,7},{24,16},{28,... | collective-permute-start | bytes 1671176 | tf_op jit(solution)/shard_map/ppermute | solution.py:26
  176.1 0.8 copy-start.3

commit v5 on v4

--- a/solution.py
+++ b/solution.py
@@ -11,41 +11,58 @@
 _ROWS_MAJOR = (((0,), (0,)), ((), ()))
 
 
-def segmented_scan(doc, state, axis, reverse, cover):
+def segmented_scan(doc, state, axis, reverse, reach, cover):
     peers = lax.axis_size(axis)
     index = lax.axis_index(axis)
     none_doc = jnp.float32(-1.0)
-    pad = jnp.broadcast_to(doc, (state.shape[0], 8, state.shape[2])).astype(jnp.float32)
-
-    def shift(value_doc, value_state, step):
+    rows = state.shape[1]
+    reach = min(reach, peers - 1)
+
+    def pack(value_doc, value_state):
+        row = jnp.broadcast_to(value_doc, (state.shape[0], 8, state.shape[2]))
+        return jnp.concatenate([value_state, row.astype(jnp.float32)], axis=1)
+
+    def shift(packed, step):
         if reverse:
             pairs = [(j, j - step) for j in range(step, peers)]
         else:
             pairs = [(j, j + step) for j in range(peers - step)]
-        row = jnp.broadcast_to(value_doc, pad.shape)
-        got = lax.ppermute(jnp.concatenate([value_state, row], axis=1), axis, pairs)
+        return lax.ppermute(packed, axis, pairs), step
+
+    def unpack(got):
+        got, step = got
         valid = (index <= peers - 1 - step) if reverse else (index >= step)
-        got_doc = jnp.where(valid, got[0, state.shape[1], 0], none_doc)
-        got_state = jnp.where(valid, got[:, : state.shape[1]], 0.0)
+        got_doc = jnp.where(valid, got[0, rows, 0], none_doc)
+        got_state = jnp.where(valid, got[:, :rows], 0.0)
         return got_doc, got_state
 
     def combine(near_doc, near_state, far_doc, far_state):
         joined = (near_doc == far_doc).astype(jnp.float32)
         return near_doc, near_state + joined * far_state
 
-    if peers == 1:
+    if reach < 1:
         return none_doc, jnp.zeros_like(state), cover()
-    got_doc, got_state = shift(doc, state, 1)
+    packed = pack(doc, state)
+    if reach <= 2:
+        arrivals = [shift(packed, step) for step in range(1, reach + 1)]
+        covered_value = cover()
+        arrivals, covered_value = lax.optimization_barrier((arrivals, covered_value))
+        ex_doc, ex_state = unpack(arrivals[0])
+        for got in arrivals[1:]:
+            ex_doc, ex_state = combine(ex_doc, ex_state, *unpack(got))
+        return ex_doc, ex_state, covered_value
+    got = shift(packed, 1)
     covered_value = cover()
-    ex_doc, ex_state, covered_value = lax.optimization_barrier((got_doc, got_state, covered_value))
+    got, covered_value = lax.optimization_barrier((got, covered_value))
+    ex_doc, ex_state = unpack(got)
     in_doc, in_state = combine(doc, state, ex_doc, ex_state)
     covered = 1
-    while covered < peers - 1:
+    while covered < reach:
         step = covered + 1
-        got_doc, got_state = shift(in_doc, in_state, step)
+        got_doc, got_state = unpack(shift(pack(in_doc, in_state), step))
         ex_doc, ex_state = combine(ex_doc, ex_state, got_doc, got_state)
         covered = covered + step
-        if covered < peers - 1:
+        if covered < reach:
             in_doc, in_state = combine(in_doc, in_state, got_doc, got_state)
     return ex_doc, ex_state, covered_value
 
@@ -63,17 +80,26 @@
     return raw + jnp.dot(q, state, preferred_element_type=jnp.float32)
 
 
-def forward_kernel(block_len, q_ref, k_ref, v_ref, g_ref, n_ref, s_ref, o_ref):
+def intra_kernel(block_len, q_ref, k_ref, v_ref, o_ref):
     causal = _causal(block_len)
-
+    for n in range(q_ref.shape[1] // block_len):
+        rows = pl.ds(n * block_len, block_len)
+        q, k, v = q_ref[0, rows, :], k_ref[0, rows, :], v_ref[0, rows, :]
+        scores = lax.dot_general(q, k, _ROWS_MINOR, preferred_element_type=jnp.float32)
+        probs = jnp.where(causal, scores, 0.0).astype(jnp.bfloat16)
+        o_ref[0, rows, :] = jnp.dot(probs, v, preferred_element_type=jnp.float32)
+
+
+def forward_kernel(block_len, i_ref, q_ref, g_ref, n_ref, s_ref, o_ref):
     @pl.when(pl.program_id(0) == 0)
     def _():
         o_ref[...] = jnp.zeros_like(o_ref)
 
     for n in range(q_ref.shape[1] // block_len):
         rows = pl.ds(n * block_len, block_len)
-        q, k, v = q_ref[0, rows, :], k_ref[0, rows, :], v_ref[0, rows, :]
-        raw = _raw_block(causal, q, k, v, s_ref[0, n])
+        raw = i_ref[0, rows, :] + jnp.dot(
+            q_ref[0, rows, :], s_ref[0, n], preferred_element_type=jnp.float32
+        )
         scaled = n_ref[0] * g_ref[0, rows, :].astype(jnp.float32)
         o_ref[rows, 0:1] += jnp.sum(raw * raw, axis=1, keepdims=True)
         o_ref[rows, 1:2] += jnp.sum(scaled * raw, axis=1, keepdims=True)
@@ -93,33 +119,37 @@
         qd_ref[0, n] = lax.dot_general(q, d, _ROWS_MAJOR, preferred_element_type=jnp.float32)
 
 
-def query_grad_kernel(block_len, k_ref, v_ref, d_ref, s_ref, dq_ref):
+def query_grad_kernel(block_len, q_ref, k_ref, v_ref, d_ref, s_ref, dq_ref, dk_ref, dv_ref):
     causal = _causal(block_len)
     for n in range(k_ref.shape[1] // block_len):
         rows = pl.ds(n * block_len, block_len)
-        k, v, d = k_ref[0, rows, :], v_ref[0, rows, :], d_ref[0, rows, :]
+        q, k, v = q_ref[0, rows, :], k_ref[0, rows, :], v_ref[0, rows, :]
+        d = d_ref[0, rows, :]
+        scores = lax.dot_general(q, k, _ROWS_MINOR, preferred_element_type=jnp.float32)
+        probs = jnp.where(causal, scores, 0.0).astype(jnp.bfloat16)
         grad_scores = lax.dot_general(d, v, _ROWS_MINOR, preferred_element_type=jnp.float32)
         grad_probs = jnp.where(causal, grad_scores, 0.0).astype(jnp.bfloat16)
         dq = jnp.dot(grad_probs, k, preferred_element_type=jnp.float32)
         dq = dq + lax.dot_general(d, s_ref[0, n], _ROWS_MINOR, preferred_element_type=jnp.float32)
         dq_ref[0, rows, :] = dq.astype(dq_ref.dtype)
-
-
-def key_value_grad_kernel(block_len, q_ref, k_ref, v_ref, d_ref, s_ref, dk_ref, dv_ref):
-    causal = _causal(block_len)
-    for n in range(q_ref.shape[1] // block_len):
-        rows = pl.ds(n * block_len, block_len)
-        q, k, v = q_ref[0, rows, :], k_ref[0, rows, :], v_ref[0, rows, :]
-        d = d_ref[0, rows, :]
+        dk_ref[0, rows, :] = lax.dot_general(
+            grad_probs, q, _ROWS_MAJOR, preferred_element_type=jnp.float32
+        )
+        dv_ref[0, rows, :] = lax.dot_general(
+            probs, d, _ROWS_MAJOR, preferred_element_type=jnp.float32
+        )
+
+
+def key_value_grad_kernel(block_len, ik_ref, iv_ref, k_ref, v_ref, s_ref, dk_ref, dv_ref):
+    for n in range(k_ref.shape[1] // block_len):
+        rows = pl.ds(n * block_len, block_len)
         state = s_ref[0, n]
-        scores = lax.dot_general(q, k, _ROWS_MINOR, preferred_element_type=jnp.float32)
-        probs = jnp.where(causal, scores, 0.0).astype(jnp.bfloat16)
-        grad_scores = lax.dot_general(d, v, _ROWS_MINOR, preferred_element_type=jnp.float32)
-        grad_probs = jnp.where(causal, grad_scores, 0.0).astype(jnp.bfloat16)
-        dk = lax.dot_general(grad_probs, q, _ROWS_MAJOR, preferred_element_type=jnp.float32)
-        dk = dk + lax.dot_general(v, state, _ROWS_MINOR, preferred_element_type=jnp.float32)
-        dv = lax.dot_general(probs, d, _ROWS_MAJOR, preferred_element_type=jnp.float32)
-        dv = dv + jnp.dot(k, state, preferred_element_type=jnp.float32)
+        dk = ik_ref[0, rows, :] + lax.dot_general(
+            v_ref[0, rows, :], state, _ROWS_MINOR, preferred_element_type=jnp.float32
+        )
+        dv = iv_ref[0, rows, :] + jnp.dot(
+            k_ref[0, rows, :], state, preferred_element_type=jnp.float32
+        )
         dk_ref[0, rows, :] = dk.astype(dk_ref.dtype)
         dv_ref[0, rows, :] = dv.astype(dv_ref.dtype)
 
@@ -170,18 +200,32 @@
     local_prefix = jnp.einsum(
         "bc,hcde->hbde", earlier_mask, key_value_block, precision=highest_precision
     )
-    prior_doc, prior_state, _ = segmented_scan(
-        doc_values[-1], device_kv, "ctx", False, lambda: jnp.float32(0.0)
+    ctx_size = lax.axis_size("ctx")
+    longest_doc = ctx_size * block_count // 2
+    reach = (longest_doc - 2) // block_count + 1
+    intra_shape = jax.ShapeDtypeStruct(queries.shape, jnp.float32)
+    prior_doc, prior_state, intra_part = segmented_scan(
+        doc_values[-1],
+        device_kv,
+        "ctx",
+        False,
+        reach,
+        lambda: per_head_call(
+            functools.partial(intra_kernel, block_len),
+            [(queries, True), (keys, True), (values, True)],
+            [(intra_shape, True)],
+            2 * pair_flops,
+        )[0],
     )
     prior_match = (doc_values == prior_doc).astype(jnp.float32)
     entering = prior_match[None, :, None, None] * prior_state[:, None, :, :]
     preceding_states = (local_prefix + entering).astype(jnp.bfloat16)
     (local_sums,) = per_head_call(
         functools.partial(forward_kernel, block_len),
-        [(queries, True), (keys, True), (values, True), (out_grad, True), (gain, True),
+        [(intra_part, True), (queries, True), (out_grad, True), (gain, True),
          (preceding_states, True)],
         [(jax.ShapeDtypeStruct((tok_count, 2), jnp.float32), False)],
-        5 * pair_flops // 2,
+        pair_flops // 2,
     )
     feature_count = head_count * head_width * lax.axis_size(("sub", "head"))
     total_sums = lax.psum(local_sums, ("sub", "head"))
@@ -200,16 +244,18 @@
     device_qd = jnp.einsum(
         "c,hcde->hde", first_match, query_grad_block, precision=highest_precision
     )
-    next_doc, next_state, (query_gradient,) = segmented_scan(
+    next_doc, next_state, (query_gradient, key_intra, value_intra) = segmented_scan(
         doc_values[0],
         device_qd,
         "ctx",
         True,
+        reach,
         lambda: per_head_call(
             functools.partial(query_grad_kernel, block_len),
-            [(keys, True), (values, True), (d_attn, True), (preceding_states, True)],
-            [(full, True)],
-            5 * pair_flops // 2,
+            [(queries, True), (keys, True), (values, True), (d_attn, True),
+             (preceding_states, True)],
+            [(full, True), (intra_shape, True), (intra_shape, True)],
+            5 * pair_flops,
         ),
     )
     local_suffix = jnp.einsum(
@@ -220,10 +266,10 @@
     following_states = (local_suffix + leaving).astype(jnp.bfloat16)
     key_gradient, value_gradient = per_head_call(
         functools.partial(key_value_grad_kernel, block_len),
-        [(queries, True), (keys, True), (values, True), (d_attn, True),
+        [(key_intra, True), (value_intra, True), (keys, True), (values, True),
          (following_states, True)],
         [(full, True), (full, True)],
-        5 * pair_flops,
+        pair_flops,
     )
     return query_gradient, key_gradient, value_gradient
 

time: 200 us -> 174 us (0.87)
  waiting for transfers between devices: 55.6 us -> 30.8 us
  Pallas kernels: 55.1 us -> 64.3 us
  other arithmetic: 18 us -> 12.4 us
  local copies, waits for them, and re-layouts: 9.71 us -> 6.68 us
    ppermute x4, waiting for transfers between devices: 55.6 us -> 30.8 us  [shift(): return (lax.ppermute(packed, axis, pairs), step)]
    pallas_call x4 -> x5, Pallas kernels: 55.1 us -> 64.3 us  [per_head_call(): pl.pallas_call(kernel, grid=(head_count,), in_specs=[spec(x.shape, h) for...]
    select_n x2 -> x0, other arithmetic: 3.76 us -> none  [shift(): got_state = jnp.where(valid, got[:, :state.shape[1]], 0.0)]
    concatenate x4 -> x2, local copies, waits for them, and re-layouts: 4.14 us -> 1.34 us  [pack(): return jnp.concatenate([value_state, row.astype(jnp.float32)], axis=1)]
    add x4 -> x2, other arithmetic: 4.42 us -> 2.56 us  [combine(): return (near_doc, near_state + joined * far_state)]
  transfers between devices with their start and end apart: 4 -> 4, of which waited for: 4 -> 3; matrix products, arithmetic and copies ran while one was open for 5% -> 6% of each run, Pallas kernels for 5% -> 16%
where the time goes in v5:
time: 174 us; the launch traced here: 173 us
  Pallas kernels  64.3 us (37%)
  waiting for transfers between devices  30.8 us (18%)
  matrix products  24.3 us (14%)
  blocking collectives  18 us (10%)
  starting transfers between devices  13.1 us (8%)
  other arithmetic  12.4 us (7%)
  local copies, waits for them, and re-layouts  6.68 us (4%)
  between operations  3.36 us (2%)
    pallas_call x5, Pallas kernels, per_head_call(): pl.pallas_call(kernel, grid=(head_count,), in_specs=[spec(x.shape, h) for...  64.3 us
    ppermute x4, waiting for transfers between devices, shift(): return (lax.ppermute(packed, axis, pairs), step)  30.8 us
    psum x1, blocking collectives, on_device(): total_sums = lax.psum(local_sums, ('sub', 'head'))  18 us
    ppermute x4, starting transfers between devices, shift(): return (lax.ppermute(packed, axis, pairs), step)  13.1 us
    dot_general x1, matrix products, on_device(): jnp.einsum('c,hcde->hde', first_match, query_grad_block, precision=highes...  5.75 us
    dot_general x1, matrix products, on_device(): jnp.einsum('bc,hcde->hbde', later_mask, query_grad_block, precision=highe...  5.51 us
    dot_general x1, matrix products, on_device(): jnp.einsum('bc,hcde->hbde', earlier_mask, key_value_block, precision=high...  5.48 us
    slice x4, local copies, waits for them, and re-layouts, unpack(): got_doc = jnp.where(valid, got[0, rows, 0], none_doc)  4.75 us
  transfers between devices with their start and end apart: 4, of which 3 were waited for; matrix products, arithmetic and copies ran while one was open for 6% of the time, Pallas kernels for 16%

profile of v5, /device:TPU:0, one launch (start us, length us, event | category | flops | bytes accessed | tf_op | source)
XLA Modules:
  0.0 172.9 jit_solution(9590566044225725786)
XLA Ops:
  0.6 0.7 convert_element_type.25
  1.3 0.6 fusion.29
  1.9 0.0 copy-start.1
  1.9 3.4 %fusion.30 = f32[8,5,128,128]{3,2,1,0:T(8,128)S(1)} fusion(bf16[8,5,256,128]{3,2,1,0:T(8,128)(2,1)} %bitcast.45, bf16[8,5,256,128]{3,2,1,0:T(8,128)(2,1)} %bitcast.46), kind=kOutput, calls=%fused_computation.41 | convolution fusion | flops 335544320 | bytes 7864320 | tf_op jit(solution)/shard_map/hnid,hnie->hnde/dot_general | solution.py:195
  5.3 0.0 copy-done.1
  5.3 4.1 %fusion.4 = f32[1,8,128,128]{3,0,2,1:T(1,128)S(1)} fusion(f32[8,5,128,128]{3,2,1,0:T(8,128)S(1)} %fusion.30, f32[]{:T(128)} %bitcast.7, s32[5]{0:T(128)S(1)} %copy-done.1), kind=kOutput, calls=%fused_computation.4 | convolution fusion | flops 7864330 | bytes 3145752 | tf_op jit(solution)/shard_map/c,hcde->hde/dot_general | solution.py:199
  9.4 0.7 concatenate.6
  10.1 5.8 %collective-permute-start = (f32[8,136,128]{2,1,0:T(8,128)S(1)}, f32[8,136,128]{2,1,0:T(8,128)}, u32[]{:S(2)}, u32[]{:S(2)}) collective-permute-start(f32[8,136,128]{2,1,0:T(8,128)S(1)} %concatenate.6), channel_id=1, source_target_pairs={{0,4},{4,8},{8,12},{1,5},{5,9},{9,13},{2,6},{6,10},{10,14},{3,7},{... | collective-permute-start | bytes 1671176 | tf_op jit(solution)/shard_map/ppermute | solution.py:30
  15.9 4.5 %collective-permute-start.1 = (f32[8,136,128]{2,1,0:T(8,128)S(1)}, f32[8,136,128]{2,1,0:T(8,128)}, u32[]{:S(2)}, u32[]{:S(2)}) collective-permute-start(f32[8,136,128]{2,1,0:T(8,128)S(1)} %concatenate.6), channel_id=1, source_target_pairs={{0,8},{4,12},{1,9},{5,13},{2,10},{6,14},{3,11},{7,15},{16,24},{20,... | collective-permute-start | bytes 1671176 | tf_op jit(solution)/shard_map/ppermute | solution.py:30
  20.4 10.1 %shard_map.85.i_ref = f32[8,1280,128]{2,1,0:T(8,128)} custom-call(bf16[8,1280,128]{2,1,0:T(8,128)(2,1)} %q_ref.7, bf16[8,1280,128]{2,1,0:T(8,128)(2,1)} %k_ref.7, bf16[8,1280,128]{2,1,0:T(8,128)(2,1)} %v_ref.7), custom_call_target="tpu_custom_call" | custom-call | flops 1342177280 | bytes 13107200 | tf_op jit(solution)/shard_map/pallas_call | solution.py:166
  30.5 5.5 %fusion.6 = f32[8,128,128,5]{2,3,1,0:T(8,128)} fusion(f32[8,5,128,128]{3,2,1,0:T(8,128)S(1)} %fusion.30, f32[5]{0:T(128)S(1)} %convert_element_type.25), kind=kOutput, calls=%fused_computation.6 | convolution fusion | flops 39321676 | bytes 5242900 | tf_op jit(solution)/shard_map/bc,hcde->hbde/dot_general | solution.py:200
  36.0 0.0 collective-permute-done
  36.0 2.9 %collective-permute-done.1 = f32[8,136,128]{2,1,0:T(8,128)} collective-permute-done((f32[8,136,128]{2,1,0:T(8,128)S(1)}, f32[8,136,128]{2,1,0:T(8,128)}, u32[]{:S(2)}, u32[]{:S(2)}) %collective-permute-start.1) | collective-permute-done | bytes 557088 | tf_op jit(solution)/shard_map/ppermute | solution.py:30
  38.9 1.2 slice.40
  40.1 1.2 slice.42
  42.6 1.3 multiply_add_fusion.1
  43.9 3.9 %fusion.9.s_ref = bf16[8,5,128,128]{3,2,1,0:T(8,128)(2,1)} fusion(f32[8,128,128,5]{2,3,1,0:T(8,128)} %fusion.6, f32[8,128,128]{2,1,0:T(8,128)S(1)} %multiply_add_fusion.1, f32[5]{0:T(128)S(1)} %compare_convert_fusion.1), kind=kLoop, calls=%fused_computation.11 | loop fusion | flops 1966080 | bytes 4456468 | tf_op jit(solution)/shard_map/convert_element_type | solution.py:222
  47.8 9.6 %shard_map.86 = f32[1280,2]{1,0:T(8,128)} custom-call(f32[8,1280,128]{2,1,0:T(8,128)} %shard_map.85.i_ref, bf16[8,1280,128]{2,1,0:T(8,128)(2,1)} %q_ref.7, bf16[8,1280,128]{2,1,0:T(8,128)(2,1)} %g_ref.3, f32[8,1,128]{2,1,0:T(1,128)} %bitcast.49, bf16[8,5,128,128]{3,2,1,0:T(8,128)(2,1)} %fusion.9.s_ref), custom_call_target="tpu_custom_call" | custom-call | flops 335544320 | bytes 11810816 | tf_op jit(solution)/shard_map/pallas_call | solution.py:166
  57.5 18.0 %psum.7 = f32[1280,2]{1,0:T(8,128)S(1)} all-reduce(f32[1280,2]{1,0:T(8,128)} %shard_map.86), channel_id=1, replica_groups=mesh['groups'=2,'ctx'=4,'sub'=2,'head'=2] {'sub','head'}, use_global_device_ids=true, to_apply=%region_0.1 | all-reduce | flops 2560 | bytes 20480 | tf_op jit(solution)/shard_map/psum | solution.py:231
  75.4 0.3 fusion.12
  75.7 1.1 pad_maximum_fusion.c_ref
  76.8 17.1 %shard_map.87 = (bf16[8,1280,128]{2,1,0:T(8,128)(2,1)}, f32[8,5,128,128]{3,2,1,0:T(8,128)}) custom-call(bf16[8,1280,128]{2,1,0:T(8,128)(2,1)} %q_ref.7, bf16[8,1280,128]{2,1,0:T(8,128)(2,1)} %k_ref.7, bf16[8,1280,128]{2,1,0:T(8,128)(2,1)} %v_ref.7, bf16[8,1280,128]{2,1,0:T(8,128)(2,1)} %g_ref.3, f32[8,1,128]{2,1,0:T(1,128)} %bitcast.50, ...), custom_call_target="tpu_custom_call" | custom-call | flops 2013265920 | bytes 17053696 | tf_op jit(solution)/shard_map/pallas_call | solution.py:166
  94.0 5.8 %fusion = f32[1,8,128,128]{3,0,2,1:T(1,128)S(1)} fusion(f32[8,5,128,128]{3,2,1,0:T(8,128)} %get-tuple-element.27, f32[]{:T(128)} %bitcast.15, s32[5]{0:T(128)S(1)} %copy-done.1), kind=kOutput, calls=%fused_computation | convolution fusion | flops 7864330 | bytes 3145752 | tf_op jit(solution)/shard_map/c,hcde->hde/dot_general | solution.py:244
  99.7 0.7 concatenate.7
  100.4 1.3 collective-permute-start.2
  101.7 1.5 collective-permute-start.3
  103.2 0.0 copy-start
  103.2 16.9 %shard_map.88 = (bf16[8,1280,128]{2,1,0:T(8,128)(2,1)}, f32[8,1280,128]{2,1,0:T(8,128)}, f32[8,1280,128]{2,1,0:T(8,128)}) custom-call(bf16[8,1280,128]{2,1,0:T(8,128)(2,1)} %q_ref.7, bf16[8,1280,128]{2,1,0:T(8,128)(2,1)} %k_ref.7, bf16[8,1280,128]{2,1,0:T(8,128)(2,1)} %v_ref.7, bf16[8,1280,128]{2,1,0:T(8,128)(2,1)} %get-tuple-element.28.d_ref, ...), custom_call_target="tpu_custom_call" | custom-call | flops 3355443200 | bytes 24903680 | tf_op jit(solution)/shard_map/pallas_call | solution.py:166
  120.2 0.0 copy-done
  120.2 5.5 %fusion.2 = f32[8,128,128,5]{2,3,1,0:T(8,128)} fusion(f32[8,5,128,128]{3,2,1,0:T(8,128)S(1)} %copy-done, f32[5]{0:T(128)S(1)} %convert_element_type.25), kind=kOutput, calls=%fused_computation.2 | convolution fusion | flops 39321676 | bytes 5242900 | tf_op jit(solution)/shard_map/bc,hcde->hbde/dot_general | solution.py:261
  125.7 2.8 %collective-permute-done.2 = f32[8,136,128]{2,1,0:T(8,128)} collective-permute-done((f32[8,136,128]{2,1,0:T(8,128)S(1)}, f32[8,136,128]{2,1,0:T(8,128)}, u32[]{:S(2)}, u32[]{:S(2)}) %collective-permute-start.2) | collective-permute-done | bytes 557088 | tf_op jit(solution)/shard_map/ppermute | solution.py:30
  128.5 25.0 %collective-permute-done.3 = f32[8,136,128]{2,1,0:T(8,128)} collective-permute-done((f32[8,136,128]{2,1,0:T(8,128)S(1)}, f32[8,136,128]{2,1,0:T(8,128)}, u32[]{:S(2)}, u32[]{:S(2)}) %collective-permute-start.3) | collective-permute-done | bytes 557088 | tf_op jit(solution)/shard_map/ppermute | solution.py:30
  153.6 1.2 slice.48
  154.7 1.2 slice.46
  157.2 1.3 multiply_add_fusion
  158.5 3.9 %fusion.8.s_ref = bf16[8,5,128,128]{3,2,1,0:T(8,128)(2,1)} fusion(f32[8,128,128,5]{2,3,1,0:T(8,128)} %fusion.2, f32[8,128,128]{2,1,0:T(8,128)S(1)} %multiply_add_fusion, f32[5]{0:T(128)S(1)} %compare_convert_fusion), kind=kLoop, calls=%fused_computation.9 | loop fusion | flops 1966080 | bytes 4456468 | tf_op jit(solution)/shard_map/convert_element_type | solution.py:266
  162.4 10.5 %shard_map.89 = (bf16[8,1280,128]{2,1,0:T(8,128)(2,1)}, bf16[8,1280,128]{2,1,0:T(8,128)(2,1)}) custom-call(f32[8,1280,128]{2,1,0:T(8,128)} %get-tuple-element.33.ik_ref, f32[8,1280,128]{2,1,0:T(8,128)} %get-tuple-element.34.iv_ref, bf16[8,1280,128]{2,1,0:T(8,128)(2,1)} %k_ref.7, bf16[8,1280,128]{2,1,0:T(8,128)(2,1)} %v_ref.7, ...), custom_call_target="tpu_custom_call" | custom-call | flops 671088640 | bytes 22282240 | tf_op jit(solution)/shard_map/pallas_call | solution.py:166
  (2 shorter events, 0.0 us)
Async XLA Ops:
  1.9 3.4 %copy-start.1 = (s32[5]{0:T(128)S(1)}, s32[5]{0:T(128)}, u32[]{:S(2)}) copy-start(s32[5]{0:T(128)} %param.11) | copy-start | bytes 64
  10.1 25.9 %collective-permute-start = (f32[8,136,128]{2,1,0:T(8,128)S(1)}, f32[8,136,128]{2,1,0:T(8,128)}, u32[]{:S(2)}, u32[]{:S(2)}) collective-permute-start(f32[8,136,128]{2,1,0:T(8,128)S(1)} %concatenate.6), channel_id=1, source_target_pairs={{0,4},{4,8},{8,12},{1,5},{5,9},{9,13},{2,6},{6,10},{10,14},{3,7},{... | collective-permute-start | bytes 1671176 | tf_op jit(solution)/shard_map/ppermute | solution.py:30
  15.9 23.0 %collective-permute-start.1 = (f32[8,136,128]{2,1,0:T(8,128)S(1)}, f32[8,136,128]{2,1,0:T(8,128)}, u32[]{:S(2)}, u32[]{:S(2)}) collective-permute-start(f32[8,136,128]{2,1,0:T(8,128)S(1)} %concatenate.6), channel_id=1, source_target_pairs={{0,8},{4,12},{1,9},{5,13},{2,10},{6,14},{3,11},{7,15},{16,24},{20,... | collective-permute-start | bytes 1671176 | tf_op jit(solution)/shard_map/ppermute | solution.py:30
  100.4 28.1 %collective-permute-start.2 = (f32[8,136,128]{2,1,0:T(8,128)S(1)}, f32[8,136,128]{2,1,0:T(8,128)}, u32[]{:S(2)}, u32[]{:S(2)}) collective-permute-start(f32[8,136,128]{2,1,0:T(8,128)S(1)} %concatenate.7), channel_id=1, source_target_pairs={{4,0},{8,4},{12,8},{5,1},{9,5},{13,9},{6,2},{10,6},{14,10},{7,3},{... | collective-permute-start | bytes 1671176 | tf_op jit(solution)/shard_map/ppermute | solution.py:30
  101.7 51.9 %collective-permute-start.3 = (f32[8,136,128]{2,1,0:T(8,128)S(1)}, f32[8,136,128]{2,1,0:T(8,128)}, u32[]{:S(2)}, u32[]{:S(2)}) collective-permute-start(f32[8,136,128]{2,1,0:T(8,128)S(1)} %concatenate.7), channel_id=1, source_target_pairs={{8,0},{12,4},{9,1},{13,5},{10,2},{14,6},{11,3},{15,7},{24,16},{28,... | collective-permute-start | bytes 1671176 | tf_op jit(solution)/shard_map/ppermute | solution.py:30
  103.2 17.0 %copy-start = (f32[8,5,128,128]{3,2,1,0:T(8,128)S(1)}, f32[8,5,128,128]{3,2,1,0:T(8,128)}, u32[]{:S(2)}) copy-start(f32[8,5,128,128]{3,2,1,0:T(8,128)} %get-tuple-element.27) | copy-start | bytes 7864324

commit v6 on v5

--- a/solution.py
+++ b/solution.py
@@ -44,12 +44,13 @@
         return none_doc, jnp.zeros_like(state), cover()
     packed = pack(doc, state)
     if reach <= 2:
-        arrivals = [shift(packed, step) for step in range(1, reach + 1)]
+        got = shift(packed, 1)
         covered_value = cover()
-        arrivals, covered_value = lax.optimization_barrier((arrivals, covered_value))
-        ex_doc, ex_state = unpack(arrivals[0])
-        for got in arrivals[1:]:
-            ex_doc, ex_state = combine(ex_doc, ex_state, *unpack(got))
+        got, covered_value = lax.optimization_barrier((got, covered_value))
+        ex_doc, ex_state = unpack(got)
+        if reach == 2:
+            in_doc, in_state = combine(doc, state, ex_doc, ex_state)
+            ex_doc, ex_state = unpack(shift(pack(in_doc, in_state), 1))
         return ex_doc, ex_state, covered_value
     got = shift(packed, 1)
     covered_value = cover()
@@ -228,9 +229,9 @@
         pair_flops // 2,
     )
     feature_count = head_count * head_width * lax.axis_size(("sub", "head"))
-    total_sums = lax.psum(local_sums, ("sub", "head"))
-    root_mean = jnp.sqrt(total_sums[:, 0] / feature_count + 1e-06)
-    inner_mean = total_sums[:, 1] / feature_count
+    total_sums = lax.psum(local_sums.T, ("sub", "head"))
+    root_mean = jnp.sqrt(total_sums[0] / feature_count + 1e-06)
+    inner_mean = total_sums[1] / feature_count
     factor = inner_mean / (root_mean * root_mean)
     coefs = jnp.stack([root_mean, factor], axis=1)
     d_attn, query_grad_block = per_head_call(

time: 174 us -> 167 us (0.960)
  waiting for transfers between devices: 30.8 us -> 16.7 us
  local copies, waits for them, and re-layouts: 6.68 us -> 10.9 us
    ppermute x4, waiting for transfers between devices: 30.8 us -> 16.7 us  [shift(): return (lax.ppermute(packed, axis, pairs), step)]
    concatenate x2 -> x4, local copies, waits for them, and re-layouts: 1.34 us -> 4.25 us  [pack(): return jnp.concatenate([value_state, row.astype(jnp.float32)], axis=1)]
    select_n x0 -> x2, other arithmetic: none -> 2.17 us  [unpack(): got_state = jnp.where(valid, got[:, :rows], 0.0)]
  transfers between devices with their start and end apart: 4 -> 4, of which waited for: 3 -> 3; matrix products, arithmetic and copies ran while one was open for 6% -> 7% of each run, Pallas kernels for 16% -> 16%
where the time goes in v6:
time: 167 us; the launch traced here: 166 us
  Pallas kernels  64.2 us (38%)
  matrix products  24.3 us (15%)
  blocking collectives  18 us (11%)
  waiting for transfers between devices  16.7 us (10%)
  starting transfers between devices  13.7 us (8%)
  other arithmetic  13.5 us (8%)
  local copies, waits for them, and re-layouts  10.9 us (7%)
  between operations  4.65 us (3%)
    pallas_call x5, Pallas kernels, per_head_call(): pl.pallas_call(kernel, grid=(head_count,), in_specs=[spec(x.shape, h) for...  64.2 us
    psum x1, blocking collectives, on_device(): total_sums = lax.psum(local_sums.T, ('sub', 'head'))  18 us
    ppermute x4, waiting for transfers between devices, shift(): return (lax.ppermute(packed, axis, pairs), step)  16.7 us
    ppermute x4, starting transfers between devices, shift(): return (lax.ppermute(packed, axis, pairs), step)  13.7 us
    dot_general x1, matrix products, on_device(): jnp.einsum('c,hcde->hde', first_match, query_grad_block, precision=highes...  5.74 us
    dot_general x1, matrix products, on_device(): jnp.einsum('bc,hcde->hbde', later_mask, query_grad_block, precision=highe...  5.52 us
    dot_general x1, matrix products, on_device(): jnp.einsum('bc,hcde->hbde', earlier_mask, key_value_block, precision=high...  5.47 us
    slice x4, local copies, waits for them, and re-layouts, unpack(): got_doc = jnp.where(valid, got[0, rows, 0], none_doc)  4.91 us
  transfers between devices with their start and end apart: 4, of which 3 were waited for; matrix products, arithmetic and copies ran while one was open for 7% of the time, Pallas kernels for 16%

profile of v6, /device:TPU:0, one launch (start us, length us, event | category | flops | bytes accessed | tf_op | source)
XLA Modules:
  0.0 165.9 jit_solution(5984487066533982203)
XLA Ops:
  0.6 0.7 convert_element_type.25
  1.3 0.6 fusion.30
  1.9 0.0 copy-start.1
  1.9 3.4 %fusion.31 = f32[8,5,128,128]{3,2,1,0:T(8,128)S(1)} fusion(bf16[8,5,256,128]{3,2,1,0:T(8,128)(2,1)} %bitcast.46, bf16[8,5,256,128]{3,2,1,0:T(8,128)(2,1)} %bitcast.47), kind=kOutput, calls=%fused_computation.45 | convolution fusion | flops 335544320 | bytes 7864320 | tf_op jit(solution)/shard_map/hnid,hnie->hnde/dot_general | solution.py:196
  5.3 0.0 copy-done.1
  5.3 4.1 %fusion.4 = f32[1,8,128,128]{3,0,2,1:T(1,128)S(1)} fusion(f32[8,5,128,128]{3,2,1,0:T(8,128)S(1)} %fusion.31, f32[]{:T(128)} %bitcast.7, s32[5]{0:T(128)S(1)} %copy-done.1), kind=kOutput, calls=%fused_computation.4 | convolution fusion | flops 7864330 | bytes 3145752 | tf_op jit(solution)/shard_map/c,hcde->hde/dot_general | solution.py:200
  9.4 1.5 concatenate.12
  10.9 5.8 %collective-permute-start = (f32[8,136,128]{2,1,0:T(8,128)}, f32[8,136,128]{2,1,0:T(8,128)}, u32[]{:S(2)}, u32[]{:S(2)}) collective-permute-start(f32[8,136,128]{2,1,0:T(8,128)} %concatenate.12), channel_id=1, source_target_pairs={{0,4},{4,8},{8,12},{1,5},{5,9},{9,13},{2,6},{6,10},{10,14},{3,7},{... | collective-permute-start | bytes 1671176 | tf_op jit(solution)/shard_map/ppermute | solution.py:30
  16.7 10.2 %shard_map.85.i_ref = f32[8,1280,128]{2,1,0:T(8,128)} custom-call(bf16[8,1280,128]{2,1,0:T(8,128)(2,1)} %q_ref.7, bf16[8,1280,128]{2,1,0:T(8,128)(2,1)} %k_ref.7, bf16[8,1280,128]{2,1,0:T(8,128)(2,1)} %v_ref.7), custom_call_target="tpu_custom_call" | custom-call | flops 1342177280 | bytes 13107200 | tf_op jit(solution)/shard_map/pallas_call | solution.py:167
  26.8 1.2 collective-permute-done
  28.0 1.2 slice.40
  30.5 1.1 multiply_add_fusion.1
  31.6 0.7 concatenate.13
  32.3 5.2 %collective-permute-start.1 = (f32[8,136,128]{2,1,0:T(8,128)S(1)}, f32[8,136,128]{2,1,0:T(8,128)}, u32[]{:S(2)}, u32[]{:S(2)}) collective-permute-start(f32[8,136,128]{2,1,0:T(8,128)S(1)} %concatenate.13), channel_id=1, source_target_pairs={{0,4},{4,8},{8,12},{1,5},{5,9},{9,13},{2,6},{6,10},{10,14},{3,7},{... | collective-permute-start | bytes 1671176 | tf_op jit(solution)/shard_map/ppermute | solution.py:30
  37.5 5.5 %fusion.6 = f32[8,128,128,5]{2,3,1,0:T(8,128)} fusion(f32[8,5,128,128]{3,2,1,0:T(8,128)S(1)} %fusion.31, f32[5]{0:T(128)S(1)} %convert_element_type.25), kind=kOutput, calls=%fused_computation.6 | convolution fusion | flops 39321676 | bytes 5242900 | tf_op jit(solution)/shard_map/bc,hcde->hbde/dot_general | solution.py:201
  43.0 4.7 %collective-permute-done.1 = f32[8,136,128]{2,1,0:T(8,128)} collective-permute-done((f32[8,136,128]{2,1,0:T(8,128)S(1)}, f32[8,136,128]{2,1,0:T(8,128)}, u32[]{:S(2)}, u32[]{:S(2)}) %collective-permute-start.1) | collective-permute-done | bytes 557088 | tf_op jit(solution)/shard_map/ppermute | solution.py:30
  47.7 1.2 slice.50
  49.6 1.1 slice_select_fusion.1
  50.7 3.9 %fusion.9.s_ref = bf16[8,5,128,128]{3,2,1,0:T(8,128)(2,1)} fusion(f32[8,128,128,5]{2,3,1,0:T(8,128)} %fusion.6, f32[8,128,128]{2,1,0:T(8,128)S(1)} %slice_select_fusion.1, f32[5]{0:T(128)S(1)} %compare_convert_fusion.1), kind=kLoop, calls=%fused_computation.11 | loop fusion | flops 1966080 | bytes 4456468 | tf_op jit(solution)/shard_map/convert_element_type | solution.py:223
  54.6 9.6 %shard_map.86 = f32[1280,2]{1,0:T(8,128)} custom-call(f32[8,1280,128]{2,1,0:T(8,128)} %shard_map.85.i_ref, bf16[8,1280,128]{2,1,0:T(8,128)(2,1)} %q_ref.7, bf16[8,1280,128]{2,1,0:T(8,128)(2,1)} %g_ref.3, f32[8,1,128]{2,1,0:T(1,128)} %bitcast.53, bf16[8,5,128,128]{3,2,1,0:T(8,128)(2,1)} %fusion.9.s_ref), custom_call_target="tpu_custom_call" | custom-call | flops 335544320 | bytes 11810816 | tf_op jit(solution)/shard_map/pallas_call | solution.py:167
  64.2 18.0 %psum.7 = f32[2,1280]{0,1:T(8,128)S(1)} all-reduce(f32[2,1280]{0,1:T(8,128)} %bitcast.52), channel_id=1, replica_groups=mesh['groups'=2,'ctx'=4,'sub'=2,'head'=2] {'sub','head'}, use_global_device_ids=true, to_apply=%region_0.1 | all-reduce | flops 2560 | bytes 20480 | tf_op jit(solution)/shard_map/psum | solution.py:232
  82.2 0.6 fusion.10
  82.9 1.1 copy.23.c_ref
  84.0 17.1 %shard_map.87 = (bf16[8,1280,128]{2,1,0:T(8,128)(2,1)}, f32[8,5,128,128]{3,2,1,0:T(8,128)}) custom-call(bf16[8,1280,128]{2,1,0:T(8,128)(2,1)} %q_ref.7, bf16[8,1280,128]{2,1,0:T(8,128)(2,1)} %k_ref.7, bf16[8,1280,128]{2,1,0:T(8,128)(2,1)} %v_ref.7, bf16[8,1280,128]{2,1,0:T(8,128)(2,1)} %g_ref.3, f32[8,1,128]{2,1,0:T(1,128)} %bitcast.54, ...), custom_call_target="tpu_custom_call" | custom-call | flops 2013265920 | bytes 17053696 | tf_op jit(solution)/shard_map/pallas_call | solution.py:167
  101.1 5.7 %fusion = f32[1,8,128,128]{3,0,2,1:T(1,128)S(1)} fusion(f32[8,5,128,128]{3,2,1,0:T(8,128)} %get-tuple-element.21, f32[]{:T(128)} %bitcast.16, s32[5]{0:T(128)S(1)} %copy-done.1), kind=kOutput, calls=%fused_computation | convolution fusion | flops 7864330 | bytes 3145752 | tf_op jit(solution)/shard_map/c,hcde->hde/dot_general | solution.py:245
  106.9 1.4 concatenate.14
  108.3 1.3 collective-permute-start.2
  109.6 16.8 %shard_map.88 = (bf16[8,1280,128]{2,1,0:T(8,128)(2,1)}, f32[8,1280,128]{2,1,0:T(8,128)}, f32[8,1280,128]{2,1,0:T(8,128)}) custom-call(bf16[8,1280,128]{2,1,0:T(8,128)(2,1)} %q_ref.7, bf16[8,1280,128]{2,1,0:T(8,128)(2,1)} %k_ref.7, bf16[8,1280,128]{2,1,0:T(8,128)(2,1)} %v_ref.7, bf16[8,1280,128]{2,1,0:T(8,128)(2,1)} %get-tuple-element.22.d_ref, ...), custom_call_target="tpu_custom_call" | custom-call | flops 3355443200 | bytes 24903680 | tf_op jit(solution)/shard_map/pallas_call | solution.py:167
  126.4 0.0 copy-start
  126.4 0.0 collective-permute-done.2
  126.4 1.3 slice.46
  129.0 1.1 multiply_add_fusion
  130.1 0.6 concatenate.15
  130.7 1.5 collective-permute-start.3
  132.3 0.0 copy-done
  132.3 5.5 %fusion.2 = f32[8,128,128,5]{2,3,1,0:T(8,128)} fusion(f32[8,5,128,128]{3,2,1,0:T(8,128)S(1)} %copy-done, f32[5]{0:T(128)S(1)} %convert_element_type.25), kind=kOutput, calls=%fused_computation.2 | convolution fusion | flops 39321676 | bytes 5242900 | tf_op jit(solution)/shard_map/bc,hcde->hbde/dot_general | solution.py:262
  137.8 10.8 %collective-permute-done.3 = f32[8,136,128]{2,1,0:T(8,128)} collective-permute-done((f32[8,136,128]{2,1,0:T(8,128)S(1)}, f32[8,136,128]{2,1,0:T(8,128)}, u32[]{:S(2)}, u32[]{:S(2)}) %collective-permute-start.3) | collective-permute-done | bytes 557088 | tf_op jit(solution)/shard_map/ppermute | solution.py:30
  148.6 1.2 slice.54
  150.4 1.1 slice_select_fusion
  151.5 3.9 %fusion.8.s_ref = bf16[8,5,128,128]{3,2,1,0:T(8,128)(2,1)} fusion(f32[8,128,128,5]{2,3,1,0:T(8,128)} %fusion.2, f32[8,128,128]{2,1,0:T(8,128)S(1)} %slice_select_fusion, f32[5]{0:T(128)S(1)} %compare_convert_fusion), kind=kLoop, calls=%fused_computation.9 | loop fusion | flops 1966080 | bytes 4456468 | tf_op jit(solution)/shard_map/convert_element_type | solution.py:267
  155.4 10.5 %shard_map.89 = (bf16[8,1280,128]{2,1,0:T(8,128)(2,1)}, bf16[8,1280,128]{2,1,0:T(8,128)(2,1)}) custom-call(f32[8,1280,128]{2,1,0:T(8,128)} %get-tuple-element.27.ik_ref, f32[8,1280,128]{2,1,0:T(8,128)} %get-tuple-element.28.iv_ref, bf16[8,1280,128]{2,1,0:T(8,128)(2,1)} %k_ref.7, bf16[8,1280,128]{2,1,0:T(8,128)(2,1)} %v_ref.7, ...), custom_call_target="tpu_custom_call" | custom-call | flops 671088640 | bytes 22282240 | tf_op jit(solution)/shard_map/pallas_call | solution.py:167
  (5 shorter events, 0.0 us)
Async XLA Ops:
  1.9 3.4 %copy-start.1 = (s32[5]{0:T(128)S(1)}, s32[5]{0:T(128)}, u32[]{:S(2)}) copy-start(s32[5]{0:T(128)} %param.11) | copy-start | bytes 64
  10.9 17.1 %collective-permute-start = (f32[8,136,128]{2,1,0:T(8,128)}, f32[8,136,128]{2,1,0:T(8,128)}, u32[]{:S(2)}, u32[]{:S(2)}) collective-permute-start(f32[8,136,128]{2,1,0:T(8,128)} %concatenate.12), channel_id=1, source_target_pairs={{0,4},{4,8},{8,12},{1,5},{5,9},{9,13},{2,6},{6,10},{10,14},{3,7},{... | collective-permute-start | bytes 1671176 | tf_op jit(solution)/shard_map/ppermute | solution.py:30
  32.3 15.4 %collective-permute-start.1 = (f32[8,136,128]{2,1,0:T(8,128)S(1)}, f32[8,136,128]{2,1,0:T(8,128)}, u32[]{:S(2)}, u32[]{:S(2)}) collective-permute-start(f32[8,136,128]{2,1,0:T(8,128)S(1)} %concatenate.13), channel_id=1, source_target_pairs={{0,4},{4,8},{8,12},{1,5},{5,9},{9,13},{2,6},{6,10},{10,14},{3,7},{... | collective-permute-start | bytes 1671176 | tf_op jit(solution)/shard_map/ppermute | solution.py:30
  108.3 18.1 %collective-permute-start.2 = (f32[8,136,128]{2,1,0:T(8,128)}, f32[8,136,128]{2,1,0:T(8,128)}, u32[]{:S(2)}, u32[]{:S(2)}) collective-permute-start(f32[8,136,128]{2,1,0:T(8,128)} %concatenate.14), channel_id=1, source_target_pairs={{4,0},{8,4},{12,8},{5,1},{9,5},{13,9},{6,2},{10,6},{14,10},{7,3},{... | collective-permute-start | bytes 1671176 | tf_op jit(solution)/shard_map/ppermute | solution.py:30
  126.4 5.9 %copy-start = (f32[8,5,128,128]{3,2,1,0:T(8,128)S(1)}, f32[8,5,128,128]{3,2,1,0:T(8,128)}, u32[]{:S(2)}) copy-start(f32[8,5,128,128]{3,2,1,0:T(8,128)} %get-tuple-element.21) | copy-start | bytes 7864324
  130.7 17.8 %collective-permute-start.3 = (f32[8,136,128]{2,1,0:T(8,128)S(1)}, f32[8,136,128]{2,1,0:T(8,128)}, u32[]{:S(2)}, u32[]{:S(2)}) collective-permute-start(f32[8,136,128]{2,1,0:T(8,128)S(1)} %concatenate.15), channel_id=1, source_target_pairs={{4,0},{8,4},{12,8},{5,1},{9,5},{13,9},{6,2},{10,6},{14,10},{7,3},{... | collective-permute-start | bytes 1671176 | tf_op jit(solution)/shard_map/ppermute | solution.py:30

commit v7 on v6

--- a/solution.py
+++ b/solution.py
@@ -68,6 +68,17 @@
     return ex_doc, ex_state, covered_value
 
 
+def masked_block_sum(mask, blocks):
+    total = mask[0] * blocks[:, 0]
+    for c in range(1, blocks.shape[1]):
+        total = total + mask[c] * blocks[:, c]
+    return total
+
+
+def masked_block_sums(mask, blocks):
+    return jnp.stack([masked_block_sum(mask[b], blocks) for b in range(mask.shape[0])], axis=1)
+
+
 def _causal(block_len):
     row_ids = lax.broadcasted_iota(jnp.int32, (block_len, block_len), 0)
     col_ids = lax.broadcasted_iota(jnp.int32, (block_len, block_len), 1)
@@ -181,7 +192,6 @@
     block_count = doc_ids.shape[0]
     block_len = tok_count // block_count
     block_shape = (head_count, block_count, block_len, head_width)
-    highest_precision = lax.Precision.HIGHEST
     key_blocks = keys.reshape(block_shape)
     value_blocks = values.reshape(block_shape)
     gain = norm_gain.reshape(head_count, 1, head_width)
@@ -197,10 +207,8 @@
         "hnid,hnie->hnde", key_blocks, value_blocks, preferred_element_type=jnp.float32
     )
     last_match = (doc_values == doc_values[-1]).astype(jnp.float32)
-    device_kv = jnp.einsum("c,hcde->hde", last_match, key_value_block, precision=highest_precision)
-    local_prefix = jnp.einsum(
-        "bc,hcde->hbde", earlier_mask, key_value_block, precision=highest_precision
-    )
+    device_kv = masked_block_sum(last_match, key_value_block)
+    local_prefix = masked_block_sums(earlier_mask, key_value_block)
     ctx_size = lax.axis_size("ctx")
     longest_doc = ctx_size * block_count // 2
     reach = (longest_doc - 2) // block_count + 1
@@ -229,9 +237,9 @@
         pair_flops // 2,
     )
     feature_count = head_count * head_width * lax.axis_size(("sub", "head"))
-    total_sums = lax.psum(local_sums.T, ("sub", "head"))
-    root_mean = jnp.sqrt(total_sums[0] / feature_count + 1e-06)
-    inner_mean = total_sums[1] / feature_count
+    total_sums = lax.psum(local_sums.T.reshape(2 * tok_count), ("sub", "head"))
+    root_mean = jnp.sqrt(total_sums[:tok_count] / feature_count + 1e-06)
+    inner_mean = total_sums[tok_count:] / feature_count
     factor = inner_mean / (root_mean * root_mean)
     coefs = jnp.stack([root_mean, factor], axis=1)
     d_attn, query_grad_block = per_head_call(
@@ -242,9 +250,7 @@
         3 * pair_flops,
     )
     first_match = (doc_values == doc_values[0]).astype(jnp.float32)
-    device_qd = jnp.einsum(
-        "c,hcde->hde", first_match, query_grad_block, precision=highest_precision
-    )
+    device_qd = masked_block_sum(first_match, query_grad_block)
     next_doc, next_state, (query_gradient, key_intra, value_intra) = segmented_scan(
         doc_values[0],
         device_qd,
@@ -259,9 +265,7 @@
             5 * pair_flops,
         ),
     )
-    local_suffix = jnp.einsum(
-        "bc,hcde->hbde", later_mask, query_grad_block, precision=highest_precision
-    )
+    local_suffix = masked_block_sums(later_mask, query_grad_block)
     next_match = (doc_values == next_doc).astype(jnp.float32)
     leaving = next_match[None, :, None, None] * next_state[:, None, :, :]
     following_states = (local_suffix + leaving).astype(jnp.bfloat16)

time: 167 us -> 183 us (1.096)
  other arithmetic: 13.5 us -> 67.3 us
  matrix products: 24.3 us -> 3.42 us
  waiting for transfers between devices: 16.7 us -> 5.55 us
  blocking collectives: 18 us -> 10.1 us
  local copies, waits for them, and re-layouts: 10.9 us -> 13.8 us
  starting transfers between devices: 13.7 us -> 11.8 us
    unnamed x0 -> x8, other arithmetic: none -> 32.8 us
    dot_general x4 -> x0, matrix products: 20.8 us -> none  [the longest x1 5.74 us: on_device(): jnp.einsum('c,hcde->hde', first_match, query_grad_block, precision=highes...]
    ppermute x4, waiting for transfers between devices: 16.7 us -> 5.55 us  [shift(): return (lax.ppermute(packed, axis, pairs), step)]
    add x0 -> x2, other arithmetic: none -> 8.33 us  [masked_block_sum(): total = total + mask[c] * blocks[:, c]]
    another operation x0 -> x2, other arithmetic: none -> 8.16 us  [masked_block_sums(): jnp.stack([masked_block_sum(mask[b], blocks) for b in range(mask.shape[0]...]
    psum x1, blocking collectives: 18 us -> 10.1 us  [on_device(): total_sums = lax.psum(local_sums.T.reshape(2 * tok_count), ('sub', 'head'))]
    add x2, other arithmetic: 2.21 us -> 8.72 us  [combine(): return (near_doc, near_state + joined * far_state)]
    slice x0 -> x4, local copies, waits for them, and re-layouts: none -> 2.8 us  [masked_block_sum(): total = mask[0] * blocks[:, 0]]
  transfers between devices with their start and end apart: 4 -> 4, of which waited for: 3 -> 2; matrix products, arithmetic and copies ran while one was open for 7% -> 24% of each run, Pallas kernels for 16% -> 15%
where the time goes in v7:
time: 183 us; the launch traced here: 181 us
  other arithmetic  67.3 us (37%)
  Pallas kernels  64.2 us (35%)
  local copies, waits for them, and re-layouts  13.8 us (8%)
  starting transfers between devices  11.8 us (6%)
  blocking collectives  10.1 us (6%)
  waiting for transfers between devices  5.55 us (3%)
  between operations  4.73 us (3%)
  matrix products  3.42 us (2%)
    pallas_call x5, Pallas kernels, per_head_call(): pl.pallas_call(kernel, grid=(head_count,), in_specs=[spec(x.shape, h) for...  64.2 us
    unnamed x8, other arithmetic  32.8 us
    ppermute x4, starting transfers between devices, shift(): return (lax.ppermute(packed, axis, pairs), step)  11.8 us
    psum x1, blocking collectives, on_device(): total_sums = lax.psum(local_sums.T.reshape(2 * tok_count), ('sub', 'head'))  10.1 us
    add x2, other arithmetic, combine(): return (near_doc, near_state + joined * far_state)  8.72 us
    add x2, other arithmetic, masked_block_sum(): total = total + mask[c] * blocks[:, c]  8.33 us
    another operation x2, other arithmetic, masked_block_sums(): jnp.stack([masked_block_sum(mask[b], blocks) for b in range(mask.shape[0]...  8.16 us
    ppermute x4, waiting for transfers between devices, shift(): return (lax.ppermute(packed, axis, pairs), step)  5.55 us
  transfers between devices with their start and end apart: 4, of which 2 were waited for; matrix products, arithmetic and copies ran while one was open for 24% of the time, Pallas kernels for 15%

profile of v7, /device:TPU:0, one launch (start us, length us, event | category | flops | bytes accessed | tf_op | source)
XLA Modules:
  0.0 180.9 jit_solution(14899970186927610501)
XLA Ops:
  0.6 0.7 convert_element_type.33
  1.3 0.6 fusion.13
  1.9 1.9 %compare_convert_fusion.3 = (f32[5]{0:T(128)S(1)}, f32[5]{0:T(128)S(1)}) fusion(f32[]{:T(128)} %bitcast, s32[5]{0:T(128)} %param.11, f32[]{:T(128)} %bitcast.30), kind=kLoop, calls=%fused_computation.36 | loop fusion | flops 25 | bytes 68 | tf_op jit(solution)/shard_map/convert_element_type | solution.py:252
  3.8 0.7 fusion.12
  4.5 3.4 %fusion = f32[8,5,128,128]{3,2,0,1:T(8,128)S(1)} fusion(bf16[8,5,256,128]{3,2,1,0:T(8,128)(2,1)} %bitcast.78, bf16[8,5,256,128]{3,2,1,0:T(8,128)(2,1)} %bitcast.79), kind=kOutput, calls=%fused_computation | convolution fusion | flops 335544320 | bytes 7864320 | tf_op jit(solution)/shard_map/hnid,hnie->hnde/dot_general | solution.py:206
  7.9 3.2 %add_bitcast_fusion.1 = f32[8,128,128]{2,1,0:T(8,128)S(1)} fusion(f32[8,5,128,128]{3,2,0,1:T(8,128)S(1)} %fusion, f32[]{:T(128)} %bitcast.35, f32[]{:T(128)} %bitcast.34, f32[]{:T(128)} %bitcast.33, f32[]{:T(128)} %bitcast.32, f32[]{:T(128)} %bitcast.31), kind=kLoop, calls=%fused_computation.8 | loop fusion | flops 1179648 | bytes 3145748 | tf_op jit(solution)/shard_map/add | solution.py:74
  11.1 0.6 concatenate.12
  11.7 5.8 %collective-permute-start = (f32[8,136,128]{2,1,0:T(8,128)S(1)}, f32[8,136,128]{2,1,0:T(8,128)}, u32[]{:S(2)}, u32[]{:S(2)}) collective-permute-start(f32[8,136,128]{2,1,0:T(8,128)S(1)} %concatenate.12), channel_id=1, source_target_pairs={{0,4},{4,8},{8,12},{1,5},{5,9},{9,13},{2,6},{6,10},{10,14},{3,7},{... | collective-permute-start | bytes 1671176 | tf_op jit(solution)/shard_map/ppermute | solution.py:30
  17.6 10.2 %shard_map.85.i_ref = f32[8,1280,128]{2,1,0:T(8,128)} custom-call(bf16[8,1280,128]{2,1,0:T(8,128)(2,1)} %q_ref.7, bf16[8,1280,128]{2,1,0:T(8,128)(2,1)} %k_ref.7, bf16[8,1280,128]{2,1,0:T(8,128)(2,1)} %v_ref.7), custom_call_target="tpu_custom_call" | custom-call | flops 1342177280 | bytes 13107200 | tf_op jit(solution)/shard_map/pallas_call | solution.py:178
  27.7 0.7 fusion.9
  28.4 4.2 %add_dynamic-update-slice_fusion.9 = f32[8,5,128,128]{3,2,0,1:T(8,128)} fusion(f32[8,5,128,128]{3,2,0,1:T(8,128)S(1)} %fusion, f32[]{:T(128)} %bitcast.9, f32[]{:T(128)} %bitcast.8, f32[]{:T(128)} %bitcast.7, f32[]{:T(128)} %bitcast.6, f32[]{:T(128)} %bitcast.3), kind=kLoop, calls=%fused_computation.20 | loop fusion | flops 1179647 | bytes 3145748
  32.6 0.7 fusion.10
  33.3 4.2 %add_dynamic-update-slice_fusion.8 = f32[8,5,128,128]{3,2,0,1:T(8,128)} fusion(f32[8,5,128,128]{3,2,0,1:T(8,128)} %add_dynamic-update-slice_fusion.9, f32[8,5,128,128]{3,2,0,1:T(8,128)S(1)} %fusion, f32[]{:T(128)} %bitcast.14, f32[]{:T(128)} %bitcast.13, f32[]{:T(128)} %bitcast.12, f32[]{:T(128)} %bitcast.11, f32[]{:T(128)} %bitcast.10), kind=kLoop, calls=%fused_computation.19 | loop fusion | flops 1179648 | bytes 3148288
  37.5 4.0 %add_dynamic-update-slice_fusion.7 = f32[8,5,128,128]{3,2,0,1:T(8,128)} fusion(f32[8,5,128,128]{3,2,0,1:T(8,128)} %add_dynamic-update-slice_fusion.8, f32[8,5,128,128]{3,2,0,1:T(8,128)S(1)} %fusion, f32[]{:T(128)} %bitcast.19, f32[]{:T(128)} %bitcast.18, f32[]{:T(128)} %bitcast.17, f32[]{:T(128)} %bitcast.16, f32[]{:T(128)} %bitcast.15), kind=kLoop, calls=%fused_computation.18 | loop fusion | flops 1179648 | bytes 3148288
  41.6 1.3 slice.446
  44.1 4.3 %multiply_add_fusion.1 = f32[8,128,128]{2,1,0:T(8,128)S(1)} fusion(f32[8,136,128]{2,1,0:T(8,128)} %collective-permute-done, f32[]{:T(128)S(6)} %convert_element_type.37, pred[]{:T(512)S(6)} %ge.7, f32[8,5,128,128]{3,2,0,1:T(8,128)S(1)} %fusion, f32[]{:T(128)} %bitcast.35, f32[]{:T(128)} %bitcast.34, f32[]{:T(128)} %bitcast.33, f32[]{:T(128)} %bitcast.32, ...), kind=kLoop, calls=%fused_computation.15 | loop fusion | flops 1572864 | bytes 3670041 | tf_op jit(solution)/shard_map/add | solution.py:41
  48.4 0.6 concatenate.13
  49.0 3.5 %collective-permute-start.1 = (f32[8,136,128]{2,1,0:T(8,128)S(1)}, f32[8,136,128]{2,1,0:T(8,128)}, u32[]{:S(2)}, u32[]{:S(2)}) collective-permute-start(f32[8,136,128]{2,1,0:T(8,128)S(1)} %concatenate.13), channel_id=1, source_target_pairs={{0,4},{4,8},{8,12},{1,5},{5,9},{9,13},{2,6},{6,10},{10,14},{3,7},{... | collective-permute-start | bytes 1671176 | tf_op jit(solution)/shard_map/ppermute | solution.py:30
  52.5 0.7 fusion.8
  53.3 4.0 %add_dynamic-update-slice_fusion.6 = f32[8,5,128,128]{3,2,0,1:T(8,128)} fusion(f32[8,5,128,128]{3,2,0,1:T(8,128)} %add_dynamic-update-slice_fusion.7, f32[8,5,128,128]{3,2,0,1:T(8,128)S(1)} %fusion, f32[]{:T(128)} %bitcast.24, f32[]{:T(128)} %bitcast.23, f32[]{:T(128)} %bitcast.22, f32[]{:T(128)} %bitcast.21, f32[]{:T(128)} %bitcast.20), kind=kLoop, calls=%fused_computation.17 | loop fusion | flops 1179648 | bytes 3148288
  57.3 4.1 %add_dynamic-update-slice_fusion.5 = f32[8,5,128,128]{3,2,0,1:T(8,128)} fusion(f32[8,5,128,128]{3,2,0,1:T(8,128)} %add_dynamic-update-slice_fusion.6, f32[8,5,128,128]{3,2,0,1:T(8,128)S(1)} %fusion, f32[]{:T(128)} %bitcast.29, f32[]{:T(128)} %bitcast.28, f32[]{:T(128)} %bitcast.27, f32[]{:T(128)} %bitcast.26, f32[]{:T(128)} %bitcast.25), kind=kLoop, calls=%fused_computation.16 | loop fusion | flops 1179648 | bytes 3148288 | tf_op jit(solution)/shard_map/stack | solution.py:79
  61.4 1.9 %collective-permute-done.1 = f32[8,136,128]{2,1,0:T(8,128)} collective-permute-done((f32[8,136,128]{2,1,0:T(8,128)S(1)}, f32[8,136,128]{2,1,0:T(8,128)}, u32[]{:S(2)}, u32[]{:S(2)}) %collective-permute-start.1) | collective-permute-done | bytes 557088 | tf_op jit(solution)/shard_map/ppermute | solution.py:30
  63.3 1.2 slice.495
  65.2 1.1 slice_select_fusion.1
  66.3 2.2 %add_convert_fusion.1 = bf16[8,5,128,128]{3,2,0,1:T(8,128)(2,1)S(1)} fusion(f32[8,5,128,128]{3,2,0,1:T(8,128)} %add_dynamic-update-slice_fusion.5, f32[8,128,128]{2,1,0:T(8,128)S(1)} %slice_select_fusion.1, f32[5]{0:T(128)S(1)} %compare_convert_fusion.1), kind=kLoop, calls=%fused_computation.4 | loop fusion | flops 1966080 | bytes 4456468 | tf_op jit(solution)/shard_map/convert_element_type | solution.py:231
  68.4 1.2 copy.38.s_ref
  69.6 9.6 %shard_map.86 = f32[1280,2]{1,0:T(8,128)} custom-call(f32[8,1280,128]{2,1,0:T(8,128)} %shard_map.85.i_ref, bf16[8,1280,128]{2,1,0:T(8,128)(2,1)} %q_ref.7, bf16[8,1280,128]{2,1,0:T(8,128)(2,1)} %g_ref.3, f32[8,1,128]{2,1,0:T(1,128)} %bitcast.81, bf16[8,5,128,128]{3,2,1,0:T(8,128)(2,1)} %copy.38.s_ref), custom_call_target="tpu_custom_call" | custom-call | flops 335544320 | bytes 11810816 | tf_op jit(solution)/shard_map/pallas_call | solution.py:178
  79.2 1.3 copy.37
  80.6 10.1 %psum.7 = f32[2560]{0:T(1024)S(1)} all-reduce(f32[2560]{0:T(1024)S(1)} %reshape.153), channel_id=1, replica_groups=mesh['groups'=2,'ctx'=4,'sub'=2,'head'=2] {'sub','head'}, use_global_device_ids=true, to_apply=%region_0.1 | all-reduce | flops 2560 | bytes 20480 | tf_op jit(solution)/shard_map/psum | solution.py:240
  90.8 1.1 copy.39.c_ref
  91.9 17.1 %shard_map.87 = (bf16[8,1280,128]{2,1,0:T(8,128)(2,1)}, f32[8,5,128,128]{3,2,1,0:T(8,128)}) custom-call(bf16[8,1280,128]{2,1,0:T(8,128)(2,1)} %q_ref.7, bf16[8,1280,128]{2,1,0:T(8,128)(2,1)} %k_ref.7, bf16[8,1280,128]{2,1,0:T(8,128)(2,1)} %v_ref.7, bf16[8,1280,128]{2,1,0:T(8,128)(2,1)} %g_ref.3, f32[8,1,128]{2,1,0:T(1,128)} %bitcast.82, ...), custom_call_target="tpu_custom_call" | custom-call | flops 2013265920 | bytes 17053696 | tf_op jit(solution)/shard_map/pallas_call | solution.py:178
  109.0 5.1 %add_bitcast_fusion = f32[8,128,128]{2,1,0:T(8,128)S(1)} fusion(f32[8,5,128,128]{3,2,1,0:T(8,128)} %get-tuple-element.21, f32[]{:T(128)} %bitcast.43, f32[]{:T(128)} %bitcast.42, f32[]{:T(128)} %bitcast.41, f32[]{:T(128)} %bitcast.40, f32[]{:T(128)} %bitcast.1), kind=kLoop, calls=%fused_computation.7 | loop fusion | flops 1179648 | bytes 3145748 | tf_op jit(solution)/shard_map/add | solution.py:74
  114.1 0.7 concatenate.14
  114.9 1.3 collective-permute-start.2
  116.2 4.2 %add_dynamic-update-slice_fusion.4 = f32[8,5,128,128]{3,2,1,0:T(8,128)} fusion(f32[8,5,128,128]{3,2,1,0:T(8,128)S(1)} %copy-done, f32[]{:T(128)} %bitcast.49, f32[]{:T(128)} %bitcast.48, f32[]{:T(128)} %bitcast.47, f32[]{:T(128)} %bitcast.46, f32[]{:T(128)} %bitcast.45), kind=kLoop, calls=%fused_computation.14 | loop fusion | flops 1179647 | bytes 3145748
  120.3 3.9 %add_dynamic-update-slice_fusion.3 = f32[8,5,128,128]{3,2,1,0:T(8,128)} fusion(f32[8,5,128,128]{3,2,1,0:T(8,128)} %add_dynamic-update-slice_fusion.4, f32[8,5,128,128]{3,2,1,0:T(8,128)S(1)} %copy-done, f32[]{:T(128)} %bitcast.54, f32[]{:T(128)} %bitcast.53, f32[]{:T(128)} %bitcast.52, f32[]{:T(128)} %bitcast.51, f32[]{:T(128)} %bitcast.50), kind=kLoop, calls=%fused_computation.13 | loop fusion | flops 1179648 | bytes 3148288
  124.2 16.8 %shard_map.88 = (bf16[8,1280,128]{2,1,0:T(8,128)(2,1)}, f32[8,1280,128]{2,1,0:T(8,128)}, f32[8,1280,128]{2,1,0:T(8,128)}) custom-call(bf16[8,1280,128]{2,1,0:T(8,128)(2,1)} %q_ref.7, bf16[8,1280,128]{2,1,0:T(8,128)(2,1)} %k_ref.7, bf16[8,1280,128]{2,1,0:T(8,128)(2,1)} %v_ref.7, bf16[8,1280,128]{2,1,0:T(8,128)(2,1)} %get-tuple-element.22.d_ref, ...), custom_call_target="tpu_custom_call" | custom-call | flops 3355443200 | bytes 24903680 | tf_op jit(solution)/shard_map/pallas_call | solution.py:178
  141.0 1.2 slice.486
  143.5 4.4 %multiply_add_fusion = f32[8,128,128]{2,1,0:T(8,128)S(1)} fusion(f32[8,136,128]{2,1,0:T(8,128)} %collective-permute-done.2, f32[]{:T(128)S(6)} %convert_element_type.41, pred[]{:T(512)S(6)} %le.7, f32[8,5,128,128]{3,2,1,0:T(8,128)S(1)} %copy-done, f32[]{:T(128)} %bitcast.43, f32[]{:T(128)} %bitcast.42, f32[]{:T(128)} %bitcast.41, f32[]{:T(128)} %bitcast.40, ...), kind=kLoop, calls=%fused_computation.9 | loop fusion | flops 1572864 | bytes 3670041 | tf_op jit(solution)/shard_map/add | solution.py:41
  147.9 0.7 concatenate.15
  148.6 1.3 collective-permute-start.3
  149.9 4.2 %add_dynamic-update-slice_fusion.2 = f32[8,5,128,128]{3,2,1,0:T(8,128)} fusion(f32[8,5,128,128]{3,2,1,0:T(8,128)} %add_dynamic-update-slice_fusion.3, f32[8,5,128,128]{3,2,1,0:T(8,128)S(1)} %copy-done, f32[]{:T(128)} %bitcast.59, f32[]{:T(128)} %bitcast.58, f32[]{:T(128)} %bitcast.57, f32[]{:T(128)} %bitcast.56, f32[]{:T(128)} %bitcast.55), kind=kLoop, calls=%fused_computation.12 | loop fusion | flops 1179648 | bytes 3148288
  154.1 4.1 %add_dynamic-update-slice_fusion.1 = f32[8,5,128,128]{3,2,1,0:T(8,128)} fusion(f32[8,5,128,128]{3,2,1,0:T(8,128)} %add_dynamic-update-slice_fusion.2, f32[8,5,128,128]{3,2,1,0:T(8,128)S(1)} %copy-done, f32[]{:T(128)} %bitcast.64, f32[]{:T(128)} %bitcast.63, f32[]{:T(128)} %bitcast.62, f32[]{:T(128)} %bitcast.61, f32[]{:T(128)} %bitcast.60), kind=kLoop, calls=%fused_computation.11 | loop fusion | flops 1179648 | bytes 3148288
  158.2 4.0 %add_dynamic-update-slice_fusion = f32[8,5,128,128]{3,2,1,0:T(8,128)} fusion(f32[8,5,128,128]{3,2,1,0:T(8,128)} %add_dynamic-update-slice_fusion.1, f32[8,5,128,128]{3,2,1,0:T(8,128)S(1)} %copy-done, f32[]{:T(128)} %bitcast.69, f32[]{:T(128)} %bitcast.68, f32[]{:T(128)} %bitcast.67, f32[]{:T(128)} %bitcast.66, f32[]{:T(128)} %bitcast.65), kind=kLoop, calls=%fused_computation.10 | loop fusion | flops 1179648 | bytes 3148288 | tf_op jit(solution)/shard_map/stack | solution.py:79
  162.3 3.7 %collective-permute-done.3 = f32[8,136,128]{2,1,0:T(8,128)S(1)} collective-permute-done((f32[8,136,128]{2,1,0:T(8,128)S(1)}, f32[8,136,128]{2,1,0:T(8,128)S(1)}, u32[]{:S(2)}, u32[]{:S(2)}) %collective-permute-start.3) | collective-permute-done | bytes 557088 | tf_op jit(solution)/shard_map/ppermute | solution.py:30
  165.9 0.5 slice.499
  167.2 3.3 %add_convert_fusion.s_ref = bf16[8,5,128,128]{3,2,1,0:T(8,128)(2,1)} fusion(f32[8,5,128,128]{3,2,1,0:T(8,128)} %add_dynamic-update-slice_fusion, f32[8,128,128]{2,1,0:T(8,128)S(1)} %slice_select_fusion, f32[5]{0:T(128)S(1)} %compare_convert_fusion), kind=kLoop, calls=%fused_computation.3 | loop fusion | flops 1966080 | bytes 4456468 | tf_op jit(solution)/shard_map/convert_element_type | solution.py:271
  170.5 10.5 %shard_map.89 = (bf16[8,1280,128]{2,1,0:T(8,128)(2,1)}, bf16[8,1280,128]{2,1,0:T(8,128)(2,1)}) custom-call(f32[8,1280,128]{2,1,0:T(8,128)} %get-tuple-element.27.ik_ref, f32[8,1280,128]{2,1,0:T(8,128)} %get-tuple-element.28.iv_ref, bf16[8,1280,128]{2,1,0:T(8,128)(2,1)} %k_ref.7, bf16[8,1280,128]{2,1,0:T(8,128)(2,1)} %v_ref.7, ...), custom_call_target="tpu_custom_call" | custom-call | flops 671088640 | bytes 22282240 | tf_op jit(solution)/shard_map/pallas_call | solution.py:178
  (15 shorter events, 0.2 us)
Async XLA Ops:
  11.7 29.9 %collective-permute-start = (f32[8,136,128]{2,1,0:T(8,128)S(1)}, f32[8,136,128]{2,1,0:T(8,128)}, u32[]{:S(2)}, u32[]{:S(2)}) collective-permute-start(f32[8,136,128]{2,1,0:T(8,128)S(1)} %concatenate.12), channel_id=1, source_target_pairs={{0,4},{4,8},{8,12},{1,5},{5,9},{9,13},{2,6},{6,10},{10,14},{3,7},{... | collective-permute-start | bytes 1671176 | tf_op jit(solution)/shard_map/ppermute | solution.py:30
  49.0 14.2 %collective-permute-start.1 = (f32[8,136,128]{2,1,0:T(8,128)S(1)}, f32[8,136,128]{2,1,0:T(8,128)}, u32[]{:S(2)}, u32[]{:S(2)}) collective-permute-start(f32[8,136,128]{2,1,0:T(8,128)S(1)} %concatenate.13), channel_id=1, source_target_pairs={{0,4},{4,8},{8,12},{1,5},{5,9},{9,13},{2,6},{6,10},{10,14},{3,7},{... | collective-permute-start | bytes 1671176 | tf_op jit(solution)/shard_map/ppermute | solution.py:30
  53.3 11.9 %copy-start.1 = (s32[5]{0:T(128)S(1)}, s32[5]{0:T(128)}, u32[]{:S(2)}) copy-start(s32[5]{0:T(128)} %param.11) | copy-start | bytes 64
  109.0 7.1 %copy-start = (f32[8,5,128,128]{3,2,1,0:T(8,128)S(1)}, f32[8,5,128,128]{3,2,1,0:T(8,128)}, u32[]{:S(2)}) copy-start(f32[8,5,128,128]{3,2,1,0:T(8,128)} %get-tuple-element.21) | copy-start | bytes 7864324
  114.9 26.2 %collective-permute-start.2 = (f32[8,136,128]{2,1,0:T(8,128)S(1)}, f32[8,136,128]{2,1,0:T(8,128)}, u32[]{:S(2)}, u32[]{:S(2)}) collective-permute-start(f32[8,136,128]{2,1,0:T(8,128)S(1)} %concatenate.14), channel_id=1, source_target_pairs={{4,0},{8,4},{12,8},{5,1},{9,5},{13,9},{6,2},{10,6},{14,10},{7,3},{... | collective-permute-start | bytes 1671176 | tf_op jit(solution)/shard_map/ppermute | solution.py:30
  148.6 17.3 %collective-permute-start.3 = (f32[8,136,128]{2,1,0:T(8,128)S(1)}, f32[8,136,128]{2,1,0:T(8,128)S(1)}, u32[]{:S(2)}, u32[]{:S(2)}) collective-permute-start(f32[8,136,128]{2,1,0:T(8,128)S(1)} %concatenate.15), channel_id=1, source_target_pairs={{4,0},{8,4},{12,8},{5,1},{9,5},{13,9},{6,2},{10,6},{14,10},{7,3},{... | collective-permute-start | bytes 1671176 | tf_op jit(solution)/shard_map/ppermute | solution.py:30

commit v8 on v7

v8 whole, which is shorter than its diff:
```python
import functools
import math

import jax
import jax.numpy as jnp
from jax import lax
from jax.experimental import pallas as pl
from jax.sharding import PartitionSpec as P

_ROWS_MINOR = (((1,), (1,)), ((), ()))
_ROWS_MAJOR = (((0,), (0,)), ((), ()))


def _causal(block_len):
    row_ids = lax.broadcasted_iota(jnp.int32, (block_len, block_len), 0)
    col_ids = lax.broadcasted_iota(jnp.int32, (block_len, block_len), 1)
    return row_ids >= col_ids


def _sum_blocks(mask_ref, first_row, parts):
    total = mask_ref[first_row : first_row + 1, :] * parts[0]
    for c in range(1, len(parts)):
        total = total + mask_ref[first_row + c : first_row + c + 1, :] * parts[c]
    return total


def _carried(state_ref, doc_ref, n, carry_ref):
    width = carry_ref.shape[2]
    joined = doc_ref[n : n + 1, :] == carry_ref[0, width : width + 1, :]
    total = state_ref[0, n] + jnp.where(joined, carry_ref[0, :width, :], 0.0)
    return total.astype(jnp.bfloat16)


def state_kernel(block_len, k_ref, v_ref, pair_ref, end_ref, row_ref, prefix_ref, pay_ref):
    count = k_ref.shape[1] // block_len
    width = k_ref.shape[2]
    parts = []
    for n in range(count):
        rows = pl.ds(n * block_len, block_len)
        parts.append(
            lax.dot_general(
                k_ref[0, rows, :], v_ref[0, rows, :], _ROWS_MAJOR,
                preferred_element_type=jnp.float32,
            )
        )
    for b in range(count):
        prefix_ref[0, b] = _sum_blocks(pair_ref, b * count, parts)
    pay_ref[0, :width, :] = _sum_blocks(end_ref, 0, parts)
    pay_ref[0, width:, :] = row_ref[...]


def combine_kernel(near_ref, far_ref, o_ref):
    width = near_ref.shape[2]
    joined = near_ref[0, width : width + 1, :] == far_ref[0, width : width + 1, :]
    o_ref[0, :width, :] = near_ref[0, :width, :] + jnp.where(
        joined, far_ref[0, :width, :], 0.0
    )
    o_ref[0, width:, :] = near_ref[0, width:, :]


def intra_kernel(block_len, q_ref, k_ref, v_ref, o_ref):
    causal = _causal(block_len)
    for n in range(q_ref.shape[1] // block_len):
        rows = pl.ds(n * block_len, block_len)
        q, k, v = q_ref[0, rows, :], k_ref[0, rows, :], v_ref[0, rows, :]
        scores = lax.dot_general(q, k, _ROWS_MINOR, preferred_element_type=jnp.float32)
        probs = jnp.where(causal, scores, 0.0).astype(jnp.bfloat16)
        o_ref[0, rows, :] = jnp.dot(probs, v, preferred_element_type=jnp.float32)


def forward_kernel(
    block_len, i_ref, q_ref, g_ref, n_ref, prefix_ref, carry_ref, doc_ref, o_ref, s_ref
):
    @pl.when(pl.program_id(0) == 0)
    def _():
        o_ref[...] = jnp.zeros_like(o_ref)

    for n in range(q_ref.shape[1] // block_len):
        rows = pl.ds(n * block_len, block_len)
        state = _carried(prefix_ref, doc_ref, n, carry_ref)
        s_ref[0, n] = state
        raw = i_ref[0, rows, :] + jnp.dot(
            q_ref[0, rows, :], state, preferred_element_type=jnp.float32
        )
        scaled = n_ref[0] * g_ref[0, rows, :].astype(jnp.float32)
        o_ref[rows, 0:1] += jnp.sum(raw * raw, axis=1, keepdims=True)
        o_ref[rows, 1:2] += jnp.sum(scaled * raw, axis=1, keepdims=True)


def grad_kernel(
    block_len, q_ref, k_ref, v_ref, g_ref, n_ref, s_ref, c_ref, pair_ref, end_ref, row_ref,
    d_ref, suffix_ref, pay_ref,
):
    causal = _causal(block_len)
    count = q_ref.shape[1] // block_len
    width = q_ref.shape[2]
    parts = []
    for n in range(count):
        rows = pl.ds(n * block_len, block_len)
        q, k, v = q_ref[0, rows, :], k_ref[0, rows, :], v_ref[0, rows, :]
        scores = lax.dot_general(q, k, _ROWS_MINOR, preferred_element_type=jnp.float32)
        probs = jnp.where(causal, scores, 0.0).astype(jnp.bfloat16)
        raw = jnp.dot(probs, v, preferred_element_type=jnp.float32)
        raw = raw + jnp.dot(q, s_ref[0, n], preferred_element_type=jnp.float32)
        scaled = n_ref[0] * g_ref[0, rows, :].astype(jnp.float32)
        root_mean = c_ref[rows, 0:1]
        factor = c_ref[rows, 1:2]
        d = ((scaled - raw * factor) / root_mean).astype(jnp.bfloat16)
        d_ref[0, rows, :] = d
        parts.append(lax.dot_general(q, d, _ROWS_MAJOR, preferred_element_type=jnp.float32))
    for b in range(count):
        suffix_ref[0, b] = _sum_blocks(pair_ref, b * count, parts)
    pay_ref[0, :width, :] = _sum_blocks(end_ref, 0, parts)
    pay_ref[0, width:, :] = row_ref[...]


def query_grad_kernel(block_len, q_ref, k_ref, v_ref, d_ref, s_ref, dq_ref, dk_ref, dv_ref):
    causal = _causal(block_len)
    for n in range(k_ref.shape[1] // block_len):
        rows = pl.ds(n * block_len, block_len)
        q, k, v = q_ref[0, rows, :], k_ref[0, rows, :], v_ref[0, rows, :]
        d = d_ref[0, rows, :]
        scores = lax.dot_general(q, k, _ROWS_MINOR, preferred_element_type=jnp.float32)
        probs = jnp.where(causal, scores, 0.0).astype(jnp.bfloat16)
        grad_scores = lax.dot_general(d, v, _ROWS_MINOR, preferred_element_type=jnp.float32)
        grad_probs = jnp.where(causal, grad_scores, 0.0).astype(jnp.bfloat16)
        dq = jnp.dot(grad_probs, k, preferred_element_type=jnp.float32)
        dq = dq + lax.dot_general(d, s_ref[0, n], _ROWS_MINOR, preferred_element_type=jnp.float32)
        dq_ref[0, rows, :] = dq.astype(dq_ref.dtype)
        dk_ref[0, rows, :] = lax.dot_general(
            grad_probs, q, _ROWS_MAJOR, preferred_element_type=jnp.float32
        )
        dv_ref[0, rows, :] = lax.dot_general(
            probs, d, _ROWS_MAJOR, preferred_element_type=jnp.float32
        )


def key_value_grad_kernel(
    block_len, ik_ref, iv_ref, k_ref, v_ref, suffix_ref, carry_ref, doc_ref, dk_ref, dv_ref
):
    for n in range(k_ref.shape[1] // block_len):
        rows = pl.ds(n * block_len, block_len)
        state = _carried(suffix_ref, doc_ref, n, carry_ref)
        dk = ik_ref[0, rows, :] + lax.dot_general(
            v_ref[0, rows, :], state, _ROWS_MINOR, preferred_element_type=jnp.float32
        )
        dv = iv_ref[0, rows, :] + jnp.dot(
            k_ref[0, rows, :], state, preferred_element_type=jnp.float32
        )
        dk_ref[0, rows, :] = dk.astype(dk_ref.dtype)
        dv_ref[0, rows, :] = dv.astype(dv_ref.dtype)


def per_head_call(kernel, inputs, outputs, flops):
    def spec(shape, per_head):
        if per_head:
            return pl.BlockSpec((1,) + shape[1:], lambda h: (h,) + (0,) * (len(shape) - 1))
        return pl.BlockSpec(shape, lambda h: (0,) * len(shape))

    head_count = inputs[0][0].shape[0]
    in_bytes = sum(x.size * x.dtype.itemsize for x, _ in inputs)
    out_bytes = sum(math.prod(o.shape) * o.dtype.itemsize for o, _ in outputs)
    return pl.pallas_call(
        kernel,
        grid=(head_count,),
        in_specs=[spec(x.shape, h) for x, h in inputs],
        out_specs=[spec(o.shape, h) for o, h in outputs],
        out_shape=[o for o, _ in outputs],
        cost_estimate=pl.CostEstimate(
            flops=flops, transcendentals=0, bytes_accessed=in_bytes + out_bytes
        ),
    )(*[x for x, _ in inputs])


def combine(near, far):
    return per_head_call(
        combine_kernel, [(near, True), (far, True)], [(near, True)], 2 * near.size
    )[0]


def carry(payload, axis, reverse, reach, cover):
    peers = lax.axis_size(axis)
    reach = min(reach, peers - 1)

    def shift(value, step):
        if reverse:
            pairs = [(j, j - step) for j in range(step, peers)]
        else:
            pairs = [(j, j + step) for j in range(peers - step)]
        return lax.ppermute(value, axis, pairs)

    if reach < 1:
        return jnp.zeros_like(payload), cover()
    got = shift(payload, 1)
    covered_value = cover()
    got, covered_value = lax.optimization_barrier((got, covered_value))
    if reach <= 2:
        if reach == 2:
            got = shift(combine(payload, got), 1)
        return got, covered_value
    earlier, inclusive = got, combine(payload, got)
    covered = 1
    while covered < reach:
        step = covered + 1
        got = shift(inclusive, step)
        earlier = combine(earlier, got)
        covered = covered + step
        if covered < reach:
            inclusive = combine(inclusive, got)
    return earlier, covered_value


def on_device(queries, keys, values, out_grad, norm_gain, doc_ids):
    head_count, tok_count, head_width = queries.shape
    block_count = doc_ids.shape[0]
    block_len = tok_count // block_count
    gain = norm_gain.reshape(head_count, 1, head_width)
    doc_values = doc_ids.astype(jnp.float32)
    block_pos = jnp.arange(block_count, dtype=jnp.int32)
    same_doc = doc_values[:, None] == doc_values[None, :]
    earlier_mask = (same_doc & (block_pos[None, :] < block_pos[:, None])).astype(jnp.float32)
    later_mask = (same_doc & (block_pos[None, :] > block_pos[:, None])).astype(jnp.float32)
    last_match = (doc_values == doc_values[-1]).astype(jnp.float32)
    first_match = (doc_values == doc_values[0]).astype(jnp.float32)

    def lanes(table, rows):
        return jnp.broadcast_to(table.reshape(rows, 1), (rows, head_width))

    earlier_rows = lanes(earlier_mask, block_count * block_count)
    later_rows = lanes(later_mask, block_count * block_count)
    last_rows = lanes(last_match, block_count)
    first_rows = lanes(first_match, block_count)
    doc_rows = lanes(doc_values + 1.0, block_count)
    last_doc_rows = jnp.broadcast_to(doc_values[-1] + 1.0, (8, head_width))
    first_doc_rows = jnp.broadcast_to(doc_values[0] + 1.0, (8, head_width))

    pair_flops = 2 * head_count * block_count * block_len * block_len * head_width
    full = jax.ShapeDtypeStruct(queries.shape, jnp.bfloat16)
    wide = jax.ShapeDtypeStruct(queries.shape, jnp.float32)
    states = jax.ShapeDtypeStruct((head_count, block_count, head_width, head_width), jnp.float32)
    payload = jax.ShapeDtypeStruct((head_count, head_width + 8, head_width), jnp.float32)
    ctx_size = lax.axis_size("ctx")
    longest_doc = ctx_size * block_count // 2
    reach = (longest_doc - 2) // block_count + 1

    local_prefix, kv_payload = per_head_call(
        functools.partial(state_kernel, block_len),
        [(keys, True), (values, True), (earlier_rows, False), (last_rows, False),
         (last_doc_rows, False)],
        [(states, True), (payload, True)],
        pair_flops // 2,
    )
    prior, intra_part = carry(
        kv_payload,
        "ctx",
        False,
        reach,
        lambda: per_head_call(
            functools.partial(intra_kernel, block_len),
            [(queries, True), (keys, True), (values, True)],
            [(wide, True)],
            2 * pair_flops,
        )[0],
    )
    local_sums, preceding_states = per_head_call(
        functools.partial(forward_kernel, block_len),
        [(intra_part, True), (queries, True), (out_grad, True), (gain, True),
         (local_prefix, True), (prior, True), (doc_rows, False)],
        [(jax.ShapeDtypeStruct((tok_count, 2), jnp.float32), False),
         (jax.ShapeDtypeStruct(states.shape, jnp.bfloat16), True)],
        pair_flops // 2,
    )
    feature_count = head_count * head_width * lax.axis_size(("sub", "head"))
    total_sums = lax.psum(local_sums.T.reshape(2 * tok_count), ("sub", "head"))
    root_mean = jnp.sqrt(total_sums[:tok_count] / feature_count + 1e-06)
    inner_mean = total_sums[tok_count:] / feature_count
    factor = inner_mean / (root_mean * root_mean)
    coefs = jnp.stack([root_mean, factor], axis=1)
    d_attn, local_suffix, qd_payload = per_head_call(
        functools.partial(grad_kernel, block_len),
        [(queries, True), (keys, True), (values, True), (out_grad, True), (gain, True),
         (preceding_states, True), (coefs, False), (later_rows, False), (first_rows, False),
         (first_doc_rows, False)],
        [(full, True), (states, True), (payload, True)],
        3 * pair_flops,
    )
    following, (query_gradient, key_intra, value_intra) = carry(
        qd_payload,
        "ctx",
        True,
        reach,
        lambda: per_head_call(
            functools.partial(query_grad_kernel, block_len),
            [(queries, True), (keys, True), (values, True), (d_attn, True),
             (preceding_states, True)],
            [(full, True), (wide, True), (wide, True)],
            5 * pair_flops,
        ),
    )
    key_gradient, value_gradient = per_head_call(
        functools.partial(key_value_grad_kernel, block_len),
        [(key_intra, True), (value_intra, True), (keys, True), (values, True),
         (local_suffix, True), (following, True), (doc_rows, False)],
        [(full, True), (full, True)],
        pair_flops,
    )
    return query_gradient, key_gradient, value_gradient


def solution(mesh):
    return jax.shard_map(
        on_device,
        mesh=mesh,
        in_specs=(
            P(("sub", "head"), ("groups", "ctx"), None),
            P(("sub", "head"), ("groups", "ctx"), None),
            P(("sub", "head"), ("groups", "ctx"), None),
            P(("sub", "head"), ("groups", "ctx"), None),
            P(("sub", "head"), None),
            P(("groups", "ctx")),
        ),
        out_specs=(
            P(("sub", "head"), ("groups", "ctx"), None),
            P(("sub", "head"), ("groups", "ctx"), None),
            P(("sub", "head"), ("groups", "ctx"), None),
        ),
        check_vma=False,
    )
```

time: 183 us -> 151 us (0.83)
  other arithmetic: 67.3 us -> 2.64 us
  waiting for transfers between devices: 5.55 us -> 28.6 us
  Pallas kernels: 64.2 us -> 83.5 us
  local copies, waits for them, and re-layouts: 13.8 us -> 10.3 us
  matrix products: 3.42 us -> 0 us
  between operations: 4.73 us -> 1.94 us
    unnamed x8 -> x0, other arithmetic: 32.8 us -> none
    ppermute x4, waiting for transfers between devices: 5.55 us -> 28.6 us  [shift(): return lax.ppermute(value, axis, pairs)]
    pallas_call x5 -> x8, Pallas kernels: 64.2 us -> 83.5 us  [per_head_call(): pl.pallas_call(kernel, grid=(head_count,), in_specs=[spec(x.shape, h) for...]
    add x4 -> x1, other arithmetic: 17 us -> 0.01 us  [on_device(): doc_rows = lanes(doc_values + 1.0, block_count)]
    another operation x2 -> x0, other arithmetic: 8.16 us -> none  [masked_block_sums(): jnp.stack([masked_block_sum(mask[b], blocks) for b in range(mask.shape[0]...]
    slice x8 -> x0, local copies, waits for them, and re-layouts: 6.96 us -> none  [the longest x4 4.16 us: unpack(): got_doc = jnp.where(valid, got[0, rows, 0], none_doc)]
    convert_element_type x4 -> x0, other arithmetic: 5.47 us -> none  [the longest x1 3.29 us: on_device(): following_states = (local_suffix + leaving).astype(jnp.bfloat16)]
    broadcast_in_dim x0 -> x7, local copies, waits for them, and re-layouts: none -> 4.59 us  [the longest x5 3.4 us: lanes(): return jnp.broadcast_to(table.reshape(rows, 1), (rows, head_width))]
  transfers between devices with their start and end apart: 4 -> 4, of which waited for: 2 -> 3; matrix products, arithmetic and copies ran while one was open for 24% -> 0% of each run, Pallas kernels for 15% -> 18%
where the time goes in v8:
time: 151 us; the launch traced here: 149 us
  Pallas kernels  83.5 us (55%)
  waiting for transfers between devices  28.6 us (19%)
  starting transfers between devices  12 us (8%)
  local copies, waits for them, and re-layouts  10.3 us (7%)
  blocking collectives  10.1 us (7%)
  other arithmetic  2.64 us (2%)
  between operations  1.94 us (1%)
    pallas_call x8, Pallas kernels, per_head_call(): pl.pallas_call(kernel, grid=(head_count,), in_specs=[spec(x.shape, h) for...  83.5 us
    ppermute x4, waiting for transfers between devices, shift(): return lax.ppermute(value, axis, pairs)  28.6 us
    ppermute x4, starting transfers between devices, shift(): return lax.ppermute(value, axis, pairs)  12 us
    psum x1, blocking collectives, on_device(): total_sums = lax.psum(local_sums.T.reshape(2 * tok_count), ('sub', 'head'))  10.1 us
    broadcast_in_dim x5, local copies, waits for them, and re-layouts, lanes(): return jnp.broadcast_to(table.reshape(rows, 1), (rows, head_width))  3.4 us
  transfers between devices with their start and end apart: 4, of which 3 were waited for; matrix products, arithmetic and copies ran while one was open for 0% of the time, Pallas kernels for 18%

profile of v8, /device:TPU:0, one launch (start us, length us, event | category | flops | bytes accessed | tf_op | source)
XLA Modules:
  0.0 149.1 jit_solution(4510070304451350720)
XLA Ops:
  0.6 0.7 convert_element_type.29
  1.3 0.6 fusion.5
  1.9 0.1 fusion.4
  2.6 1.9 %compare_convert_fusion = (f32[5]{0:T(128)S(1)}, f32[5]{0:T(128)S(1)}) fusion(f32[]{:T(128)} %bitcast.3, s32[5]{0:T(128)} %param.11, f32[]{:T(128)} %bitcast.1), kind=kLoop, calls=%fused_computation.12 | loop fusion | flops 25 | bytes 68 | tf_op jit(solution)/shard_map/convert_element_type | solution.py:224
  4.5 0.1 reshape.86
  4.5 0.6 broadcast_in_dim.16.row_ref
  5.1 0.7 broadcast_in_dim.15.end_ref
  5.8 0.7 broadcast_in_dim.14.pair_ref
  6.5 7.6 %shard_map.85 = (f32[8,5,128,128]{3,2,1,0:T(8,128)}, f32[8,136,128]{2,1,0:T(8,128)}) custom-call(bf16[8,1280,128]{2,1,0:T(8,128)(2,1)} %k_ref.9, bf16[8,1280,128]{2,1,0:T(8,128)(2,1)} %v_ref.9, f32[25,128]{1,0:T(8,128)} %broadcast_in_dim.14.pair_ref, f32[5,128]{1,0:T(8,128)} %broadcast_in_dim.15.end_ref, f32[8,128]{1,0:T(8,128)} %broadcast_in_dim.16.row_ref), custom_call_target="tpu_custom_call" | custom-call | flops 335544320 | bytes 8440832 | tf_op jit(solution)/shard_map/pallas_call | solution.py:163
  14.1 0.0 copy-start.4
  14.1 5.1 %collective-permute-start = (f32[8,136,128]{2,1,0:T(8,128)}, f32[8,136,128]{2,1,0:T(8,128)S(1)}, u32[]{:S(2)}, u32[]{:S(2)}) collective-permute-start(f32[8,136,128]{2,1,0:T(8,128)} %get-tuple-element.21.near_ref), channel_id=1, source_target_pairs={{0,4},{4,8},{8,12},{1,5},{5,9},{9,13},{2,6},{6,10},{10,14},{3,7},{... | collective-permute-start | bytes 1671176 | tf_op jit(solution)/shard_map/ppermute | solution.py:190
  19.2 10.2 %shard_map.86.i_ref = f32[8,1280,128]{2,1,0:T(8,128)} custom-call(bf16[8,1280,128]{2,1,0:T(8,128)(2,1)} %q_ref.7, bf16[8,1280,128]{2,1,0:T(8,128)(2,1)} %k_ref.9, bf16[8,1280,128]{2,1,0:T(8,128)(2,1)} %v_ref.9), custom_call_target="tpu_custom_call" | custom-call | flops 1342177280 | bytes 13107200 | tf_op jit(solution)/shard_map/pallas_call | solution.py:163
  29.3 2.0 %collective-permute-done.far_ref = f32[8,136,128]{2,1,0:T(8,128)S(1)} collective-permute-done((f32[8,136,128]{2,1,0:T(8,128)}, f32[8,136,128]{2,1,0:T(8,128)S(1)}, u32[]{:S(2)}, u32[]{:S(2)}) %collective-permute-start) | collective-permute-done | bytes 557088 | tf_op jit(solution)/shard_map/ppermute | solution.py:190
  31.3 0.0 copy-start.2
  31.3 0.8 copy-done.2
  32.1 5.1 %shard_map.87 = f32[8,136,128]{2,1,0:T(8,128)} custom-call(f32[8,136,128]{2,1,0:T(8,128)} %get-tuple-element.21.near_ref, f32[8,136,128]{2,1,0:T(8,128)} %copy-done.2), custom_call_target="tpu_custom_call" | custom-call | flops 278528 | bytes 1671168 | tf_op jit(solution)/shard_map/pallas_call | solution.py:163
  37.2 4.3 %collective-permute-start.1 = (f32[8,136,128]{2,1,0:T(8,128)}, f32[8,136,128]{2,1,0:T(8,128)S(1)}, u32[]{:S(2)}, u32[]{:S(2)}) collective-permute-start(f32[8,136,128]{2,1,0:T(8,128)} %shard_map.87), channel_id=1, source_target_pairs={{0,4},{4,8},{8,12},{1,5},{5,9},{9,13},{2,6},{6,10},{10,14},{3,7},{... | collective-permute-start | bytes 1671176 | tf_op jit(solution)/shard_map/ppermute | solution.py:190
  42.1 0.1 reshape.87
  42.2 0.0 copy-done.4
  42.2 10.6 %collective-permute-done.1.carry_ref = f32[8,136,128]{2,1,0:T(8,128)S(1)} collective-permute-done((f32[8,136,128]{2,1,0:T(8,128)}, f32[8,136,128]{2,1,0:T(8,128)S(1)}, u32[]{:S(2)}, u32[]{:S(2)}) %collective-permute-start.1) | collective-permute-done | bytes 557088 | tf_op jit(solution)/shard_map/ppermute | solution.py:190
  52.8 0.0 copy-start
  52.8 0.7 broadcast_in_dim.17.doc_ref
  53.6 0.1 copy-done
  53.7 10.2 %shard_map.88 = (f32[1280,2]{1,0:T(8,128)}, bf16[8,5,128,128]{3,2,1,0:T(8,128)(2,1)}) custom-call(f32[8,1280,128]{2,1,0:T(8,128)} %shard_map.86.i_ref, bf16[8,1280,128]{2,1,0:T(8,128)(2,1)} %q_ref.7, bf16[8,1280,128]{2,1,0:T(8,128)(2,1)} %g_ref.3, f32[8,1,128]{2,1,0:T(1,128)} %bitcast.5, f32[8,5,128,128]{3,2,1,0:T(8,128)} %get-tuple-element.23.prefix_ref, ...), custom_call_target="tpu_custom_call" | custom-call | flops 335544320 | bytes 14991872 | tf_op jit(solution)/shard_map/pallas_call | solution.py:163
  63.8 1.3 copy.12
  65.2 10.1 %psum.7 = f32[2560]{0:T(1024)S(1)} all-reduce(f32[2560]{0:T(1024)S(1)} %reshape.85), channel_id=1, replica_groups=mesh['groups'=2,'ctx'=4,'sub'=2,'head'=2] {'sub','head'}, use_global_device_ids=true, to_apply=%region_0.0 | all-reduce | flops 2560 | bytes 20480 | tf_op jit(solution)/shard_map/psum | solution.py:274
  75.4 1.1 copy.13.c_ref
  76.5 0.7 broadcast_in_dim.19.end_ref
  77.1 0.6 broadcast_in_dim.20.row_ref
  77.7 0.7 broadcast_in_dim.18.pair_ref
  78.4 17.5 %shard_map.89 = (bf16[8,1280,128]{2,1,0:T(8,128)(2,1)}, f32[8,5,128,128]{3,2,1,0:T(8,128)}, f32[8,136,128]{2,1,0:T(8,128)}) custom-call(bf16[8,1280,128]{2,1,0:T(8,128)(2,1)} %q_ref.7, bf16[8,1280,128]{2,1,0:T(8,128)(2,1)} %k_ref.9, bf16[8,1280,128]{2,1,0:T(8,128)(2,1)} %v_ref.9, bf16[8,1280,128]{2,1,0:T(8,128)(2,1)} %g_ref.3, f32[8,1,128]{2,1,0:T(1,128)} %bitcast.6, ...), custom_call_target="tpu_custom_call" | custom-call | flops 2013265920 | bytes 17630208 | tf_op jit(solution)/shard_map/pallas_call | solution.py:163
  95.9 1.3 collective-permute-start.2
  97.2 16.8 %shard_map.90 = (bf16[8,1280,128]{2,1,0:T(8,128)(2,1)}, f32[8,1280,128]{2,1,0:T(8,128)}, f32[8,1280,128]{2,1,0:T(8,128)}) custom-call(bf16[8,1280,128]{2,1,0:T(8,128)(2,1)} %q_ref.7, bf16[8,1280,128]{2,1,0:T(8,128)(2,1)} %k_ref.9, bf16[8,1280,128]{2,1,0:T(8,128)(2,1)} %v_ref.9, bf16[8,1280,128]{2,1,0:T(8,128)(2,1)} %get-tuple-element.28.d_ref, ...), custom_call_target="tpu_custom_call" | custom-call | flops 3355443200 | bytes 24903680 | tf_op jit(solution)/shard_map/pallas_call | solution.py:163
  114.0 0.0 collective-permute-done.2.far_ref
  114.0 0.0 copy-start.1
  114.0 0.8 copy-done.1
  114.8 5.1 %shard_map.91 = f32[8,136,128]{2,1,0:T(8,128)} custom-call(f32[8,136,128]{2,1,0:T(8,128)} %get-tuple-element.27.near_ref, f32[8,136,128]{2,1,0:T(8,128)} %copy-done.1), custom_call_target="tpu_custom_call" | custom-call | flops 278528 | bytes 1671168 | tf_op jit(solution)/shard_map/pallas_call | solution.py:163
  119.9 1.3 collective-permute-start.3
  121.2 16.0 %collective-permute-done.3.carry_ref = f32[8,136,128]{2,1,0:T(8,128)S(1)} collective-permute-done((f32[8,136,128]{2,1,0:T(8,128)}, f32[8,136,128]{2,1,0:T(8,128)S(1)}, u32[]{:S(2)}, u32[]{:S(2)}) %collective-permute-start.3) | collective-permute-done | bytes 557088 | tf_op jit(solution)/shard_map/ppermute | solution.py:190
  137.2 0.0 copy-start.3
  137.2 0.8 copy-done.3
  138.0 11.0 %shard_map.92 = (bf16[8,1280,128]{2,1,0:T(8,128)(2,1)}, bf16[8,1280,128]{2,1,0:T(8,128)(2,1)}) custom-call(f32[8,1280,128]{2,1,0:T(8,128)} %get-tuple-element.33.ik_ref, f32[8,1280,128]{2,1,0:T(8,128)} %get-tuple-element.34.iv_ref, bf16[8,1280,128]{2,1,0:T(8,128)(2,1)} %k_ref.9, bf16[8,1280,128]{2,1,0:T(8,128)(2,1)} %v_ref.9, ...), custom_call_target="tpu_custom_call" | custom-call | flops 671088640 | bytes 24152576 | tf_op jit(solution)/shard_map/pallas_call | solution.py:163
  (6 shorter events, 0.1 us)
Async XLA Ops:
  14.1 28.1 %copy-start.4 = (s32[5]{0:T(128)S(1)}, s32[5]{0:T(128)}, u32[]{:S(2)}) copy-start(s32[5]{0:T(128)} %param.11) | copy-start | bytes 64
  14.1 17.2 %collective-permute-start = (f32[8,136,128]{2,1,0:T(8,128)}, f32[8,136,128]{2,1,0:T(8,128)S(1)}, u32[]{:S(2)}, u32[]{:S(2)}) collective-permute-start(f32[8,136,128]{2,1,0:T(8,128)} %get-tuple-element.21.near_ref), channel_id=1, source_target_pairs={{0,4},{4,8},{8,12},{1,5},{5,9},{9,13},{2,6},{6,10},{10,14},{3,7},{... | collective-permute-start | bytes 1671176 | tf_op jit(solution)/shard_map/ppermute | solution.py:190
  31.3 0.8 copy-start.2
  37.2 15.6 %collective-permute-start.1 = (f32[8,136,128]{2,1,0:T(8,128)}, f32[8,136,128]{2,1,0:T(8,128)S(1)}, u32[]{:S(2)}, u32[]{:S(2)}) collective-permute-start(f32[8,136,128]{2,1,0:T(8,128)} %shard_map.87), channel_id=1, source_target_pairs={{0,4},{4,8},{8,12},{1,5},{5,9},{9,13},{2,6},{6,10},{10,14},{3,7},{... | collective-permute-start | bytes 1671176 | tf_op jit(solution)/shard_map/ppermute | solution.py:190
  52.8 0.8 copy-start
  95.9 18.1 %collective-permute-start.2 = (f32[8,136,128]{2,1,0:T(8,128)}, f32[8,136,128]{2,1,0:T(8,128)S(1)}, u32[]{:S(2)}, u32[]{:S(2)}) collective-permute-start(f32[8,136,128]{2,1,0:T(8,128)} %get-tuple-element.27.near_ref), channel_id=1, source_target_pairs={{4,0},{8,4},{12,8},{5,1},{9,5},{13,9},{6,2},{10,6},{14,10},{7,3},{... | collective-permute-start | bytes 1671176 | tf_op jit(solution)/shard_map/ppermute | solution.py:190
  114.0 0.8 copy-start.1
  119.9 17.3 %collective-permute-start.3 = (f32[8,136,128]{2,1,0:T(8,128)}, f32[8,136,128]{2,1,0:T(8,128)S(1)}, u32[]{:S(2)}, u32[]{:S(2)}) collective-permute-start(f32[8,136,128]{2,1,0:T(8,128)} %shard_map.91), channel_id=1, source_target_pairs={{4,0},{8,4},{12,8},{5,1},{9,5},{13,9},{6,2},{10,6},{14,10},{7,3},{... | collective-permute-start | bytes 1671176 | tf_op jit(solution)/shard_map/ppermute | solution.py:190
  137.2 0.8 copy-start.3

commit v9 on v8

--- a/solution.py
+++ b/solution.py
@@ -51,11 +51,12 @@
 
 def combine_kernel(near_ref, far_ref, o_ref):
     width = near_ref.shape[2]
-    joined = near_ref[0, width : width + 1, :] == far_ref[0, width : width + 1, :]
-    o_ref[0, :width, :] = near_ref[0, :width, :] + jnp.where(
-        joined, far_ref[0, :width, :], 0.0
-    )
-    o_ref[0, width:, :] = near_ref[0, width:, :]
+    for h in range(near_ref.shape[0]):
+        joined = near_ref[h, width : width + 1, :] == far_ref[h, width : width + 1, :]
+        o_ref[h, :width, :] = near_ref[h, :width, :] + jnp.where(
+            joined, far_ref[h, :width, :], 0.0
+        )
+        o_ref[h, width:, :] = near_ref[h, width:, :]
 
 
 def intra_kernel(block_len, q_ref, k_ref, v_ref, o_ref):
@@ -173,9 +174,13 @@
 
 
 def combine(near, far):
-    return per_head_call(
-        combine_kernel, [(near, True), (far, True)], [(near, True)], 2 * near.size
-    )[0]
+    return pl.pallas_call(
+        combine_kernel,
+        out_shape=jax.ShapeDtypeStruct(near.shape, near.dtype),
+        cost_estimate=pl.CostEstimate(
+            flops=2 * near.size, transcendentals=0, bytes_accessed=3 * near.size * 4
+        ),
+    )(near, far)
 
 
 def carry(payload, axis, reverse, reach, cover):
@@ -271,7 +276,12 @@
         pair_flops // 2,
     )
     feature_count = head_count * head_width * lax.axis_size(("sub", "head"))
-    total_sums = lax.psum(local_sums.T.reshape(2 * tok_count), ("sub", "head"))
+    total_sums = local_sums.T.reshape(2 * tok_count)
+    for axis in ("head", "sub"):
+        if lax.axis_size(axis) == 2:
+            total_sums = total_sums + lax.ppermute(total_sums, axis, [(0, 1), (1, 0)])
+        elif lax.axis_size(axis) > 2:
+            total_sums = lax.psum(total_sums, axis)
     root_mean = jnp.sqrt(total_sums[:tok_count] / feature_count + 1e-06)
     inner_mean = total_sums[tok_count:] / feature_count
     factor = inner_mean / (root_mean * root_mean)

time: 151 us -> 139 us (0.921)
  blocking collectives: 10.1 us -> 0 us
  Pallas kernels: 83.5 us -> 77.4 us
  waiting for transfers between devices: 28.6 us -> 31.5 us
    pallas_call x8 -> x6, Pallas kernels: 83.5 us -> 73.2 us  [per_head_call(): pl.pallas_call(kernel, grid=(head_count,), in_specs=[spec(x.shape, h) for...]
    psum x1 -> x0, blocking collectives: 10.1 us -> none  [on_device(): total_sums = lax.psum(local_sums.T.reshape(2 * tok_count), ('sub', 'head'))]
    pallas_call x0 -> x2, Pallas kernels: none -> 4.21 us  [combine(): pl.pallas_call(combine_kernel, out_shape=jax.ShapeDtypeStruct(near.shape,...]
    ppermute x0 -> x2, waiting for transfers between devices: none -> 2.6 us  [on_device(): total_sums = total_sums + lax.ppermute(total_sums, axis, [(0, 1), (1, 0)])]
    ppermute x0 -> x2, starting transfers between devices: none -> 1.56 us  [on_device(): total_sums = total_sums + lax.ppermute(total_sums, axis, [(0, 1), (1, 0)])]
  transfers between devices with their start and end apart: 4 -> 6, of which waited for: 3 -> 5; matrix products, arithmetic and copies ran while one was open for 0% -> 0% of each run, Pallas kernels for 18% -> 20%
where the time goes in v9:
time: 139 us; the launch traced here: 138 us
  Pallas kernels  77.4 us (56%)
  waiting for transfers between devices  31.5 us (23%)
  starting transfers between devices  13.5 us (10%)
  local copies, waits for them, and re-layouts  10.3 us (7%)
  other arithmetic  2.77 us (2%)
  between operations  2.09 us (2%)
    pallas_call x6, Pallas kernels, per_head_call(): pl.pallas_call(kernel, grid=(head_count,), in_specs=[spec(x.shape, h) for...  73.2 us
    ppermute x4, waiting for transfers between devices, shift(): return lax.ppermute(value, axis, pairs)  28.9 us
    ppermute x4, starting transfers between devices, shift(): return lax.ppermute(value, axis, pairs)  12 us
    pallas_call x2, Pallas kernels, combine(): pl.pallas_call(combine_kernel, out_shape=jax.ShapeDtypeStruct(near.shape,...  4.21 us
    broadcast_in_dim x5, local copies, waits for them, and re-layouts, lanes(): return jnp.broadcast_to(table.reshape(rows, 1), (rows, head_width))  3.44 us
  transfers between devices with their start and end apart: 6, of which 5 were waited for; matrix products, arithmetic and copies ran while one was open for 0% of the time, Pallas kernels for 20%

profile of v9, /device:TPU:0, one launch (start us, length us, event | category | flops | bytes accessed | tf_op | source)
XLA Modules:
  0.0 137.6 jit_solution(2692009935509445197)
XLA Ops:
  0.6 0.7 convert_element_type.29
  1.3 0.6 fusion.5
  1.9 0.1 fusion.4
  2.6 2.0 %compare_convert_fusion = (f32[5]{0:T(128)S(1)}, f32[5]{0:T(128)S(1)}) fusion(f32[]{:T(128)} %bitcast.3, s32[5]{0:T(128)} %param.11, f32[]{:T(128)} %bitcast.1), kind=kLoop, calls=%fused_computation.12 | loop fusion | flops 25 | bytes 68 | tf_op jit(solution)/shard_map/convert_element_type | solution.py:229
  4.6 0.1 reshape.86
  4.7 0.6 broadcast_in_dim.16.row_ref
  5.3 0.7 broadcast_in_dim.15.end_ref
  5.9 0.7 broadcast_in_dim.14.pair_ref
  6.6 7.6 %shard_map.85 = (f32[8,5,128,128]{3,2,1,0:T(8,128)}, f32[8,136,128]{2,1,0:T(8,128)}) custom-call(bf16[8,1280,128]{2,1,0:T(8,128)(2,1)} %k_ref.9, bf16[8,1280,128]{2,1,0:T(8,128)(2,1)} %v_ref.9, f32[25,128]{1,0:T(8,128)} %broadcast_in_dim.14.pair_ref, f32[5,128]{1,0:T(8,128)} %broadcast_in_dim.15.end_ref, f32[8,128]{1,0:T(8,128)} %broadcast_in_dim.16.row_ref), custom_call_target="tpu_custom_call" | custom-call | flops 335544320 | bytes 8440832 | tf_op jit(solution)/shard_map/pallas_call | solution.py:164
  14.2 0.0 copy-start.4
  14.2 5.1 %collective-permute-start = (f32[8,136,128]{2,1,0:T(8,128)}, f32[8,136,128]{2,1,0:T(8,128)S(1)}, u32[]{:S(2)}, u32[]{:S(2)}) collective-permute-start(f32[8,136,128]{2,1,0:T(8,128)} %get-tuple-element.21.near_ref), channel_id=1, source_target_pairs={{0,4},{4,8},{8,12},{1,5},{5,9},{9,13},{2,6},{6,10},{10,14},{3,7},{... | collective-permute-start | bytes 1671176 | tf_op jit(solution)/shard_map/ppermute | solution.py:195
  19.3 10.2 %shard_map.86.i_ref = f32[8,1280,128]{2,1,0:T(8,128)} custom-call(bf16[8,1280,128]{2,1,0:T(8,128)(2,1)} %q_ref.7, bf16[8,1280,128]{2,1,0:T(8,128)(2,1)} %k_ref.9, bf16[8,1280,128]{2,1,0:T(8,128)(2,1)} %v_ref.9), custom_call_target="tpu_custom_call" | custom-call | flops 1342177280 | bytes 13107200 | tf_op jit(solution)/shard_map/pallas_call | solution.py:164
  29.5 2.0 %collective-permute-done.far_ref = f32[8,136,128]{2,1,0:T(8,128)S(1)} collective-permute-done((f32[8,136,128]{2,1,0:T(8,128)}, f32[8,136,128]{2,1,0:T(8,128)S(1)}, u32[]{:S(2)}, u32[]{:S(2)}) %collective-permute-start) | collective-permute-done | bytes 557088 | tf_op jit(solution)/shard_map/ppermute | solution.py:195
  31.5 0.0 copy-start.2
  31.5 0.8 copy-done.2
  32.3 2.1 %shard_map.87 = f32[8,136,128]{2,1,0:T(8,128)} custom-call(f32[8,136,128]{2,1,0:T(8,128)} %get-tuple-element.21.near_ref, f32[8,136,128]{2,1,0:T(8,128)} %copy-done.2), custom_call_target="tpu_custom_call" | custom-call | flops 278528 | bytes 1671168 | tf_op jit(solution)/shard_map/pallas_call | solution.py:177
  34.4 4.3 %collective-permute-start.1 = (f32[8,136,128]{2,1,0:T(8,128)}, f32[8,136,128]{2,1,0:T(8,128)S(1)}, u32[]{:S(2)}, u32[]{:S(2)}) collective-permute-start(f32[8,136,128]{2,1,0:T(8,128)} %shard_map.87), channel_id=1, source_target_pairs={{0,4},{4,8},{8,12},{1,5},{5,9},{9,13},{2,6},{6,10},{10,14},{3,7},{... | collective-permute-start | bytes 1671176 | tf_op jit(solution)/shard_map/ppermute | solution.py:195
  38.7 0.0 copy-done.4
  38.7 11.3 %collective-permute-done.1.carry_ref = f32[8,136,128]{2,1,0:T(8,128)S(1)} collective-permute-done((f32[8,136,128]{2,1,0:T(8,128)}, f32[8,136,128]{2,1,0:T(8,128)S(1)}, u32[]{:S(2)}, u32[]{:S(2)}) %collective-permute-start.1) | collective-permute-done | bytes 557088 | tf_op jit(solution)/shard_map/ppermute | solution.py:195
  50.0 0.0 copy-start
  50.0 0.8 broadcast_in_dim.17.doc_ref
  50.8 0.0 copy-done
  50.8 10.2 %shard_map.88 = (f32[1280,2]{1,0:T(8,128)}, bf16[8,5,128,128]{3,2,1,0:T(8,128)(2,1)}) custom-call(f32[8,1280,128]{2,1,0:T(8,128)} %shard_map.86.i_ref, bf16[8,1280,128]{2,1,0:T(8,128)(2,1)} %q_ref.7, bf16[8,1280,128]{2,1,0:T(8,128)(2,1)} %g_ref.3, f32[8,1,128]{2,1,0:T(1,128)} %bitcast.5, f32[8,5,128,128]{3,2,1,0:T(8,128)} %get-tuple-element.23.prefix_ref, ...), custom_call_target="tpu_custom_call" | custom-call | flops 335544320 | bytes 14991872 | tf_op jit(solution)/shard_map/pallas_call | solution.py:164
  61.0 1.3 copy.12
  62.3 0.1 collective-permute-start.2
  62.4 1.2 collective-permute-done.2
  63.5 1.5 %collective-permute-start.3 = (f32[2560]{0:T(1024)S(1)}, f32[2560]{0:T(1024)S(1)}, u32[]{:S(2)}, u32[]{:S(2)}) collective-permute-start(f32[2560]{0:T(1024)S(1)} %add.23), channel_id=1, source_target_pairs={{0,2},{2,0},{1,3},{3,1},{4,6},{6,4},{5,7},{7,5},{8,10},{10,8},{9,1... | collective-permute-start | bytes 30728 | tf_op jit(solution)/shard_map/ppermute | solution.py:282
  65.7 0.1 reshape.87
  65.8 1.4 %collective-permute-done.3 = f32[2560]{0:T(1024)S(1)} collective-permute-done((f32[2560]{0:T(1024)S(1)}, f32[2560]{0:T(1024)S(1)}, u32[]{:S(2)}, u32[]{:S(2)}) %collective-permute-start.3) | collective-permute-done | bytes 10272 | tf_op jit(solution)/shard_map/ppermute | solution.py:282
  67.3 1.1 copy.13.c_ref
  68.4 0.7 broadcast_in_dim.19.end_ref
  69.1 0.6 broadcast_in_dim.20.row_ref
  69.7 0.7 broadcast_in_dim.18.pair_ref
  70.3 17.5 %shard_map.89 = (bf16[8,1280,128]{2,1,0:T(8,128)(2,1)}, f32[8,5,128,128]{3,2,1,0:T(8,128)}, f32[8,136,128]{2,1,0:T(8,128)}) custom-call(bf16[8,1280,128]{2,1,0:T(8,128)(2,1)} %q_ref.7, bf16[8,1280,128]{2,1,0:T(8,128)(2,1)} %k_ref.9, bf16[8,1280,128]{2,1,0:T(8,128)(2,1)} %v_ref.9, bf16[8,1280,128]{2,1,0:T(8,128)(2,1)} %g_ref.3, f32[8,1,128]{2,1,0:T(1,128)} %bitcast.6, ...), custom_call_target="tpu_custom_call" | custom-call | flops 2013265920 | bytes 17630208 | tf_op jit(solution)/shard_map/pallas_call | solution.py:164
  87.9 1.3 collective-permute-start.4
  89.2 16.8 %shard_map.90 = (bf16[8,1280,128]{2,1,0:T(8,128)(2,1)}, f32[8,1280,128]{2,1,0:T(8,128)}, f32[8,1280,128]{2,1,0:T(8,128)}) custom-call(bf16[8,1280,128]{2,1,0:T(8,128)(2,1)} %q_ref.7, bf16[8,1280,128]{2,1,0:T(8,128)(2,1)} %k_ref.9, bf16[8,1280,128]{2,1,0:T(8,128)(2,1)} %v_ref.9, bf16[8,1280,128]{2,1,0:T(8,128)(2,1)} %get-tuple-element.28.d_ref, ...), custom_call_target="tpu_custom_call" | custom-call | flops 3355443200 | bytes 24903680 | tf_op jit(solution)/shard_map/pallas_call | solution.py:164
  106.0 0.0 collective-permute-done.4.far_ref
  106.0 0.0 copy-start.1
  106.0 0.8 copy-done.1
  106.8 2.1 %shard_map.91 = f32[8,136,128]{2,1,0:T(8,128)} custom-call(f32[8,136,128]{2,1,0:T(8,128)} %get-tuple-element.27.near_ref, f32[8,136,128]{2,1,0:T(8,128)} %copy-done.1), custom_call_target="tpu_custom_call" | custom-call | flops 278528 | bytes 1671168 | tf_op jit(solution)/shard_map/pallas_call | solution.py:177
  108.9 1.3 collective-permute-start.5
  110.2 15.6 %collective-permute-done.5.carry_ref = f32[8,136,128]{2,1,0:T(8,128)S(1)} collective-permute-done((f32[8,136,128]{2,1,0:T(8,128)}, f32[8,136,128]{2,1,0:T(8,128)S(1)}, u32[]{:S(2)}, u32[]{:S(2)}) %collective-permute-start.5) | collective-permute-done | bytes 557088 | tf_op jit(solution)/shard_map/ppermute | solution.py:195
  125.8 0.0 copy-start.3
  125.8 0.8 copy-done.3
  126.6 11.0 %shard_map.92 = (bf16[8,1280,128]{2,1,0:T(8,128)(2,1)}, bf16[8,1280,128]{2,1,0:T(8,128)(2,1)}) custom-call(f32[8,1280,128]{2,1,0:T(8,128)} %get-tuple-element.33.ik_ref, f32[8,1280,128]{2,1,0:T(8,128)} %get-tuple-element.34.iv_ref, bf16[8,1280,128]{2,1,0:T(8,128)(2,1)} %k_ref.9, bf16[8,1280,128]{2,1,0:T(8,128)(2,1)} %v_ref.9, ...), custom_call_target="tpu_custom_call" | custom-call | flops 671088640 | bytes 24152576 | tf_op jit(solution)/shard_map/pallas_call | solution.py:164
  (8 shorter events, 0.1 us)
Async XLA Ops:
  14.2 24.5 %copy-start.4 = (s32[5]{0:T(128)S(1)}, s32[5]{0:T(128)}, u32[]{:S(2)}) copy-start(s32[5]{0:T(128)} %param.11) | copy-start | bytes 64
  14.2 17.2 %collective-permute-start = (f32[8,136,128]{2,1,0:T(8,128)}, f32[8,136,128]{2,1,0:T(8,128)S(1)}, u32[]{:S(2)}, u32[]{:S(2)}) collective-permute-start(f32[8,136,128]{2,1,0:T(8,128)} %get-tuple-element.21.near_ref), channel_id=1, source_target_pairs={{0,4},{4,8},{8,12},{1,5},{5,9},{9,13},{2,6},{6,10},{10,14},{3,7},{... | collective-permute-start | bytes 1671176 | tf_op jit(solution)/shard_map/ppermute | solution.py:195
  31.5 0.8 copy-start.2
  34.4 15.6 %collective-permute-start.1 = (f32[8,136,128]{2,1,0:T(8,128)}, f32[8,136,128]{2,1,0:T(8,128)S(1)}, u32[]{:S(2)}, u32[]{:S(2)}) collective-permute-start(f32[8,136,128]{2,1,0:T(8,128)} %shard_map.87), channel_id=1, source_target_pairs={{0,4},{4,8},{8,12},{1,5},{5,9},{9,13},{2,6},{6,10},{10,14},{3,7},{... | collective-permute-start | bytes 1671176 | tf_op jit(solution)/shard_map/ppermute | solution.py:195
  50.0 0.8 copy-start
  62.3 1.2 collective-permute-start.2
  63.5 3.7 %collective-permute-start.3 = (f32[2560]{0:T(1024)S(1)}, f32[2560]{0:T(1024)S(1)}, u32[]{:S(2)}, u32[]{:S(2)}) collective-permute-start(f32[2560]{0:T(1024)S(1)} %add.23), channel_id=1, source_target_pairs={{0,2},{2,0},{1,3},{3,1},{4,6},{6,4},{5,7},{7,5},{8,10},{10,8},{9,1... | collective-permute-start | bytes 30728 | tf_op jit(solution)/shard_map/ppermute | solution.py:282
  87.9 18.1 %collective-permute-start.4 = (f32[8,136,128]{2,1,0:T(8,128)}, f32[8,136,128]{2,1,0:T(8,128)S(1)}, u32[]{:S(2)}, u32[]{:S(2)}) collective-permute-start(f32[8,136,128]{2,1,0:T(8,128)} %get-tuple-element.27.near_ref), channel_id=1, source_target_pairs={{4,0},{8,4},{12,8},{5,1},{9,5},{13,9},{6,2},{10,6},{14,10},{7,3},{... | collective-permute-start | bytes 1671176 | tf_op jit(solution)/shard_map/ppermute | solution.py:195
  106.0 0.8 copy-start.1
  108.9 16.9 %collective-permute-start.5 = (f32[8,136,128]{2,1,0:T(8,128)}, f32[8,136,128]{2,1,0:T(8,128)S(1)}, u32[]{:S(2)}, u32[]{:S(2)}) collective-permute-start(f32[8,136,128]{2,1,0:T(8,128)} %shard_map.91), channel_id=1, source_target_pairs={{4,0},{8,4},{12,8},{5,1},{9,5},{13,9},{6,2},{10,6},{14,10},{7,3},{... | collective-permute-start | bytes 1671176 | tf_op jit(solution)/shard_map/ppermute | solution.py:195
  125.8 0.8 copy-start.3

commit v10 on v9

--- a/solution.py
+++ b/solution.py
@@ -70,7 +70,7 @@
 
 
 def forward_kernel(
-    block_len, i_ref, q_ref, g_ref, n_ref, prefix_ref, carry_ref, doc_ref, o_ref, s_ref
+    block_len, i_ref, q_ref, g_ref, n_ref, prefix_ref, carry_ref, doc_ref, o_ref, s_ref, r_ref
 ):
     @pl.when(pl.program_id(0) == 0)
     def _():
@@ -83,26 +83,23 @@
         raw = i_ref[0, rows, :] + jnp.dot(
             q_ref[0, rows, :], state, preferred_element_type=jnp.float32
         )
+        r_ref[0, rows, :] = raw
         scaled = n_ref[0] * g_ref[0, rows, :].astype(jnp.float32)
         o_ref[rows, 0:1] += jnp.sum(raw * raw, axis=1, keepdims=True)
         o_ref[rows, 1:2] += jnp.sum(scaled * raw, axis=1, keepdims=True)
 
 
 def grad_kernel(
-    block_len, q_ref, k_ref, v_ref, g_ref, n_ref, s_ref, c_ref, pair_ref, end_ref, row_ref,
+    block_len, q_ref, r_ref, g_ref, n_ref, c_ref, pair_ref, end_ref, row_ref,
     d_ref, suffix_ref, pay_ref,
 ):
-    causal = _causal(block_len)
     count = q_ref.shape[1] // block_len
     width = q_ref.shape[2]
     parts = []
     for n in range(count):
         rows = pl.ds(n * block_len, block_len)
-        q, k, v = q_ref[0, rows, :], k_ref[0, rows, :], v_ref[0, rows, :]
-        scores = lax.dot_general(q, k, _ROWS_MINOR, preferred_element_type=jnp.float32)
-        probs = jnp.where(causal, scores, 0.0).astype(jnp.bfloat16)
-        raw = jnp.dot(probs, v, preferred_element_type=jnp.float32)
-        raw = raw + jnp.dot(q, s_ref[0, n], preferred_element_type=jnp.float32)
+        q = q_ref[0, rows, :]
+        raw = r_ref[0, rows, :]
         scaled = n_ref[0] * g_ref[0, rows, :].astype(jnp.float32)
         root_mean = c_ref[rows, 0:1]
         factor = c_ref[rows, 1:2]
@@ -267,12 +264,12 @@
             2 * pair_flops,
         )[0],
     )
-    local_sums, preceding_states = per_head_call(
+    local_sums, preceding_states, raw_attn = per_head_call(
         functools.partial(forward_kernel, block_len),
         [(intra_part, True), (queries, True), (out_grad, True), (gain, True),
          (local_prefix, True), (prior, True), (doc_rows, False)],
         [(jax.ShapeDtypeStruct((tok_count, 2), jnp.float32), False),
-         (jax.ShapeDtypeStruct(states.shape, jnp.bfloat16), True)],
+         (jax.ShapeDtypeStruct(states.shape, jnp.bfloat16), True), (wide, True)],
         pair_flops // 2,
     )
     feature_count = head_count * head_width * lax.axis_size(("sub", "head"))
@@ -288,11 +285,10 @@
     coefs = jnp.stack([root_mean, factor], axis=1)
     d_attn, local_suffix, qd_payload = per_head_call(
         functools.partial(grad_kernel, block_len),
-        [(queries, True), (keys, True), (values, True), (out_grad, True), (gain, True),
-         (preceding_states, True), (coefs, False), (later_rows, False), (first_rows, False),
-         (first_doc_rows, False)],
+        [(queries, True), (raw_attn, True), (out_grad, True), (gain, True),
+         (coefs, False), (later_rows, False), (first_rows, False), (first_doc_rows, False)],
         [(full, True), (states, True), (payload, True)],
-        3 * pair_flops,
+        pair_flops // 2,
     )
     following, (query_gradient, key_intra, value_intra) = carry(
         qd_payload,

time: 139 us -> 133 us (0.957)
  Pallas kernels: 77.4 us -> 71.6 us
    pallas_call x6, Pallas kernels: 73.2 us -> 67.4 us  [per_head_call(): pl.pallas_call(kernel, grid=(head_count,), in_specs=[spec(x.shape, h) for...]
  transfers between devices with their start and end apart: 6 -> 6, of which waited for: 5 -> 5; matrix products, arithmetic and copies ran while one was open for 0% -> 0% of each run, Pallas kernels for 20% -> 21%
where the time goes in v10:
time: 133 us; the launch traced here: 132 us
  Pallas kernels  71.6 us (54%)
  waiting for transfers between devices  31.5 us (24%)
  starting transfers between devices  13.5 us (10%)
  local copies, waits for them, and re-layouts  10.3 us (8%)
  other arithmetic  2.71 us (2%)
  between operations  2.04 us (2%)
    pallas_call x6, Pallas kernels, per_head_call(): pl.pallas_call(kernel, grid=(head_count,), in_specs=[spec(x.shape, h) for...  67.4 us
    ppermute x4, waiting for transfers between devices, shift(): return lax.ppermute(value, axis, pairs)  28.8 us
    ppermute x4, starting transfers between devices, shift(): return lax.ppermute(value, axis, pairs)  11.9 us
    pallas_call x2, Pallas kernels, combine(): pl.pallas_call(combine_kernel, out_shape=jax.ShapeDtypeStruct(near.shape,...  4.19 us
    broadcast_in_dim x5, local copies, waits for them, and re-layouts, lanes(): return jnp.broadcast_to(table.reshape(rows, 1), (rows, head_width))  3.41 us
    ppermute x2, waiting for transfers between devices, on_device(): total_sums = total_sums + lax.ppermute(total_sums, axis, [(0, 1), (1, 0)])  2.66 us
  transfers between devices with their start and end apart: 6, of which 5 were waited for; matrix products, arithmetic and copies ran while one was open for 0% of the time, Pallas kernels for 21%

profile of v10, /device:TPU:0, one launch (start us, length us, event | category | flops | bytes accessed | tf_op | source)
XLA Modules:
  0.0 131.6 jit_solution(15012980685828011872)
XLA Ops:
  0.6 0.7 convert_element_type.29
  1.3 0.6 fusion.5
  1.9 0.1 fusion.4
  2.6 1.9 %compare_convert_fusion = (f32[5]{0:T(128)S(1)}, f32[5]{0:T(128)S(1)}) fusion(f32[]{:T(128)} %bitcast.3, s32[5]{0:T(128)} %param.11, f32[]{:T(128)} %bitcast), kind=kLoop, calls=%fused_computation.12 | loop fusion | flops 25 | bytes 68 | tf_op jit(solution)/shard_map/convert_element_type | solution.py:226
  4.5 0.1 reshape.86
  4.6 0.6 broadcast_in_dim.16.row_ref
  5.2 0.7 broadcast_in_dim.15.end_ref
  5.9 0.7 broadcast_in_dim.14.pair_ref
  6.5 7.6 %shard_map.85 = (f32[8,5,128,128]{3,2,1,0:T(8,128)}, f32[8,136,128]{2,1,0:T(8,128)}) custom-call(bf16[8,1280,128]{2,1,0:T(8,128)(2,1)} %k_ref.7, bf16[8,1280,128]{2,1,0:T(8,128)(2,1)} %v_ref.7, f32[25,128]{1,0:T(8,128)} %broadcast_in_dim.14.pair_ref, f32[5,128]{1,0:T(8,128)} %broadcast_in_dim.15.end_ref, f32[8,128]{1,0:T(8,128)} %broadcast_in_dim.16.row_ref), custom_call_target="tpu_custom_call" | custom-call | flops 335544320 | bytes 8440832 | tf_op jit(solution)/shard_map/pallas_call | solution.py:161
  14.1 0.0 copy-start.4
  14.1 5.1 %collective-permute-start = (f32[8,136,128]{2,1,0:T(8,128)}, f32[8,136,128]{2,1,0:T(8,128)S(1)}, u32[]{:S(2)}, u32[]{:S(2)}) collective-permute-start(f32[8,136,128]{2,1,0:T(8,128)} %get-tuple-element.22.near_ref), channel_id=1, source_target_pairs={{0,4},{4,8},{8,12},{1,5},{5,9},{9,13},{2,6},{6,10},{10,14},{3,7},{... | collective-permute-start | bytes 1671176 | tf_op jit(solution)/shard_map/ppermute | solution.py:192
  19.2 10.2 %shard_map.86.i_ref = f32[8,1280,128]{2,1,0:T(8,128)} custom-call(bf16[8,1280,128]{2,1,0:T(8,128)(2,1)} %q_ref.7, bf16[8,1280,128]{2,1,0:T(8,128)(2,1)} %k_ref.7, bf16[8,1280,128]{2,1,0:T(8,128)(2,1)} %v_ref.7), custom_call_target="tpu_custom_call" | custom-call | flops 1342177280 | bytes 13107200 | tf_op jit(solution)/shard_map/pallas_call | solution.py:161
  29.4 2.0 %collective-permute-done.far_ref = f32[8,136,128]{2,1,0:T(8,128)S(1)} collective-permute-done((f32[8,136,128]{2,1,0:T(8,128)}, f32[8,136,128]{2,1,0:T(8,128)S(1)}, u32[]{:S(2)}, u32[]{:S(2)}) %collective-permute-start) | collective-permute-done | bytes 557088 | tf_op jit(solution)/shard_map/ppermute | solution.py:192
  31.4 0.0 copy-start.2
  31.4 0.8 copy-done.2
  32.2 2.1 %shard_map.87 = f32[8,136,128]{2,1,0:T(8,128)} custom-call(f32[8,136,128]{2,1,0:T(8,128)} %get-tuple-element.22.near_ref, f32[8,136,128]{2,1,0:T(8,128)} %copy-done.2), custom_call_target="tpu_custom_call" | custom-call | flops 278528 | bytes 1671168 | tf_op jit(solution)/shard_map/pallas_call | solution.py:174
  34.3 4.3 %collective-permute-start.1 = (f32[8,136,128]{2,1,0:T(8,128)}, f32[8,136,128]{2,1,0:T(8,128)S(1)}, u32[]{:S(2)}, u32[]{:S(2)}) collective-permute-start(f32[8,136,128]{2,1,0:T(8,128)} %shard_map.87), channel_id=1, source_target_pairs={{0,4},{4,8},{8,12},{1,5},{5,9},{9,13},{2,6},{6,10},{10,14},{3,7},{... | collective-permute-start | bytes 1671176 | tf_op jit(solution)/shard_map/ppermute | solution.py:192
  38.6 0.0 copy-done.4
  38.6 11.3 %collective-permute-done.1.carry_ref = f32[8,136,128]{2,1,0:T(8,128)S(1)} collective-permute-done((f32[8,136,128]{2,1,0:T(8,128)}, f32[8,136,128]{2,1,0:T(8,128)S(1)}, u32[]{:S(2)}, u32[]{:S(2)}) %collective-permute-start.1) | collective-permute-done | bytes 557088 | tf_op jit(solution)/shard_map/ppermute | solution.py:192
  49.9 0.0 copy-start
  49.9 0.7 broadcast_in_dim.17.doc_ref
  50.6 0.1 copy-done
  50.7 11.2 %shard_map.88 = (f32[1280,2]{1,0:T(8,128)}, bf16[8,5,128,128]{3,2,1,0:T(8,128)(2,1)}, f32[8,1280,128]{2,1,0:T(8,128)}) custom-call(f32[8,1280,128]{2,1,0:T(8,128)} %shard_map.86.i_ref, bf16[8,1280,128]{2,1,0:T(8,128)(2,1)} %q_ref.7, bf16[8,1280,128]{2,1,0:T(8,128)(2,1)} %g_ref.3, f32[8,1,128]{2,1,0:T(1,128)} %bitcast.5, ...), custom_call_target="tpu_custom_call" | custom-call | flops 335544320 | bytes 20234752 | tf_op jit(solution)/shard_map/pallas_call | solution.py:161
  61.9 1.3 copy.12
  63.2 0.1 collective-permute-start.2
  63.3 1.2 collective-permute-done.2
  64.5 1.5 %collective-permute-start.3 = (f32[2560]{0:T(1024)S(1)}, f32[2560]{0:T(1024)S(1)}, u32[]{:S(2)}, u32[]{:S(2)}) collective-permute-start(f32[2560]{0:T(1024)S(1)} %add.23), channel_id=1, source_target_pairs={{0,2},{2,0},{1,3},{3,1},{4,6},{6,4},{5,7},{7,5},{8,10},{10,8},{9,1... | collective-permute-start | bytes 30728 | tf_op jit(solution)/shard_map/ppermute | solution.py:279
  66.6 0.1 reshape.87
  66.7 1.5 %collective-permute-done.3 = f32[2560]{0:T(1024)S(1)} collective-permute-done((f32[2560]{0:T(1024)S(1)}, f32[2560]{0:T(1024)S(1)}, u32[]{:S(2)}, u32[]{:S(2)}) %collective-permute-start.3) | collective-permute-done | bytes 10272 | tf_op jit(solution)/shard_map/ppermute | solution.py:279
  68.2 1.1 copy.13.c_ref
  69.3 0.7 broadcast_in_dim.19.end_ref
  70.0 0.6 broadcast_in_dim.20.row_ref
  70.6 0.7 broadcast_in_dim.18.pair_ref
  71.3 10.6 %shard_map.89 = (bf16[8,1280,128]{2,1,0:T(8,128)(2,1)}, f32[8,5,128,128]{3,2,1,0:T(8,128)}, f32[8,136,128]{2,1,0:T(8,128)}) custom-call(bf16[8,1280,128]{2,1,0:T(8,128)(2,1)} %q_ref.7, f32[8,1280,128]{2,1,0:T(8,128)} %get-tuple-element.26.r_ref, bf16[8,1280,128]{2,1,0:T(8,128)(2,1)} %g_ref.3, f32[8,1,128]{2,1,0:T(1,128)} %bitcast.6, f32[1280,2]{1,0:T(8,128)} %copy.13.c_ref, ...), custom_call_target="tpu_custom_call" | custom-call | flops 335544320 | bytes 16319488 | tf_op jit(solution)/shard_map/pallas_call | solution.py:161
  81.9 1.3 collective-permute-start.4
  83.2 16.8 %shard_map.90 = (bf16[8,1280,128]{2,1,0:T(8,128)(2,1)}, f32[8,1280,128]{2,1,0:T(8,128)}, f32[8,1280,128]{2,1,0:T(8,128)}) custom-call(bf16[8,1280,128]{2,1,0:T(8,128)(2,1)} %q_ref.7, bf16[8,1280,128]{2,1,0:T(8,128)(2,1)} %k_ref.7, bf16[8,1280,128]{2,1,0:T(8,128)(2,1)} %v_ref.7, bf16[8,1280,128]{2,1,0:T(8,128)(2,1)} %get-tuple-element.29.d_ref, ...), custom_call_target="tpu_custom_call" | custom-call | flops 3355443200 | bytes 24903680 | tf_op jit(solution)/shard_map/pallas_call | solution.py:161
  100.0 0.0 collective-permute-done.4.far_ref
  100.0 0.0 copy-start.1
  100.0 0.8 copy-done.1
  100.8 2.1 %shard_map.91 = f32[8,136,128]{2,1,0:T(8,128)} custom-call(f32[8,136,128]{2,1,0:T(8,128)} %get-tuple-element.28.near_ref, f32[8,136,128]{2,1,0:T(8,128)} %copy-done.1), custom_call_target="tpu_custom_call" | custom-call | flops 278528 | bytes 1671168 | tf_op jit(solution)/shard_map/pallas_call | solution.py:174
  102.9 1.3 collective-permute-start.5
  104.2 15.6 %collective-permute-done.5.carry_ref = f32[8,136,128]{2,1,0:T(8,128)S(1)} collective-permute-done((f32[8,136,128]{2,1,0:T(8,128)}, f32[8,136,128]{2,1,0:T(8,128)S(1)}, u32[]{:S(2)}, u32[]{:S(2)}) %collective-permute-start.5) | collective-permute-done | bytes 557088 | tf_op jit(solution)/shard_map/ppermute | solution.py:192
  119.8 0.0 copy-start.3
  119.8 0.8 copy-done.3
  120.6 11.0 %shard_map.92 = (bf16[8,1280,128]{2,1,0:T(8,128)(2,1)}, bf16[8,1280,128]{2,1,0:T(8,128)(2,1)}) custom-call(f32[8,1280,128]{2,1,0:T(8,128)} %get-tuple-element.35.ik_ref, f32[8,1280,128]{2,1,0:T(8,128)} %get-tuple-element.36.iv_ref, bf16[8,1280,128]{2,1,0:T(8,128)(2,1)} %k_ref.7, bf16[8,1280,128]{2,1,0:T(8,128)(2,1)} %v_ref.7, ...), custom_call_target="tpu_custom_call" | custom-call | flops 671088640 | bytes 24152576 | tf_op jit(solution)/shard_map/pallas_call | solution.py:161
  (8 shorter events, 0.1 us)
Async XLA Ops:
  14.1 24.5 %copy-start.4 = (s32[5]{0:T(128)S(1)}, s32[5]{0:T(128)}, u32[]{:S(2)}) copy-start(s32[5]{0:T(128)} %param.11) | copy-start | bytes 64
  14.1 17.2 %collective-permute-start = (f32[8,136,128]{2,1,0:T(8,128)}, f32[8,136,128]{2,1,0:T(8,128)S(1)}, u32[]{:S(2)}, u32[]{:S(2)}) collective-permute-start(f32[8,136,128]{2,1,0:T(8,128)} %get-tuple-element.22.near_ref), channel_id=1, source_target_pairs={{0,4},{4,8},{8,12},{1,5},{5,9},{9,13},{2,6},{6,10},{10,14},{3,7},{... | collective-permute-start | bytes 1671176 | tf_op jit(solution)/shard_map/ppermute | solution.py:192
  31.4 0.8 copy-start.2
  34.3 15.6 %collective-permute-start.1 = (f32[8,136,128]{2,1,0:T(8,128)}, f32[8,136,128]{2,1,0:T(8,128)S(1)}, u32[]{:S(2)}, u32[]{:S(2)}) collective-permute-start(f32[8,136,128]{2,1,0:T(8,128)} %shard_map.87), channel_id=1, source_target_pairs={{0,4},{4,8},{8,12},{1,5},{5,9},{9,13},{2,6},{6,10},{10,14},{3,7},{... | collective-permute-start | bytes 1671176 | tf_op jit(solution)/shard_map/ppermute | solution.py:192
  49.9 0.8 copy-start
  63.2 1.2 collective-permute-start.2
  64.5 3.7 %collective-permute-start.3 = (f32[2560]{0:T(1024)S(1)}, f32[2560]{0:T(1024)S(1)}, u32[]{:S(2)}, u32[]{:S(2)}) collective-permute-start(f32[2560]{0:T(1024)S(1)} %add.23), channel_id=1, source_target_pairs={{0,2},{2,0},{1,3},{3,1},{4,6},{6,4},{5,7},{7,5},{8,10},{10,8},{9,1... | collective-permute-start | bytes 30728 | tf_op jit(solution)/shard_map/ppermute | solution.py:279
  81.9 18.1 %collective-permute-start.4 = (f32[8,136,128]{2,1,0:T(8,128)}, f32[8,136,128]{2,1,0:T(8,128)S(1)}, u32[]{:S(2)}, u32[]{:S(2)}) collective-permute-start(f32[8,136,128]{2,1,0:T(8,128)} %get-tuple-element.28.near_ref), channel_id=1, source_target_pairs={{4,0},{8,4},{12,8},{5,1},{9,5},{13,9},{6,2},{10,6},{14,10},{7,3},{... | collective-permute-start | bytes 1671176 | tf_op jit(solution)/shard_map/ppermute | solution.py:192
  100.0 0.8 copy-start.1
  102.9 16.9 %collective-permute-start.5 = (f32[8,136,128]{2,1,0:T(8,128)}, f32[8,136,128]{2,1,0:T(8,128)S(1)}, u32[]{:S(2)}, u32[]{:S(2)}) collective-permute-start(f32[8,136,128]{2,1,0:T(8,128)} %shard_map.91), channel_id=1, source_target_pairs={{4,0},{8,4},{12,8},{5,1},{9,5},{13,9},{6,2},{10,6},{14,10},{7,3},{... | collective-permute-start | bytes 1671176 | tf_op jit(solution)/shard_map/ppermute | solution.py:192
  119.8 0.8 copy-start.3

commit v11 on v10

--- a/solution.py
+++ b/solution.py
@@ -31,11 +31,9 @@
     return total.astype(jnp.bfloat16)
 
 
-def state_kernel(block_len, k_ref, v_ref, pair_ref, end_ref, row_ref, prefix_ref, pay_ref):
-    count = k_ref.shape[1] // block_len
-    width = k_ref.shape[2]
+def _key_value_parts(block_len, k_ref, v_ref):
     parts = []
-    for n in range(count):
+    for n in range(k_ref.shape[1] // block_len):
         rows = pl.ds(n * block_len, block_len)
         parts.append(
             lax.dot_general(
@@ -43,10 +41,21 @@
                 preferred_element_type=jnp.float32,
             )
         )
+    return parts
+
+
+def payload_kernel(block_len, k_ref, v_ref, end_ref, row_ref, pay_ref):
+    width = k_ref.shape[2]
+    parts = _key_value_parts(block_len, k_ref, v_ref)
+    pay_ref[0, :width, :] = _sum_blocks(end_ref, 0, parts)
+    pay_ref[0, width:, :] = row_ref[...]
+
+
+def prefix_kernel(block_len, k_ref, v_ref, pair_ref, prefix_ref):
+    parts = _key_value_parts(block_len, k_ref, v_ref)
+    count = len(parts)
     for b in range(count):
         prefix_ref[0, b] = _sum_blocks(pair_ref, b * count, parts)
-    pay_ref[0, :width, :] = _sum_blocks(end_ref, 0, parts)
-    pay_ref[0, width:, :] = row_ref[...]
 
 
 def combine_kernel(near_ref, far_ref, o_ref):
@@ -245,25 +254,29 @@
     longest_doc = ctx_size * block_count // 2
     reach = (longest_doc - 2) // block_count + 1
 
-    local_prefix, kv_payload = per_head_call(
-        functools.partial(state_kernel, block_len),
-        [(keys, True), (values, True), (earlier_rows, False), (last_rows, False),
-         (last_doc_rows, False)],
-        [(states, True), (payload, True)],
+    (kv_payload,) = per_head_call(
+        functools.partial(payload_kernel, block_len),
+        [(keys, True), (values, True), (last_rows, False), (last_doc_rows, False)],
+        [(payload, True)],
         pair_flops // 2,
     )
-    prior, intra_part = carry(
-        kv_payload,
-        "ctx",
-        False,
-        reach,
-        lambda: per_head_call(
+
+    def forward_cover():
+        (intra,) = per_head_call(
             functools.partial(intra_kernel, block_len),
             [(queries, True), (keys, True), (values, True)],
             [(wide, True)],
             2 * pair_flops,
-        )[0],
-    )
+        )
+        (prefix,) = per_head_call(
+            functools.partial(prefix_kernel, block_len),
+            [(keys, True), (values, True), (earlier_rows, False)],
+            [(states, True)],
+            pair_flops // 2,
+        )
+        return intra, prefix
+
+    prior, (intra_part, local_prefix) = carry(kv_payload, "ctx", False, reach, forward_cover)
     local_sums, preceding_states, raw_attn = per_head_call(
         functools.partial(forward_kernel, block_len),
         [(intra_part, True), (queries, True), (out_grad, True), (gain, True),

time: 133 us -> 138 us (1.038)
  Pallas kernels: 71.6 us -> 78.4 us
  waiting for transfers between devices: 31.5 us -> 30 us
    pallas_call x6 -> x7, Pallas kernels: 67.4 us -> 74.2 us  [per_head_call(): pl.pallas_call(kernel, grid=(head_count,), in_specs=[spec(x.shape, h) for...]
    ppermute x4, waiting for transfers between devices: 28.8 us -> 27.4 us  [shift(): return lax.ppermute(value, axis, pairs)]
  transfers between devices with their start and end apart: 6 -> 6, of which waited for: 5 -> 4; matrix products, arithmetic and copies ran while one was open for 0% -> 1% of each run, Pallas kernels for 21% -> 25%
where the time goes in v11:
time: 138 us; the launch traced here: 136 us
  Pallas kernels  78.4 us (57%)
  waiting for transfers between devices  30 us (22%)
  starting transfers between devices  12.5 us (9%)
  local copies, waits for them, and re-layouts  10.3 us (7%)
  other arithmetic  2.77 us (2%)
  between operations  2.1 us (2%)
    pallas_call x7, Pallas kernels, per_head_call(): pl.pallas_call(kernel, grid=(head_count,), in_specs=[spec(x.shape, h) for...  74.2 us
    ppermute x4, waiting for transfers between devices, shift(): return lax.ppermute(value, axis, pairs)  27.4 us
    ppermute x4, starting transfers between devices, shift(): return lax.ppermute(value, axis, pairs)  11 us
    pallas_call x2, Pallas kernels, combine(): pl.pallas_call(combine_kernel, out_shape=jax.ShapeDtypeStruct(near.shape,...  4.18 us
    broadcast_in_dim x5, local copies, waits for them, and re-layouts, lanes(): return jnp.broadcast_to(table.reshape(rows, 1), (rows, head_width))  3.42 us
  transfers between devices with their start and end apart: 6, of which 4 were waited for; matrix products, arithmetic and copies ran while one was open for 1% of the time, Pallas kernels for 25%

profile of v11, /device:TPU:0, one launch (start us, length us, event | category | flops | bytes accessed | tf_op | source)
XLA Modules:
  0.0 136.2 jit_solution(16714657093684208252)
XLA Ops:
  0.6 0.7 convert_element_type.29
  1.3 0.6 fusion.5
  2.5 2.0 %compare_convert_fusion = (f32[5]{0:T(128)S(1)}, f32[5]{0:T(128)S(1)}) fusion(f32[]{:T(128)} %bitcast.3, s32[5]{0:T(128)} %param.11, f32[]{:T(128)} %bitcast), kind=kLoop, calls=%fused_computation.12 | loop fusion | flops 25 | bytes 68 | tf_op jit(solution)/shard_map/convert_element_type | solution.py:235
  4.5 0.6 broadcast_in_dim.15.row_ref
  5.1 0.7 broadcast_in_dim.14.end_ref
  5.8 6.9 %shard_map.85.near_ref = f32[8,136,128]{2,1,0:T(8,128)} custom-call(bf16[8,1280,128]{2,1,0:T(8,128)(2,1)} %k_ref.9, bf16[8,1280,128]{2,1,0:T(8,128)(2,1)} %v_ref.9, f32[5,128]{1,0:T(8,128)} %broadcast_in_dim.14.end_ref, f32[8,128]{1,0:T(8,128)} %broadcast_in_dim.15.row_ref), custom_call_target="tpu_custom_call" | custom-call | flops 335544320 | bytes 5806592 | tf_op jit(solution)/shard_map/pallas_call | solution.py:170
  12.7 4.9 %collective-permute-start = (f32[8,136,128]{2,1,0:T(8,128)}, f32[8,136,128]{2,1,0:T(8,128)S(1)}, u32[]{:S(2)}, u32[]{:S(2)}) collective-permute-start(f32[8,136,128]{2,1,0:T(8,128)} %shard_map.85.near_ref), channel_id=1, source_target_pairs={{0,4},{4,8},{8,12},{1,5},{5,9},{9,13},{2,6},{6,10},{10,14},{3,7},{... | collective-permute-start | bytes 1671176 | tf_op jit(solution)/shard_map/ppermute | solution.py:201
  17.7 0.1 fusion.4
  17.8 0.1 reshape.86
  17.9 0.7 broadcast_in_dim.16.pair_ref
  18.5 7.4 %shard_map.87.prefix_ref = f32[8,5,128,128]{3,2,1,0:T(8,128)} custom-call(bf16[8,1280,128]{2,1,0:T(8,128)(2,1)} %k_ref.9, bf16[8,1280,128]{2,1,0:T(8,128)(2,1)} %v_ref.9, f32[25,128]{1,0:T(8,128)} %broadcast_in_dim.16.pair_ref), custom_call_target="tpu_custom_call" | custom-call | flops 335544320 | bytes 7877120 | tf_op jit(solution)/shard_map/pallas_call | solution.py:170
  26.0 0.0 copy-start.4
  26.0 10.2 %shard_map.86.i_ref = f32[8,1280,128]{2,1,0:T(8,128)} custom-call(bf16[8,1280,128]{2,1,0:T(8,128)(2,1)} %q_ref.7, bf16[8,1280,128]{2,1,0:T(8,128)(2,1)} %k_ref.9, bf16[8,1280,128]{2,1,0:T(8,128)(2,1)} %v_ref.9), custom_call_target="tpu_custom_call" | custom-call | flops 1342177280 | bytes 13107200 | tf_op jit(solution)/shard_map/pallas_call | solution.py:170
  36.1 0.0 collective-permute-done.far_ref
  36.1 0.0 copy-start.1
  36.1 0.8 copy-done.1
  36.9 2.1 %shard_map.88 = f32[8,136,128]{2,1,0:T(8,128)} custom-call(f32[8,136,128]{2,1,0:T(8,128)} %shard_map.85.near_ref, f32[8,136,128]{2,1,0:T(8,128)} %copy-done.1), custom_call_target="tpu_custom_call" | custom-call | flops 278528 | bytes 1671168 | tf_op jit(solution)/shard_map/pallas_call | solution.py:183
  39.0 3.5 %collective-permute-start.1 = (f32[8,136,128]{2,1,0:T(8,128)}, f32[8,136,128]{2,1,0:T(8,128)S(1)}, u32[]{:S(2)}, u32[]{:S(2)}) collective-permute-start(f32[8,136,128]{2,1,0:T(8,128)} %shard_map.88), channel_id=1, source_target_pairs={{0,4},{4,8},{8,12},{1,5},{5,9},{9,13},{2,6},{6,10},{10,14},{3,7},{... | collective-permute-start | bytes 1671176 | tf_op jit(solution)/shard_map/ppermute | solution.py:201
  42.5 0.0 copy-done.4
  42.5 11.8 %collective-permute-done.1.carry_ref = f32[8,136,128]{2,1,0:T(8,128)S(1)} collective-permute-done((f32[8,136,128]{2,1,0:T(8,128)}, f32[8,136,128]{2,1,0:T(8,128)S(1)}, u32[]{:S(2)}, u32[]{:S(2)}) %collective-permute-start.1) | collective-permute-done | bytes 557088 | tf_op jit(solution)/shard_map/ppermute | solution.py:201
  54.4 0.0 copy-start
  54.4 0.7 broadcast_in_dim.17.doc_ref
  55.1 0.1 copy-done
  55.2 11.2 %shard_map.89 = (f32[1280,2]{1,0:T(8,128)}, bf16[8,5,128,128]{3,2,1,0:T(8,128)(2,1)}, f32[8,1280,128]{2,1,0:T(8,128)}) custom-call(f32[8,1280,128]{2,1,0:T(8,128)} %shard_map.86.i_ref, bf16[8,1280,128]{2,1,0:T(8,128)(2,1)} %q_ref.7, bf16[8,1280,128]{2,1,0:T(8,128)(2,1)} %g_ref.3, f32[8,1,128]{2,1,0:T(1,128)} %bitcast.5, ...), custom_call_target="tpu_custom_call" | custom-call | flops 335544320 | bytes 20234752 | tf_op jit(solution)/shard_map/pallas_call | solution.py:170
  66.4 1.3 copy.12
  67.7 0.1 collective-permute-start.2
  67.8 1.2 collective-permute-done.2
  69.0 1.5 %collective-permute-start.3 = (f32[2560]{0:T(1024)S(1)}, f32[2560]{0:T(1024)S(1)}, u32[]{:S(2)}, u32[]{:S(2)}) collective-permute-start(f32[2560]{0:T(1024)S(1)} %add.23), channel_id=1, source_target_pairs={{0,2},{2,0},{1,3},{3,1},{4,6},{6,4},{5,7},{7,5},{8,10},{10,8},{9,1... | collective-permute-start | bytes 30728 | tf_op jit(solution)/shard_map/ppermute | solution.py:292
  71.2 0.1 reshape.87
  71.2 1.4 %collective-permute-done.3 = f32[2560]{0:T(1024)S(1)} collective-permute-done((f32[2560]{0:T(1024)S(1)}, f32[2560]{0:T(1024)S(1)}, u32[]{:S(2)}, u32[]{:S(2)}) %collective-permute-start.3) | collective-permute-done | bytes 10272 | tf_op jit(solution)/shard_map/ppermute | solution.py:292
  72.7 1.1 copy.13.c_ref
  73.8 0.7 broadcast_in_dim.19.end_ref
  74.5 0.6 broadcast_in_dim.20.row_ref
  75.1 0.7 broadcast_in_dim.18.pair_ref
  75.8 10.6 %shard_map.90 = (bf16[8,1280,128]{2,1,0:T(8,128)(2,1)}, f32[8,5,128,128]{3,2,1,0:T(8,128)}, f32[8,136,128]{2,1,0:T(8,128)}) custom-call(bf16[8,1280,128]{2,1,0:T(8,128)(2,1)} %q_ref.7, f32[8,1280,128]{2,1,0:T(8,128)} %get-tuple-element.24.r_ref, bf16[8,1280,128]{2,1,0:T(8,128)(2,1)} %g_ref.3, f32[8,1,128]{2,1,0:T(1,128)} %bitcast.6, f32[1280,2]{1,0:T(8,128)} %copy.13.c_ref, ...), custom_call_target="tpu_custom_call" | custom-call | flops 335544320 | bytes 16319488 | tf_op jit(solution)/shard_map/pallas_call | solution.py:170
  86.4 1.3 collective-permute-start.4
  87.7 16.8 %shard_map.91 = (bf16[8,1280,128]{2,1,0:T(8,128)(2,1)}, f32[8,1280,128]{2,1,0:T(8,128)}, f32[8,1280,128]{2,1,0:T(8,128)}) custom-call(bf16[8,1280,128]{2,1,0:T(8,128)(2,1)} %q_ref.7, bf16[8,1280,128]{2,1,0:T(8,128)(2,1)} %k_ref.9, bf16[8,1280,128]{2,1,0:T(8,128)(2,1)} %v_ref.9, bf16[8,1280,128]{2,1,0:T(8,128)(2,1)} %get-tuple-element.27.d_ref, ...), custom_call_target="tpu_custom_call" | custom-call | flops 3355443200 | bytes 24903680 | tf_op jit(solution)/shard_map/pallas_call | solution.py:170
  104.5 0.0 collective-permute-done.4.far_ref
  104.5 0.0 copy-start.2
  104.5 0.8 copy-done.2
  105.3 2.1 %shard_map.92 = f32[8,136,128]{2,1,0:T(8,128)} custom-call(f32[8,136,128]{2,1,0:T(8,128)} %get-tuple-element.26.near_ref, f32[8,136,128]{2,1,0:T(8,128)} %copy-done.2), custom_call_target="tpu_custom_call" | custom-call | flops 278528 | bytes 1671168 | tf_op jit(solution)/shard_map/pallas_call | solution.py:183
  107.4 1.3 collective-permute-start.5
  108.7 15.6 %collective-permute-done.5.carry_ref = f32[8,136,128]{2,1,0:T(8,128)S(1)} collective-permute-done((f32[8,136,128]{2,1,0:T(8,128)}, f32[8,136,128]{2,1,0:T(8,128)S(1)}, u32[]{:S(2)}, u32[]{:S(2)}) %collective-permute-start.5) | collective-permute-done | bytes 557088 | tf_op jit(solution)/shard_map/ppermute | solution.py:201
  124.3 0.0 copy-start.3
  124.3 0.8 copy-done.3
  125.1 11.0 %shard_map.93 = (bf16[8,1280,128]{2,1,0:T(8,128)(2,1)}, bf16[8,1280,128]{2,1,0:T(8,128)(2,1)}) custom-call(f32[8,1280,128]{2,1,0:T(8,128)} %get-tuple-element.33.ik_ref, f32[8,1280,128]{2,1,0:T(8,128)} %get-tuple-element.34.iv_ref, bf16[8,1280,128]{2,1,0:T(8,128)(2,1)} %k_ref.9, bf16[8,1280,128]{2,1,0:T(8,128)(2,1)} %v_ref.9, ...), custom_call_target="tpu_custom_call" | custom-call | flops 671088640 | bytes 24152576 | tf_op jit(solution)/shard_map/pallas_call | solution.py:170
  (8 shorter events, 0.1 us)
Async XLA Ops:
  12.7 23.4 %collective-permute-start = (f32[8,136,128]{2,1,0:T(8,128)}, f32[8,136,128]{2,1,0:T(8,128)S(1)}, u32[]{:S(2)}, u32[]{:S(2)}) collective-permute-start(f32[8,136,128]{2,1,0:T(8,128)} %shard_map.85.near_ref), channel_id=1, source_target_pairs={{0,4},{4,8},{8,12},{1,5},{5,9},{9,13},{2,6},{6,10},{10,14},{3,7},{... | collective-permute-start | bytes 1671176 | tf_op jit(solution)/shard_map/ppermute | solution.py:201
  26.0 16.6 %copy-start.4 = (s32[5]{0:T(128)S(1)}, s32[5]{0:T(128)}, u32[]{:S(2)}) copy-start(s32[5]{0:T(128)} %param.11) | copy-start | bytes 64
  36.1 0.8 copy-start.1
  39.0 15.3 %collective-permute-start.1 = (f32[8,136,128]{2,1,0:T(8,128)}, f32[8,136,128]{2,1,0:T(8,128)S(1)}, u32[]{:S(2)}, u32[]{:S(2)}) collective-permute-start(f32[8,136,128]{2,1,0:T(8,128)} %shard_map.88), channel_id=1, source_target_pairs={{0,4},{4,8},{8,12},{1,5},{5,9},{9,13},{2,6},{6,10},{10,14},{3,7},{... | collective-permute-start | bytes 1671176 | tf_op jit(solution)/shard_map/ppermute | solution.py:201
  54.4 0.8 copy-start
  67.7 1.2 collective-permute-start.2
  69.0 3.7 %collective-permute-start.3 = (f32[2560]{0:T(1024)S(1)}, f32[2560]{0:T(1024)S(1)}, u32[]{:S(2)}, u32[]{:S(2)}) collective-permute-start(f32[2560]{0:T(1024)S(1)} %add.23), channel_id=1, source_target_pairs={{0,2},{2,0},{1,3},{3,1},{4,6},{6,4},{5,7},{7,5},{8,10},{10,8},{9,1... | collective-permute-start | bytes 30728 | tf_op jit(solution)/shard_map/ppermute | solution.py:292
  86.4 18.1 %collective-permute-start.4 = (f32[8,136,128]{2,1,0:T(8,128)}, f32[8,136,128]{2,1,0:T(8,128)S(1)}, u32[]{:S(2)}, u32[]{:S(2)}) collective-permute-start(f32[8,136,128]{2,1,0:T(8,128)} %get-tuple-element.26.near_ref), channel_id=1, source_target_pairs={{4,0},{8,4},{12,8},{5,1},{9,5},{13,9},{6,2},{10,6},{14,10},{7,3},{... | collective-permute-start | bytes 1671176 | tf_op jit(solution)/shard_map/ppermute | solution.py:201
  104.5 0.8 copy-start.2
  107.4 16.9 %collective-permute-start.5 = (f32[8,136,128]{2,1,0:T(8,128)}, f32[8,136,128]{2,1,0:T(8,128)S(1)}, u32[]{:S(2)}, u32[]{:S(2)}) collective-permute-start(f32[8,136,128]{2,1,0:T(8,128)} %shard_map.92), channel_id=1, source_target_pairs={{4,0},{8,4},{12,8},{5,1},{9,5},{13,9},{6,2},{10,6},{14,10},{7,3},{... | collective-permute-start | bytes 1671176 | tf_op jit(solution)/shard_map/ppermute | solution.py:201
  124.3 0.8 copy-start.3

commit v12 on v10

--- a/solution.py
+++ b/solution.py
@@ -149,25 +149,37 @@
         dv_ref[0, rows, :] = dv.astype(dv_ref.dtype)
 
 
-def per_head_call(kernel, inputs, outputs, flops):
-    def spec(shape, per_head):
+def per_head_call(kernel, inputs, outputs, flops, heads=None, into=()):
+    def spec(shape, per_head, first):
         if per_head:
-            return pl.BlockSpec((1,) + shape[1:], lambda h: (h,) + (0,) * (len(shape) - 1))
+            return pl.BlockSpec(
+                (1,) + shape[1:], lambda h: (h + first,) + (0,) * (len(shape) - 1)
+            )
         return pl.BlockSpec(shape, lambda h: (0,) * len(shape))
 
     head_count = inputs[0][0].shape[0]
-    in_bytes = sum(x.size * x.dtype.itemsize for x, _ in inputs)
-    out_bytes = sum(math.prod(o.shape) * o.dtype.itemsize for o, _ in outputs)
+    first, count = heads if heads is not None else (0, head_count)
+    share = count / head_count
+    in_bytes = sum(x.size * x.dtype.itemsize for x, _ in inputs) * share
+    out_bytes = sum(math.prod(o.shape) * o.dtype.itemsize for o, _ in outputs) * share
+    skip = len(inputs)
+
+    def body(*refs):
+        kernel(*refs[:skip], *refs[skip + len(into):])
+
     return pl.pallas_call(
-        kernel,
-        grid=(head_count,),
-        in_specs=[spec(x.shape, h) for x, h in inputs],
-        out_specs=[spec(o.shape, h) for o, h in outputs],
+        body,
+        grid=(count,),
+        in_specs=[spec(x.shape, h, first) for x, h in inputs]
+        + [pl.BlockSpec(memory_space=pl.ANY) for _ in into],
+        out_specs=[spec(o.shape, h, first) for o, h in outputs],
         out_shape=[o for o, _ in outputs],
+        input_output_aliases={skip + i: i for i in range(len(into))},
         cost_estimate=pl.CostEstimate(
-            flops=flops, transcendentals=0, bytes_accessed=in_bytes + out_bytes
-        ),
-    )(*[x for x, _ in inputs])
+            flops=int(flops * share), transcendentals=0,
+            bytes_accessed=int(in_bytes + out_bytes),
+        ),
+    )(*[x for x, _ in inputs], *into)
 
 
 def combine(near, far):
@@ -191,15 +203,19 @@
             pairs = [(j, j + step) for j in range(peers - step)]
         return lax.ppermute(value, axis, pairs)
 
+    first_cover, second_cover = cover
     if reach < 1:
-        return jnp.zeros_like(payload), cover()
+        return jnp.zeros_like(payload), second_cover(first_cover())
     got = shift(payload, 1)
-    covered_value = cover()
+    covered_value = first_cover()
     got, covered_value = lax.optimization_barrier((got, covered_value))
     if reach <= 2:
         if reach == 2:
             got = shift(combine(payload, got), 1)
-        return got, covered_value
+            covered_value = second_cover(covered_value)
+            got, covered_value = lax.optimization_barrier((got, covered_value))
+            return got, covered_value
+        return got, second_cover(covered_value)
     earlier, inclusive = got, combine(payload, got)
     covered = 1
     while covered < reach:
@@ -209,7 +225,7 @@
         covered = covered + step
         if covered < reach:
             inclusive = combine(inclusive, got)
-    return earlier, covered_value
+    return earlier, second_cover(covered_value)
 
 
 def on_device(queries, keys, values, out_grad, norm_gain, doc_ids):
@@ -257,12 +273,15 @@
         "ctx",
         False,
         reach,
-        lambda: per_head_call(
-            functools.partial(intra_kernel, block_len),
-            [(queries, True), (keys, True), (values, True)],
-            [(wide, True)],
-            2 * pair_flops,
-        )[0],
+        (
+            lambda: per_head_call(
+                functools.partial(intra_kernel, block_len),
+                [(queries, True), (keys, True), (values, True)],
+                [(wide, True)],
+                2 * pair_flops,
+            )[0],
+            lambda intra: intra,
+        ),
     )
     local_sums, preceding_states, raw_attn = per_head_call(
         functools.partial(forward_kernel, block_len),
@@ -290,17 +309,27 @@
         [(full, True), (states, True), (payload, True)],
         pair_flops // 2,
     )
+    half = head_count // 2
+
+    def query_grads(heads, into):
+        return per_head_call(
+            functools.partial(query_grad_kernel, block_len),
+            [(queries, True), (keys, True), (values, True), (d_attn, True),
+             (preceding_states, True)],
+            [(full, True), (wide, True), (wide, True)],
+            5 * pair_flops,
+            heads=heads,
+            into=into,
+        )
+
     following, (query_gradient, key_intra, value_intra) = carry(
         qd_payload,
         "ctx",
         True,
         reach,
-        lambda: per_head_call(
-            functools.partial(query_grad_kernel, block_len),
-            [(queries, True), (keys, True), (values, True), (d_attn, True),
-             (preceding_states, True)],
-            [(full, True), (wide, True), (wide, True)],
-            5 * pair_flops,
+        (
+            lambda: query_grads((0, half), ()),
+            lambda done: query_grads((half, head_count - half), tuple(done)),
         ),
     )
     key_gradient, value_gradient = per_head_call(

time: 133 us -> 129 us (0.970)
  waiting for transfers between devices: 31.5 us -> 25.3 us
  Pallas kernels: 71.6 us -> 73.9 us
    ppermute x4, waiting for transfers between devices: 28.8 us -> 22.7 us  [shift(): return lax.ppermute(value, axis, pairs)]
    pallas_call x6 -> x7, Pallas kernels: 67.4 us -> 69.7 us  [per_head_call(): pl.pallas_call(body, grid=(count,), in_specs=[spec(x.shape, h, first) for...]
  transfers between devices with their start and end apart: 6 -> 6, of which waited for: 5 -> 6; matrix products, arithmetic and copies ran while one was open for 0% -> 0% of each run, Pallas kernels for 21% -> 23%
where the time goes in v12:
time: 129 us; the launch traced here: 128 us
  Pallas kernels  73.9 us (57%)
  waiting for transfers between devices  25.3 us (20%)
  starting transfers between devices  13.5 us (10%)
  local copies, waits for them, and re-layouts  10.3 us (8%)
  other arithmetic  2.75 us (2%)
  between operations  2.07 us (2%)
    pallas_call x7, Pallas kernels, per_head_call(): pl.pallas_call(body, grid=(count,), in_specs=[spec(x.shape, h, first) for...  69.7 us
    ppermute x4, waiting for transfers between devices, shift(): return lax.ppermute(value, axis, pairs)  22.7 us
    ppermute x4, starting transfers between devices, shift(): return lax.ppermute(value, axis, pairs)  11.9 us
    pallas_call x2, Pallas kernels, combine(): pl.pallas_call(combine_kernel, out_shape=jax.ShapeDtypeStruct(near.shape,...  4.21 us
    broadcast_in_dim x5, local copies, waits for them, and re-layouts, lanes(): return jnp.broadcast_to(table.reshape(rows, 1), (rows, head_width))  3.43 us
    ppermute x2, waiting for transfers between devices, on_device(): total_sums = total_sums + lax.ppermute(total_sums, axis, [(0, 1), (1, 0)])  2.61 us
  transfers between devices with their start and end apart: 6, of which 6 were waited for; matrix products, arithmetic and copies ran while one was open for 0% of the time, Pallas kernels for 23%

profile of v12, /device:TPU:0, one launch (start us, length us, event | category | flops | bytes accessed | tf_op | source)
XLA Modules:
  0.0 127.9 jit_solution(4528433507900123375)
XLA Ops:
  0.6 0.7 convert_element_type.29
  1.3 0.6 fusion.5
  1.9 0.1 fusion.4
  2.6 2.0 %compare_convert_fusion = (f32[5]{0:T(128)S(1)}, f32[5]{0:T(128)S(1)}) fusion(f32[]{:T(128)} %bitcast.3, s32[5]{0:T(128)} %param.11, f32[]{:T(128)} %bitcast), kind=kLoop, calls=%fused_computation.12 | loop fusion | flops 25 | bytes 68 | tf_op jit(solution)/shard_map/convert_element_type | solution.py:242
  4.6 0.1 reshape.86
  4.7 0.6 broadcast_in_dim.16.refs_4_
  5.2 0.7 broadcast_in_dim.15.refs_3_
  5.9 0.7 broadcast_in_dim.14.refs_2_
  6.6 7.6 %shard_map.85 = (f32[8,5,128,128]{3,2,1,0:T(8,128)}, f32[8,136,128]{2,1,0:T(8,128)}) custom-call(bf16[8,1280,128]{2,1,0:T(8,128)(2,1)} %refs_2_.11, bf16[8,1280,128]{2,1,0:T(8,128)(2,1)} %refs_3_.1, f32[25,128]{1,0:T(8,128)} %broadcast_in_dim.14.refs_2_, f32[5,128]{1,0:T(8,128)} %broadcast_in_dim.15.refs_3_, f32[8,128]{1,0:T(8,128)} %broadcast_in_dim.16.refs_4_), custom_call_target="tpu_custom_call" | custom-call | flops 335544320 | bytes 8440832 | tf_op jit(solution)/shard_map/pallas_call | solution.py:170
  14.2 0.0 copy-start.4
  14.2 5.1 %collective-permute-start = (f32[8,136,128]{2,1,0:T(8,128)}, f32[8,136,128]{2,1,0:T(8,128)S(1)}, u32[]{:S(2)}, u32[]{:S(2)}) collective-permute-start(f32[8,136,128]{2,1,0:T(8,128)} %get-tuple-element.31.near_ref), channel_id=1, source_target_pairs={{0,4},{4,8},{8,12},{1,5},{5,9},{9,13},{2,6},{6,10},{10,14},{3,7},{... | collective-permute-start | bytes 1671176 | tf_op jit(solution)/shard_map/ppermute | solution.py:204
  19.3 10.2 %shard_map.86.refs_0_ = f32[8,1280,128]{2,1,0:T(8,128)} custom-call(bf16[8,1280,128]{2,1,0:T(8,128)(2,1)} %refs_0_.9, bf16[8,1280,128]{2,1,0:T(8,128)(2,1)} %refs_2_.11, bf16[8,1280,128]{2,1,0:T(8,128)(2,1)} %refs_3_.1), custom_call_target="tpu_custom_call" | custom-call | flops 1342177280 | bytes 13107200 | tf_op jit(solution)/shard_map/pallas_call | solution.py:170
  29.5 2.0 %collective-permute-done.far_ref = f32[8,136,128]{2,1,0:T(8,128)S(1)} collective-permute-done((f32[8,136,128]{2,1,0:T(8,128)}, f32[8,136,128]{2,1,0:T(8,128)S(1)}, u32[]{:S(2)}, u32[]{:S(2)}) %collective-permute-start) | collective-permute-done | bytes 557088 | tf_op jit(solution)/shard_map/ppermute | solution.py:204
  31.4 0.0 copy-start.2
  31.4 0.8 copy-done.2
  32.2 2.1 %shard_map.87 = f32[8,136,128]{2,1,0:T(8,128)} custom-call(f32[8,136,128]{2,1,0:T(8,128)} %get-tuple-element.31.near_ref, f32[8,136,128]{2,1,0:T(8,128)} %copy-done.2), custom_call_target="tpu_custom_call" | custom-call | flops 278528 | bytes 1671168 | tf_op jit(solution)/shard_map/pallas_call | solution.py:186
  34.3 4.3 %collective-permute-start.1 = (f32[8,136,128]{2,1,0:T(8,128)}, f32[8,136,128]{2,1,0:T(8,128)S(1)}, u32[]{:S(2)}, u32[]{:S(2)}) collective-permute-start(f32[8,136,128]{2,1,0:T(8,128)} %shard_map.87), channel_id=1, source_target_pairs={{0,4},{4,8},{8,12},{1,5},{5,9},{9,13},{2,6},{6,10},{10,14},{3,7},{... | collective-permute-start | bytes 1671176 | tf_op jit(solution)/shard_map/ppermute | solution.py:204
  38.6 0.0 copy-done.4
  38.7 11.3 %collective-permute-done.1.refs_5_ = f32[8,136,128]{2,1,0:T(8,128)S(1)} collective-permute-done((f32[8,136,128]{2,1,0:T(8,128)}, f32[8,136,128]{2,1,0:T(8,128)S(1)}, u32[]{:S(2)}, u32[]{:S(2)}) %collective-permute-start.1) | collective-permute-done | bytes 557088 | tf_op jit(solution)/shard_map/ppermute | solution.py:204
  49.9 0.0 copy-start
  49.9 0.8 broadcast_in_dim.17.refs_6_
  50.7 0.0 copy-done
  50.7 11.2 %shard_map.88 = (f32[1280,2]{1,0:T(8,128)}, bf16[8,5,128,128]{3,2,1,0:T(8,128)(2,1)}, f32[8,1280,128]{2,1,0:T(8,128)}) custom-call(f32[8,1280,128]{2,1,0:T(8,128)} %shard_map.86.refs_0_, bf16[8,1280,128]{2,1,0:T(8,128)(2,1)} %refs_0_.9, bf16[8,1280,128]{2,1,0:T(8,128)(2,1)} %refs_2_.8, f32[8,1,128]{2,1,0:T(1,128)} %bitcast.5, ...), custom_call_target="tpu_custom_call" | custom-call | flops 335544320 | bytes 20234752 | tf_op jit(solution)/shard_map/pallas_call | solution.py:170
  61.9 1.3 %copy.15 = f32[2,1280]{1,0:T(2,128)S(1)} copy(f32[2,1280]{0,1:T(8,128)} %bitcast.4) | data formatting | bytes 20480 | tf_op jit(solution)/shard_map/transpose | solution.py:295
  63.3 0.1 collective-permute-start.2
  63.3 1.2 collective-permute-done.2
  64.5 1.5 %collective-permute-start.3 = (f32[2560]{0:T(1024)S(1)}, f32[2560]{0:T(1024)S(1)}, u32[]{:S(2)}, u32[]{:S(2)}) collective-permute-start(f32[2560]{0:T(1024)S(1)} %add.23), channel_id=1, source_target_pairs={{0,2},{2,0},{1,3},{3,1},{4,6},{6,4},{5,7},{7,5},{8,10},{10,8},{9,1... | collective-permute-start | bytes 30728 | tf_op jit(solution)/shard_map/ppermute | solution.py:298
  66.7 0.1 reshape.87
  66.7 1.4 %collective-permute-done.3 = f32[2560]{0:T(1024)S(1)} collective-permute-done((f32[2560]{0:T(1024)S(1)}, f32[2560]{0:T(1024)S(1)}, u32[]{:S(2)}, u32[]{:S(2)}) %collective-permute-start.3) | collective-permute-done | bytes 10272 | tf_op jit(solution)/shard_map/ppermute | solution.py:298
  68.3 1.1 copy.16.refs_4_
  69.4 0.7 broadcast_in_dim.19.refs_6_
  70.0 0.6 broadcast_in_dim.20.refs_7_
  70.6 0.7 broadcast_in_dim.18.refs_5_
  71.3 10.6 %shard_map.89 = (bf16[8,1280,128]{2,1,0:T(8,128)(2,1)}, f32[8,5,128,128]{3,2,1,0:T(8,128)}, f32[8,136,128]{2,1,0:T(8,128)}) custom-call(bf16[8,1280,128]{2,1,0:T(8,128)(2,1)} %refs_0_.9, f32[8,1280,128]{2,1,0:T(8,128)} %get-tuple-element.37.refs_1_, bf16[8,1280,128]{2,1,0:T(8,128)(2,1)} %refs_2_.8, f32[8,1,128]{2,1,0:T(1,128)} %bitcast.6, ...), custom_call_target="tpu_custom_call" | custom-call | flops 335544320 | bytes 16319488 | tf_op jit(solution)/shard_map/pallas_call | solution.py:170
  81.9 1.3 %collective-permute-start.4 = (f32[8,136,128]{2,1,0:T(8,128)}, f32[8,136,128]{2,1,0:T(8,128)S(1)}, u32[]{:S(2)}, u32[]{:S(2)}) collective-permute-start(f32[8,136,128]{2,1,0:T(8,128)} %get-tuple-element.39.near_ref), channel_id=1, source_target_pairs={{4,0},{8,4},{12,8},{5,1},{9,5},{13,9},{6,2},{10,6},{14,10},{7,3},{... | collective-permute-start | bytes 1671176 | tf_op jit(solution)/shard_map/ppermute | solution.py:204
  83.2 9.6 %shard_map.90 = (bf16[8,1280,128]{2,1,0:T(8,128)(2,1)}, f32[8,1280,128]{2,1,0:T(8,128)}, f32[8,1280,128]{2,1,0:T(8,128)}) custom-call(bf16[8,1280,128]{2,1,0:T(8,128)(2,1)} %refs_0_.9, bf16[8,1280,128]{2,1,0:T(8,128)(2,1)} %refs_2_.11, bf16[8,1280,128]{2,1,0:T(8,128)(2,1)} %refs_3_.1, bf16[8,1280,128]{2,1,0:T(8,128)(2,1)} %get-tuple-element.40.refs_3_, ...), custom_call_target="tpu_custom_call" | custom-call | flops 1677721600 | bytes 12451840 | tf_op jit(solution)/shard_map/pallas_call | solution.py:170
  92.8 5.4 %collective-permute-done.4.far_ref = f32[8,136,128]{2,1,0:T(8,128)S(1)} collective-permute-done((f32[8,136,128]{2,1,0:T(8,128)}, f32[8,136,128]{2,1,0:T(8,128)S(1)}, u32[]{:S(2)}, u32[]{:S(2)}) %collective-permute-start.4) | collective-permute-done | bytes 557088 | tf_op jit(solution)/shard_map/ppermute | solution.py:204
  98.2 0.0 copy-start.1
  98.2 0.8 copy-done.1
  99.0 2.1 %shard_map.91 = f32[8,136,128]{2,1,0:T(8,128)} custom-call(f32[8,136,128]{2,1,0:T(8,128)} %get-tuple-element.39.near_ref, f32[8,136,128]{2,1,0:T(8,128)} %copy-done.1), custom_call_target="tpu_custom_call" | custom-call | flops 278528 | bytes 1671168 | tf_op jit(solution)/shard_map/pallas_call | solution.py:186
  101.1 1.3 %collective-permute-start.5 = (f32[8,136,128]{2,1,0:T(8,128)}, f32[8,136,128]{2,1,0:T(8,128)S(1)}, u32[]{:S(2)}, u32[]{:S(2)}) collective-permute-start(f32[8,136,128]{2,1,0:T(8,128)} %shard_map.91), channel_id=1, source_target_pairs={{4,0},{8,4},{12,8},{5,1},{9,5},{13,9},{6,2},{10,6},{14,10},{7,3},{... | collective-permute-start | bytes 1671176 | tf_op jit(solution)/shard_map/ppermute | solution.py:204
  102.4 9.6 %shard_map.92 = (bf16[8,1280,128]{2,1,0:T(8,128)(2,1)}, f32[8,1280,128]{2,1,0:T(8,128)}, f32[8,1280,128]{2,1,0:T(8,128)}) custom-call(bf16[8,1280,128]{2,1,0:T(8,128)(2,1)} %refs_0_.9, bf16[8,1280,128]{2,1,0:T(8,128)(2,1)} %refs_2_.11, bf16[8,1280,128]{2,1,0:T(8,128)(2,1)} %refs_3_.1, ...), custom_call_target="tpu_custom_call", output_to_operand_aliasing={{0}: (5, {}), {1}: (6, {}), {2}: (7, {})} | custom-call | flops 1677721600 | bytes 12451840 | tf_op jit(solution)/shard_map/pallas_call | solution.py:170
  112.0 4.1 %collective-permute-done.5.refs_5_ = f32[8,136,128]{2,1,0:T(8,128)S(1)} collective-permute-done((f32[8,136,128]{2,1,0:T(8,128)}, f32[8,136,128]{2,1,0:T(8,128)S(1)}, u32[]{:S(2)}, u32[]{:S(2)}) %collective-permute-start.5) | collective-permute-done | bytes 557088 | tf_op jit(solution)/shard_map/ppermute | solution.py:204
  116.1 0.0 copy-start.3
  116.1 0.8 copy-done.3
  116.9 11.0 %shard_map.93 = (bf16[8,1280,128]{2,1,0:T(8,128)(2,1)}, bf16[8,1280,128]{2,1,0:T(8,128)(2,1)}) custom-call(f32[8,1280,128]{2,1,0:T(8,128)} %get-tuple-element.53.refs_0_, f32[8,1280,128]{2,1,0:T(8,128)} %get-tuple-element.54.refs_1_, bf16[8,1280,128]{2,1,0:T(8,128)(2,1)} %refs_2_.11, bf16[8,1280,128]{2,1,0:T(8,128)(2,1)} %refs_3_.1, ...), custom_call_target="tpu_custom_call" | custom-call | flops 671088640 | bytes 24152576 | tf_op jit(solution)/shard_map/pallas_call | solution.py:170
  (8 shorter events, 0.1 us)
Async XLA Ops:
  14.2 24.5 %copy-start.4 = (s32[5]{0:T(128)S(1)}, s32[5]{0:T(128)}, u32[]{:S(2)}) copy-start(s32[5]{0:T(128)} %param.11) | copy-start | bytes 64
  14.2 17.2 %collective-permute-start = (f32[8,136,128]{2,1,0:T(8,128)}, f32[8,136,128]{2,1,0:T(8,128)S(1)}, u32[]{:S(2)}, u32[]{:S(2)}) collective-permute-start(f32[8,136,128]{2,1,0:T(8,128)} %get-tuple-element.31.near_ref), channel_id=1, source_target_pairs={{0,4},{4,8},{8,12},{1,5},{5,9},{9,13},{2,6},{6,10},{10,14},{3,7},{... | collective-permute-start | bytes 1671176 | tf_op jit(solution)/shard_map/ppermute | solution.py:204
  31.4 0.8 copy-start.2
  34.3 15.6 %collective-permute-start.1 = (f32[8,136,128]{2,1,0:T(8,128)}, f32[8,136,128]{2,1,0:T(8,128)S(1)}, u32[]{:S(2)}, u32[]{:S(2)}) collective-permute-start(f32[8,136,128]{2,1,0:T(8,128)} %shard_map.87), channel_id=1, source_target_pairs={{0,4},{4,8},{8,12},{1,5},{5,9},{9,13},{2,6},{6,10},{10,14},{3,7},{... | collective-permute-start | bytes 1671176 | tf_op jit(solution)/shard_map/ppermute | solution.py:204
  49.9 0.8 copy-start
  63.3 1.2 collective-permute-start.2
  64.5 3.7 %collective-permute-start.3 = (f32[2560]{0:T(1024)S(1)}, f32[2560]{0:T(1024)S(1)}, u32[]{:S(2)}, u32[]{:S(2)}) collective-permute-start(f32[2560]{0:T(1024)S(1)} %add.23), channel_id=1, source_target_pairs={{0,2},{2,0},{1,3},{3,1},{4,6},{6,4},{5,7},{7,5},{8,10},{10,8},{9,1... | collective-permute-start | bytes 30728 | tf_op jit(solution)/shard_map/ppermute | solution.py:298
  81.9 16.3 %collective-permute-start.4 = (f32[8,136,128]{2,1,0:T(8,128)}, f32[8,136,128]{2,1,0:T(8,128)S(1)}, u32[]{:S(2)}, u32[]{:S(2)}) collective-permute-start(f32[8,136,128]{2,1,0:T(8,128)} %get-tuple-element.39.near_ref), channel_id=1, source_target_pairs={{4,0},{8,4},{12,8},{5,1},{9,5},{13,9},{6,2},{10,6},{14,10},{7,3},{... | collective-permute-start | bytes 1671176 | tf_op jit(solution)/shard_map/ppermute | solution.py:204
  98.2 0.8 copy-start.1
  101.1 15.0 %collective-permute-start.5 = (f32[8,136,128]{2,1,0:T(8,128)}, f32[8,136,128]{2,1,0:T(8,128)S(1)}, u32[]{:S(2)}, u32[]{:S(2)}) collective-permute-start(f32[8,136,128]{2,1,0:T(8,128)} %shard_map.91), channel_id=1, source_target_pairs={{4,0},{8,4},{12,8},{5,1},{9,5},{13,9},{6,2},{10,6},{14,10},{7,3},{... | collective-permute-start | bytes 1671176 | tf_op jit(solution)/shard_map/ppermute | solution.py:204
  116.1 0.8 copy-start.3

commit v13 on v12

--- a/solution.py
+++ b/solution.py
@@ -70,7 +70,7 @@
 
 
 def forward_kernel(
-    block_len, i_ref, q_ref, g_ref, n_ref, prefix_ref, carry_ref, doc_ref, o_ref, s_ref, r_ref
+    block_len, i_ref, q_ref, g_ref, n_ref, prefix_ref, carry_ref, doc_ref, o_ref, s_ref
 ):
     @pl.when(pl.program_id(0) == 0)
     def _():
@@ -83,14 +83,13 @@
         raw = i_ref[0, rows, :] + jnp.dot(
             q_ref[0, rows, :], state, preferred_element_type=jnp.float32
         )
-        r_ref[0, rows, :] = raw
         scaled = n_ref[0] * g_ref[0, rows, :].astype(jnp.float32)
         o_ref[rows, 0:1] += jnp.sum(raw * raw, axis=1, keepdims=True)
         o_ref[rows, 1:2] += jnp.sum(scaled * raw, axis=1, keepdims=True)
 
 
 def grad_kernel(
-    block_len, q_ref, r_ref, g_ref, n_ref, c_ref, pair_ref, end_ref, row_ref,
+    block_len, q_ref, i_ref, s_ref, g_ref, n_ref, c_ref, pair_ref, end_ref, row_ref,
     d_ref, suffix_ref, pay_ref,
 ):
     count = q_ref.shape[1] // block_len
@@ -99,7 +98,7 @@
     for n in range(count):
         rows = pl.ds(n * block_len, block_len)
         q = q_ref[0, rows, :]
-        raw = r_ref[0, rows, :]
+        raw = i_ref[0, rows, :] + jnp.dot(q, s_ref[0, n], preferred_element_type=jnp.float32)
         scaled = n_ref[0] * g_ref[0, rows, :].astype(jnp.float32)
         root_mean = c_ref[rows, 0:1]
         factor = c_ref[rows, 1:2]
@@ -283,12 +282,12 @@
             lambda intra: intra,
         ),
     )
-    local_sums, preceding_states, raw_attn = per_head_call(
+    local_sums, preceding_states = per_head_call(
         functools.partial(forward_kernel, block_len),
         [(intra_part, True), (queries, True), (out_grad, True), (gain, True),
          (local_prefix, True), (prior, True), (doc_rows, False)],
         [(jax.ShapeDtypeStruct((tok_count, 2), jnp.float32), False),
-         (jax.ShapeDtypeStruct(states.shape, jnp.bfloat16), True), (wide, True)],
+         (jax.ShapeDtypeStruct(states.shape, jnp.bfloat16), True)],
         pair_flops // 2,
     )
     feature_count = head_count * head_width * lax.axis_size(("sub", "head"))
@@ -304,7 +303,8 @@
     coefs = jnp.stack([root_mean, factor], axis=1)
     d_attn, local_suffix, qd_payload = per_head_call(
         functools.partial(grad_kernel, block_len),
-        [(queries, True), (raw_attn, True), (out_grad, True), (gain, True),
+        [(queries, True), (intra_part, True), (preceding_states, True), (out_grad, True),
+         (gain, True),
          (coefs, False), (later_rows, False), (first_rows, False), (first_doc_rows, False)],
         [(full, True), (states, True), (payload, True)],
         pair_flops // 2,

time: 129 us -> 128 us (level)
  no operation moved by 1% of the time
where the time goes in v13:
time: 128 us; the launch traced here: 127 us
  Pallas kernels  73.2 us (57%)
  waiting for transfers between devices  25.5 us (20%)
  starting transfers between devices  13.5 us (11%)
  local copies, waits for them, and re-layouts  10.3 us (8%)
  other arithmetic  2.65 us (2%)
  between operations  1.97 us (2%)
    pallas_call x7, Pallas kernels, per_head_call(): pl.pallas_call(body, grid=(count,), in_specs=[spec(x.shape, h, first) for...  69 us
    ppermute x4, waiting for transfers between devices, shift(): return lax.ppermute(value, axis, pairs)  22.8 us
    ppermute x4, starting transfers between devices, shift(): return lax.ppermute(value, axis, pairs)  11.9 us
    pallas_call x2, Pallas kernels, combine(): pl.pallas_call(combine_kernel, out_shape=jax.ShapeDtypeStruct(near.shape,...  4.21 us
    broadcast_in_dim x5, local copies, waits for them, and re-layouts, lanes(): return jnp.broadcast_to(table.reshape(rows, 1), (rows, head_width))  3.43 us
    ppermute x2, waiting for transfers between devices, on_device(): total_sums = total_sums + lax.ppermute(total_sums, axis, [(0, 1), (1, 0)])  2.72 us
  transfers between devices with their start and end apart: 6, of which 6 were waited for; matrix products, arithmetic and copies ran while one was open for 0% of the time, Pallas kernels for 23%

profile of v13, /device:TPU:0, one launch (start us, length us, event | category | flops | bytes accessed | tf_op | source)
XLA Modules:
  0.0 127.0 jit_solution(264635237643502961)
XLA Ops:
  0.6 0.7 convert_element_type.29
  1.3 0.6 fusion.5
  1.9 0.1 fusion.4
  2.6 1.9 %compare_convert_fusion = (f32[5]{0:T(128)S(1)}, f32[5]{0:T(128)S(1)}) fusion(f32[]{:T(128)} %bitcast.3, s32[5]{0:T(128)} %param.11, f32[]{:T(128)} %bitcast), kind=kLoop, calls=%fused_computation.12 | loop fusion | flops 25 | bytes 68 | tf_op jit(solution)/shard_map/convert_element_type | solution.py:241
  4.5 0.1 reshape.86
  4.6 0.6 broadcast_in_dim.16.refs_4_
  5.1 0.7 broadcast_in_dim.15.refs_3_
  5.8 0.7 broadcast_in_dim.14.refs_2_
  6.5 7.6 %shard_map.85 = (f32[8,5,128,128]{3,2,1,0:T(8,128)}, f32[8,136,128]{2,1,0:T(8,128)}) custom-call(bf16[8,1280,128]{2,1,0:T(8,128)(2,1)} %refs_2_.9, bf16[8,1280,128]{2,1,0:T(8,128)(2,1)} %refs_3_.3, f32[25,128]{1,0:T(8,128)} %broadcast_in_dim.14.refs_2_, f32[5,128]{1,0:T(8,128)} %broadcast_in_dim.15.refs_3_, f32[8,128]{1,0:T(8,128)} %broadcast_in_dim.16.refs_4_), custom_call_target="tpu_custom_call" | custom-call | flops 335544320 | bytes 8440832 | tf_op jit(solution)/shard_map/pallas_call | solution.py:169
  14.1 0.0 copy-start.4
  14.1 5.1 %collective-permute-start = (f32[8,136,128]{2,1,0:T(8,128)}, f32[8,136,128]{2,1,0:T(8,128)S(1)}, u32[]{:S(2)}, u32[]{:S(2)}) collective-permute-start(f32[8,136,128]{2,1,0:T(8,128)} %get-tuple-element.30.near_ref), channel_id=1, source_target_pairs={{0,4},{4,8},{8,12},{1,5},{5,9},{9,13},{2,6},{6,10},{10,14},{3,7},{... | collective-permute-start | bytes 1671176 | tf_op jit(solution)/shard_map/ppermute | solution.py:203
  19.2 10.2 %shard_map.86.refs_0_.refs_1_ = f32[8,1280,128]{2,1,0:T(8,128)} custom-call(bf16[8,1280,128]{2,1,0:T(8,128)(2,1)} %refs_0_.9, bf16[8,1280,128]{2,1,0:T(8,128)(2,1)} %refs_2_.9, bf16[8,1280,128]{2,1,0:T(8,128)(2,1)} %refs_3_.3), custom_call_target="tpu_custom_call" | custom-call | flops 1342177280 | bytes 13107200 | tf_op jit(solution)/shard_map/pallas_call | solution.py:169
  29.3 2.0 %collective-permute-done.far_ref = f32[8,136,128]{2,1,0:T(8,128)S(1)} collective-permute-done((f32[8,136,128]{2,1,0:T(8,128)}, f32[8,136,128]{2,1,0:T(8,128)S(1)}, u32[]{:S(2)}, u32[]{:S(2)}) %collective-permute-start) | collective-permute-done | bytes 557088 | tf_op jit(solution)/shard_map/ppermute | solution.py:203
  31.3 0.0 copy-start.2
  31.3 0.8 copy-done.2
  32.1 2.1 %shard_map.87 = f32[8,136,128]{2,1,0:T(8,128)} custom-call(f32[8,136,128]{2,1,0:T(8,128)} %get-tuple-element.30.near_ref, f32[8,136,128]{2,1,0:T(8,128)} %copy-done.2), custom_call_target="tpu_custom_call" | custom-call | flops 278528 | bytes 1671168 | tf_op jit(solution)/shard_map/pallas_call | solution.py:185
  34.2 4.3 %collective-permute-start.1 = (f32[8,136,128]{2,1,0:T(8,128)}, f32[8,136,128]{2,1,0:T(8,128)S(1)}, u32[]{:S(2)}, u32[]{:S(2)}) collective-permute-start(f32[8,136,128]{2,1,0:T(8,128)} %shard_map.87), channel_id=1, source_target_pairs={{0,4},{4,8},{8,12},{1,5},{5,9},{9,13},{2,6},{6,10},{10,14},{3,7},{... | collective-permute-start | bytes 1671176 | tf_op jit(solution)/shard_map/ppermute | solution.py:203
  38.5 0.0 copy-done.4
  38.6 11.3 %collective-permute-done.1.refs_5_ = f32[8,136,128]{2,1,0:T(8,128)S(1)} collective-permute-done((f32[8,136,128]{2,1,0:T(8,128)}, f32[8,136,128]{2,1,0:T(8,128)S(1)}, u32[]{:S(2)}, u32[]{:S(2)}) %collective-permute-start.1) | collective-permute-done | bytes 557088 | tf_op jit(solution)/shard_map/ppermute | solution.py:203
  49.8 0.0 copy-start
  49.8 0.8 broadcast_in_dim.17.refs_6_
  50.6 0.0 copy-done
  50.6 10.2 %shard_map.88 = (f32[1280,2]{1,0:T(8,128)}, bf16[8,5,128,128]{3,2,1,0:T(8,128)(2,1)}) custom-call(f32[8,1280,128]{2,1,0:T(8,128)} %shard_map.86.refs_0_.refs_1_, bf16[8,1280,128]{2,1,0:T(8,128)(2,1)} %refs_0_.9, bf16[8,1280,128]{2,1,0:T(8,128)(2,1)} %refs_3_.2, f32[8,1,128]{2,1,0:T(1,128)} %bitcast.5, f32[8,5,128,128]{3,2,1,0:T(8,128)} %get-tuple-element.34.refs_4_, ...), custom_call_target="tpu_custom_call" | custom-call | flops 335544320 | bytes 14991872 | tf_op jit(solution)/shard_map/pallas_call | solution.py:169
  60.8 1.3 %copy.15 = f32[2,1280]{1,0:T(2,128)S(1)} copy(f32[2,1280]{0,1:T(8,128)} %bitcast.4) | data formatting | bytes 20480 | tf_op jit(solution)/shard_map/transpose | solution.py:294
  62.2 0.1 collective-permute-start.2
  62.3 1.2 collective-permute-done.2
  63.4 1.5 %collective-permute-start.3 = (f32[2560]{0:T(1024)S(1)}, f32[2560]{0:T(1024)S(1)}, u32[]{:S(2)}, u32[]{:S(2)}) collective-permute-start(f32[2560]{0:T(1024)S(1)} %add.23), channel_id=1, source_target_pairs={{0,2},{2,0},{1,3},{3,1},{4,6},{6,4},{5,7},{7,5},{8,10},{10,8},{9,1... | collective-permute-start | bytes 30728 | tf_op jit(solution)/shard_map/ppermute | solution.py:297
  65.5 0.1 reshape.87
  65.6 1.6 %collective-permute-done.3 = f32[2560]{0:T(1024)S(1)} collective-permute-done((f32[2560]{0:T(1024)S(1)}, f32[2560]{0:T(1024)S(1)}, u32[]{:S(2)}, u32[]{:S(2)}) %collective-permute-start.3) | collective-permute-done | bytes 10272 | tf_op jit(solution)/shard_map/ppermute | solution.py:297
  67.2 1.1 copy.16.refs_5_
  68.3 0.7 broadcast_in_dim.19.refs_7_
  69.0 0.6 broadcast_in_dim.20.refs_8_
  69.5 0.7 broadcast_in_dim.18.refs_6_
  70.2 10.8 %shard_map.89 = (bf16[8,1280,128]{2,1,0:T(8,128)(2,1)}, f32[8,5,128,128]{3,2,1,0:T(8,128)}, f32[8,136,128]{2,1,0:T(8,128)}) custom-call(bf16[8,1280,128]{2,1,0:T(8,128)(2,1)} %refs_0_.9, f32[8,1280,128]{2,1,0:T(8,128)} %shard_map.86.refs_0_.refs_1_, bf16[8,5,128,128]{3,2,1,0:T(8,128)(2,1)} %get-tuple-element.36.refs_2_.refs_4_, ...), custom_call_target="tpu_custom_call" | custom-call | flops 335544320 | bytes 17630208 | tf_op jit(solution)/shard_map/pallas_call | solution.py:169
  81.1 1.3 %collective-permute-start.4 = (f32[8,136,128]{2,1,0:T(8,128)}, f32[8,136,128]{2,1,0:T(8,128)S(1)}, u32[]{:S(2)}, u32[]{:S(2)}) collective-permute-start(f32[8,136,128]{2,1,0:T(8,128)} %get-tuple-element.38.near_ref), channel_id=1, source_target_pairs={{4,0},{8,4},{12,8},{5,1},{9,5},{13,9},{6,2},{10,6},{14,10},{7,3},{... | collective-permute-start | bytes 1671176 | tf_op jit(solution)/shard_map/ppermute | solution.py:203
  82.3 9.6 %shard_map.90 = (bf16[8,1280,128]{2,1,0:T(8,128)(2,1)}, f32[8,1280,128]{2,1,0:T(8,128)}, f32[8,1280,128]{2,1,0:T(8,128)}) custom-call(bf16[8,1280,128]{2,1,0:T(8,128)(2,1)} %refs_0_.9, bf16[8,1280,128]{2,1,0:T(8,128)(2,1)} %refs_2_.9, bf16[8,1280,128]{2,1,0:T(8,128)(2,1)} %refs_3_.3, bf16[8,1280,128]{2,1,0:T(8,128)(2,1)} %get-tuple-element.39.refs_3_, ...), custom_call_target="tpu_custom_call" | custom-call | flops 1677721600 | bytes 12451840 | tf_op jit(solution)/shard_map/pallas_call | solution.py:169
  91.9 5.4 %collective-permute-done.4.far_ref = f32[8,136,128]{2,1,0:T(8,128)S(1)} collective-permute-done((f32[8,136,128]{2,1,0:T(8,128)}, f32[8,136,128]{2,1,0:T(8,128)S(1)}, u32[]{:S(2)}, u32[]{:S(2)}) %collective-permute-start.4) | collective-permute-done | bytes 557088 | tf_op jit(solution)/shard_map/ppermute | solution.py:203
  97.3 0.0 copy-start.1
  97.3 0.8 copy-done.1
  98.2 2.1 %shard_map.91 = f32[8,136,128]{2,1,0:T(8,128)} custom-call(f32[8,136,128]{2,1,0:T(8,128)} %get-tuple-element.38.near_ref, f32[8,136,128]{2,1,0:T(8,128)} %copy-done.1), custom_call_target="tpu_custom_call" | custom-call | flops 278528 | bytes 1671168 | tf_op jit(solution)/shard_map/pallas_call | solution.py:185
  100.3 1.3 %collective-permute-start.5 = (f32[8,136,128]{2,1,0:T(8,128)}, f32[8,136,128]{2,1,0:T(8,128)S(1)}, u32[]{:S(2)}, u32[]{:S(2)}) collective-permute-start(f32[8,136,128]{2,1,0:T(8,128)} %shard_map.91), channel_id=1, source_target_pairs={{4,0},{8,4},{12,8},{5,1},{9,5},{13,9},{6,2},{10,6},{14,10},{7,3},{... | collective-permute-start | bytes 1671176 | tf_op jit(solution)/shard_map/ppermute | solution.py:203
  101.6 9.6 %shard_map.92 = (bf16[8,1280,128]{2,1,0:T(8,128)(2,1)}, f32[8,1280,128]{2,1,0:T(8,128)}, f32[8,1280,128]{2,1,0:T(8,128)}) custom-call(bf16[8,1280,128]{2,1,0:T(8,128)(2,1)} %refs_0_.9, bf16[8,1280,128]{2,1,0:T(8,128)(2,1)} %refs_2_.9, bf16[8,1280,128]{2,1,0:T(8,128)(2,1)} %refs_3_.3, ...), custom_call_target="tpu_custom_call", output_to_operand_aliasing={{0}: (5, {}), {1}: (6, {}), {2}: (7, {})} | custom-call | flops 1677721600 | bytes 12451840 | tf_op jit(solution)/shard_map/pallas_call | solution.py:169
  111.1 4.1 %collective-permute-done.5.refs_5_ = f32[8,136,128]{2,1,0:T(8,128)S(1)} collective-permute-done((f32[8,136,128]{2,1,0:T(8,128)}, f32[8,136,128]{2,1,0:T(8,128)S(1)}, u32[]{:S(2)}, u32[]{:S(2)}) %collective-permute-start.5) | collective-permute-done | bytes 557088 | tf_op jit(solution)/shard_map/ppermute | solution.py:203
  115.3 0.0 copy-start.3
  115.3 0.8 copy-done.3
  116.1 11.0 %shard_map.93 = (bf16[8,1280,128]{2,1,0:T(8,128)(2,1)}, bf16[8,1280,128]{2,1,0:T(8,128)(2,1)}) custom-call(f32[8,1280,128]{2,1,0:T(8,128)} %get-tuple-element.51.refs_0_, f32[8,1280,128]{2,1,0:T(8,128)} %get-tuple-element.52.refs_1_, bf16[8,1280,128]{2,1,0:T(8,128)(2,1)} %refs_2_.9, bf16[8,1280,128]{2,1,0:T(8,128)(2,1)} %refs_3_.3, ...), custom_call_target="tpu_custom_call" | custom-call | flops 671088640 | bytes 24152576 | tf_op jit(solution)/shard_map/pallas_call | solution.py:169
  (8 shorter events, 0.1 us)
Async XLA Ops:
  14.1 24.5 %copy-start.4 = (s32[5]{0:T(128)S(1)}, s32[5]{0:T(128)}, u32[]{:S(2)}) copy-start(s32[5]{0:T(128)} %param.11) | copy-start | bytes 64
  14.1 17.2 %collective-permute-start = (f32[8,136,128]{2,1,0:T(8,128)}, f32[8,136,128]{2,1,0:T(8,128)S(1)}, u32[]{:S(2)}, u32[]{:S(2)}) collective-permute-start(f32[8,136,128]{2,1,0:T(8,128)} %get-tuple-element.30.near_ref), channel_id=1, source_target_pairs={{0,4},{4,8},{8,12},{1,5},{5,9},{9,13},{2,6},{6,10},{10,14},{3,7},{... | collective-permute-start | bytes 1671176 | tf_op jit(solution)/shard_map/ppermute | solution.py:203
  31.3 0.8 copy-start.2
  34.2 15.6 %collective-permute-start.1 = (f32[8,136,128]{2,1,0:T(8,128)}, f32[8,136,128]{2,1,0:T(8,128)S(1)}, u32[]{:S(2)}, u32[]{:S(2)}) collective-permute-start(f32[8,136,128]{2,1,0:T(8,128)} %shard_map.87), channel_id=1, source_target_pairs={{0,4},{4,8},{8,12},{1,5},{5,9},{9,13},{2,6},{6,10},{10,14},{3,7},{... | collective-permute-start | bytes 1671176 | tf_op jit(solution)/shard_map/ppermute | solution.py:203
  49.8 0.8 copy-start
  62.2 1.2 collective-permute-start.2
  63.4 3.7 %collective-permute-start.3 = (f32[2560]{0:T(1024)S(1)}, f32[2560]{0:T(1024)S(1)}, u32[]{:S(2)}, u32[]{:S(2)}) collective-permute-start(f32[2560]{0:T(1024)S(1)} %add.23), channel_id=1, source_target_pairs={{0,2},{2,0},{1,3},{3,1},{4,6},{6,4},{5,7},{7,5},{8,10},{10,8},{9,1... | collective-permute-start | bytes 30728 | tf_op jit(solution)/shard_map/ppermute | solution.py:297
  81.1 16.3 %collective-permute-start.4 = (f32[8,136,128]{2,1,0:T(8,128)}, f32[8,136,128]{2,1,0:T(8,128)S(1)}, u32[]{:S(2)}, u32[]{:S(2)}) collective-permute-start(f32[8,136,128]{2,1,0:T(8,128)} %get-tuple-element.38.near_ref), channel_id=1, source_target_pairs={{4,0},{8,4},{12,8},{5,1},{9,5},{13,9},{6,2},{10,6},{14,10},{7,3},{... | collective-permute-start | bytes 1671176 | tf_op jit(solution)/shard_map/ppermute | solution.py:203
  97.3 0.8 copy-start.1
  100.3 15.0 %collective-permute-start.5 = (f32[8,136,128]{2,1,0:T(8,128)}, f32[8,136,128]{2,1,0:T(8,128)S(1)}, u32[]{:S(2)}, u32[]{:S(2)}) collective-permute-start(f32[8,136,128]{2,1,0:T(8,128)} %shard_map.91), channel_id=1, source_target_pairs={{4,0},{8,4},{12,8},{5,1},{9,5},{13,9},{6,2},{10,6},{14,10},{7,3},{... | collective-permute-start | bytes 1671176 | tf_op jit(solution)/shard_map/ppermute | solution.py:203
  115.3 0.8 copy-start.3

commit v14 on v13

--- a/solution.py
+++ b/solution.py
@@ -5,6 +5,7 @@
 import jax.numpy as jnp
 from jax import lax
 from jax.experimental import pallas as pl
+from jax.experimental.pallas import tpu as pltpu
 from jax.sharding import PartitionSpec as P
 
 _ROWS_MINOR = (((1,), (1,)), ((), ()))
@@ -17,21 +18,25 @@
     return row_ids >= col_ids
 
 
-def _sum_blocks(mask_ref, first_row, parts):
-    total = mask_ref[first_row : first_row + 1, :] * parts[0]
-    for c in range(1, len(parts)):
-        total = total + mask_ref[first_row + c : first_row + c + 1, :] * parts[c]
+def _doc_sum(doc_ref, parts, keep):
+    total = jnp.zeros_like(parts[0])
+    for c in range(len(parts)):
+        total = total + jnp.where(keep(c), parts[c], 0.0)
     return total
+
+
+def _doc_row(doc_ref, n, shape):
+    return jnp.full(shape, doc_ref[n].astype(jnp.float32) + 1.0, jnp.float32)
 
 
 def _carried(state_ref, doc_ref, n, carry_ref):
     width = carry_ref.shape[2]
-    joined = doc_ref[n : n + 1, :] == carry_ref[0, width : width + 1, :]
+    joined = carry_ref[0, width : width + 1, :] == doc_ref[n].astype(jnp.float32) + 1.0
     total = state_ref[0, n] + jnp.where(joined, carry_ref[0, :width, :], 0.0)
     return total.astype(jnp.bfloat16)
 
 
-def state_kernel(block_len, k_ref, v_ref, pair_ref, end_ref, row_ref, prefix_ref, pay_ref):
+def state_kernel(block_len, doc_ref, k_ref, v_ref, prefix_ref, pay_ref):
     count = k_ref.shape[1] // block_len
     width = k_ref.shape[2]
     parts = []
@@ -44,9 +49,11 @@
             )
         )
     for b in range(count):
-        prefix_ref[0, b] = _sum_blocks(pair_ref, b * count, parts)
-    pay_ref[0, :width, :] = _sum_blocks(end_ref, 0, parts)
-    pay_ref[0, width:, :] = row_ref[...]
+        prefix_ref[0, b] = _doc_sum(
+            doc_ref, parts, lambda c: jnp.logical_and(c < b, doc_ref[c] == doc_ref[b])
+        )
+    pay_ref[0, :width, :] = _doc_sum(doc_ref, parts, lambda c: doc_ref[c] == doc_ref[count - 1])
+    pay_ref[0, width:, :] = _doc_row(doc_ref, count - 1, (8, width))
 
 
 def combine_kernel(near_ref, far_ref, o_ref):
@@ -70,7 +77,7 @@
 
 
 def forward_kernel(
-    block_len, i_ref, q_ref, g_ref, n_ref, prefix_ref, carry_ref, doc_ref, o_ref, s_ref
+    block_len, doc_ref, i_ref, q_ref, g_ref, n_ref, prefix_ref, carry_ref, o_ref, s_ref
 ):
     @pl.when(pl.program_id(0) == 0)
     def _():
@@ -89,8 +96,7 @@
 
 
 def grad_kernel(
-    block_len, q_ref, i_ref, s_ref, g_ref, n_ref, c_ref, pair_ref, end_ref, row_ref,
-    d_ref, suffix_ref, pay_ref,
+    block_len, doc_ref, q_ref, i_ref, s_ref, g_ref, n_ref, c_ref, d_ref, suffix_ref, pay_ref
 ):
     count = q_ref.shape[1] // block_len
     width = q_ref.shape[2]
@@ -106,9 +112,11 @@
         d_ref[0, rows, :] = d
         parts.append(lax.dot_general(q, d, _ROWS_MAJOR, preferred_element_type=jnp.float32))
     for b in range(count):
-        suffix_ref[0, b] = _sum_blocks(pair_ref, b * count, parts)
-    pay_ref[0, :width, :] = _sum_blocks(end_ref, 0, parts)
-    pay_ref[0, width:, :] = row_ref[...]
+        suffix_ref[0, b] = _doc_sum(
+            doc_ref, parts, lambda c: jnp.logical_and(c > b, doc_ref[c] == doc_ref[b])
+        )
+    pay_ref[0, :width, :] = _doc_sum(doc_ref, parts, lambda c: doc_ref[c] == doc_ref[0])
+    pay_ref[0, width:, :] = _doc_row(doc_ref, 0, (8, width))
 
 
 def query_grad_kernel(block_len, q_ref, k_ref, v_ref, d_ref, s_ref, dq_ref, dk_ref, dv_ref):
@@ -133,7 +141,7 @@
 
 
 def key_value_grad_kernel(
-    block_len, ik_ref, iv_ref, k_ref, v_ref, suffix_ref, carry_ref, doc_ref, dk_ref, dv_ref
+    block_len, doc_ref, ik_ref, iv_ref, k_ref, v_ref, suffix_ref, carry_ref, dk_ref, dv_ref
 ):
     for n in range(k_ref.shape[1] // block_len):
         rows = pl.ds(n * block_len, block_len)
@@ -148,37 +156,42 @@
         dv_ref[0, rows, :] = dv.astype(dv_ref.dtype)
 
 
-def per_head_call(kernel, inputs, outputs, flops, heads=None, into=()):
+def per_head_call(kernel, inputs, outputs, flops, heads=None, into=(), scalars=None):
     def spec(shape, per_head, first):
         if per_head:
             return pl.BlockSpec(
-                (1,) + shape[1:], lambda h: (h + first,) + (0,) * (len(shape) - 1)
+                (1,) + shape[1:], lambda h, *_: (h + first,) + (0,) * (len(shape) - 1)
             )
-        return pl.BlockSpec(shape, lambda h: (0,) * len(shape))
+        return pl.BlockSpec(shape, lambda h, *_: (0,) * len(shape))
 
     head_count = inputs[0][0].shape[0]
     first, count = heads if heads is not None else (0, head_count)
     share = count / head_count
     in_bytes = sum(x.size * x.dtype.itemsize for x, _ in inputs) * share
     out_bytes = sum(math.prod(o.shape) * o.dtype.itemsize for o, _ in outputs) * share
-    skip = len(inputs)
+    lead = 0 if scalars is None else 1
+    skip = lead + len(inputs)
 
     def body(*refs):
         kernel(*refs[:skip], *refs[skip + len(into):])
 
-    return pl.pallas_call(
-        body,
+    grid_spec = pltpu.PrefetchScalarGridSpec(
+        num_scalar_prefetch=lead,
         grid=(count,),
         in_specs=[spec(x.shape, h, first) for x, h in inputs]
         + [pl.BlockSpec(memory_space=pl.ANY) for _ in into],
         out_specs=[spec(o.shape, h, first) for o, h in outputs],
+    )
+    return pl.pallas_call(
+        body,
+        grid_spec=grid_spec,
         out_shape=[o for o, _ in outputs],
         input_output_aliases={skip + i: i for i in range(len(into))},
         cost_estimate=pl.CostEstimate(
             flops=int(flops * share), transcendentals=0,
             bytes_accessed=int(in_bytes + out_bytes),
         ),
-    )(*[x for x, _ in inputs], *into)
+    )(*([] if scalars is None else [scalars]), *[x for x, _ in inputs], *into)
 
 
 def combine(near, far):
@@ -232,25 +245,6 @@
     block_count = doc_ids.shape[0]
     block_len = tok_count // block_count
     gain = norm_gain.reshape(head_count, 1, head_width)
-    doc_values = doc_ids.astype(jnp.float32)
-    block_pos = jnp.arange(block_count, dtype=jnp.int32)
-    same_doc = doc_values[:, None] == doc_values[None, :]
-    earlier_mask = (same_doc & (block_pos[None, :] < block_pos[:, None])).astype(jnp.float32)
-    later_mask = (same_doc & (block_pos[None, :] > block_pos[:, None])).astype(jnp.float32)
-    last_match = (doc_values == doc_values[-1]).astype(jnp.float32)
-    first_match = (doc_values == doc_values[0]).astype(jnp.float32)
-
-    def lanes(table, rows):
-        return jnp.broadcast_to(table.reshape(rows, 1), (rows, head_width))
-
-    earlier_rows = lanes(earlier_mask, block_count * block_count)
-    later_rows = lanes(later_mask, block_count * block_count)
-    last_rows = lanes(last_match, block_count)
-    first_rows = lanes(first_match, block_count)
-    doc_rows = lanes(doc_values + 1.0, block_count)
-    last_doc_rows = jnp.broadcast_to(doc_values[-1] + 1.0, (8, head_width))
-    first_doc_rows = jnp.broadcast_to(doc_values[0] + 1.0, (8, head_width))
-
     pair_flops = 2 * head_count * block_count * block_len * block_len * head_width
     full = jax.ShapeDtypeStruct(queries.shape, jnp.bfloat16)
     wide = jax.ShapeDtypeStruct(queries.shape, jnp.float32)
@@ -262,10 +256,10 @@
 
     local_prefix, kv_payload = per_head_call(
         functools.partial(state_kernel, block_len),
-        [(keys, True), (values, True), (earlier_rows, False), (last_rows, False),
-         (last_doc_rows, False)],
+        [(keys, True), (values, True)],
         [(states, True), (payload, True)],
         pair_flops // 2,
+        scalars=doc_ids,
     )
     prior, intra_part = carry(
         kv_payload,
@@ -285,10 +279,11 @@
     local_sums, preceding_states = per_head_call(
         functools.partial(forward_kernel, block_len),
         [(intra_part, True), (queries, True), (out_grad, True), (gain, True),
-         (local_prefix, True), (prior, True), (doc_rows, False)],
+         (local_prefix, True), (prior, True)],
         [(jax.ShapeDtypeStruct((tok_count, 2), jnp.float32), False),
          (jax.ShapeDtypeStruct(states.shape, jnp.bfloat16), True)],
         pair_flops // 2,
+        scalars=doc_ids,
     )
     feature_count = head_count * head_width * lax.axis_size(("sub", "head"))
     total_sums = local_sums.T.reshape(2 * tok_count)
@@ -305,9 +300,10 @@
         functools.partial(grad_kernel, block_len),
         [(queries, True), (intra_part, True), (preceding_states, True), (out_grad, True),
          (gain, True),
-         (coefs, False), (later_rows, False), (first_rows, False), (first_doc_rows, False)],
+         (coefs, False)],
         [(full, True), (states, True), (payload, True)],
         pair_flops // 2,
+        scalars=doc_ids,
     )
     half = head_count // 2
 
@@ -335,9 +331,10 @@
     key_gradient, value_gradient = per_head_call(
         functools.partial(key_value_grad_kernel, block_len),
         [(key_intra, True), (value_intra, True), (keys, True), (values, True),
-         (local_suffix, True), (following, True), (doc_rows, False)],
+         (local_suffix, True), (following, True)],
         [(full, True), (full, True)],
         pair_flops,
+        scalars=doc_ids,
     )
     return query_gradient, key_gradient, value_gradient
 

time: 128 us -> 123 us (0.961)
  local copies, waits for them, and re-layouts: 10.3 us -> 5.71 us
  other arithmetic: 2.65 us -> 0.04 us
  Pallas kernels: 73.2 us -> 75.6 us
    broadcast_in_dim x7 -> x0, local copies, waits for them, and re-layouts: 4.61 us -> none  [the longest x5 3.43 us: lanes(): return jnp.broadcast_to(table.reshape(rows, 1), (rows, head_width))]
    convert_element_type x3 -> x0, other arithmetic: 2.61 us -> none  [the longest x1 1.87 us: on_device(): first_match = (doc_values == doc_values[0]).astype(jnp.float32)]
    pallas_call x7, Pallas kernels: 69 us -> 71.3 us  [per_head_call(): pl.pallas_call(body, grid_spec=grid_spec, out_shape=[o for o, _ in output...]
    unnamed x10 -> x8, local copies, waits for them, and re-layouts: 2.49 us -> 3.28 us
  transfers between devices with their start and end apart: 6 -> 6, of which waited for: 6 -> 6; matrix products, arithmetic and copies ran while one was open for 0% -> 0% of each run, Pallas kernels for 23% -> 24%
where the time goes in v14:
time: 123 us; the launch traced here: 122 us
  Pallas kernels  75.6 us (61%)
  waiting for transfers between devices  26 us (21%)
  starting transfers between devices  13.5 us (11%)
  local copies, waits for them, and re-layouts  5.71 us (5%)
    pallas_call x7, Pallas kernels, per_head_call(): pl.pallas_call(body, grid_spec=grid_spec, out_shape=[o for o, _ in output...  71.3 us
    ppermute x4, waiting for transfers between devices, shift(): return lax.ppermute(value, axis, pairs)  22.7 us
    ppermute x4, starting transfers between devices, shift(): return lax.ppermute(value, axis, pairs)  11.8 us
    pallas_call x2, Pallas kernels, combine(): pl.pallas_call(combine_kernel, out_shape=jax.ShapeDtypeStruct(near.shape,...  4.22 us
    ppermute x2, waiting for transfers between devices, on_device(): total_sums = total_sums + lax.ppermute(total_sums, axis, [(0, 1), (1, 0)])  3.28 us
    unnamed x8, local copies, waits for them, and re-layouts  3.28 us
  transfers between devices with their start and end apart: 6, of which 6 were waited for; matrix products, arithmetic and copies ran while one was open for 0% of the time, Pallas kernels for 24%

profile of v14, /device:TPU:0, one launch (start us, length us, event | category | flops | bytes accessed | tf_op | source)
XLA Modules:
  0.0 121.5 jit_solution(16049346949378169756)
XLA Ops:
  0.6 8.1 %shard_map.85 = (f32[8,5,128,128]{3,2,1,0:T(8,128)}, f32[8,136,128]{2,1,0:T(8,128)}) custom-call(s32[5]{0:T(128)} %refs_0_.13, bf16[8,1280,128]{2,1,0:T(8,128)(2,1)} %refs_3_.3, bf16[8,1280,128]{2,1,0:T(8,128)(2,1)} %refs_4_.3), custom_call_target="tpu_custom_call" | custom-call | flops 335544320 | bytes 8421376 | tf_op jit(solution)/shard_map/pallas_call | solution.py:185
  8.7 5.0 %collective-permute-start = (f32[8,136,128]{2,1,0:T(8,128)}, f32[8,136,128]{2,1,0:T(8,128)S(1)}, u32[]{:S(2)}, u32[]{:S(2)}) collective-permute-start(f32[8,136,128]{2,1,0:T(8,128)} %get-tuple-element.30.near_ref), channel_id=1, source_target_pairs={{0,4},{4,8},{8,12},{1,5},{5,9},{9,13},{2,6},{6,10},{10,14},{3,7},{... | collective-permute-start | bytes 1671176 | tf_op jit(solution)/shard_map/ppermute | solution.py:216
  13.7 10.2 %shard_map.86.refs_1_.refs_2_ = f32[8,1280,128]{2,1,0:T(8,128)} custom-call(bf16[8,1280,128]{2,1,0:T(8,128)(2,1)} %refs_0_.12, bf16[8,1280,128]{2,1,0:T(8,128)(2,1)} %refs_3_.3, bf16[8,1280,128]{2,1,0:T(8,128)(2,1)} %refs_4_.3), custom_call_target="tpu_custom_call" | custom-call | flops 1342177280 | bytes 13107200 | tf_op jit(solution)/shard_map/pallas_call | solution.py:185
  23.8 2.0 %collective-permute-done.far_ref = f32[8,136,128]{2,1,0:T(8,128)S(1)} collective-permute-done((f32[8,136,128]{2,1,0:T(8,128)}, f32[8,136,128]{2,1,0:T(8,128)S(1)}, u32[]{:S(2)}, u32[]{:S(2)}) %collective-permute-start) | collective-permute-done | bytes 557088 | tf_op jit(solution)/shard_map/ppermute | solution.py:216
  25.8 0.0 copy-start.3
  25.8 0.8 copy-done.3
  26.6 2.1 %shard_map.87 = f32[8,136,128]{2,1,0:T(8,128)} custom-call(f32[8,136,128]{2,1,0:T(8,128)} %get-tuple-element.30.near_ref, f32[8,136,128]{2,1,0:T(8,128)} %copy-done.3), custom_call_target="tpu_custom_call" | custom-call | flops 278528 | bytes 1671168 | tf_op jit(solution)/shard_map/pallas_call | solution.py:198
  28.7 4.3 %collective-permute-start.1 = (f32[8,136,128]{2,1,0:T(8,128)}, f32[8,136,128]{2,1,0:T(8,128)S(1)}, u32[]{:S(2)}, u32[]{:S(2)}) collective-permute-start(f32[8,136,128]{2,1,0:T(8,128)} %shard_map.87), channel_id=1, source_target_pairs={{0,4},{4,8},{8,12},{1,5},{5,9},{9,13},{2,6},{6,10},{10,14},{3,7},{... | collective-permute-start | bytes 1671176 | tf_op jit(solution)/shard_map/ppermute | solution.py:216
  33.0 11.2 %collective-permute-done.1.refs_6_ = f32[8,136,128]{2,1,0:T(8,128)S(1)} collective-permute-done((f32[8,136,128]{2,1,0:T(8,128)}, f32[8,136,128]{2,1,0:T(8,128)S(1)}, u32[]{:S(2)}, u32[]{:S(2)}) %collective-permute-start.1) | collective-permute-done | bytes 557088 | tf_op jit(solution)/shard_map/ppermute | solution.py:216
  44.3 0.0 copy-start.1
  44.3 0.8 copy-done.1
  45.1 10.8 %shard_map.88 = (f32[1280,2]{1,0:T(8,128)}, bf16[8,5,128,128]{3,2,1,0:T(8,128)(2,1)}) custom-call(s32[5]{0:T(128)} %refs_0_.13, f32[8,1280,128]{2,1,0:T(8,128)} %shard_map.86.refs_1_.refs_2_, bf16[8,1280,128]{2,1,0:T(8,128)(2,1)} %refs_0_.12, bf16[8,1280,128]{2,1,0:T(8,128)(2,1)} %refs_4_.2, f32[8,1,128]{2,1,0:T(1,128)} %bitcast.3, ...), custom_call_target="tpu_custom_call" | custom-call | flops 335544320 | bytes 14989312 | tf_op jit(solution)/shard_map/pallas_call | solution.py:185
  55.9 1.3 %copy.15 = f32[2,1280]{1,0:T(2,128)S(1)} copy(f32[2,1280]{0,1:T(8,128)} %bitcast.2) | data formatting | bytes 20480 | tf_op jit(solution)/shard_map/transpose | solution.py:289
  57.2 0.1 collective-permute-start.2
  57.3 1.2 collective-permute-done.2
  58.4 1.6 %collective-permute-start.3 = (f32[2560]{0:T(1024)S(1)}, f32[2560]{0:T(1024)S(1)}, u32[]{:S(2)}, u32[]{:S(2)}) collective-permute-start(f32[2560]{0:T(1024)S(1)} %add.12), channel_id=1, source_target_pairs={{0,2},{2,0},{1,3},{3,1},{4,6},{6,4},{5,7},{7,5},{8,10},{10,8},{9,1... | collective-permute-start | bytes 30728 | tf_op jit(solution)/shard_map/ppermute | solution.py:292
  60.0 2.1 %collective-permute-done.3 = f32[2560]{0:T(1024)S(1)} collective-permute-done((f32[2560]{0:T(1024)S(1)}, f32[2560]{0:T(1024)S(1)}, u32[]{:S(2)}, u32[]{:S(2)}) %collective-permute-start.3) | collective-permute-done | bytes 10272 | tf_op jit(solution)/shard_map/ppermute | solution.py:292
  62.2 1.1 copy.16.refs_6_
  63.3 11.6 %shard_map.89 = (bf16[8,1280,128]{2,1,0:T(8,128)(2,1)}, f32[8,5,128,128]{3,2,1,0:T(8,128)}, f32[8,136,128]{2,1,0:T(8,128)}) custom-call(s32[5]{0:T(128)} %refs_0_.13, bf16[8,1280,128]{2,1,0:T(8,128)(2,1)} %refs_0_.12, f32[8,1280,128]{2,1,0:T(8,128)} %shard_map.86.refs_1_.refs_2_, bf16[8,5,128,128]{3,2,1,0:T(8,128)(2,1)} %get-tuple-element.36.refs_3_.refs_4_, ...), custom_call_target="tpu_custom_call" | custom-call | flops 335544320 | bytes 17610752 | tf_op jit(solution)/shard_map/pallas_call | solution.py:185
  74.9 1.3 %collective-permute-start.4 = (f32[8,136,128]{2,1,0:T(8,128)}, f32[8,136,128]{2,1,0:T(8,128)S(1)}, u32[]{:S(2)}, u32[]{:S(2)}) collective-permute-start(f32[8,136,128]{2,1,0:T(8,128)} %get-tuple-element.38.near_ref), channel_id=1, source_target_pairs={{4,0},{8,4},{12,8},{5,1},{9,5},{13,9},{6,2},{10,6},{14,10},{7,3},{... | collective-permute-start | bytes 1671176 | tf_op jit(solution)/shard_map/ppermute | solution.py:216
  76.2 9.6 %shard_map.90 = (bf16[8,1280,128]{2,1,0:T(8,128)(2,1)}, f32[8,1280,128]{2,1,0:T(8,128)}, f32[8,1280,128]{2,1,0:T(8,128)}) custom-call(bf16[8,1280,128]{2,1,0:T(8,128)(2,1)} %refs_0_.12, bf16[8,1280,128]{2,1,0:T(8,128)(2,1)} %refs_3_.3, bf16[8,1280,128]{2,1,0:T(8,128)(2,1)} %refs_4_.3, bf16[8,1280,128]{2,1,0:T(8,128)(2,1)} %get-tuple-element.39.refs_3_, ...), custom_call_target="tpu_custom_call" | custom-call | flops 1677721600 | bytes 12451840 | tf_op jit(solution)/shard_map/pallas_call | solution.py:185
  85.8 5.4 %collective-permute-done.4.far_ref = f32[8,136,128]{2,1,0:T(8,128)S(1)} collective-permute-done((f32[8,136,128]{2,1,0:T(8,128)}, f32[8,136,128]{2,1,0:T(8,128)S(1)}, u32[]{:S(2)}, u32[]{:S(2)}) %collective-permute-start.4) | collective-permute-done | bytes 557088 | tf_op jit(solution)/shard_map/ppermute | solution.py:216
  91.2 0.0 copy-start.2
  91.2 0.8 copy-done.2
  92.0 2.1 %shard_map.91 = f32[8,136,128]{2,1,0:T(8,128)} custom-call(f32[8,136,128]{2,1,0:T(8,128)} %get-tuple-element.38.near_ref, f32[8,136,128]{2,1,0:T(8,128)} %copy-done.2), custom_call_target="tpu_custom_call" | custom-call | flops 278528 | bytes 1671168 | tf_op jit(solution)/shard_map/pallas_call | solution.py:198
  94.1 1.3 %collective-permute-start.5 = (f32[8,136,128]{2,1,0:T(8,128)}, f32[8,136,128]{2,1,0:T(8,128)S(1)}, u32[]{:S(2)}, u32[]{:S(2)}) collective-permute-start(f32[8,136,128]{2,1,0:T(8,128)} %shard_map.91), channel_id=1, source_target_pairs={{4,0},{8,4},{12,8},{5,1},{9,5},{13,9},{6,2},{10,6},{14,10},{7,3},{... | collective-permute-start | bytes 1671176 | tf_op jit(solution)/shard_map/ppermute | solution.py:216
  95.4 9.6 %shard_map.92 = (bf16[8,1280,128]{2,1,0:T(8,128)(2,1)}, f32[8,1280,128]{2,1,0:T(8,128)}, f32[8,1280,128]{2,1,0:T(8,128)}) custom-call(bf16[8,1280,128]{2,1,0:T(8,128)(2,1)} %refs_0_.12, bf16[8,1280,128]{2,1,0:T(8,128)(2,1)} %refs_3_.3, bf16[8,1280,128]{2,1,0:T(8,128)(2,1)} %refs_4_.3, ...), custom_call_target="tpu_custom_call", output_to_operand_aliasing={{0}: (5, {}), {1}: (6, {}), {2}: (7, {})} | custom-call | flops 1677721600 | bytes 12451840 | tf_op jit(solution)/shard_map/pallas_call | solution.py:185
  105.0 4.1 %collective-permute-done.5.refs_6_ = f32[8,136,128]{2,1,0:T(8,128)S(1)} collective-permute-done((f32[8,136,128]{2,1,0:T(8,128)}, f32[8,136,128]{2,1,0:T(8,128)S(1)}, u32[]{:S(2)}, u32[]{:S(2)}) %collective-permute-start.5) | collective-permute-done | bytes 557088 | tf_op jit(solution)/shard_map/ppermute | solution.py:216
  109.1 0.0 copy-start
  109.1 0.8 copy-done
  110.0 11.6 %shard_map.93 = (bf16[8,1280,128]{2,1,0:T(8,128)(2,1)}, bf16[8,1280,128]{2,1,0:T(8,128)(2,1)}) custom-call(s32[5]{0:T(128)} %refs_0_.13, f32[8,1280,128]{2,1,0:T(8,128)} %get-tuple-element.51.refs_1_, f32[8,1280,128]{2,1,0:T(8,128)} %get-tuple-element.52.refs_2_, bf16[8,1280,128]{2,1,0:T(8,128)(2,1)} %refs_3_.3, bf16[8,1280,128]{2,1,0:T(8,128)(2,1)} %refs_4_.3, ...), custom_call_target="tpu_custom_call" | custom-call | flops 671088640 | bytes 24150016 | tf_op jit(solution)/shard_map/pallas_call | solution.py:185
  (7 shorter events, 0.1 us)
Async XLA Ops:
  8.7 17.1 %collective-permute-start = (f32[8,136,128]{2,1,0:T(8,128)}, f32[8,136,128]{2,1,0:T(8,128)S(1)}, u32[]{:S(2)}, u32[]{:S(2)}) collective-permute-start(f32[8,136,128]{2,1,0:T(8,128)} %get-tuple-element.30.near_ref), channel_id=1, source_target_pairs={{0,4},{4,8},{8,12},{1,5},{5,9},{9,13},{2,6},{6,10},{10,14},{3,7},{... | collective-permute-start | bytes 1671176 | tf_op jit(solution)/shard_map/ppermute | solution.py:216
  25.8 0.8 copy-start.3
  28.7 15.6 %collective-permute-start.1 = (f32[8,136,128]{2,1,0:T(8,128)}, f32[8,136,128]{2,1,0:T(8,128)S(1)}, u32[]{:S(2)}, u32[]{:S(2)}) collective-permute-start(f32[8,136,128]{2,1,0:T(8,128)} %shard_map.87), channel_id=1, source_target_pairs={{0,4},{4,8},{8,12},{1,5},{5,9},{9,13},{2,6},{6,10},{10,14},{3,7},{... | collective-permute-start | bytes 1671176 | tf_op jit(solution)/shard_map/ppermute | solution.py:216
  44.3 0.8 copy-start.1
  57.2 1.2 %collective-permute-start.2 = (f32[2560]{0:T(1024)S(1)}, f32[2560]{0:T(1024)S(1)}, u32[]{:S(2)}, u32[]{:S(2)}) collective-permute-start(f32[2560]{0:T(1024)S(1)} %reshape.13), channel_id=1, source_target_pairs={{0,1},{1,0},{2,3},{3,2},{4,5},{5,4},{6,7},{7,6},{8,9},{9,8},{10,11... | collective-permute-start | bytes 30728 | tf_op jit(solution)/shard_map/ppermute | solution.py:292
  58.4 3.7 %collective-permute-start.3 = (f32[2560]{0:T(1024)S(1)}, f32[2560]{0:T(1024)S(1)}, u32[]{:S(2)}, u32[]{:S(2)}) collective-permute-start(f32[2560]{0:T(1024)S(1)} %add.12), channel_id=1, source_target_pairs={{0,2},{2,0},{1,3},{3,1},{4,6},{6,4},{5,7},{7,5},{8,10},{10,8},{9,1... | collective-permute-start | bytes 30728 | tf_op jit(solution)/shard_map/ppermute | solution.py:292
  74.9 16.3 %collective-permute-start.4 = (f32[8,136,128]{2,1,0:T(8,128)}, f32[8,136,128]{2,1,0:T(8,128)S(1)}, u32[]{:S(2)}, u32[]{:S(2)}) collective-permute-start(f32[8,136,128]{2,1,0:T(8,128)} %get-tuple-element.38.near_ref), channel_id=1, source_target_pairs={{4,0},{8,4},{12,8},{5,1},{9,5},{13,9},{6,2},{10,6},{14,10},{7,3},{... | collective-permute-start | bytes 1671176 | tf_op jit(solution)/shard_map/ppermute | solution.py:216
  91.2 0.8 copy-start.2
  94.1 15.0 %collective-permute-start.5 = (f32[8,136,128]{2,1,0:T(8,128)}, f32[8,136,128]{2,1,0:T(8,128)S(1)}, u32[]{:S(2)}, u32[]{:S(2)}) collective-permute-start(f32[8,136,128]{2,1,0:T(8,128)} %shard_map.91), channel_id=1, source_target_pairs={{4,0},{8,4},{12,8},{5,1},{9,5},{13,9},{6,2},{10,6},{14,10},{7,3},{... | collective-permute-start | bytes 1671176 | tf_op jit(solution)/shard_map/ppermute | solution.py:216
  109.1 0.8 copy-start

commit v15 on v14

--- a/solution.py
+++ b/solution.py
@@ -36,24 +36,21 @@
     return total.astype(jnp.bfloat16)
 
 
-def state_kernel(block_len, doc_ref, k_ref, v_ref, prefix_ref, pay_ref):
-    count = k_ref.shape[1] // block_len
-    width = k_ref.shape[2]
-    parts = []
-    for n in range(count):
-        rows = pl.ds(n * block_len, block_len)
-        parts.append(
-            lax.dot_general(
-                k_ref[0, rows, :], v_ref[0, rows, :], _ROWS_MAJOR,
-                preferred_element_type=jnp.float32,
-            )
-        )
+def payload_kernel(doc_ref, kv_ref, pay_ref):
+    count = kv_ref.shape[1]
+    width = kv_ref.shape[2]
+    parts = [kv_ref[0, c] for c in range(count)]
+    pay_ref[0, :width, :] = _doc_sum(doc_ref, parts, lambda c: doc_ref[c] == doc_ref[count - 1])
+    pay_ref[0, width:, :] = _doc_row(doc_ref, count - 1, (8, width))
+
+
+def prefix_kernel(doc_ref, kv_ref, prefix_ref):
+    count = kv_ref.shape[1]
+    parts = [kv_ref[0, c] for c in range(count)]
     for b in range(count):
         prefix_ref[0, b] = _doc_sum(
             doc_ref, parts, lambda c: jnp.logical_and(c < b, doc_ref[c] == doc_ref[b])
         )
-    pay_ref[0, :width, :] = _doc_sum(doc_ref, parts, lambda c: doc_ref[c] == doc_ref[count - 1])
-    pay_ref[0, width:, :] = _doc_row(doc_ref, count - 1, (8, width))
 
 
 def combine_kernel(near_ref, far_ref, o_ref):
@@ -254,14 +251,17 @@
     longest_doc = ctx_size * block_count // 2
     reach = (longest_doc - 2) // block_count + 1
 
-    local_prefix, kv_payload = per_head_call(
-        functools.partial(state_kernel, block_len),
-        [(keys, True), (values, True)],
-        [(states, True), (payload, True)],
-        pair_flops // 2,
-        scalars=doc_ids,
-    )
-    prior, intra_part = carry(
+    block_shape = (head_count, block_count, block_len, head_width)
+    key_value_block = jnp.einsum(
+        "hnid,hnie->hnde",
+        keys.reshape(block_shape),
+        values.reshape(block_shape),
+        preferred_element_type=jnp.float32,
+    )
+    (kv_payload,) = per_head_call(
+        payload_kernel, [(key_value_block, True)], [(payload, True)], 0, scalars=doc_ids
+    )
+    prior, (intra_part, local_prefix) = carry(
         kv_payload,
         "ctx",
         False,
@@ -273,7 +273,13 @@
                 [(wide, True)],
                 2 * pair_flops,
             )[0],
-            lambda intra: intra,
+            lambda intra: (
+                intra,
+                per_head_call(
+                    prefix_kernel, [(key_value_block, True)], [(states, True)], 0,
+                    scalars=doc_ids,
+                )[0],
+            ),
         ),
     )
     local_sums, preceding_states = per_head_call(

time: 123 us -> 126 us (1.024)
  waiting for transfers between devices: 26 us -> 19.6 us
  matrix products: 0 us -> 4.91 us
  Pallas kernels: 75.6 us -> 80.2 us
    ppermute x4, waiting for transfers between devices: 22.7 us -> 16.2 us  [shift(): return lax.ppermute(value, axis, pairs)]
    dot_general x0 -> x1, matrix products: none -> 4.91 us  [on_device(): jnp.einsum('hnid,hnie->hnde', keys.reshape(block_shape), values.reshape(b...]
    pallas_call x7 -> x8, Pallas kernels: 71.3 us -> 76 us  [per_head_call(): pl.pallas_call(body, grid_spec=grid_spec, out_shape=[o for o, _ in output...]
  transfers between devices with their start and end apart: 6 -> 6, of which waited for: 6 -> 6; matrix products, arithmetic and copies ran while one was open for 0% -> 0% of each run, Pallas kernels for 24% -> 29%
where the time goes in v15:
time: 126 us; the launch traced here: 124 us
  Pallas kernels  80.2 us (64%)
  waiting for transfers between devices  19.6 us (16%)
  starting transfers between devices  13.4 us (11%)
  local copies, waits for them, and re-layouts  5.66 us (4%)
  matrix products  4.91 us (4%)
    pallas_call x8, Pallas kernels, per_head_call(): pl.pallas_call(body, grid_spec=grid_spec, out_shape=[o for o, _ in output...  76 us
    ppermute x4, waiting for transfers between devices, shift(): return lax.ppermute(value, axis, pairs)  16.2 us
    ppermute x4, starting transfers between devices, shift(): return lax.ppermute(value, axis, pairs)  11.8 us
    dot_general x1, matrix products, on_device(): jnp.einsum('hnid,hnie->hnde', keys.reshape(block_shape), values.reshape(b...  4.91 us
    pallas_call x2, Pallas kernels, combine(): pl.pallas_call(combine_kernel, out_shape=jax.ShapeDtypeStruct(near.shape,...  4.24 us
    ppermute x2, waiting for transfers between devices, on_device(): total_sums = total_sums + lax.ppermute(total_sums, axis, [(0, 1), (1, 0)])  3.36 us
    unnamed x8, local copies, waits for them, and re-layouts  3.22 us
  transfers between devices with their start and end apart: 6, of which 6 were waited for; matrix products, arithmetic and copies ran while one was open for 0% of the time, Pallas kernels for 29%

profile of v15, /device:TPU:0, one launch (start us, length us, event | category | flops | bytes accessed | tf_op | source)
XLA Modules:
  0.0 124.5 jit_solution(13268982519974823465)
XLA Ops:
  0.6 4.9 %fusion.3.refs_1_ = f32[8,5,128,128]{3,2,1,0:T(8,128)} fusion(bf16[8,5,256,128]{3,2,1,0:T(8,128)(2,1)} %bitcast.6, bf16[8,5,256,128]{3,2,1,0:T(8,128)(2,1)} %bitcast.7), kind=kOutput, calls=%fused_computation.6 | convolution fusion | flops 335544320 | bytes 7864320 | tf_op jit(solution)/shard_map/hnid,hnie->hnde/dot_general | solution.py:255
  5.5 6.1 %shard_map.85.near_ref = f32[8,136,128]{2,1,0:T(8,128)} custom-call(s32[5]{0:T(128)} %refs_0_.15, f32[8,5,128,128]{3,2,1,0:T(8,128)} %fusion.3.refs_1_), custom_call_target="tpu_custom_call" | custom-call | bytes 3178496 | tf_op jit(solution)/shard_map/pallas_call | solution.py:182
  11.6 5.0 %collective-permute-start = (f32[8,136,128]{2,1,0:T(8,128)}, f32[8,136,128]{2,1,0:T(8,128)S(1)}, u32[]{:S(2)}, u32[]{:S(2)}) collective-permute-start(f32[8,136,128]{2,1,0:T(8,128)} %shard_map.85.near_ref), channel_id=1, source_target_pairs={{0,4},{4,8},{8,12},{1,5},{5,9},{9,13},{2,6},{6,10},{10,14},{3,7},{... | collective-permute-start | bytes 1671176 | tf_op jit(solution)/shard_map/ppermute | solution.py:213
  16.6 10.2 %shard_map.86.refs_1_.refs_2_ = f32[8,1280,128]{2,1,0:T(8,128)} custom-call(bf16[8,1280,128]{2,1,0:T(8,128)(2,1)} %refs_0_.14, bf16[8,1280,128]{2,1,0:T(8,128)(2,1)} %refs_3_.3, bf16[8,1280,128]{2,1,0:T(8,128)(2,1)} %refs_4_.3), custom_call_target="tpu_custom_call" | custom-call | flops 1342177280 | bytes 13107200 | tf_op jit(solution)/shard_map/pallas_call | solution.py:182
  26.8 2.0 %collective-permute-done.far_ref = f32[8,136,128]{2,1,0:T(8,128)S(1)} collective-permute-done((f32[8,136,128]{2,1,0:T(8,128)}, f32[8,136,128]{2,1,0:T(8,128)S(1)}, u32[]{:S(2)}, u32[]{:S(2)}) %collective-permute-start) | collective-permute-done | bytes 557088 | tf_op jit(solution)/shard_map/ppermute | solution.py:213
  28.7 0.0 copy-start.3
  28.7 0.8 copy-done.3
  29.6 2.1 %shard_map.87 = f32[8,136,128]{2,1,0:T(8,128)} custom-call(f32[8,136,128]{2,1,0:T(8,128)} %shard_map.85.near_ref, f32[8,136,128]{2,1,0:T(8,128)} %copy-done.3), custom_call_target="tpu_custom_call" | custom-call | flops 278528 | bytes 1671168 | tf_op jit(solution)/shard_map/pallas_call | solution.py:195
  31.7 4.3 %collective-permute-start.1 = (f32[8,136,128]{2,1,0:T(8,128)}, f32[8,136,128]{2,1,0:T(8,128)S(1)}, u32[]{:S(2)}, u32[]{:S(2)}) collective-permute-start(f32[8,136,128]{2,1,0:T(8,128)} %shard_map.87), channel_id=1, source_target_pairs={{0,4},{4,8},{8,12},{1,5},{5,9},{9,13},{2,6},{6,10},{10,14},{3,7},{... | collective-permute-start | bytes 1671176 | tf_op jit(solution)/shard_map/ppermute | solution.py:213
  36.0 6.6 %shard_map.88.refs_5_ = f32[8,5,128,128]{3,2,1,0:T(8,128)} custom-call(s32[5]{0:T(128)} %refs_0_.15, f32[8,5,128,128]{3,2,1,0:T(8,128)} %fusion.3.refs_1_), custom_call_target="tpu_custom_call" | custom-call | bytes 5242880 | tf_op jit(solution)/shard_map/pallas_call | solution.py:182
  42.6 4.7 %collective-permute-done.1.refs_6_ = f32[8,136,128]{2,1,0:T(8,128)S(1)} collective-permute-done((f32[8,136,128]{2,1,0:T(8,128)}, f32[8,136,128]{2,1,0:T(8,128)S(1)}, u32[]{:S(2)}, u32[]{:S(2)}) %collective-permute-start.1) | collective-permute-done | bytes 557088 | tf_op jit(solution)/shard_map/ppermute | solution.py:213
  47.3 0.0 copy-start.1
  47.3 0.8 copy-done.1
  48.1 10.8 %shard_map.89 = (f32[1280,2]{1,0:T(8,128)}, bf16[8,5,128,128]{3,2,1,0:T(8,128)(2,1)}) custom-call(s32[5]{0:T(128)} %refs_0_.15, f32[8,1280,128]{2,1,0:T(8,128)} %shard_map.86.refs_1_.refs_2_, bf16[8,1280,128]{2,1,0:T(8,128)(2,1)} %refs_0_.14, bf16[8,1280,128]{2,1,0:T(8,128)(2,1)} %refs_4_.2, f32[8,1,128]{2,1,0:T(1,128)} %bitcast.9, ...), custom_call_target="tpu_custom_call" | custom-call | flops 335544320 | bytes 14989312 | tf_op jit(solution)/shard_map/pallas_call | solution.py:182
  58.8 1.3 %copy.18 = f32[2,1280]{1,0:T(2,128)S(1)} copy(f32[2,1280]{0,1:T(8,128)} %bitcast.8) | data formatting | bytes 20480 | tf_op jit(solution)/shard_map/transpose | solution.py:295
  60.2 0.1 collective-permute-start.2
  60.2 1.2 collective-permute-done.2
  61.4 1.5 %collective-permute-start.3 = (f32[2560]{0:T(1024)S(1)}, f32[2560]{0:T(1024)S(1)}, u32[]{:S(2)}, u32[]{:S(2)}) collective-permute-start(f32[2560]{0:T(1024)S(1)} %add.12), channel_id=1, source_target_pairs={{0,2},{2,0},{1,3},{3,1},{4,6},{6,4},{5,7},{7,5},{8,10},{10,8},{9,1... | collective-permute-start | bytes 30728 | tf_op jit(solution)/shard_map/ppermute | solution.py:298
  62.9 2.2 %collective-permute-done.3 = f32[2560]{0:T(1024)S(1)} collective-permute-done((f32[2560]{0:T(1024)S(1)}, f32[2560]{0:T(1024)S(1)}, u32[]{:S(2)}, u32[]{:S(2)}) %collective-permute-start.3) | collective-permute-done | bytes 10272 | tf_op jit(solution)/shard_map/ppermute | solution.py:298
  65.2 1.1 copy.19.refs_6_
  66.3 11.6 %shard_map.90 = (bf16[8,1280,128]{2,1,0:T(8,128)(2,1)}, f32[8,5,128,128]{3,2,1,0:T(8,128)}, f32[8,136,128]{2,1,0:T(8,128)}) custom-call(s32[5]{0:T(128)} %refs_0_.15, bf16[8,1280,128]{2,1,0:T(8,128)(2,1)} %refs_0_.14, f32[8,1280,128]{2,1,0:T(8,128)} %shard_map.86.refs_1_.refs_2_, bf16[8,5,128,128]{3,2,1,0:T(8,128)(2,1)} %get-tuple-element.34.refs_3_.refs_4_, ...), custom_call_target="tpu_custom_call" | custom-call | flops 335544320 | bytes 17610752 | tf_op jit(solution)/shard_map/pallas_call | solution.py:182
  77.9 1.3 %collective-permute-start.4 = (f32[8,136,128]{2,1,0:T(8,128)}, f32[8,136,128]{2,1,0:T(8,128)S(1)}, u32[]{:S(2)}, u32[]{:S(2)}) collective-permute-start(f32[8,136,128]{2,1,0:T(8,128)} %get-tuple-element.36.near_ref), channel_id=1, source_target_pairs={{4,0},{8,4},{12,8},{5,1},{9,5},{13,9},{6,2},{10,6},{14,10},{7,3},{... | collective-permute-start | bytes 1671176 | tf_op jit(solution)/shard_map/ppermute | solution.py:213
  79.2 9.6 %shard_map.91 = (bf16[8,1280,128]{2,1,0:T(8,128)(2,1)}, f32[8,1280,128]{2,1,0:T(8,128)}, f32[8,1280,128]{2,1,0:T(8,128)}) custom-call(bf16[8,1280,128]{2,1,0:T(8,128)(2,1)} %refs_0_.14, bf16[8,1280,128]{2,1,0:T(8,128)(2,1)} %refs_3_.3, bf16[8,1280,128]{2,1,0:T(8,128)(2,1)} %refs_4_.3, bf16[8,1280,128]{2,1,0:T(8,128)(2,1)} %get-tuple-element.37.refs_3_, ...), custom_call_target="tpu_custom_call" | custom-call | flops 1677721600 | bytes 12451840 | tf_op jit(solution)/shard_map/pallas_call | solution.py:182
  88.7 5.4 %collective-permute-done.4.far_ref = f32[8,136,128]{2,1,0:T(8,128)S(1)} collective-permute-done((f32[8,136,128]{2,1,0:T(8,128)}, f32[8,136,128]{2,1,0:T(8,128)S(1)}, u32[]{:S(2)}, u32[]{:S(2)}) %collective-permute-start.4) | collective-permute-done | bytes 557088 | tf_op jit(solution)/shard_map/ppermute | solution.py:213
  94.2 0.0 copy-start.2
  94.2 0.8 copy-done.2
  95.0 2.1 %shard_map.92 = f32[8,136,128]{2,1,0:T(8,128)} custom-call(f32[8,136,128]{2,1,0:T(8,128)} %get-tuple-element.36.near_ref, f32[8,136,128]{2,1,0:T(8,128)} %copy-done.2), custom_call_target="tpu_custom_call" | custom-call | flops 278528 | bytes 1671168 | tf_op jit(solution)/shard_map/pallas_call | solution.py:195
  97.1 1.3 %collective-permute-start.5 = (f32[8,136,128]{2,1,0:T(8,128)}, f32[8,136,128]{2,1,0:T(8,128)S(1)}, u32[]{:S(2)}, u32[]{:S(2)}) collective-permute-start(f32[8,136,128]{2,1,0:T(8,128)} %shard_map.92), channel_id=1, source_target_pairs={{4,0},{8,4},{12,8},{5,1},{9,5},{13,9},{6,2},{10,6},{14,10},{7,3},{... | collective-permute-start | bytes 1671176 | tf_op jit(solution)/shard_map/ppermute | solution.py:213
  98.4 9.6 %shard_map.93 = (bf16[8,1280,128]{2,1,0:T(8,128)(2,1)}, f32[8,1280,128]{2,1,0:T(8,128)}, f32[8,1280,128]{2,1,0:T(8,128)}) custom-call(bf16[8,1280,128]{2,1,0:T(8,128)(2,1)} %refs_0_.14, bf16[8,1280,128]{2,1,0:T(8,128)(2,1)} %refs_3_.3, bf16[8,1280,128]{2,1,0:T(8,128)(2,1)} %refs_4_.3, ...), custom_call_target="tpu_custom_call", output_to_operand_aliasing={{0}: (5, {}), {1}: (6, {}), {2}: (7, {})} | custom-call | flops 1677721600 | bytes 12451840 | tf_op jit(solution)/shard_map/pallas_call | solution.py:182
  107.9 4.1 %collective-permute-done.5.refs_6_ = f32[8,136,128]{2,1,0:T(8,128)S(1)} collective-permute-done((f32[8,136,128]{2,1,0:T(8,128)}, f32[8,136,128]{2,1,0:T(8,128)S(1)}, u32[]{:S(2)}, u32[]{:S(2)}) %collective-permute-start.5) | collective-permute-done | bytes 557088 | tf_op jit(solution)/shard_map/ppermute | solution.py:213
  112.1 0.0 copy-start
  112.1 0.8 copy-done
  112.9 11.6 %shard_map.94 = (bf16[8,1280,128]{2,1,0:T(8,128)(2,1)}, bf16[8,1280,128]{2,1,0:T(8,128)(2,1)}) custom-call(s32[5]{0:T(128)} %refs_0_.15, f32[8,1280,128]{2,1,0:T(8,128)} %get-tuple-element.49.refs_1_, f32[8,1280,128]{2,1,0:T(8,128)} %get-tuple-element.50.refs_2_, bf16[8,1280,128]{2,1,0:T(8,128)(2,1)} %refs_3_.3, bf16[8,1280,128]{2,1,0:T(8,128)(2,1)} %refs_4_.3, ...), custom_call_target="tpu_custom_call" | custom-call | flops 671088640 | bytes 24150016 | tf_op jit(solution)/shard_map/pallas_call | solution.py:182
  (7 shorter events, 0.1 us)
Async XLA Ops:
  11.6 17.1 %collective-permute-start = (f32[8,136,128]{2,1,0:T(8,128)}, f32[8,136,128]{2,1,0:T(8,128)S(1)}, u32[]{:S(2)}, u32[]{:S(2)}) collective-permute-start(f32[8,136,128]{2,1,0:T(8,128)} %shard_map.85.near_ref), channel_id=1, source_target_pairs={{0,4},{4,8},{8,12},{1,5},{5,9},{9,13},{2,6},{6,10},{10,14},{3,7},{... | collective-permute-start | bytes 1671176 | tf_op jit(solution)/shard_map/ppermute | solution.py:213
  28.7 0.8 copy-start.3
  31.7 15.6 %collective-permute-start.1 = (f32[8,136,128]{2,1,0:T(8,128)}, f32[8,136,128]{2,1,0:T(8,128)S(1)}, u32[]{:S(2)}, u32[]{:S(2)}) collective-permute-start(f32[8,136,128]{2,1,0:T(8,128)} %shard_map.87), channel_id=1, source_target_pairs={{0,4},{4,8},{8,12},{1,5},{5,9},{9,13},{2,6},{6,10},{10,14},{3,7},{... | collective-permute-start | bytes 1671176 | tf_op jit(solution)/shard_map/ppermute | solution.py:213
  47.3 0.8 copy-start.1
  60.2 1.2 collective-permute-start.2
  61.4 3.7 %collective-permute-start.3 = (f32[2560]{0:T(1024)S(1)}, f32[2560]{0:T(1024)S(1)}, u32[]{:S(2)}, u32[]{:S(2)}) collective-permute-start(f32[2560]{0:T(1024)S(1)} %add.12), channel_id=1, source_target_pairs={{0,2},{2,0},{1,3},{3,1},{4,6},{6,4},{5,7},{7,5},{8,10},{10,8},{9,1... | collective-permute-start | bytes 30728 | tf_op jit(solution)/shard_map/ppermute | solution.py:298
  77.9 16.3 %collective-permute-start.4 = (f32[8,136,128]{2,1,0:T(8,128)}, f32[8,136,128]{2,1,0:T(8,128)S(1)}, u32[]{:S(2)}, u32[]{:S(2)}) collective-permute-start(f32[8,136,128]{2,1,0:T(8,128)} %get-tuple-element.36.near_ref), channel_id=1, source_target_pairs={{4,0},{8,4},{12,8},{5,1},{9,5},{13,9},{6,2},{10,6},{14,10},{7,3},{... | collective-permute-start | bytes 1671176 | tf_op jit(solution)/shard_map/ppermute | solution.py:213
  94.2 0.8 copy-start.2
  97.1 15.0 %collective-permute-start.5 = (f32[8,136,128]{2,1,0:T(8,128)}, f32[8,136,128]{2,1,0:T(8,128)S(1)}, u32[]{:S(2)}, u32[]{:S(2)}) collective-permute-start(f32[8,136,128]{2,1,0:T(8,128)} %shard_map.92), channel_id=1, source_target_pairs={{4,0},{8,4},{12,8},{5,1},{9,5},{13,9},{6,2},{10,6},{14,10},{7,3},{... | collective-permute-start | bytes 1671176 | tf_op jit(solution)/shard_map/ppermute | solution.py:213
  112.1 0.8 copy-start

commit v16 on v14

--- a/solution.py
+++ b/solution.py
@@ -29,31 +29,32 @@
     return jnp.full(shape, doc_ref[n].astype(jnp.float32) + 1.0, jnp.float32)
 
 
-def _carried(state_ref, doc_ref, n, carry_ref):
+def _carried(state_ref, doc_ref, n, carry_ref, j):
     width = carry_ref.shape[2]
-    joined = carry_ref[0, width : width + 1, :] == doc_ref[n].astype(jnp.float32) + 1.0
-    total = state_ref[0, n] + jnp.where(joined, carry_ref[0, :width, :], 0.0)
+    joined = carry_ref[j, width : width + 1, :] == doc_ref[n].astype(jnp.float32) + 1.0
+    total = state_ref[j, n] + jnp.where(joined, carry_ref[j, :width, :], 0.0)
     return total.astype(jnp.bfloat16)
 
 
 def state_kernel(block_len, doc_ref, k_ref, v_ref, prefix_ref, pay_ref):
-    count = k_ref.shape[1] // block_len
-    width = k_ref.shape[2]
-    parts = []
-    for n in range(count):
-        rows = pl.ds(n * block_len, block_len)
-        parts.append(
-            lax.dot_general(
-                k_ref[0, rows, :], v_ref[0, rows, :], _ROWS_MAJOR,
-                preferred_element_type=jnp.float32,
-            )
-        )
-    for b in range(count):
-        prefix_ref[0, b] = _doc_sum(
-            doc_ref, parts, lambda c: jnp.logical_and(c < b, doc_ref[c] == doc_ref[b])
-        )
-    pay_ref[0, :width, :] = _doc_sum(doc_ref, parts, lambda c: doc_ref[c] == doc_ref[count - 1])
-    pay_ref[0, width:, :] = _doc_row(doc_ref, count - 1, (8, width))
+    for j in range(k_ref.shape[0]):
+        count = k_ref.shape[1] // block_len
+        width = k_ref.shape[2]
+        parts = []
+        for n in range(count):
+            rows = pl.ds(n * block_len, block_len)
+            parts.append(
+                lax.dot_general(
+                    k_ref[j, rows, :], v_ref[j, rows, :], _ROWS_MAJOR,
+                    preferred_element_type=jnp.float32,
+                )
+            )
+        for b in range(count):
+            prefix_ref[j, b] = _doc_sum(
+                doc_ref, parts, lambda c: jnp.logical_and(c < b, doc_ref[c] == doc_ref[b])
+            )
+        pay_ref[j, :width, :] = _doc_sum(doc_ref, parts, lambda c: doc_ref[c] == doc_ref[count - 1])
+        pay_ref[j, width:, :] = _doc_row(doc_ref, count - 1, (8, width))
 
 
 def combine_kernel(near_ref, far_ref, o_ref):
@@ -67,13 +68,14 @@
 
 
 def intra_kernel(block_len, q_ref, k_ref, v_ref, o_ref):
-    causal = _causal(block_len)
-    for n in range(q_ref.shape[1] // block_len):
-        rows = pl.ds(n * block_len, block_len)
-        q, k, v = q_ref[0, rows, :], k_ref[0, rows, :], v_ref[0, rows, :]
-        scores = lax.dot_general(q, k, _ROWS_MINOR, preferred_element_type=jnp.float32)
-        probs = jnp.where(causal, scores, 0.0).astype(jnp.bfloat16)
-        o_ref[0, rows, :] = jnp.dot(probs, v, preferred_element_type=jnp.float32)
+    for j in range(q_ref.shape[0]):
+        causal = _causal(block_len)
+        for n in range(q_ref.shape[1] // block_len):
+            rows = pl.ds(n * block_len, block_len)
+            q, k, v = q_ref[j, rows, :], k_ref[j, rows, :], v_ref[j, rows, :]
+            scores = lax.dot_general(q, k, _ROWS_MINOR, preferred_element_type=jnp.float32)
+            probs = jnp.where(causal, scores, 0.0).astype(jnp.bfloat16)
+            o_ref[j, rows, :] = jnp.dot(probs, v, preferred_element_type=jnp.float32)
 
 
 def forward_kernel(
@@ -83,89 +85,96 @@
     def _():
         o_ref[...] = jnp.zeros_like(o_ref)
 
-    for n in range(q_ref.shape[1] // block_len):
-        rows = pl.ds(n * block_len, block_len)
-        state = _carried(prefix_ref, doc_ref, n, carry_ref)
-        s_ref[0, n] = state
-        raw = i_ref[0, rows, :] + jnp.dot(
-            q_ref[0, rows, :], state, preferred_element_type=jnp.float32
-        )
-        scaled = n_ref[0] * g_ref[0, rows, :].astype(jnp.float32)
-        o_ref[rows, 0:1] += jnp.sum(raw * raw, axis=1, keepdims=True)
-        o_ref[rows, 1:2] += jnp.sum(scaled * raw, axis=1, keepdims=True)
+    for j in range(q_ref.shape[0]):
+        for n in range(q_ref.shape[1] // block_len):
+            rows = pl.ds(n * block_len, block_len)
+            state = _carried(prefix_ref, doc_ref, n, carry_ref, j)
+            s_ref[j, n] = state
+            raw = i_ref[j, rows, :] + jnp.dot(
+                q_ref[j, rows, :], state, preferred_element_type=jnp.float32
+            )
+            scaled = n_ref[j] * g_ref[j, rows, :].astype(jnp.float32)
+            o_ref[rows, 0:1] += jnp.sum(raw * raw, axis=1, keepdims=True)
+            o_ref[rows, 1:2] += jnp.sum(scaled * raw, axis=1, keepdims=True)
 
 
 def grad_kernel(
     block_len, doc_ref, q_ref, i_ref, s_ref, g_ref, n_ref, c_ref, d_ref, suffix_ref, pay_ref
 ):
-    count = q_ref.shape[1] // block_len
-    width = q_ref.shape[2]
-    parts = []
-    for n in range(count):
-        rows = pl.ds(n * block_len, block_len)
-        q = q_ref[0, rows, :]
-        raw = i_ref[0, rows, :] + jnp.dot(q, s_ref[0, n], preferred_element_type=jnp.float32)
-        scaled = n_ref[0] * g_ref[0, rows, :].astype(jnp.float32)
-        root_mean = c_ref[rows, 0:1]
-        factor = c_ref[rows, 1:2]
-        d = ((scaled - raw * factor) / root_mean).astype(jnp.bfloat16)
-        d_ref[0, rows, :] = d
-        parts.append(lax.dot_general(q, d, _ROWS_MAJOR, preferred_element_type=jnp.float32))
-    for b in range(count):
-        suffix_ref[0, b] = _doc_sum(
-            doc_ref, parts, lambda c: jnp.logical_and(c > b, doc_ref[c] == doc_ref[b])
-        )
-    pay_ref[0, :width, :] = _doc_sum(doc_ref, parts, lambda c: doc_ref[c] == doc_ref[0])
-    pay_ref[0, width:, :] = _doc_row(doc_ref, 0, (8, width))
+    for j in range(q_ref.shape[0]):
+        count = q_ref.shape[1] // block_len
+        width = q_ref.shape[2]
+        parts = []
+        for n in range(count):
+            rows = pl.ds(n * block_len, block_len)
+            q = q_ref[j, rows, :]
+            raw = i_ref[j, rows, :] + jnp.dot(q, s_ref[j, n], preferred_element_type=jnp.float32)
+            scaled = n_ref[j] * g_ref[j, rows, :].astype(jnp.float32)
+            root_mean = c_ref[rows, 0:1]
+            factor = c_ref[rows, 1:2]
+            d = ((scaled - raw * factor) / root_mean).astype(jnp.bfloat16)
+            d_ref[j, rows, :] = d
+            parts.append(lax.dot_general(q, d, _ROWS_MAJOR, preferred_element_type=jnp.float32))
+        for b in range(count):
+            suffix_ref[j, b] = _doc_sum(
+                doc_ref, parts, lambda c: jnp.logical_and(c > b, doc_ref[c] == doc_ref[b])
+            )
+        pay_ref[j, :width, :] = _doc_sum(doc_ref, parts, lambda c: doc_ref[c] == doc_ref[0])
+        pay_ref[j, width:, :] = _doc_row(doc_ref, 0, (8, width))
 
 
 def query_grad_kernel(block_len, q_ref, k_ref, v_ref, d_ref, s_ref, dq_ref, dk_ref, dv_ref):
-    causal = _causal(block_len)
-    for n in range(k_ref.shape[1] // block_len):
-        rows = pl.ds(n * block_len, block_len)
-        q, k, v = q_ref[0, rows, :], k_ref[0, rows, :], v_ref[0, rows, :]
-        d = d_ref[0, rows, :]
-        scores = lax.dot_general(q, k, _ROWS_MINOR, preferred_element_type=jnp.float32)
-        probs = jnp.where(causal, scores, 0.0).astype(jnp.bfloat16)
-        grad_scores = lax.dot_general(d, v, _ROWS_MINOR, preferred_element_type=jnp.float32)
-        grad_probs = jnp.where(causal, grad_scores, 0.0).astype(jnp.bfloat16)
-        dq = jnp.dot(grad_probs, k, preferred_element_type=jnp.float32)
-        dq = dq + lax.dot_general(d, s_ref[0, n], _ROWS_MINOR, preferred_element_type=jnp.float32)
-        dq_ref[0, rows, :] = dq.astype(dq_ref.dtype)
-        dk_ref[0, rows, :] = lax.dot_general(
-            grad_probs, q, _ROWS_MAJOR, preferred_element_type=jnp.float32
-        )
-        dv_ref[0, rows, :] = lax.dot_general(
-            probs, d, _ROWS_MAJOR, preferred_element_type=jnp.float32
-        )
+    for j in range(q_ref.shape[0]):
+        causal = _causal(block_len)
+        for n in range(k_ref.shape[1] // block_len):
+            rows = pl.ds(n * block_len, block_len)
+            q, k, v = q_ref[j, rows, :], k_ref[j, rows, :], v_ref[j, rows, :]
+            d = d_ref[j, rows, :]
+            scores = lax.dot_general(q, k, _ROWS_MINOR, preferred_element_type=jnp.float32)
+            probs = jnp.where(causal, scores, 0.0).astype(jnp.bfloat16)
+            grad_scores = lax.dot_general(d, v, _ROWS_MINOR, preferred_element_type=jnp.float32)
+            grad_probs = jnp.where(causal, grad_scores, 0.0).astype(jnp.bfloat16)
+            dq = jnp.dot(grad_probs, k, preferred_element_type=jnp.float32)
+            dq = dq + lax.dot_general(d, s_ref[j, n], _ROWS_MINOR, preferred_element_type=jnp.float32)
+            dq_ref[j, rows, :] = dq.astype(dq_ref.dtype)
+            dk_ref[j, rows, :] = lax.dot_general(
+                grad_probs, q, _ROWS_MAJOR, preferred_element_type=jnp.float32
+            )
+            dv_ref[j, rows, :] = lax.dot_general(
+                probs, d, _ROWS_MAJOR, preferred_element_type=jnp.float32
+            )
 
 
 def key_value_grad_kernel(
     block_len, doc_ref, ik_ref, iv_ref, k_ref, v_ref, suffix_ref, carry_ref, dk_ref, dv_ref
 ):
-    for n in range(k_ref.shape[1] // block_len):
-        rows = pl.ds(n * block_len, block_len)
-        state = _carried(suffix_ref, doc_ref, n, carry_ref)
-        dk = ik_ref[0, rows, :] + lax.dot_general(
-            v_ref[0, rows, :], state, _ROWS_MINOR, preferred_element_type=jnp.float32
-        )
-        dv = iv_ref[0, rows, :] + jnp.dot(
-            k_ref[0, rows, :], state, preferred_element_type=jnp.float32
-        )
-        dk_ref[0, rows, :] = dk.astype(dk_ref.dtype)
-        dv_ref[0, rows, :] = dv.astype(dv_ref.dtype)
+    for j in range(ik_ref.shape[0]):
+        for n in range(k_ref.shape[1] // block_len):
+            rows = pl.ds(n * block_len, block_len)
+            state = _carried(suffix_ref, doc_ref, n, carry_ref, j)
+            dk = ik_ref[j, rows, :] + lax.dot_general(
+                v_ref[j, rows, :], state, _ROWS_MINOR, preferred_element_type=jnp.float32
+            )
+            dv = iv_ref[j, rows, :] + jnp.dot(
+                k_ref[j, rows, :], state, preferred_element_type=jnp.float32
+            )
+            dk_ref[j, rows, :] = dk.astype(dk_ref.dtype)
+            dv_ref[j, rows, :] = dv.astype(dv_ref.dtype)
 
 
 def per_head_call(kernel, inputs, outputs, flops, heads=None, into=(), scalars=None):
+    head_count = inputs[0][0].shape[0]
+    first, count = heads if heads is not None else (0, head_count)
+    group = math.gcd(math.gcd(first, count), 2)
+
     def spec(shape, per_head, first):
         if per_head:
             return pl.BlockSpec(
-                (1,) + shape[1:], lambda h, *_: (h + first,) + (0,) * (len(shape) - 1)
+                (group,) + shape[1:],
+                lambda h, *_: (h + first // group,) + (0,) * (len(shape) - 1),
             )
         return pl.BlockSpec(shape, lambda h, *_: (0,) * len(shape))
 
-    head_count = inputs[0][0].shape[0]
-    first, count = heads if heads is not None else (0, head_count)
     share = count / head_count
     in_bytes = sum(x.size * x.dtype.itemsize for x, _ in inputs) * share
     out_bytes = sum(math.prod(o.shape) * o.dtype.itemsize for o, _ in outputs) * share
@@ -177,7 +186,7 @@
 
     grid_spec = pltpu.PrefetchScalarGridSpec(
         num_scalar_prefetch=lead,
-        grid=(count,),
+        grid=(count // group,),
         in_specs=[spec(x.shape, h, first) for x, h in inputs]
         + [pl.BlockSpec(memory_space=pl.ANY) for _ in into],
         out_specs=[spec(o.shape, h, first) for o, h in outputs],

time: 123 us -> 115 us (0.935)
  Pallas kernels: 75.6 us -> 67.2 us
  waiting for transfers between devices: 26 us -> 27.4 us
    pallas_call x7, Pallas kernels: 71.3 us -> 62.9 us  [per_head_call(): pl.pallas_call(body, grid_spec=grid_spec, out_shape=[o for o, _ in output...]
    ppermute x4, waiting for transfers between devices: 22.7 us -> 24.1 us  [shift(): return lax.ppermute(value, axis, pairs)]
  transfers between devices with their start and end apart: 6 -> 6, of which waited for: 6 -> 6; matrix products, arithmetic and copies ran while one was open for 0% -> 0% of each run, Pallas kernels for 24% -> 25%
where the time goes in v16:
time: 115 us; the launch traced here: 114 us
  Pallas kernels  67.2 us (58%)
  waiting for transfers between devices  27.4 us (24%)
  starting transfers between devices  13.4 us (12%)
  local copies, waits for them, and re-layouts  5.71 us (5%)
    pallas_call x7, Pallas kernels, per_head_call(): pl.pallas_call(body, grid_spec=grid_spec, out_shape=[o for o, _ in output...  62.9 us
    ppermute x4, waiting for transfers between devices, shift(): return lax.ppermute(value, axis, pairs)  24.1 us
    ppermute x4, starting transfers between devices, shift(): return lax.ppermute(value, axis, pairs)  11.8 us
    pallas_call x2, Pallas kernels, combine(): pl.pallas_call(combine_kernel, out_shape=jax.ShapeDtypeStruct(near.shape,...  4.22 us
    ppermute x2, waiting for transfers between devices, on_device(): total_sums = total_sums + lax.ppermute(total_sums, axis, [(0, 1), (1, 0)])  3.37 us
    unnamed x8, local copies, waits for them, and re-layouts  3.28 us
  transfers between devices with their start and end apart: 6, of which 6 were waited for; matrix products, arithmetic and copies ran while one was open for 0% of the time, Pallas kernels for 25%

profile of v16, /device:TPU:0, one launch (start us, length us, event | category | flops | bytes accessed | tf_op | source)
XLA Modules:
  0.0 114.4 jit_solution(5166833078353312264)
XLA Ops:
  0.6 5.9 %shard_map.85 = (f32[8,5,128,128]{3,2,1,0:T(8,128)}, f32[8,136,128]{2,1,0:T(8,128)}) custom-call(s32[5]{0:T(128)} %refs_0_.13, bf16[8,1280,128]{2,1,0:T(8,128)(2,1)} %refs_3_.3, bf16[8,1280,128]{2,1,0:T(8,128)(2,1)} %refs_4_.3), custom_call_target="tpu_custom_call" | custom-call | flops 335544320 | bytes 8421376 | tf_op jit(solution)/shard_map/pallas_call | solution.py:194
  6.5 4.9 %collective-permute-start = (f32[8,136,128]{2,1,0:T(8,128)}, f32[8,136,128]{2,1,0:T(8,128)S(1)}, u32[]{:S(2)}, u32[]{:S(2)}) collective-permute-start(f32[8,136,128]{2,1,0:T(8,128)} %get-tuple-element.30.near_ref), channel_id=1, source_target_pairs={{0,4},{4,8},{8,12},{1,5},{5,9},{9,13},{2,6},{6,10},{10,14},{3,7},{... | collective-permute-start | bytes 1671176 | tf_op jit(solution)/shard_map/ppermute | solution.py:225
  11.5 7.9 %shard_map.86.refs_1_.refs_2_ = f32[8,1280,128]{2,1,0:T(8,128)} custom-call(bf16[8,1280,128]{2,1,0:T(8,128)(2,1)} %refs_0_.12, bf16[8,1280,128]{2,1,0:T(8,128)(2,1)} %refs_3_.3, bf16[8,1280,128]{2,1,0:T(8,128)(2,1)} %refs_4_.3), custom_call_target="tpu_custom_call" | custom-call | flops 1342177280 | bytes 13107200 | tf_op jit(solution)/shard_map/pallas_call | solution.py:194
  19.4 4.2 %collective-permute-done.far_ref = f32[8,136,128]{2,1,0:T(8,128)S(1)} collective-permute-done((f32[8,136,128]{2,1,0:T(8,128)}, f32[8,136,128]{2,1,0:T(8,128)S(1)}, u32[]{:S(2)}, u32[]{:S(2)}) %collective-permute-start) | collective-permute-done | bytes 557088 | tf_op jit(solution)/shard_map/ppermute | solution.py:225
  23.6 0.0 copy-start.3
  23.6 0.8 copy-done.3
  24.4 2.1 %shard_map.87 = f32[8,136,128]{2,1,0:T(8,128)} custom-call(f32[8,136,128]{2,1,0:T(8,128)} %get-tuple-element.30.near_ref, f32[8,136,128]{2,1,0:T(8,128)} %copy-done.3), custom_call_target="tpu_custom_call" | custom-call | flops 278528 | bytes 1671168 | tf_op jit(solution)/shard_map/pallas_call | solution.py:207
  26.6 4.3 %collective-permute-start.1 = (f32[8,136,128]{2,1,0:T(8,128)}, f32[8,136,128]{2,1,0:T(8,128)S(1)}, u32[]{:S(2)}, u32[]{:S(2)}) collective-permute-start(f32[8,136,128]{2,1,0:T(8,128)} %shard_map.87), channel_id=1, source_target_pairs={{0,4},{4,8},{8,12},{1,5},{5,9},{9,13},{2,6},{6,10},{10,14},{3,7},{... | collective-permute-start | bytes 1671176 | tf_op jit(solution)/shard_map/ppermute | solution.py:225
  30.9 11.3 %collective-permute-done.1.refs_6_ = f32[8,136,128]{2,1,0:T(8,128)S(1)} collective-permute-done((f32[8,136,128]{2,1,0:T(8,128)}, f32[8,136,128]{2,1,0:T(8,128)S(1)}, u32[]{:S(2)}, u32[]{:S(2)}) %collective-permute-start.1) | collective-permute-done | bytes 557088 | tf_op jit(solution)/shard_map/ppermute | solution.py:225
  42.1 0.0 copy-start.1
  42.1 0.8 copy-done.1
  43.0 8.7 %shard_map.88 = (f32[1280,2]{1,0:T(8,128)}, bf16[8,5,128,128]{3,2,1,0:T(8,128)(2,1)}) custom-call(s32[5]{0:T(128)} %refs_0_.13, f32[8,1280,128]{2,1,0:T(8,128)} %shard_map.86.refs_1_.refs_2_, bf16[8,1280,128]{2,1,0:T(8,128)(2,1)} %refs_0_.12, bf16[8,1280,128]{2,1,0:T(8,128)(2,1)} %refs_4_.2, f32[8,1,128]{2,1,0:T(1,128)} %bitcast.3, ...), custom_call_target="tpu_custom_call" | custom-call | flops 335544320 | bytes 14989312 | tf_op jit(solution)/shard_map/pallas_call | solution.py:194
  51.7 1.3 %copy.15 = f32[2,1280]{1,0:T(2,128)S(1)} copy(f32[2,1280]{0,1:T(8,128)} %bitcast.2) | data formatting | bytes 20480 | tf_op jit(solution)/shard_map/transpose | solution.py:298
  53.0 0.1 collective-permute-start.2
  53.1 1.2 %collective-permute-done.2 = f32[2560]{0:T(1024)S(1)} collective-permute-done((f32[2560]{0:T(1024)S(1)}, f32[2560]{0:T(1024)S(1)}, u32[]{:S(2)}, u32[]{:S(2)}) %collective-permute-start.2) | collective-permute-done | bytes 10272 | tf_op jit(solution)/shard_map/ppermute | solution.py:301
  54.3 1.5 %collective-permute-start.3 = (f32[2560]{0:T(1024)S(1)}, f32[2560]{0:T(1024)S(1)}, u32[]{:S(2)}, u32[]{:S(2)}) collective-permute-start(f32[2560]{0:T(1024)S(1)} %add.12), channel_id=1, source_target_pairs={{0,2},{2,0},{1,3},{3,1},{4,6},{6,4},{5,7},{7,5},{8,10},{10,8},{9,1... | collective-permute-start | bytes 30728 | tf_op jit(solution)/shard_map/ppermute | solution.py:301
  55.8 2.2 %collective-permute-done.3 = f32[2560]{0:T(1024)S(1)} collective-permute-done((f32[2560]{0:T(1024)S(1)}, f32[2560]{0:T(1024)S(1)}, u32[]{:S(2)}, u32[]{:S(2)}) %collective-permute-start.3) | collective-permute-done | bytes 10272 | tf_op jit(solution)/shard_map/ppermute | solution.py:301
  58.1 1.1 copy.16.refs_6_
  59.2 10.5 %shard_map.89 = (bf16[8,1280,128]{2,1,0:T(8,128)(2,1)}, f32[8,5,128,128]{3,2,1,0:T(8,128)}, f32[8,136,128]{2,1,0:T(8,128)}) custom-call(s32[5]{0:T(128)} %refs_0_.13, bf16[8,1280,128]{2,1,0:T(8,128)(2,1)} %refs_0_.12, f32[8,1280,128]{2,1,0:T(8,128)} %shard_map.86.refs_1_.refs_2_, bf16[8,5,128,128]{3,2,1,0:T(8,128)(2,1)} %get-tuple-element.36.refs_3_.refs_4_, ...), custom_call_target="tpu_custom_call" | custom-call | flops 335544320 | bytes 17610752 | tf_op jit(solution)/shard_map/pallas_call | solution.py:194
  69.7 1.3 %collective-permute-start.4 = (f32[8,136,128]{2,1,0:T(8,128)}, f32[8,136,128]{2,1,0:T(8,128)S(1)}, u32[]{:S(2)}, u32[]{:S(2)}) collective-permute-start(f32[8,136,128]{2,1,0:T(8,128)} %get-tuple-element.38.near_ref), channel_id=1, source_target_pairs={{4,0},{8,4},{12,8},{5,1},{9,5},{13,9},{6,2},{10,6},{14,10},{7,3},{... | collective-permute-start | bytes 1671176 | tf_op jit(solution)/shard_map/ppermute | solution.py:225
  71.0 10.1 %shard_map.90 = (bf16[8,1280,128]{2,1,0:T(8,128)(2,1)}, f32[8,1280,128]{2,1,0:T(8,128)}, f32[8,1280,128]{2,1,0:T(8,128)}) custom-call(bf16[8,1280,128]{2,1,0:T(8,128)(2,1)} %refs_0_.12, bf16[8,1280,128]{2,1,0:T(8,128)(2,1)} %refs_3_.3, bf16[8,1280,128]{2,1,0:T(8,128)(2,1)} %refs_4_.3, bf16[8,1280,128]{2,1,0:T(8,128)(2,1)} %get-tuple-element.39.refs_3_, ...), custom_call_target="tpu_custom_call" | custom-call | flops 1677721600 | bytes 12451840 | tf_op jit(solution)/shard_map/pallas_call | solution.py:194
  81.1 4.9 %collective-permute-done.4.far_ref = f32[8,136,128]{2,1,0:T(8,128)S(1)} collective-permute-done((f32[8,136,128]{2,1,0:T(8,128)}, f32[8,136,128]{2,1,0:T(8,128)S(1)}, u32[]{:S(2)}, u32[]{:S(2)}) %collective-permute-start.4) | collective-permute-done | bytes 557088 | tf_op jit(solution)/shard_map/ppermute | solution.py:225
  86.0 0.0 copy-start.2
  86.0 0.8 copy-done.2
  86.8 2.1 %shard_map.91 = f32[8,136,128]{2,1,0:T(8,128)} custom-call(f32[8,136,128]{2,1,0:T(8,128)} %get-tuple-element.38.near_ref, f32[8,136,128]{2,1,0:T(8,128)} %copy-done.2), custom_call_target="tpu_custom_call" | custom-call | flops 278528 | bytes 1671168 | tf_op jit(solution)/shard_map/pallas_call | solution.py:207
  88.9 1.3 %collective-permute-start.5 = (f32[8,136,128]{2,1,0:T(8,128)}, f32[8,136,128]{2,1,0:T(8,128)S(1)}, u32[]{:S(2)}, u32[]{:S(2)}) collective-permute-start(f32[8,136,128]{2,1,0:T(8,128)} %shard_map.91), channel_id=1, source_target_pairs={{4,0},{8,4},{12,8},{5,1},{9,5},{13,9},{6,2},{10,6},{14,10},{7,3},{... | collective-permute-start | bytes 1671176 | tf_op jit(solution)/shard_map/ppermute | solution.py:225
  90.2 10.1 %shard_map.92 = (bf16[8,1280,128]{2,1,0:T(8,128)(2,1)}, f32[8,1280,128]{2,1,0:T(8,128)}, f32[8,1280,128]{2,1,0:T(8,128)}) custom-call(bf16[8,1280,128]{2,1,0:T(8,128)(2,1)} %refs_0_.12, bf16[8,1280,128]{2,1,0:T(8,128)(2,1)} %refs_3_.3, bf16[8,1280,128]{2,1,0:T(8,128)(2,1)} %refs_4_.3, ...), custom_call_target="tpu_custom_call", output_to_operand_aliasing={{0}: (5, {}), {1}: (6, {}), {2}: (7, {})} | custom-call | flops 1677721600 | bytes 12451840 | tf_op jit(solution)/shard_map/pallas_call | solution.py:194
  100.3 3.6 %collective-permute-done.5.refs_6_ = f32[8,136,128]{2,1,0:T(8,128)S(1)} collective-permute-done((f32[8,136,128]{2,1,0:T(8,128)}, f32[8,136,128]{2,1,0:T(8,128)S(1)}, u32[]{:S(2)}, u32[]{:S(2)}) %collective-permute-start.5) | collective-permute-done | bytes 557088 | tf_op jit(solution)/shard_map/ppermute | solution.py:225
  103.9 0.0 copy-start
  103.9 0.8 copy-done
  104.7 9.7 %shard_map.93 = (bf16[8,1280,128]{2,1,0:T(8,128)(2,1)}, bf16[8,1280,128]{2,1,0:T(8,128)(2,1)}) custom-call(s32[5]{0:T(128)} %refs_0_.13, f32[8,1280,128]{2,1,0:T(8,128)} %get-tuple-element.51.refs_1_, f32[8,1280,128]{2,1,0:T(8,128)} %get-tuple-element.52.refs_2_, bf16[8,1280,128]{2,1,0:T(8,128)(2,1)} %refs_3_.3, bf16[8,1280,128]{2,1,0:T(8,128)(2,1)} %refs_4_.3, ...), custom_call_target="tpu_custom_call" | custom-call | flops 671088640 | bytes 24150016 | tf_op jit(solution)/shard_map/pallas_call | solution.py:194
  (7 shorter events, 0.1 us)
Async XLA Ops:
  6.5 17.1 %collective-permute-start = (f32[8,136,128]{2,1,0:T(8,128)}, f32[8,136,128]{2,1,0:T(8,128)S(1)}, u32[]{:S(2)}, u32[]{:S(2)}) collective-permute-start(f32[8,136,128]{2,1,0:T(8,128)} %get-tuple-element.30.near_ref), channel_id=1, source_target_pairs={{0,4},{4,8},{8,12},{1,5},{5,9},{9,13},{2,6},{6,10},{10,14},{3,7},{... | collective-permute-start | bytes 1671176 | tf_op jit(solution)/shard_map/ppermute | solution.py:225
  23.6 0.8 copy-start.3
  26.6 15.6 %collective-permute-start.1 = (f32[8,136,128]{2,1,0:T(8,128)}, f32[8,136,128]{2,1,0:T(8,128)S(1)}, u32[]{:S(2)}, u32[]{:S(2)}) collective-permute-start(f32[8,136,128]{2,1,0:T(8,128)} %shard_map.87), channel_id=1, source_target_pairs={{0,4},{4,8},{8,12},{1,5},{5,9},{9,13},{2,6},{6,10},{10,14},{3,7},{... | collective-permute-start | bytes 1671176 | tf_op jit(solution)/shard_map/ppermute | solution.py:225
  42.1 0.8 copy-start.1
  53.0 1.2 %collective-permute-start.2 = (f32[2560]{0:T(1024)S(1)}, f32[2560]{0:T(1024)S(1)}, u32[]{:S(2)}, u32[]{:S(2)}) collective-permute-start(f32[2560]{0:T(1024)S(1)} %reshape.13), channel_id=1, source_target_pairs={{0,1},{1,0},{2,3},{3,2},{4,5},{5,4},{6,7},{7,6},{8,9},{9,8},{10,11... | collective-permute-start | bytes 30728 | tf_op jit(solution)/shard_map/ppermute | solution.py:301
  54.3 3.7 %collective-permute-start.3 = (f32[2560]{0:T(1024)S(1)}, f32[2560]{0:T(1024)S(1)}, u32[]{:S(2)}, u32[]{:S(2)}) collective-permute-start(f32[2560]{0:T(1024)S(1)} %add.12), channel_id=1, source_target_pairs={{0,2},{2,0},{1,3},{3,1},{4,6},{6,4},{5,7},{7,5},{8,10},{10,8},{9,1... | collective-permute-start | bytes 30728 | tf_op jit(solution)/shard_map/ppermute | solution.py:301
  69.7 16.3 %collective-permute-start.4 = (f32[8,136,128]{2,1,0:T(8,128)}, f32[8,136,128]{2,1,0:T(8,128)S(1)}, u32[]{:S(2)}, u32[]{:S(2)}) collective-permute-start(f32[8,136,128]{2,1,0:T(8,128)} %get-tuple-element.38.near_ref), channel_id=1, source_target_pairs={{4,0},{8,4},{12,8},{5,1},{9,5},{13,9},{6,2},{10,6},{14,10},{7,3},{... | collective-permute-start | bytes 1671176 | tf_op jit(solution)/shard_map/ppermute | solution.py:225
  86.0 0.8 copy-start.2
  88.9 15.0 %collective-permute-start.5 = (f32[8,136,128]{2,1,0:T(8,128)}, f32[8,136,128]{2,1,0:T(8,128)S(1)}, u32[]{:S(2)}, u32[]{:S(2)}) collective-permute-start(f32[8,136,128]{2,1,0:T(8,128)} %shard_map.91), channel_id=1, source_target_pairs={{4,0},{8,4},{12,8},{5,1},{9,5},{13,9},{6,2},{10,6},{14,10},{7,3},{... | collective-permute-start | bytes 1671176 | tf_op jit(solution)/shard_map/ppermute | solution.py:225
  103.9 0.8 copy-start

commit v17 on v16

--- a/solution.py
+++ b/solution.py
@@ -165,7 +165,7 @@
 def per_head_call(kernel, inputs, outputs, flops, heads=None, into=(), scalars=None):
     head_count = inputs[0][0].shape[0]
     first, count = heads if heads is not None else (0, head_count)
-    group = math.gcd(math.gcd(first, count), 2)
+    group = math.gcd(math.gcd(first, count), 4 if count >= 8 else 2)
 
     def spec(shape, per_head, first):
         if per_head:
@@ -296,11 +296,14 @@
     )
     feature_count = head_count * head_width * lax.axis_size(("sub", "head"))
     total_sums = local_sums.T.reshape(2 * tok_count)
-    for axis in ("head", "sub"):
-        if lax.axis_size(axis) == 2:
-            total_sums = total_sums + lax.ppermute(total_sums, axis, [(0, 1), (1, 0)])
-        elif lax.axis_size(axis) > 2:
-            total_sums = lax.psum(total_sums, axis)
+    if lax.axis_size("head") == 2 and lax.axis_size("sub") == 2:
+        partners = [
+            lax.ppermute(total_sums, ("sub", "head"), [(k, k ^ flip) for k in range(4)])
+            for flip in (1, 2, 3)
+        ]
+        total_sums = (total_sums + partners[0]) + (partners[1] + partners[2])
+    else:
+        total_sums = lax.psum(total_sums, ("sub", "head"))
     root_mean = jnp.sqrt(total_sums[:tok_count] / feature_count + 1e-06)
     inner_mean = total_sums[tok_count:] / feature_count
     factor = inner_mean / (root_mean * root_mean)

time: 115 us -> 116 us (level)
  waiting for transfers between devices: 27.4 us -> 29.3 us
  Pallas kernels: 67.2 us -> 65.7 us
    ppermute x4, waiting for transfers between devices: 24.1 us -> 27.4 us  [shift(): return lax.ppermute(value, axis, pairs)]
    ppermute x2 -> x3, waiting for transfers between devices: 3.37 us -> 1.91 us  [on_device(): lax.ppermute(total_sums, ('sub', 'head'), [(k, k ^ flip) for k in range(4)])]
    pallas_call x7, Pallas kernels: 62.9 us -> 61.5 us  [per_head_call(): pl.pallas_call(body, grid_spec=grid_spec, out_shape=[o for o, _ in output...]
  transfers between devices with their start and end apart: 6 -> 7, of which waited for: 6 -> 6; matrix products, arithmetic and copies ran while one was open for 0% -> 0% of each run, Pallas kernels for 25% -> 24%
where the time goes in v17:
time: 116 us; the launch traced here: 115 us
  Pallas kernels  65.7 us (57%)
  waiting for transfers between devices  29.3 us (25%)
  starting transfers between devices  13.9 us (12%)
  local copies, waits for them, and re-layouts  5.74 us (5%)
    pallas_call x7, Pallas kernels, per_head_call(): pl.pallas_call(body, grid_spec=grid_spec, out_shape=[o for o, _ in output...  61.5 us
    ppermute x4, waiting for transfers between devices, shift(): return lax.ppermute(value, axis, pairs)  27.4 us
    ppermute x4, starting transfers between devices, shift(): return lax.ppermute(value, axis, pairs)  12 us
    pallas_call x2, Pallas kernels, combine(): pl.pallas_call(combine_kernel, out_shape=jax.ShapeDtypeStruct(near.shape,...  4.24 us
    unnamed x8, local copies, waits for them, and re-layouts  3.3 us
  transfers between devices with their start and end apart: 7, of which 6 were waited for; matrix products, arithmetic and copies ran while one was open for 0% of the time, Pallas kernels for 24%

profile of v17, /device:TPU:0, one launch (start us, length us, event | category | flops | bytes accessed | tf_op | source)
XLA Modules:
  0.0 115.5 jit_solution(7329199486074677042)
XLA Ops:
  0.6 4.9 %shard_map.85 = (f32[8,5,128,128]{3,2,1,0:T(8,128)}, f32[8,136,128]{2,1,0:T(8,128)}) custom-call(s32[5]{0:T(128)} %refs_0_.13, bf16[8,1280,128]{2,1,0:T(8,128)(2,1)} %refs_3_.3, bf16[8,1280,128]{2,1,0:T(8,128)(2,1)} %refs_4_.3), custom_call_target="tpu_custom_call" | custom-call | flops 335544320 | bytes 8421376 | tf_op jit(solution)/shard_map/pallas_call | solution.py:194
  5.5 5.0 %collective-permute-start = (f32[8,136,128]{2,1,0:T(8,128)}, f32[8,136,128]{2,1,0:T(8,128)S(1)}, u32[]{:S(2)}, u32[]{:S(2)}) collective-permute-start(f32[8,136,128]{2,1,0:T(8,128)} %get-tuple-element.30.near_ref), channel_id=1, source_target_pairs={{0,4},{4,8},{8,12},{1,5},{5,9},{9,13},{2,6},{6,10},{10,14},{3,7},{... | collective-permute-start | bytes 1671176 | tf_op jit(solution)/shard_map/ppermute | solution.py:225
  10.5 7.2 %shard_map.86.refs_1_.refs_2_ = f32[8,1280,128]{2,1,0:T(8,128)} custom-call(bf16[8,1280,128]{2,1,0:T(8,128)(2,1)} %refs_0_.12, bf16[8,1280,128]{2,1,0:T(8,128)(2,1)} %refs_3_.3, bf16[8,1280,128]{2,1,0:T(8,128)(2,1)} %refs_4_.3), custom_call_target="tpu_custom_call" | custom-call | flops 1342177280 | bytes 13107200 | tf_op jit(solution)/shard_map/pallas_call | solution.py:194
  17.6 5.0 %collective-permute-done.far_ref = f32[8,136,128]{2,1,0:T(8,128)S(1)} collective-permute-done((f32[8,136,128]{2,1,0:T(8,128)}, f32[8,136,128]{2,1,0:T(8,128)S(1)}, u32[]{:S(2)}, u32[]{:S(2)}) %collective-permute-start) | collective-permute-done | bytes 557088 | tf_op jit(solution)/shard_map/ppermute | solution.py:225
  22.6 0.0 copy-start.3
  22.6 0.8 copy-done.3
  23.4 2.1 %shard_map.87 = f32[8,136,128]{2,1,0:T(8,128)} custom-call(f32[8,136,128]{2,1,0:T(8,128)} %get-tuple-element.30.near_ref, f32[8,136,128]{2,1,0:T(8,128)} %copy-done.3), custom_call_target="tpu_custom_call" | custom-call | flops 278528 | bytes 1671168 | tf_op jit(solution)/shard_map/pallas_call | solution.py:207
  25.5 4.3 %collective-permute-start.1 = (f32[8,136,128]{2,1,0:T(8,128)}, f32[8,136,128]{2,1,0:T(8,128)S(1)}, u32[]{:S(2)}, u32[]{:S(2)}) collective-permute-start(f32[8,136,128]{2,1,0:T(8,128)} %shard_map.87), channel_id=1, source_target_pairs={{0,4},{4,8},{8,12},{1,5},{5,9},{9,13},{2,6},{6,10},{10,14},{3,7},{... | collective-permute-start | bytes 1671176 | tf_op jit(solution)/shard_map/ppermute | solution.py:225
  29.9 11.3 %collective-permute-done.1.refs_6_ = f32[8,136,128]{2,1,0:T(8,128)S(1)} collective-permute-done((f32[8,136,128]{2,1,0:T(8,128)}, f32[8,136,128]{2,1,0:T(8,128)S(1)}, u32[]{:S(2)}, u32[]{:S(2)}) %collective-permute-start.1) | collective-permute-done | bytes 557088 | tf_op jit(solution)/shard_map/ppermute | solution.py:225
  41.1 0.0 copy-start.1
  41.1 0.8 copy-done.1
  42.0 8.2 %shard_map.88 = (f32[1280,2]{1,0:T(8,128)}, bf16[8,5,128,128]{3,2,1,0:T(8,128)(2,1)}) custom-call(s32[5]{0:T(128)} %refs_0_.13, f32[8,1280,128]{2,1,0:T(8,128)} %shard_map.86.refs_1_.refs_2_, bf16[8,1280,128]{2,1,0:T(8,128)(2,1)} %refs_0_.12, bf16[8,1280,128]{2,1,0:T(8,128)(2,1)} %refs_4_.2, f32[8,1,128]{2,1,0:T(1,128)} %bitcast.3, ...), custom_call_target="tpu_custom_call" | custom-call | flops 335544320 | bytes 14989312 | tf_op jit(solution)/shard_map/pallas_call | solution.py:194
  50.2 1.3 %copy.15 = f32[2,1280]{1,0:T(2,128)S(1)} copy(f32[2,1280]{0,1:T(8,128)} %bitcast.2) | data formatting | bytes 20480 | tf_op jit(solution)/shard_map/transpose | solution.py:298
  51.5 0.1 collective-permute-start.4
  51.6 1.6 %collective-permute-start.3 = (f32[2560]{0:T(1024)S(1)}, f32[2560]{0:T(1024)S(1)}, u32[]{:S(2)}, u32[]{:S(2)}) collective-permute-start(f32[2560]{0:T(1024)S(1)} %reshape.13), channel_id=1, source_target_pairs={{0,2},{1,3},{2,0},{3,1},{4,6},{5,7},{6,4},{7,5},{8,10},{9,11},{10,... | collective-permute-start | bytes 30728 | tf_op jit(solution)/shard_map/ppermute | solution.py:301
  53.2 0.3 collective-permute-start.2
  53.5 1.3 %collective-permute-done.4 = f32[2560]{0:T(1024)S(1)} collective-permute-done((f32[2560]{0:T(1024)S(1)}, f32[2560]{0:T(1024)S(1)}, u32[]{:S(2)}, u32[]{:S(2)}) %collective-permute-start.4) | collective-permute-done | bytes 10272 | tf_op jit(solution)/shard_map/ppermute | solution.py:301
  54.8 0.6 collective-permute-done.3
  55.4 0.0 collective-permute-done.2
  55.5 1.1 copy.16.refs_6_
  56.6 10.8 %shard_map.89 = (bf16[8,1280,128]{2,1,0:T(8,128)(2,1)}, f32[8,5,128,128]{3,2,1,0:T(8,128)}, f32[8,136,128]{2,1,0:T(8,128)}) custom-call(s32[5]{0:T(128)} %refs_0_.13, bf16[8,1280,128]{2,1,0:T(8,128)(2,1)} %refs_0_.12, f32[8,1280,128]{2,1,0:T(8,128)} %shard_map.86.refs_1_.refs_2_, bf16[8,5,128,128]{3,2,1,0:T(8,128)(2,1)} %get-tuple-element.36.refs_3_.refs_4_, ...), custom_call_target="tpu_custom_call" | custom-call | flops 335544320 | bytes 17610752 | tf_op jit(solution)/shard_map/pallas_call | solution.py:194
  67.4 1.3 %collective-permute-start.5 = (f32[8,136,128]{2,1,0:T(8,128)}, f32[8,136,128]{2,1,0:T(8,128)S(1)}, u32[]{:S(2)}, u32[]{:S(2)}) collective-permute-start(f32[8,136,128]{2,1,0:T(8,128)} %get-tuple-element.38.near_ref), channel_id=1, source_target_pairs={{4,0},{8,4},{12,8},{5,1},{9,5},{13,9},{6,2},{10,6},{14,10},{7,3},{... | collective-permute-start | bytes 1671176 | tf_op jit(solution)/shard_map/ppermute | solution.py:225
  68.7 10.1 %shard_map.90 = (bf16[8,1280,128]{2,1,0:T(8,128)(2,1)}, f32[8,1280,128]{2,1,0:T(8,128)}, f32[8,1280,128]{2,1,0:T(8,128)}) custom-call(bf16[8,1280,128]{2,1,0:T(8,128)(2,1)} %refs_0_.12, bf16[8,1280,128]{2,1,0:T(8,128)(2,1)} %refs_3_.3, bf16[8,1280,128]{2,1,0:T(8,128)(2,1)} %refs_4_.3, bf16[8,1280,128]{2,1,0:T(8,128)(2,1)} %get-tuple-element.39.refs_3_, ...), custom_call_target="tpu_custom_call" | custom-call | flops 1677721600 | bytes 12451840 | tf_op jit(solution)/shard_map/pallas_call | solution.py:194
  78.7 6.3 %collective-permute-done.5.far_ref = f32[8,136,128]{2,1,0:T(8,128)S(1)} collective-permute-done((f32[8,136,128]{2,1,0:T(8,128)}, f32[8,136,128]{2,1,0:T(8,128)S(1)}, u32[]{:S(2)}, u32[]{:S(2)}) %collective-permute-start.5) | collective-permute-done | bytes 557088 | tf_op jit(solution)/shard_map/ppermute | solution.py:225
  85.0 0.0 copy-start.2
  85.0 0.8 copy-done.2
  85.9 2.1 %shard_map.91 = f32[8,136,128]{2,1,0:T(8,128)} custom-call(f32[8,136,128]{2,1,0:T(8,128)} %get-tuple-element.38.near_ref, f32[8,136,128]{2,1,0:T(8,128)} %copy-done.2), custom_call_target="tpu_custom_call" | custom-call | flops 278528 | bytes 1671168 | tf_op jit(solution)/shard_map/pallas_call | solution.py:207
  88.0 1.5 %collective-permute-start.6 = (f32[8,136,128]{2,1,0:T(8,128)}, f32[8,136,128]{2,1,0:T(8,128)S(1)}, u32[]{:S(2)}, u32[]{:S(2)}) collective-permute-start(f32[8,136,128]{2,1,0:T(8,128)} %shard_map.91), channel_id=1, source_target_pairs={{4,0},{8,4},{12,8},{5,1},{9,5},{13,9},{6,2},{10,6},{14,10},{7,3},{... | collective-permute-start | bytes 1671176 | tf_op jit(solution)/shard_map/ppermute | solution.py:225
  89.4 10.1 %shard_map.92 = (bf16[8,1280,128]{2,1,0:T(8,128)(2,1)}, f32[8,1280,128]{2,1,0:T(8,128)}, f32[8,1280,128]{2,1,0:T(8,128)}) custom-call(bf16[8,1280,128]{2,1,0:T(8,128)(2,1)} %refs_0_.12, bf16[8,1280,128]{2,1,0:T(8,128)(2,1)} %refs_3_.3, bf16[8,1280,128]{2,1,0:T(8,128)(2,1)} %refs_4_.3, ...), custom_call_target="tpu_custom_call", output_to_operand_aliasing={{0}: (5, {}), {1}: (6, {}), {2}: (7, {})} | custom-call | flops 1677721600 | bytes 12451840 | tf_op jit(solution)/shard_map/pallas_call | solution.py:194
  99.5 4.9 %collective-permute-done.6.refs_6_ = f32[8,136,128]{2,1,0:T(8,128)S(1)} collective-permute-done((f32[8,136,128]{2,1,0:T(8,128)}, f32[8,136,128]{2,1,0:T(8,128)S(1)}, u32[]{:S(2)}, u32[]{:S(2)}) %collective-permute-start.6) | collective-permute-done | bytes 557088 | tf_op jit(solution)/shard_map/ppermute | solution.py:225
  104.4 0.0 copy-start
  104.4 0.8 copy-done
  105.2 10.3 %shard_map.93 = (bf16[8,1280,128]{2,1,0:T(8,128)(2,1)}, bf16[8,1280,128]{2,1,0:T(8,128)(2,1)}) custom-call(s32[5]{0:T(128)} %refs_0_.13, f32[8,1280,128]{2,1,0:T(8,128)} %get-tuple-element.51.refs_1_, f32[8,1280,128]{2,1,0:T(8,128)} %get-tuple-element.52.refs_2_, bf16[8,1280,128]{2,1,0:T(8,128)(2,1)} %refs_3_.3, bf16[8,1280,128]{2,1,0:T(8,128)(2,1)} %refs_4_.3, ...), custom_call_target="tpu_custom_call" | custom-call | flops 671088640 | bytes 24150016 | tf_op jit(solution)/shard_map/pallas_call | solution.py:194
  (6 shorter events, 0.1 us)
Async XLA Ops:
  5.5 17.1 %collective-permute-start = (f32[8,136,128]{2,1,0:T(8,128)}, f32[8,136,128]{2,1,0:T(8,128)S(1)}, u32[]{:S(2)}, u32[]{:S(2)}) collective-permute-start(f32[8,136,128]{2,1,0:T(8,128)} %get-tuple-element.30.near_ref), channel_id=1, source_target_pairs={{0,4},{4,8},{8,12},{1,5},{5,9},{9,13},{2,6},{6,10},{10,14},{3,7},{... | collective-permute-start | bytes 1671176 | tf_op jit(solution)/shard_map/ppermute | solution.py:225
  22.6 0.8 copy-start.3
  25.5 15.6 %collective-permute-start.1 = (f32[8,136,128]{2,1,0:T(8,128)}, f32[8,136,128]{2,1,0:T(8,128)S(1)}, u32[]{:S(2)}, u32[]{:S(2)}) collective-permute-start(f32[8,136,128]{2,1,0:T(8,128)} %shard_map.87), channel_id=1, source_target_pairs={{0,4},{4,8},{8,12},{1,5},{5,9},{9,13},{2,6},{6,10},{10,14},{3,7},{... | collective-permute-start | bytes 1671176 | tf_op jit(solution)/shard_map/ppermute | solution.py:225
  41.1 0.8 copy-start.1
  51.5 3.3 %collective-permute-start.4 = (f32[2560]{0:T(1024)S(1)}, f32[2560]{0:T(1024)S(1)}, u32[]{:S(2)}, u32[]{:S(2)}) collective-permute-start(f32[2560]{0:T(1024)S(1)} %reshape.13), channel_id=1, source_target_pairs={{0,3},{1,2},{2,1},{3,0},{4,7},{5,6},{6,5},{7,4},{8,11},{9,10},{10,... | collective-permute-start | bytes 30728 | tf_op jit(solution)/shard_map/ppermute | solution.py:301
  51.6 3.8 %collective-permute-start.3 = (f32[2560]{0:T(1024)S(1)}, f32[2560]{0:T(1024)S(1)}, u32[]{:S(2)}, u32[]{:S(2)}) collective-permute-start(f32[2560]{0:T(1024)S(1)} %reshape.13), channel_id=1, source_target_pairs={{0,2},{1,3},{2,0},{3,1},{4,6},{5,7},{6,4},{7,5},{8,10},{9,11},{10,... | collective-permute-start | bytes 30728 | tf_op jit(solution)/shard_map/ppermute | solution.py:301
  53.2 2.2 %collective-permute-start.2 = (f32[2560]{0:T(1024)S(1)}, f32[2560]{0:T(1024)S(1)}, u32[]{:S(2)}, u32[]{:S(2)}) collective-permute-start(f32[2560]{0:T(1024)S(1)} %reshape.13), channel_id=1, source_target_pairs={{0,1},{1,0},{2,3},{3,2},{4,5},{5,4},{6,7},{7,6},{8,9},{9,8},{10,11... | collective-permute-start | bytes 30728 | tf_op jit(solution)/shard_map/ppermute | solution.py:301
  67.4 17.6 %collective-permute-start.5 = (f32[8,136,128]{2,1,0:T(8,128)}, f32[8,136,128]{2,1,0:T(8,128)S(1)}, u32[]{:S(2)}, u32[]{:S(2)}) collective-permute-start(f32[8,136,128]{2,1,0:T(8,128)} %get-tuple-element.38.near_ref), channel_id=1, source_target_pairs={{4,0},{8,4},{12,8},{5,1},{9,5},{13,9},{6,2},{10,6},{14,10},{7,3},{... | collective-permute-start | bytes 1671176 | tf_op jit(solution)/shard_map/ppermute | solution.py:225
  85.0 0.8 copy-start.2
  88.0 16.4 %collective-permute-start.6 = (f32[8,136,128]{2,1,0:T(8,128)}, f32[8,136,128]{2,1,0:T(8,128)S(1)}, u32[]{:S(2)}, u32[]{:S(2)}) collective-permute-start(f32[8,136,128]{2,1,0:T(8,128)} %shard_map.91), channel_id=1, source_target_pairs={{4,0},{8,4},{12,8},{5,1},{9,5},{13,9},{6,2},{10,6},{14,10},{7,3},{... | collective-permute-start | bytes 1671176 | tf_op jit(solution)/shard_map/ppermute | solution.py:225
  104.4 0.8 copy-start

commit v18 on v17

--- a/solution.py
+++ b/solution.py
@@ -162,10 +162,12 @@
             dv_ref[j, rows, :] = dv.astype(dv_ref.dtype)
 
 
-def per_head_call(kernel, inputs, outputs, flops, heads=None, into=(), scalars=None):
+def per_head_call(
+    kernel, inputs, outputs, flops, heads=None, into=(), scalars=None, per_step=2
+):
     head_count = inputs[0][0].shape[0]
     first, count = heads if heads is not None else (0, head_count)
-    group = math.gcd(math.gcd(first, count), 4 if count >= 8 else 2)
+    group = math.gcd(math.gcd(first, count), per_step)
 
     def spec(shape, per_head, first):
         if per_head:
@@ -269,6 +271,7 @@
         [(states, True), (payload, True)],
         pair_flops // 2,
         scalars=doc_ids,
+        per_step=4,
     )
     prior, intra_part = carry(
         kv_payload,
@@ -281,6 +284,7 @@
                 [(queries, True), (keys, True), (values, True)],
                 [(wide, True)],
                 2 * pair_flops,
+                per_step=4,
             )[0],
             lambda intra: intra,
         ),
@@ -293,6 +297,7 @@
          (jax.ShapeDtypeStruct(states.shape, jnp.bfloat16), True)],
         pair_flops // 2,
         scalars=doc_ids,
+        per_step=4,
     )
     feature_count = head_count * head_width * lax.axis_size(("sub", "head"))
     total_sums = local_sums.T.reshape(2 * tok_count)

time: 116 us -> 115 us (level)
  no operation moved by 1% of the time
where the time goes in v18:
time: 115 us
  Pallas kernels  64.9 us (56%)
  waiting for transfers between devices  29.3 us (25%)
  starting transfers between devices  13.9 us (12%)
  local copies, waits for them, and re-layouts  5.74 us (5%)
    pallas_call x7, Pallas kernels, per_head_call(): pl.pallas_call(body, grid_spec=grid_spec, out_shape=[o for o, _ in output...  60.6 us
    ppermute x4, waiting for transfers between devices, shift(): return lax.ppermute(value, axis, pairs)  27.4 us
    ppermute x4, starting transfers between devices, shift(): return lax.ppermute(value, axis, pairs)  12 us
    pallas_call x2, Pallas kernels, combine(): pl.pallas_call(combine_kernel, out_shape=jax.ShapeDtypeStruct(near.shape,...  4.24 us
    unnamed x8, local copies, waits for them, and re-layouts  3.3 us
  transfers between devices with their start and end apart: 7, of which 6 were waited for; matrix products, arithmetic and copies ran while one was open for 0% of the time, Pallas kernels for 24%

profile of v18, /device:TPU:0, one launch (start us, length us, event | category | flops | bytes accessed | tf_op | source)
XLA Modules:
  0.0 114.6 jit_solution(8253278394828705163)
XLA Ops:
  0.6 4.9 %shard_map.85 = (f32[8,5,128,128]{3,2,1,0:T(8,128)}, f32[8,136,128]{2,1,0:T(8,128)}) custom-call(s32[5]{0:T(128)} %refs_0_.13, bf16[8,1280,128]{2,1,0:T(8,128)(2,1)} %refs_3_.3, bf16[8,1280,128]{2,1,0:T(8,128)(2,1)} %refs_4_.3), custom_call_target="tpu_custom_call" | custom-call | flops 335544320 | bytes 8421376 | tf_op jit(solution)/shard_map/pallas_call | solution.py:196
  5.5 5.0 %collective-permute-start = (f32[8,136,128]{2,1,0:T(8,128)}, f32[8,136,128]{2,1,0:T(8,128)S(1)}, u32[]{:S(2)}, u32[]{:S(2)}) collective-permute-start(f32[8,136,128]{2,1,0:T(8,128)} %get-tuple-element.30.near_ref), channel_id=1, source_target_pairs={{0,4},{4,8},{8,12},{1,5},{5,9},{9,13},{2,6},{6,10},{10,14},{3,7},{... | collective-permute-start | bytes 1671176 | tf_op jit(solution)/shard_map/ppermute | solution.py:227
  10.5 7.2 %shard_map.86.refs_1_.refs_2_ = f32[8,1280,128]{2,1,0:T(8,128)} custom-call(bf16[8,1280,128]{2,1,0:T(8,128)(2,1)} %refs_0_.12, bf16[8,1280,128]{2,1,0:T(8,128)(2,1)} %refs_3_.3, bf16[8,1280,128]{2,1,0:T(8,128)(2,1)} %refs_4_.3), custom_call_target="tpu_custom_call" | custom-call | flops 1342177280 | bytes 13107200 | tf_op jit(solution)/shard_map/pallas_call | solution.py:196
  17.6 5.0 %collective-permute-done.far_ref = f32[8,136,128]{2,1,0:T(8,128)S(1)} collective-permute-done((f32[8,136,128]{2,1,0:T(8,128)}, f32[8,136,128]{2,1,0:T(8,128)S(1)}, u32[]{:S(2)}, u32[]{:S(2)}) %collective-permute-start) | collective-permute-done | bytes 557088 | tf_op jit(solution)/shard_map/ppermute | solution.py:227
  22.6 0.0 copy-start.3
  22.6 0.8 copy-done.3
  23.4 2.1 %shard_map.87 = f32[8,136,128]{2,1,0:T(8,128)} custom-call(f32[8,136,128]{2,1,0:T(8,128)} %get-tuple-element.30.near_ref, f32[8,136,128]{2,1,0:T(8,128)} %copy-done.3), custom_call_target="tpu_custom_call" | custom-call | flops 278528 | bytes 1671168 | tf_op jit(solution)/shard_map/pallas_call | solution.py:209
  25.5 4.3 %collective-permute-start.1 = (f32[8,136,128]{2,1,0:T(8,128)}, f32[8,136,128]{2,1,0:T(8,128)S(1)}, u32[]{:S(2)}, u32[]{:S(2)}) collective-permute-start(f32[8,136,128]{2,1,0:T(8,128)} %shard_map.87), channel_id=1, source_target_pairs={{0,4},{4,8},{8,12},{1,5},{5,9},{9,13},{2,6},{6,10},{10,14},{3,7},{... | collective-permute-start | bytes 1671176 | tf_op jit(solution)/shard_map/ppermute | solution.py:227
  29.9 11.3 %collective-permute-done.1.refs_6_ = f32[8,136,128]{2,1,0:T(8,128)S(1)} collective-permute-done((f32[8,136,128]{2,1,0:T(8,128)}, f32[8,136,128]{2,1,0:T(8,128)S(1)}, u32[]{:S(2)}, u32[]{:S(2)}) %collective-permute-start.1) | collective-permute-done | bytes 557088 | tf_op jit(solution)/shard_map/ppermute | solution.py:227
  41.1 0.0 copy-start.1
  41.1 0.8 copy-done.1
  42.0 8.2 %shard_map.88 = (f32[1280,2]{1,0:T(8,128)}, bf16[8,5,128,128]{3,2,1,0:T(8,128)(2,1)}) custom-call(s32[5]{0:T(128)} %refs_0_.13, f32[8,1280,128]{2,1,0:T(8,128)} %shard_map.86.refs_1_.refs_2_, bf16[8,1280,128]{2,1,0:T(8,128)(2,1)} %refs_0_.12, bf16[8,1280,128]{2,1,0:T(8,128)(2,1)} %refs_4_.2, f32[8,1,128]{2,1,0:T(1,128)} %bitcast.3, ...), custom_call_target="tpu_custom_call" | custom-call | flops 335544320 | bytes 14989312 | tf_op jit(solution)/shard_map/pallas_call | solution.py:196
  50.2 1.3 %copy.15 = f32[2,1280]{1,0:T(2,128)S(1)} copy(f32[2,1280]{0,1:T(8,128)} %bitcast.2) | data formatting | bytes 20480 | tf_op jit(solution)/shard_map/transpose | solution.py:303
  51.5 0.1 collective-permute-start.4
  51.6 1.6 %collective-permute-start.3 = (f32[2560]{0:T(1024)S(1)}, f32[2560]{0:T(1024)S(1)}, u32[]{:S(2)}, u32[]{:S(2)}) collective-permute-start(f32[2560]{0:T(1024)S(1)} %reshape.13), channel_id=1, source_target_pairs={{0,2},{1,3},{2,0},{3,1},{4,6},{5,7},{6,4},{7,5},{8,10},{9,11},{10,... | collective-permute-start | bytes 30728 | tf_op jit(solution)/shard_map/ppermute | solution.py:306
  53.2 0.3 collective-permute-start.2
  53.5 1.3 %collective-permute-done.4 = f32[2560]{0:T(1024)S(1)} collective-permute-done((f32[2560]{0:T(1024)S(1)}, f32[2560]{0:T(1024)S(1)}, u32[]{:S(2)}, u32[]{:S(2)}) %collective-permute-start.4) | collective-permute-done | bytes 10272 | tf_op jit(solution)/shard_map/ppermute | solution.py:306
  54.8 0.6 collective-permute-done.3
  55.4 0.0 collective-permute-done.2
  55.5 1.1 copy.16.refs_6_
  56.6 10.5 %shard_map.89 = (bf16[8,1280,128]{2,1,0:T(8,128)(2,1)}, f32[8,5,128,128]{3,2,1,0:T(8,128)}, f32[8,136,128]{2,1,0:T(8,128)}) custom-call(s32[5]{0:T(128)} %refs_0_.13, bf16[8,1280,128]{2,1,0:T(8,128)(2,1)} %refs_0_.12, f32[8,1280,128]{2,1,0:T(8,128)} %shard_map.86.refs_1_.refs_2_, bf16[8,5,128,128]{3,2,1,0:T(8,128)(2,1)} %get-tuple-element.36.refs_3_.refs_4_, ...), custom_call_target="tpu_custom_call" | custom-call | flops 335544320 | bytes 17610752 | tf_op jit(solution)/shard_map/pallas_call | solution.py:196
  67.1 1.3 %collective-permute-start.5 = (f32[8,136,128]{2,1,0:T(8,128)}, f32[8,136,128]{2,1,0:T(8,128)S(1)}, u32[]{:S(2)}, u32[]{:S(2)}) collective-permute-start(f32[8,136,128]{2,1,0:T(8,128)} %get-tuple-element.38.near_ref), channel_id=1, source_target_pairs={{4,0},{8,4},{12,8},{5,1},{9,5},{13,9},{6,2},{10,6},{14,10},{7,3},{... | collective-permute-start | bytes 1671176 | tf_op jit(solution)/shard_map/ppermute | solution.py:227
  68.4 10.1 %shard_map.90 = (bf16[8,1280,128]{2,1,0:T(8,128)(2,1)}, f32[8,1280,128]{2,1,0:T(8,128)}, f32[8,1280,128]{2,1,0:T(8,128)}) custom-call(bf16[8,1280,128]{2,1,0:T(8,128)(2,1)} %refs_0_.12, bf16[8,1280,128]{2,1,0:T(8,128)(2,1)} %refs_3_.3, bf16[8,1280,128]{2,1,0:T(8,128)(2,1)} %refs_4_.3, bf16[8,1280,128]{2,1,0:T(8,128)(2,1)} %get-tuple-element.39.refs_3_, ...), custom_call_target="tpu_custom_call" | custom-call | flops 1677721600 | bytes 12451840 | tf_op jit(solution)/shard_map/pallas_call | solution.py:196
  78.4 6.3 %collective-permute-done.5.far_ref = f32[8,136,128]{2,1,0:T(8,128)S(1)} collective-permute-done((f32[8,136,128]{2,1,0:T(8,128)}, f32[8,136,128]{2,1,0:T(8,128)S(1)}, u32[]{:S(2)}, u32[]{:S(2)}) %collective-permute-start.5) | collective-permute-done | bytes 557088 | tf_op jit(solution)/shard_map/ppermute | solution.py:227
  84.7 0.0 copy-start.2
  84.7 0.8 copy-done.2
  85.6 2.1 %shard_map.91 = f32[8,136,128]{2,1,0:T(8,128)} custom-call(f32[8,136,128]{2,1,0:T(8,128)} %get-tuple-element.38.near_ref, f32[8,136,128]{2,1,0:T(8,128)} %copy-done.2), custom_call_target="tpu_custom_call" | custom-call | flops 278528 | bytes 1671168 | tf_op jit(solution)/shard_map/pallas_call | solution.py:209
  87.7 1.5 %collective-permute-start.6 = (f32[8,136,128]{2,1,0:T(8,128)}, f32[8,136,128]{2,1,0:T(8,128)S(1)}, u32[]{:S(2)}, u32[]{:S(2)}) collective-permute-start(f32[8,136,128]{2,1,0:T(8,128)} %shard_map.91), channel_id=1, source_target_pairs={{4,0},{8,4},{12,8},{5,1},{9,5},{13,9},{6,2},{10,6},{14,10},{7,3},{... | collective-permute-start | bytes 1671176 | tf_op jit(solution)/shard_map/ppermute | solution.py:227
  89.1 10.1 %shard_map.92 = (bf16[8,1280,128]{2,1,0:T(8,128)(2,1)}, f32[8,1280,128]{2,1,0:T(8,128)}, f32[8,1280,128]{2,1,0:T(8,128)}) custom-call(bf16[8,1280,128]{2,1,0:T(8,128)(2,1)} %refs_0_.12, bf16[8,1280,128]{2,1,0:T(8,128)(2,1)} %refs_3_.3, bf16[8,1280,128]{2,1,0:T(8,128)(2,1)} %refs_4_.3, ...), custom_call_target="tpu_custom_call", output_to_operand_aliasing={{0}: (5, {}), {1}: (6, {}), {2}: (7, {})} | custom-call | flops 1677721600 | bytes 12451840 | tf_op jit(solution)/shard_map/pallas_call | solution.py:196
  99.2 4.9 %collective-permute-done.6.refs_6_ = f32[8,136,128]{2,1,0:T(8,128)S(1)} collective-permute-done((f32[8,136,128]{2,1,0:T(8,128)}, f32[8,136,128]{2,1,0:T(8,128)S(1)}, u32[]{:S(2)}, u32[]{:S(2)}) %collective-permute-start.6) | collective-permute-done | bytes 557088 | tf_op jit(solution)/shard_map/ppermute | solution.py:227
  104.1 0.0 copy-start
  104.1 0.8 copy-done
  104.9 9.7 %shard_map.93 = (bf16[8,1280,128]{2,1,0:T(8,128)(2,1)}, bf16[8,1280,128]{2,1,0:T(8,128)(2,1)}) custom-call(s32[5]{0:T(128)} %refs_0_.13, f32[8,1280,128]{2,1,0:T(8,128)} %get-tuple-element.51.refs_1_, f32[8,1280,128]{2,1,0:T(8,128)} %get-tuple-element.52.refs_2_, bf16[8,1280,128]{2,1,0:T(8,128)(2,1)} %refs_3_.3, bf16[8,1280,128]{2,1,0:T(8,128)(2,1)} %refs_4_.3, ...), custom_call_target="tpu_custom_call" | custom-call | flops 671088640 | bytes 24150016 | tf_op jit(solution)/shard_map/pallas_call | solution.py:196
  (6 shorter events, 0.1 us)
Async XLA Ops:
  5.5 17.1 %collective-permute-start = (f32[8,136,128]{2,1,0:T(8,128)}, f32[8,136,128]{2,1,0:T(8,128)S(1)}, u32[]{:S(2)}, u32[]{:S(2)}) collective-permute-start(f32[8,136,128]{2,1,0:T(8,128)} %get-tuple-element.30.near_ref), channel_id=1, source_target_pairs={{0,4},{4,8},{8,12},{1,5},{5,9},{9,13},{2,6},{6,10},{10,14},{3,7},{... | collective-permute-start | bytes 1671176 | tf_op jit(solution)/shard_map/ppermute | solution.py:227
  22.6 0.8 copy-start.3
  25.5 15.6 %collective-permute-start.1 = (f32[8,136,128]{2,1,0:T(8,128)}, f32[8,136,128]{2,1,0:T(8,128)S(1)}, u32[]{:S(2)}, u32[]{:S(2)}) collective-permute-start(f32[8,136,128]{2,1,0:T(8,128)} %shard_map.87), channel_id=1, source_target_pairs={{0,4},{4,8},{8,12},{1,5},{5,9},{9,13},{2,6},{6,10},{10,14},{3,7},{... | collective-permute-start | bytes 1671176 | tf_op jit(solution)/shard_map/ppermute | solution.py:227
  41.1 0.8 copy-start.1
  51.5 3.3 %collective-permute-start.4 = (f32[2560]{0:T(1024)S(1)}, f32[2560]{0:T(1024)S(1)}, u32[]{:S(2)}, u32[]{:S(2)}) collective-permute-start(f32[2560]{0:T(1024)S(1)} %reshape.13), channel_id=1, source_target_pairs={{0,3},{1,2},{2,1},{3,0},{4,7},{5,6},{6,5},{7,4},{8,11},{9,10},{10,... | collective-permute-start | bytes 30728 | tf_op jit(solution)/shard_map/ppermute | solution.py:306
  51.6 3.8 %collective-permute-start.3 = (f32[2560]{0:T(1024)S(1)}, f32[2560]{0:T(1024)S(1)}, u32[]{:S(2)}, u32[]{:S(2)}) collective-permute-start(f32[2560]{0:T(1024)S(1)} %reshape.13), channel_id=1, source_target_pairs={{0,2},{1,3},{2,0},{3,1},{4,6},{5,7},{6,4},{7,5},{8,10},{9,11},{10,... | collective-permute-start | bytes 30728 | tf_op jit(solution)/shard_map/ppermute | solution.py:306
  53.2 2.2 %collective-permute-start.2 = (f32[2560]{0:T(1024)S(1)}, f32[2560]{0:T(1024)S(1)}, u32[]{:S(2)}, u32[]{:S(2)}) collective-permute-start(f32[2560]{0:T(1024)S(1)} %reshape.13), channel_id=1, source_target_pairs={{0,1},{1,0},{2,3},{3,2},{4,5},{5,4},{6,7},{7,6},{8,9},{9,8},{10,11... | collective-permute-start | bytes 30728 | tf_op jit(solution)/shard_map/ppermute | solution.py:306
  67.1 17.7 %collective-permute-start.5 = (f32[8,136,128]{2,1,0:T(8,128)}, f32[8,136,128]{2,1,0:T(8,128)S(1)}, u32[]{:S(2)}, u32[]{:S(2)}) collective-permute-start(f32[8,136,128]{2,1,0:T(8,128)} %get-tuple-element.38.near_ref), channel_id=1, source_target_pairs={{4,0},{8,4},{12,8},{5,1},{9,5},{13,9},{6,2},{10,6},{14,10},{7,3},{... | collective-permute-start | bytes 1671176 | tf_op jit(solution)/shard_map/ppermute | solution.py:227
  84.7 0.8 copy-start.2
  87.7 16.4 %collective-permute-start.6 = (f32[8,136,128]{2,1,0:T(8,128)}, f32[8,136,128]{2,1,0:T(8,128)S(1)}, u32[]{:S(2)}, u32[]{:S(2)}) collective-permute-start(f32[8,136,128]{2,1,0:T(8,128)} %shard_map.91), channel_id=1, source_target_pairs={{4,0},{8,4},{12,8},{5,1},{9,5},{13,9},{6,2},{10,6},{14,10},{7,3},{... | collective-permute-start | bytes 1671176 | tf_op jit(solution)/shard_map/ppermute | solution.py:227
  104.1 0.8 copy-start

commit v19 on v18

--- a/solution.py
+++ b/solution.py
@@ -29,10 +29,14 @@
     return jnp.full(shape, doc_ref[n].astype(jnp.float32) + 1.0, jnp.float32)
 
 
-def _carried(state_ref, doc_ref, n, carry_ref, j):
-    width = carry_ref.shape[2]
-    joined = carry_ref[j, width : width + 1, :] == doc_ref[n].astype(jnp.float32) + 1.0
-    total = state_ref[j, n] + jnp.where(joined, carry_ref[j, :width, :], 0.0)
+def _carried(state_ref, doc_ref, n, near_ref, far_ref, j):
+    width = near_ref.shape[2]
+    near_doc = near_ref[j, width : width + 1, :]
+    carried = near_ref[j, :width, :] + jnp.where(
+        near_doc == far_ref[j, width : width + 1, :], far_ref[j, :width, :], 0.0
+    )
+    joined = near_doc == doc_ref[n].astype(jnp.float32) + 1.0
+    total = state_ref[j, n] + jnp.where(joined, carried, 0.0)
     return total.astype(jnp.bfloat16)
 
 
@@ -79,7 +83,7 @@
 
 
 def forward_kernel(
-    block_len, doc_ref, i_ref, q_ref, g_ref, n_ref, prefix_ref, carry_ref, o_ref, s_ref
+    block_len, doc_ref, i_ref, q_ref, g_ref, n_ref, prefix_ref, near_ref, far_ref, o_ref, s_ref
 ):
     @pl.when(pl.program_id(0) == 0)
     def _():
@@ -88,7 +92,7 @@
     for j in range(q_ref.shape[0]):
         for n in range(q_ref.shape[1] // block_len):
             rows = pl.ds(n * block_len, block_len)
-            state = _carried(prefix_ref, doc_ref, n, carry_ref, j)
+            state = _carried(prefix_ref, doc_ref, n, near_ref, far_ref, j)
             s_ref[j, n] = state
             raw = i_ref[j, rows, :] + jnp.dot(
                 q_ref[j, rows, :], state, preferred_element_type=jnp.float32
@@ -146,12 +150,13 @@
 
 
 def key_value_grad_kernel(
-    block_len, doc_ref, ik_ref, iv_ref, k_ref, v_ref, suffix_ref, carry_ref, dk_ref, dv_ref
+    block_len, doc_ref, ik_ref, iv_ref, k_ref, v_ref, suffix_ref, near_ref, far_ref, dk_ref,
+    dv_ref,
 ):
     for j in range(ik_ref.shape[0]):
         for n in range(k_ref.shape[1] // block_len):
             rows = pl.ds(n * block_len, block_len)
-            state = _carried(suffix_ref, doc_ref, n, carry_ref, j)
+            state = _carried(suffix_ref, doc_ref, n, near_ref, far_ref, j)
             dk = ik_ref[j, rows, :] + lax.dot_general(
                 v_ref[j, rows, :], state, _ROWS_MINOR, preferred_element_type=jnp.float32
             )
@@ -227,18 +232,19 @@
         return lax.ppermute(value, axis, pairs)
 
     first_cover, second_cover = cover
+    none = jnp.zeros_like(payload)
     if reach < 1:
-        return jnp.zeros_like(payload), second_cover(first_cover())
+        return (none, none), second_cover(first_cover())
     got = shift(payload, 1)
     covered_value = first_cover()
     got, covered_value = lax.optimization_barrier((got, covered_value))
     if reach <= 2:
         if reach == 2:
-            got = shift(combine(payload, got), 1)
+            beyond = shift(got, 1)
             covered_value = second_cover(covered_value)
-            got, covered_value = lax.optimization_barrier((got, covered_value))
-            return got, covered_value
-        return got, second_cover(covered_value)
+            beyond, covered_value = lax.optimization_barrier((beyond, covered_value))
+            return (got, beyond), covered_value
+        return (got, none), second_cover(covered_value)
     earlier, inclusive = got, combine(payload, got)
     covered = 1
     while covered < reach:
@@ -248,7 +254,7 @@
         covered = covered + step
         if covered < reach:
             inclusive = combine(inclusive, got)
-    return earlier, second_cover(covered_value)
+    return (earlier, none), second_cover(covered_value)
 
 
 def on_device(queries, keys, values, out_grad, norm_gain, doc_ids):
@@ -292,7 +298,7 @@
     local_sums, preceding_states = per_head_call(
         functools.partial(forward_kernel, block_len),
         [(intra_part, True), (queries, True), (out_grad, True), (gain, True),
-         (local_prefix, True), (prior, True)],
+         (local_prefix, True), (prior[0], True), (prior[1], True)],
         [(jax.ShapeDtypeStruct((tok_count, 2), jnp.float32), False),
          (jax.ShapeDtypeStruct(states.shape, jnp.bfloat16), True)],
         pair_flops // 2,
@@ -348,7 +354,7 @@
     key_gradient, value_gradient = per_head_call(
         functools.partial(key_value_grad_kernel, block_len),
         [(key_intra, True), (value_intra, True), (keys, True), (values, True),
-         (local_suffix, True), (following, True)],
+         (local_suffix, True), (following[0], True), (following[1], True)],
         [(full, True), (full, True)],
         pair_flops,
         scalars=doc_ids,

time: 115 us -> 109 us (0.948)
  Pallas kernels: 64.9 us -> 61 us
  local copies, waits for them, and re-layouts: 5.74 us -> 4.08 us
    pallas_call x2 -> x0, Pallas kernels: 4.24 us -> none  [combine(): pl.pallas_call(combine_kernel, out_shape=jax.ShapeDtypeStruct(near.shape,...]
    unnamed x8, local copies, waits for them, and re-layouts: 3.3 us -> 1.64 us
  transfers between devices with their start and end apart: 7 -> 7, of which waited for: 6 -> 6; matrix products, arithmetic and copies ran while one was open for 0% -> 0% of each run, Pallas kernels for 24% -> 25%
where the time goes in v19:
time: 109 us
  Pallas kernels  61 us (56%)
  waiting for transfers between devices  28.9 us (27%)
  starting transfers between devices  13.9 us (13%)
  local copies, waits for them, and re-layouts  4.08 us (4%)
    pallas_call x7, Pallas kernels, per_head_call(): pl.pallas_call(body, grid_spec=grid_spec, out_shape=[o for o, _ in output...  61 us
    ppermute x4, waiting for transfers between devices, shift(): return lax.ppermute(value, axis, pairs)  27 us
    ppermute x4, starting transfers between devices, shift(): return lax.ppermute(value, axis, pairs)  12 us
  transfers between devices with their start and end apart: 7, of which 6 were waited for; matrix products, arithmetic and copies ran while one was open for 0% of the time, Pallas kernels for 25%

profile of v19, /device:TPU:0, one launch (start us, length us, event | category | flops | bytes accessed | tf_op | source)
XLA Modules:
  0.0 108.6 jit_solution(14899503491449102784)
XLA Ops:
  0.6 4.9 %shard_map.85 = (f32[8,5,128,128]{3,2,1,0:T(8,128)}, f32[8,136,128]{2,1,0:T(8,128)}) custom-call(s32[5]{0:T(128)} %refs_0_.13, bf16[8,1280,128]{2,1,0:T(8,128)(2,1)} %refs_3_.3, bf16[8,1280,128]{2,1,0:T(8,128)(2,1)} %refs_4_.3), custom_call_target="tpu_custom_call" | custom-call | flops 335544320 | bytes 8421376 | tf_op jit(solution)/shard_map/pallas_call | solution.py:201
  5.5 5.0 %collective-permute-start = (f32[8,136,128]{2,1,0:T(8,128)}, f32[8,136,128]{2,1,0:T(8,128)S(1)}, u32[]{:S(2)}, u32[]{:S(2)}) collective-permute-start(f32[8,136,128]{2,1,0:T(8,128)} %get-tuple-element.30), channel_id=1, source_target_pairs={{0,4},{4,8},{8,12},{1,5},{5,9},{9,13},{2,6},{6,10},{10,14},{3,7},{... | collective-permute-start | bytes 1671176 | tf_op jit(solution)/shard_map/ppermute | solution.py:232
  10.5 7.2 %shard_map.86.refs_1_.refs_2_ = f32[8,1280,128]{2,1,0:T(8,128)} custom-call(bf16[8,1280,128]{2,1,0:T(8,128)(2,1)} %refs_0_.12, bf16[8,1280,128]{2,1,0:T(8,128)(2,1)} %refs_3_.3, bf16[8,1280,128]{2,1,0:T(8,128)(2,1)} %refs_4_.3), custom_call_target="tpu_custom_call" | custom-call | flops 1342177280 | bytes 13107200 | tf_op jit(solution)/shard_map/pallas_call | solution.py:201
  17.6 5.0 %collective-permute-done.refs_6_ = f32[8,136,128]{2,1,0:T(8,128)S(1)} collective-permute-done((f32[8,136,128]{2,1,0:T(8,128)}, f32[8,136,128]{2,1,0:T(8,128)S(1)}, u32[]{:S(2)}, u32[]{:S(2)}) %collective-permute-start) | collective-permute-done | bytes 557088 | tf_op jit(solution)/shard_map/ppermute | solution.py:232
  22.6 0.0 copy-start.2
  22.6 4.3 %collective-permute-start.1 = (f32[8,136,128]{2,1,0:T(8,128)S(1)}, f32[8,136,128]{2,1,0:T(8,128)S(1)}, u32[]{:S(2)}, u32[]{:S(2)}) collective-permute-start(f32[8,136,128]{2,1,0:T(8,128)S(1)} %collective-permute-done.refs_6_), channel_id=1, source_target_pairs={{0,4},{4,8},{8,12},{1,5},{5,9},{9,13},{2,6},{6,10},{10,14},{3,7},{... | collective-permute-start | bytes 1671176 | tf_op jit(solution)/shard_map/ppermute | solution.py:232
  26.9 11.0 %collective-permute-done.1.refs_7_ = f32[8,136,128]{2,1,0:T(8,128)S(1)} collective-permute-done((f32[8,136,128]{2,1,0:T(8,128)S(1)}, f32[8,136,128]{2,1,0:T(8,128)S(1)}, u32[]{:S(2)}, u32[]{:S(2)}) %collective-permute-start.1) | collective-permute-done | bytes 557088 | tf_op jit(solution)/shard_map/ppermute | solution.py:232
  37.9 0.0 copy-start.3
  37.9 0.0 copy-done.2
  37.9 0.8 copy-done.3
  38.7 8.4 %shard_map.87 = (f32[1280,2]{1,0:T(8,128)}, bf16[8,5,128,128]{3,2,1,0:T(8,128)(2,1)}) custom-call(s32[5]{0:T(128)} %refs_0_.13, f32[8,1280,128]{2,1,0:T(8,128)} %shard_map.86.refs_1_.refs_2_, bf16[8,1280,128]{2,1,0:T(8,128)(2,1)} %refs_0_.12, bf16[8,1280,128]{2,1,0:T(8,128)(2,1)} %refs_4_.2, f32[8,1,128]{2,1,0:T(1,128)} %bitcast.3, ...), custom_call_target="tpu_custom_call" | custom-call | flops 335544320 | bytes 15546368 | tf_op jit(solution)/shard_map/pallas_call | solution.py:201
  47.1 1.3 %copy.15 = f32[2,1280]{1,0:T(2,128)S(1)} copy(f32[2,1280]{0,1:T(8,128)} %bitcast.2) | data formatting | bytes 20480 | tf_op jit(solution)/shard_map/transpose | solution.py:309
  48.4 0.1 collective-permute-start.4
  48.5 1.6 %collective-permute-start.3 = (f32[2560]{0:T(1024)S(1)}, f32[2560]{0:T(1024)S(1)}, u32[]{:S(2)}, u32[]{:S(2)}) collective-permute-start(f32[2560]{0:T(1024)S(1)} %reshape.13), channel_id=1, source_target_pairs={{0,2},{1,3},{2,0},{3,1},{4,6},{5,7},{6,4},{7,5},{8,10},{9,11},{10,... | collective-permute-start | bytes 30728 | tf_op jit(solution)/shard_map/ppermute | solution.py:312
  50.0 0.3 collective-permute-start.2
  50.3 1.3 %collective-permute-done.4 = f32[2560]{0:T(1024)S(1)} collective-permute-done((f32[2560]{0:T(1024)S(1)}, f32[2560]{0:T(1024)S(1)}, u32[]{:S(2)}, u32[]{:S(2)}) %collective-permute-start.4) | collective-permute-done | bytes 10272 | tf_op jit(solution)/shard_map/ppermute | solution.py:312
  51.7 0.6 collective-permute-done.3
  52.2 0.0 collective-permute-done.2
  52.3 1.1 %copy.16.refs_6_ = f32[1280,2]{1,0:T(8,128)} copy(f32[1280,2]{0,1:T(2,128)S(1)} %pad_maximum_fusion) | data formatting | bytes 20480 | tf_op jit(solution)/shard_map/stack | solution.py:321
  53.4 10.5 %shard_map.88 = (bf16[8,1280,128]{2,1,0:T(8,128)(2,1)}, f32[8,5,128,128]{3,2,1,0:T(8,128)}, f32[8,136,128]{2,1,0:T(8,128)}) custom-call(s32[5]{0:T(128)} %refs_0_.13, bf16[8,1280,128]{2,1,0:T(8,128)(2,1)} %refs_0_.12, f32[8,1280,128]{2,1,0:T(8,128)} %shard_map.86.refs_1_.refs_2_, bf16[8,5,128,128]{3,2,1,0:T(8,128)(2,1)} %get-tuple-element.36.refs_3_.refs_4_, ...), custom_call_target="tpu_custom_call" | custom-call | flops 335544320 | bytes 17610752 | tf_op jit(solution)/shard_map/pallas_call | solution.py:201
  63.9 1.3 %collective-permute-start.5 = (f32[8,136,128]{2,1,0:T(8,128)}, f32[8,136,128]{2,1,0:T(8,128)S(1)}, u32[]{:S(2)}, u32[]{:S(2)}) collective-permute-start(f32[8,136,128]{2,1,0:T(8,128)} %get-tuple-element.38), channel_id=1, source_target_pairs={{4,0},{8,4},{12,8},{5,1},{9,5},{13,9},{6,2},{10,6},{14,10},{7,3},{... | collective-permute-start | bytes 1671176 | tf_op jit(solution)/shard_map/ppermute | solution.py:232
  65.2 10.1 %shard_map.89 = (bf16[8,1280,128]{2,1,0:T(8,128)(2,1)}, f32[8,1280,128]{2,1,0:T(8,128)}, f32[8,1280,128]{2,1,0:T(8,128)}) custom-call(bf16[8,1280,128]{2,1,0:T(8,128)(2,1)} %refs_0_.12, bf16[8,1280,128]{2,1,0:T(8,128)(2,1)} %refs_3_.3, bf16[8,1280,128]{2,1,0:T(8,128)(2,1)} %refs_4_.3, bf16[8,1280,128]{2,1,0:T(8,128)(2,1)} %get-tuple-element.39.refs_3_, ...), custom_call_target="tpu_custom_call" | custom-call | flops 1677721600 | bytes 12451840 | tf_op jit(solution)/shard_map/pallas_call | solution.py:201
  75.4 6.4 %collective-permute-done.5.refs_6_ = f32[8,136,128]{2,1,0:T(8,128)S(1)} collective-permute-done((f32[8,136,128]{2,1,0:T(8,128)}, f32[8,136,128]{2,1,0:T(8,128)S(1)}, u32[]{:S(2)}, u32[]{:S(2)}) %collective-permute-start.5) | collective-permute-done | bytes 557088 | tf_op jit(solution)/shard_map/ppermute | solution.py:232
  81.7 0.0 copy-start
  81.7 1.5 %collective-permute-start.6 = (f32[8,136,128]{2,1,0:T(8,128)S(1)}, f32[8,136,128]{2,1,0:T(8,128)S(1)}, u32[]{:S(2)}, u32[]{:S(2)}) collective-permute-start(f32[8,136,128]{2,1,0:T(8,128)S(1)} %collective-permute-done.5.refs_6_), channel_id=1, source_target_pairs={{4,0},{8,4},{12,8},{5,1},{9,5},{13,9},{6,2},{10,6},{14,10},{7,3},{... | collective-permute-start | bytes 1671176 | tf_op jit(solution)/shard_map/ppermute | solution.py:232
  83.2 10.1 %shard_map.90 = (bf16[8,1280,128]{2,1,0:T(8,128)(2,1)}, f32[8,1280,128]{2,1,0:T(8,128)}, f32[8,1280,128]{2,1,0:T(8,128)}) custom-call(bf16[8,1280,128]{2,1,0:T(8,128)(2,1)} %refs_0_.12, bf16[8,1280,128]{2,1,0:T(8,128)(2,1)} %refs_3_.3, bf16[8,1280,128]{2,1,0:T(8,128)(2,1)} %refs_4_.3, ...), custom_call_target="tpu_custom_call", output_to_operand_aliasing={{0}: (5, {}), {1}: (6, {}), {2}: (7, {})} | custom-call | flops 1677721600 | bytes 12451840 | tf_op jit(solution)/shard_map/pallas_call | solution.py:201
  93.3 0.0 copy-done
  93.3 4.7 %collective-permute-done.6.refs_7_ = f32[8,136,128]{2,1,0:T(8,128)S(1)} collective-permute-done((f32[8,136,128]{2,1,0:T(8,128)S(1)}, f32[8,136,128]{2,1,0:T(8,128)S(1)}, u32[]{:S(2)}, u32[]{:S(2)}) %collective-permute-start.6) | collective-permute-done | bytes 557088 | tf_op jit(solution)/shard_map/ppermute | solution.py:232
  97.9 0.0 copy-start.1
  97.9 0.8 copy-done.1
  98.7 9.8 %shard_map.91 = (bf16[8,1280,128]{2,1,0:T(8,128)(2,1)}, bf16[8,1280,128]{2,1,0:T(8,128)(2,1)}) custom-call(s32[5]{0:T(128)} %refs_0_.13, f32[8,1280,128]{2,1,0:T(8,128)} %get-tuple-element.51.refs_1_, f32[8,1280,128]{2,1,0:T(8,128)} %get-tuple-element.52.refs_2_, bf16[8,1280,128]{2,1,0:T(8,128)(2,1)} %refs_3_.3, bf16[8,1280,128]{2,1,0:T(8,128)(2,1)} %refs_4_.3, ...), custom_call_target="tpu_custom_call" | custom-call | flops 671088640 | bytes 24707072 | tf_op jit(solution)/shard_map/pallas_call | solution.py:201
  (6 shorter events, 0.1 us)
Async XLA Ops:
  5.5 17.1 %collective-permute-start = (f32[8,136,128]{2,1,0:T(8,128)}, f32[8,136,128]{2,1,0:T(8,128)S(1)}, u32[]{:S(2)}, u32[]{:S(2)}) collective-permute-start(f32[8,136,128]{2,1,0:T(8,128)} %get-tuple-element.30), channel_id=1, source_target_pairs={{0,4},{4,8},{8,12},{1,5},{5,9},{9,13},{2,6},{6,10},{10,14},{3,7},{... | collective-permute-start | bytes 1671176 | tf_op jit(solution)/shard_map/ppermute | solution.py:232
  22.6 15.3 %copy-start.2 = (f32[8,136,128]{2,1,0:T(8,128)}, f32[8,136,128]{2,1,0:T(8,128)S(1)}, u32[]{:S(2)}) copy-start(f32[8,136,128]{2,1,0:T(8,128)S(1)} %collective-permute-done.refs_6_) | copy-start | bytes 1671172
  22.6 15.3 %collective-permute-start.1 = (f32[8,136,128]{2,1,0:T(8,128)S(1)}, f32[8,136,128]{2,1,0:T(8,128)S(1)}, u32[]{:S(2)}, u32[]{:S(2)}) collective-permute-start(f32[8,136,128]{2,1,0:T(8,128)S(1)} %collective-permute-done.refs_6_), channel_id=1, source_target_pairs={{0,4},{4,8},{8,12},{1,5},{5,9},{9,13},{2,6},{6,10},{10,14},{3,7},{... | collective-permute-start | bytes 1671176 | tf_op jit(solution)/shard_map/ppermute | solution.py:232
  37.9 0.8 copy-start.3
  48.4 3.3 %collective-permute-start.4 = (f32[2560]{0:T(1024)S(1)}, f32[2560]{0:T(1024)S(1)}, u32[]{:S(2)}, u32[]{:S(2)}) collective-permute-start(f32[2560]{0:T(1024)S(1)} %reshape.13), channel_id=1, source_target_pairs={{0,3},{1,2},{2,1},{3,0},{4,7},{5,6},{6,5},{7,4},{8,11},{9,10},{10,... | collective-permute-start | bytes 30728 | tf_op jit(solution)/shard_map/ppermute | solution.py:312
  48.5 3.8 %collective-permute-start.3 = (f32[2560]{0:T(1024)S(1)}, f32[2560]{0:T(1024)S(1)}, u32[]{:S(2)}, u32[]{:S(2)}) collective-permute-start(f32[2560]{0:T(1024)S(1)} %reshape.13), channel_id=1, source_target_pairs={{0,2},{1,3},{2,0},{3,1},{4,6},{5,7},{6,4},{7,5},{8,10},{9,11},{10,... | collective-permute-start | bytes 30728 | tf_op jit(solution)/shard_map/ppermute | solution.py:312
  50.0 2.2 %collective-permute-start.2 = (f32[2560]{0:T(1024)S(1)}, f32[2560]{0:T(1024)S(1)}, u32[]{:S(2)}, u32[]{:S(2)}) collective-permute-start(f32[2560]{0:T(1024)S(1)} %reshape.13), channel_id=1, source_target_pairs={{0,1},{1,0},{2,3},{3,2},{4,5},{5,4},{6,7},{7,6},{8,9},{9,8},{10,11... | collective-permute-start | bytes 30728 | tf_op jit(solution)/shard_map/ppermute | solution.py:312
  63.9 17.8 %collective-permute-start.5 = (f32[8,136,128]{2,1,0:T(8,128)}, f32[8,136,128]{2,1,0:T(8,128)S(1)}, u32[]{:S(2)}, u32[]{:S(2)}) collective-permute-start(f32[8,136,128]{2,1,0:T(8,128)} %get-tuple-element.38), channel_id=1, source_target_pairs={{4,0},{8,4},{12,8},{5,1},{9,5},{13,9},{6,2},{10,6},{14,10},{7,3},{... | collective-permute-start | bytes 1671176 | tf_op jit(solution)/shard_map/ppermute | solution.py:232
  81.7 11.6 %copy-start = (f32[8,136,128]{2,1,0:T(8,128)}, f32[8,136,128]{2,1,0:T(8,128)S(1)}, u32[]{:S(2)}) copy-start(f32[8,136,128]{2,1,0:T(8,128)S(1)} %collective-permute-done.5.refs_6_) | copy-start | bytes 1671172
  81.7 16.2 %collective-permute-start.6 = (f32[8,136,128]{2,1,0:T(8,128)S(1)}, f32[8,136,128]{2,1,0:T(8,128)S(1)}, u32[]{:S(2)}, u32[]{:S(2)}) collective-permute-start(f32[8,136,128]{2,1,0:T(8,128)S(1)} %collective-permute-done.5.refs_6_), channel_id=1, source_target_pairs={{4,0},{8,4},{12,8},{5,1},{9,5},{13,9},{6,2},{10,6},{14,10},{7,3},{... | collective-permute-start | bytes 1671176 | tf_op jit(solution)/shard_map/ppermute | solution.py:232
  97.9 0.8 copy-start.1

commit v20 on v19

--- a/solution.py
+++ b/solution.py
@@ -168,7 +168,7 @@
 
 
 def per_head_call(
-    kernel, inputs, outputs, flops, heads=None, into=(), scalars=None, per_step=2
+    kernel, inputs, outputs, flops, heads=None, into=(), scalars=None, per_step=2, local=()
 ):
     head_count = inputs[0][0].shape[0]
     first, count = heads if heads is not None else (0, head_count)
@@ -196,7 +196,9 @@
         grid=(count // group,),
         in_specs=[spec(x.shape, h, first) for x, h in inputs]
         + [pl.BlockSpec(memory_space=pl.ANY) for _ in into],
-        out_specs=[spec(o.shape, h, first) for o, h in outputs],
+        out_specs=[
+            spec(o.shape, h, 0 if i in local else first) for i, (o, h) in enumerate(outputs)
+        ],
     )
     return pl.pallas_call(
         body,
@@ -218,6 +220,15 @@
             flops=2 * near.size, transcendentals=0, bytes_accessed=3 * near.size * 4
         ),
     )(near, far)
+
+
+def shift_along(value, axis, step, reverse):
+    peers = lax.axis_size(axis)
+    if reverse:
+        pairs = [(j, j - step) for j in range(step, peers)]
+    else:
+        pairs = [(j, j + step) for j in range(peers - step)]
+    return lax.ppermute(value, axis, pairs)
 
 
 def carry(payload, axis, reverse, reach, cover):
@@ -319,16 +330,21 @@
     inner_mean = total_sums[tok_count:] / feature_count
     factor = inner_mean / (root_mean * root_mean)
     coefs = jnp.stack([root_mean, factor], axis=1)
-    d_attn, local_suffix, qd_payload = per_head_call(
-        functools.partial(grad_kernel, block_len),
-        [(queries, True), (intra_part, True), (preceding_states, True), (out_grad, True),
-         (gain, True),
-         (coefs, False)],
-        [(full, True), (states, True), (payload, True)],
-        pair_flops // 2,
-        scalars=doc_ids,
-    )
     half = head_count // 2
+
+    def grads(heads, into):
+        return per_head_call(
+            functools.partial(grad_kernel, block_len),
+            [(queries, True), (intra_part, True), (preceding_states, True), (out_grad, True),
+             (gain, True), (coefs, False)],
+            [(full, True), (states, True),
+             (jax.ShapeDtypeStruct((heads[1],) + payload.shape[1:], jnp.float32), True)],
+            pair_flops // 2,
+            scalars=doc_ids,
+            heads=heads,
+            into=into,
+            local=(2,),
+        )
 
     def query_grads(heads, into):
         return per_head_call(
@@ -341,16 +357,47 @@
             into=into,
         )
 
-    following, (query_gradient, key_intra, value_intra) = carry(
-        qd_payload,
-        "ctx",
-        True,
-        reach,
-        (
-            lambda: query_grads((0, half), ()),
-            lambda done: query_grads((half, head_count - half), tuple(done)),
-        ),
-    )
+    reach_now = min(reach, ctx_size - 1)
+    if 1 <= reach_now <= 2 and half * 2 == head_count and half % 2 == 0:
+        first_heads, second_heads = (0, half), (half, head_count - half)
+        d_attn, local_suffix, first_payload = grads(first_heads, ())
+        first_near = shift_along(first_payload, "ctx", 1, True)
+        d_attn, local_suffix, second_payload = grads(second_heads, (d_attn, local_suffix))
+        first_near, d_attn, local_suffix, second_payload = lax.optimization_barrier(
+            (first_near, d_attn, local_suffix, second_payload)
+        )
+        second_near = shift_along(second_payload, "ctx", 1, True)
+        if reach_now == 2:
+            first_far = shift_along(first_near, "ctx", 1, True)
+        else:
+            first_far = jnp.zeros_like(first_near)
+        done = query_grads(first_heads, ())
+        first_far, second_near, done = lax.optimization_barrier(
+            (first_far, second_near, done)
+        )
+        if reach_now == 2:
+            second_far = shift_along(second_near, "ctx", 1, True)
+        else:
+            second_far = jnp.zeros_like(second_near)
+        done = query_grads(second_heads, tuple(done))
+        second_far, done = lax.optimization_barrier((second_far, done))
+        query_gradient, key_intra, value_intra = done
+        following = (
+            jnp.concatenate([first_near, second_near], axis=0),
+            jnp.concatenate([first_far, second_far], axis=0),
+        )
+    else:
+        d_attn, local_suffix, qd_payload = grads((0, head_count), ())
+        following, (query_gradient, key_intra, value_intra) = carry(
+            qd_payload,
+            "ctx",
+            True,
+            reach,
+            (
+                lambda: query_grads((0, half), ()),
+                lambda done: query_grads((half, head_count - half), tuple(done)),
+            ),
+        )
     key_gradient, value_gradient = per_head_call(
         functools.partial(key_value_grad_kernel, block_len),
         [(key_intra, True), (value_intra, True), (keys, True), (values, True),

time: 109 us -> 112 us (1.028)
  waiting for transfers between devices: 28.9 us -> 25.4 us
  Pallas kernels: 61 us -> 63.9 us
  starting transfers between devices: 13.9 us -> 16.5 us
  other arithmetic: 0.03 us -> 1.74 us
    ppermute x4 -> x2, waiting for transfers between devices: 27 us -> 15.9 us  [shift(): return lax.ppermute(value, axis, pairs)]
    ppermute x0 -> x4, waiting for transfers between devices: none -> 7.53 us  [shift_along(): return lax.ppermute(value, axis, pairs)]
    ppermute x0 -> x4, starting transfers between devices: none -> 5.31 us  [shift_along(): return lax.ppermute(value, axis, pairs)]
    pallas_call x7 -> x8, Pallas kernels: 61 us -> 63.9 us  [per_head_call(): pl.pallas_call(body, grid_spec=grid_spec, out_shape=[o for o, _ in output...]
    ppermute x4 -> x2, starting transfers between devices: 12 us -> 9.26 us  [shift(): return lax.ppermute(value, axis, pairs)]
    concatenate x0 -> x2, other arithmetic: none -> 1.71 us  [the longest x1 0.87 us: on_device(): jnp.concatenate([first_near, second_near], axis=0)]
  transfers between devices with their start and end apart: 7 -> 9, of which waited for: 6 -> 6; matrix products, arithmetic and copies ran while one was open for 0% -> 1% of each run, Pallas kernels for 25% -> 31%
where the time goes in v20:
time: 112 us; the launch traced here: 111 us
  Pallas kernels  63.9 us (57%)
  waiting for transfers between devices  25.4 us (23%)
  starting transfers between devices  16.5 us (15%)
  local copies, waits for them, and re-layouts  3.25 us (3%)
  other arithmetic  1.74 us (2%)
    pallas_call x8, Pallas kernels, per_head_call(): pl.pallas_call(body, grid_spec=grid_spec, out_shape=[o for o, _ in output...  63.9 us
    ppermute x2, waiting for transfers between devices, shift(): return lax.ppermute(value, axis, pairs)  15.9 us
    ppermute x2, starting transfers between devices, shift(): return lax.ppermute(value, axis, pairs)  9.26 us
    ppermute x4, waiting for transfers between devices, shift_along(): return lax.ppermute(value, axis, pairs)  7.53 us
    ppermute x4, starting transfers between devices, shift_along(): return lax.ppermute(value, axis, pairs)  5.31 us
  transfers between devices with their start and end apart: 9, of which 6 were waited for; matrix products, arithmetic and copies ran while one was open for 1% of the time, Pallas kernels for 31%

profile of v20, /device:TPU:0, one launch (start us, length us, event | category | flops | bytes accessed | tf_op | source)
XLA Modules:
  0.0 111.5 jit_solution(1460564288025084700)
XLA Ops:
  0.6 4.9 %shard_map.85 = (f32[8,5,128,128]{3,2,1,0:T(8,128)}, f32[8,136,128]{2,1,0:T(8,128)}) custom-call(s32[5]{0:T(128)} %refs_0_.15, bf16[8,1280,128]{2,1,0:T(8,128)(2,1)} %refs_3_.3, bf16[8,1280,128]{2,1,0:T(8,128)(2,1)} %refs_4_.5), custom_call_target="tpu_custom_call" | custom-call | flops 335544320 | bytes 8421376 | tf_op jit(solution)/shard_map/pallas_call | solution.py:203
  5.5 5.0 %collective-permute-start = (f32[8,136,128]{2,1,0:T(8,128)}, f32[8,136,128]{2,1,0:T(8,128)S(1)}, u32[]{:S(2)}, u32[]{:S(2)}) collective-permute-start(f32[8,136,128]{2,1,0:T(8,128)} %get-tuple-element.38), channel_id=1, source_target_pairs={{0,4},{4,8},{8,12},{1,5},{5,9},{9,13},{2,6},{6,10},{10,14},{3,7},{... | collective-permute-start | bytes 1671176 | tf_op jit(solution)/shard_map/ppermute | solution.py:243
  10.5 7.2 %shard_map.86.refs_1_.refs_2_ = f32[8,1280,128]{2,1,0:T(8,128)} custom-call(bf16[8,1280,128]{2,1,0:T(8,128)(2,1)} %refs_0_.14, bf16[8,1280,128]{2,1,0:T(8,128)(2,1)} %refs_3_.3, bf16[8,1280,128]{2,1,0:T(8,128)(2,1)} %refs_4_.5), custom_call_target="tpu_custom_call" | custom-call | flops 1342177280 | bytes 13107200 | tf_op jit(solution)/shard_map/pallas_call | solution.py:203
  17.6 5.0 %collective-permute-done.refs_6_ = f32[8,136,128]{2,1,0:T(8,128)S(1)} collective-permute-done((f32[8,136,128]{2,1,0:T(8,128)}, f32[8,136,128]{2,1,0:T(8,128)S(1)}, u32[]{:S(2)}, u32[]{:S(2)}) %collective-permute-start) | collective-permute-done | bytes 557088 | tf_op jit(solution)/shard_map/ppermute | solution.py:243
  22.6 0.0 copy-start
  22.6 4.3 %collective-permute-start.1 = (f32[8,136,128]{2,1,0:T(8,128)S(1)}, f32[8,136,128]{2,1,0:T(8,128)S(1)}, u32[]{:S(2)}, u32[]{:S(2)}) collective-permute-start(f32[8,136,128]{2,1,0:T(8,128)S(1)} %collective-permute-done.refs_6_), channel_id=1, source_target_pairs={{0,4},{4,8},{8,12},{1,5},{5,9},{9,13},{2,6},{6,10},{10,14},{3,7},{... | collective-permute-start | bytes 1671176 | tf_op jit(solution)/shard_map/ppermute | solution.py:243
  26.9 11.0 %collective-permute-done.1.refs_7_ = f32[8,136,128]{2,1,0:T(8,128)S(1)} collective-permute-done((f32[8,136,128]{2,1,0:T(8,128)S(1)}, f32[8,136,128]{2,1,0:T(8,128)S(1)}, u32[]{:S(2)}, u32[]{:S(2)}) %collective-permute-start.1) | collective-permute-done | bytes 557088 | tf_op jit(solution)/shard_map/ppermute | solution.py:243
  37.9 0.0 copy-start.1
  37.9 0.0 copy-done
  37.9 0.8 copy-done.1
  38.7 8.4 %shard_map.87 = (f32[1280,2]{1,0:T(8,128)}, bf16[8,5,128,128]{3,2,1,0:T(8,128)(2,1)}) custom-call(s32[5]{0:T(128)} %refs_0_.15, f32[8,1280,128]{2,1,0:T(8,128)} %shard_map.86.refs_1_.refs_2_, bf16[8,1280,128]{2,1,0:T(8,128)(2,1)} %refs_0_.14, bf16[8,1280,128]{2,1,0:T(8,128)(2,1)} %refs_4_.4, f32[8,1,128]{2,1,0:T(1,128)} %bitcast.3, ...), custom_call_target="tpu_custom_call" | custom-call | flops 335544320 | bytes 15546368 | tf_op jit(solution)/shard_map/pallas_call | solution.py:203
  47.1 1.3 %copy.17 = f32[2,1280]{1,0:T(2,128)S(1)} copy(f32[2,1280]{0,1:T(8,128)} %bitcast.2) | data formatting | bytes 20480 | tf_op jit(solution)/shard_map/transpose | solution.py:320
  48.4 0.1 collective-permute-start.4
  48.5 1.6 %collective-permute-start.3 = (f32[2560]{0:T(1024)S(1)}, f32[2560]{0:T(1024)S(1)}, u32[]{:S(2)}, u32[]{:S(2)}) collective-permute-start(f32[2560]{0:T(1024)S(1)} %reshape.13), channel_id=1, source_target_pairs={{0,2},{1,3},{2,0},{3,1},{4,6},{5,7},{6,4},{7,5},{8,10},{9,11},{10,... | collective-permute-start | bytes 30728 | tf_op jit(solution)/shard_map/ppermute | solution.py:323
  50.0 0.3 collective-permute-start.2
  50.3 1.3 %collective-permute-done.4 = f32[2560]{0:T(1024)S(1)} collective-permute-done((f32[2560]{0:T(1024)S(1)}, f32[2560]{0:T(1024)S(1)}, u32[]{:S(2)}, u32[]{:S(2)}) %collective-permute-start.4) | collective-permute-done | bytes 10272 | tf_op jit(solution)/shard_map/ppermute | solution.py:323
  51.7 0.6 collective-permute-done.3
  52.2 0.0 collective-permute-done.2
  52.3 1.1 copy.18.refs_6_
  53.4 6.7 %shard_map.88 = (bf16[8,1280,128]{2,1,0:T(8,128)(2,1)}, f32[8,5,128,128]{3,2,1,0:T(8,128)}, f32[4,136,128]{2,1,0:T(8,128)}) custom-call(s32[5]{0:T(128)} %refs_0_.15, bf16[8,1280,128]{2,1,0:T(8,128)(2,1)} %refs_0_.14, f32[8,1280,128]{2,1,0:T(8,128)} %shard_map.86.refs_1_.refs_2_, bf16[8,5,128,128]{3,2,1,0:T(8,128)(2,1)} %get-tuple-element.44.refs_3_.refs_4_, ...), custom_call_target="tpu_custom_call" | custom-call | flops 167772160 | bytes 8666112 | tf_op jit(solution)/shard_map/pallas_call | solution.py:203
  60.1 1.3 %collective-permute-start.5 = (f32[4,136,128]{2,1,0:T(8,128)}, f32[4,136,128]{2,1,0:T(8,128)S(1)}, u32[]{:S(2)}, u32[]{:S(2)}) collective-permute-start(f32[4,136,128]{2,1,0:T(8,128)} %get-tuple-element.46), channel_id=1, source_target_pairs={{4,0},{8,4},{12,8},{5,1},{9,5},{13,9},{6,2},{10,6},{14,10},{7,3},{... | collective-permute-start | bytes 835592 | tf_op jit(solution)/shard_map/ppermute | solution.py:231
  61.4 6.7 %shard_map.89 = (bf16[8,1280,128]{2,1,0:T(8,128)(2,1)}, f32[8,5,128,128]{3,2,1,0:T(8,128)}, f32[4,136,128]{2,1,0:T(8,128)}) custom-call(s32[5]{0:T(128)} %refs_0_.15, bf16[8,1280,128]{2,1,0:T(8,128)(2,1)} %refs_0_.14, f32[8,1280,128]{2,1,0:T(8,128)} %shard_map.86.refs_1_.refs_2_, ...), custom_call_target="tpu_custom_call", output_to_operand_aliasing={{0}: (7, {}), {1}: (8, {})} | custom-call | flops 167772160 | bytes 8666112 | tf_op jit(solution)/shard_map/pallas_call | solution.py:203
  68.2 3.8 %collective-permute-done.5 = f32[4,136,128]{2,1,0:T(8,128)S(1)} collective-permute-done((f32[4,136,128]{2,1,0:T(8,128)}, f32[4,136,128]{2,1,0:T(8,128)S(1)}, u32[]{:S(2)}, u32[]{:S(2)}) %collective-permute-start.5) | collective-permute-done | bytes 278560 | tf_op jit(solution)/shard_map/ppermute | solution.py:231
  71.9 1.3 %collective-permute-start.7 = (f32[4,136,128]{2,1,0:T(8,128)}, f32[4,136,128]{2,1,0:T(8,128)S(1)}, u32[]{:S(2)}, u32[]{:S(2)}) collective-permute-start(f32[4,136,128]{2,1,0:T(8,128)} %get-tuple-element.53), channel_id=1, source_target_pairs={{4,0},{8,4},{12,8},{5,1},{9,5},{13,9},{6,2},{10,6},{14,10},{7,3},{... | collective-permute-start | bytes 835592 | tf_op jit(solution)/shard_map/ppermute | solution.py:231
  73.2 1.3 %collective-permute-start.6 = (f32[4,136,128]{2,1,0:T(8,128)S(1)}, f32[4,136,128]{2,1,0:T(8,128)S(1)}, u32[]{:S(2)}, u32[]{:S(2)}) collective-permute-start(f32[4,136,128]{2,1,0:T(8,128)S(1)} %collective-permute-done.5), channel_id=1, source_target_pairs={{4,0},{8,4},{12,8},{5,1},{9,5},{13,9},{6,2},{10,6},{14,10},{7,3},{... | collective-permute-start | bytes 835592 | tf_op jit(solution)/shard_map/ppermute | solution.py:231
  74.5 10.1 %shard_map.90 = (bf16[8,1280,128]{2,1,0:T(8,128)(2,1)}, f32[8,1280,128]{2,1,0:T(8,128)}, f32[8,1280,128]{2,1,0:T(8,128)}) custom-call(bf16[8,1280,128]{2,1,0:T(8,128)(2,1)} %refs_0_.14, bf16[8,1280,128]{2,1,0:T(8,128)(2,1)} %refs_3_.3, bf16[8,1280,128]{2,1,0:T(8,128)(2,1)} %refs_4_.5, bf16[8,1280,128]{2,1,0:T(8,128)(2,1)} %get-tuple-element.54.refs_3_, ...), custom_call_target="tpu_custom_call" | custom-call | flops 1677721600 | bytes 12451840 | tf_op jit(solution)/shard_map/pallas_call | solution.py:203
  84.6 0.0 collective-permute-done.7
  84.6 3.8 %collective-permute-done.6 = f32[4,136,128]{2,1,0:T(8,128)S(1)} collective-permute-done((f32[4,136,128]{2,1,0:T(8,128)S(1)}, f32[4,136,128]{2,1,0:T(8,128)S(1)}, u32[]{:S(2)}, u32[]{:S(2)}) %collective-permute-start.6) | collective-permute-done | bytes 278560 | tf_op jit(solution)/shard_map/ppermute | solution.py:231
  88.4 1.5 %collective-permute-start.8 = (f32[4,136,128]{2,1,0:T(8,128)S(1)}, f32[4,136,128]{2,1,0:T(8,128)S(1)}, u32[]{:S(2)}, u32[]{:S(2)}) collective-permute-start(f32[4,136,128]{2,1,0:T(8,128)S(1)} %collective-permute-done.7), channel_id=1, source_target_pairs={{4,0},{8,4},{12,8},{5,1},{9,5},{13,9},{6,2},{10,6},{14,10},{7,3},{... | collective-permute-start | bytes 835592 | tf_op jit(solution)/shard_map/ppermute | solution.py:231
  89.8 0.9 pad_maximum_fusion.refs_6_
  90.7 10.1 %shard_map.91 = (bf16[8,1280,128]{2,1,0:T(8,128)(2,1)}, f32[8,1280,128]{2,1,0:T(8,128)}, f32[8,1280,128]{2,1,0:T(8,128)}) custom-call(bf16[8,1280,128]{2,1,0:T(8,128)(2,1)} %refs_0_.14, bf16[8,1280,128]{2,1,0:T(8,128)(2,1)} %refs_3_.3, bf16[8,1280,128]{2,1,0:T(8,128)(2,1)} %refs_4_.5, ...), custom_call_target="tpu_custom_call", output_to_operand_aliasing={{0}: (5, {}), {1}: (6, {}), {2}: (7, {})} | custom-call | flops 1677721600 | bytes 12451840 | tf_op jit(solution)/shard_map/pallas_call | solution.py:203
  100.8 0.0 collective-permute-done.8
  100.8 0.8 pad_maximum_fusion.1.refs_7_
  101.6 9.8 %shard_map.92 = (bf16[8,1280,128]{2,1,0:T(8,128)(2,1)}, bf16[8,1280,128]{2,1,0:T(8,128)(2,1)}) custom-call(s32[5]{0:T(128)} %refs_0_.15, f32[8,1280,128]{2,1,0:T(8,128)} %get-tuple-element.66.refs_1_, f32[8,1280,128]{2,1,0:T(8,128)} %get-tuple-element.67.refs_2_, bf16[8,1280,128]{2,1,0:T(8,128)(2,1)} %refs_3_.3, bf16[8,1280,128]{2,1,0:T(8,128)(2,1)} %refs_4_.5, ...), custom_call_target="tpu_custom_call" | custom-call | flops 671088640 | bytes 24707072 | tf_op jit(solution)/shard_map/pallas_call | solution.py:203
  (6 shorter events, 0.1 us)
Async XLA Ops:
  5.5 17.1 %collective-permute-start = (f32[8,136,128]{2,1,0:T(8,128)}, f32[8,136,128]{2,1,0:T(8,128)S(1)}, u32[]{:S(2)}, u32[]{:S(2)}) collective-permute-start(f32[8,136,128]{2,1,0:T(8,128)} %get-tuple-element.38), channel_id=1, source_target_pairs={{0,4},{4,8},{8,12},{1,5},{5,9},{9,13},{2,6},{6,10},{10,14},{3,7},{... | collective-permute-start | bytes 1671176 | tf_op jit(solution)/shard_map/ppermute | solution.py:243
  22.6 15.3 %copy-start = (f32[8,136,128]{2,1,0:T(8,128)}, f32[8,136,128]{2,1,0:T(8,128)S(1)}, u32[]{:S(2)}) copy-start(f32[8,136,128]{2,1,0:T(8,128)S(1)} %collective-permute-done.refs_6_) | copy-start | bytes 1671172
  22.6 15.3 %collective-permute-start.1 = (f32[8,136,128]{2,1,0:T(8,128)S(1)}, f32[8,136,128]{2,1,0:T(8,128)S(1)}, u32[]{:S(2)}, u32[]{:S(2)}) collective-permute-start(f32[8,136,128]{2,1,0:T(8,128)S(1)} %collective-permute-done.refs_6_), channel_id=1, source_target_pairs={{0,4},{4,8},{8,12},{1,5},{5,9},{9,13},{2,6},{6,10},{10,14},{3,7},{... | collective-permute-start | bytes 1671176 | tf_op jit(solution)/shard_map/ppermute | solution.py:243
  37.9 0.8 copy-start.1
  48.4 3.3 %collective-permute-start.4 = (f32[2560]{0:T(1024)S(1)}, f32[2560]{0:T(1024)S(1)}, u32[]{:S(2)}, u32[]{:S(2)}) collective-permute-start(f32[2560]{0:T(1024)S(1)} %reshape.13), channel_id=1, source_target_pairs={{0,3},{1,2},{2,1},{3,0},{4,7},{5,6},{6,5},{7,4},{8,11},{9,10},{10,... | collective-permute-start | bytes 30728 | tf_op jit(solution)/shard_map/ppermute | solution.py:323
  48.5 3.8 %collective-permute-start.3 = (f32[2560]{0:T(1024)S(1)}, f32[2560]{0:T(1024)S(1)}, u32[]{:S(2)}, u32[]{:S(2)}) collective-permute-start(f32[2560]{0:T(1024)S(1)} %reshape.13), channel_id=1, source_target_pairs={{0,2},{1,3},{2,0},{3,1},{4,6},{5,7},{6,4},{7,5},{8,10},{9,11},{10,... | collective-permute-start | bytes 30728 | tf_op jit(solution)/shard_map/ppermute | solution.py:323
  50.0 2.2 %collective-permute-start.2 = (f32[2560]{0:T(1024)S(1)}, f32[2560]{0:T(1024)S(1)}, u32[]{:S(2)}, u32[]{:S(2)}) collective-permute-start(f32[2560]{0:T(1024)S(1)} %reshape.13), channel_id=1, source_target_pairs={{0,1},{1,0},{2,3},{3,2},{4,5},{5,4},{6,7},{7,6},{8,9},{9,8},{10,11... | collective-permute-start | bytes 30728 | tf_op jit(solution)/shard_map/ppermute | solution.py:323
  60.1 11.8 %collective-permute-start.5 = (f32[4,136,128]{2,1,0:T(8,128)}, f32[4,136,128]{2,1,0:T(8,128)S(1)}, u32[]{:S(2)}, u32[]{:S(2)}) collective-permute-start(f32[4,136,128]{2,1,0:T(8,128)} %get-tuple-element.46), channel_id=1, source_target_pairs={{4,0},{8,4},{12,8},{5,1},{9,5},{13,9},{6,2},{10,6},{14,10},{7,3},{... | collective-permute-start | bytes 835592 | tf_op jit(solution)/shard_map/ppermute | solution.py:231
  71.9 12.7 %collective-permute-start.7 = (f32[4,136,128]{2,1,0:T(8,128)}, f32[4,136,128]{2,1,0:T(8,128)S(1)}, u32[]{:S(2)}, u32[]{:S(2)}) collective-permute-start(f32[4,136,128]{2,1,0:T(8,128)} %get-tuple-element.53), channel_id=1, source_target_pairs={{4,0},{8,4},{12,8},{5,1},{9,5},{13,9},{6,2},{10,6},{14,10},{7,3},{... | collective-permute-start | bytes 835592 | tf_op jit(solution)/shard_map/ppermute | solution.py:231
  73.2 15.1 %collective-permute-start.6 = (f32[4,136,128]{2,1,0:T(8,128)S(1)}, f32[4,136,128]{2,1,0:T(8,128)S(1)}, u32[]{:S(2)}, u32[]{:S(2)}) collective-permute-start(f32[4,136,128]{2,1,0:T(8,128)S(1)} %collective-permute-done.5), channel_id=1, source_target_pairs={{4,0},{8,4},{12,8},{5,1},{9,5},{13,9},{6,2},{10,6},{14,10},{7,3},{... | collective-permute-start | bytes 835592 | tf_op jit(solution)/shard_map/ppermute | solution.py:231
  88.4 12.4 %collective-permute-start.8 = (f32[4,136,128]{2,1,0:T(8,128)S(1)}, f32[4,136,128]{2,1,0:T(8,128)S(1)}, u32[]{:S(2)}, u32[]{:S(2)}) collective-permute-start(f32[4,136,128]{2,1,0:T(8,128)S(1)} %collective-permute-done.7), channel_id=1, source_target_pairs={{4,0},{8,4},{12,8},{5,1},{9,5},{13,9},{6,2},{10,6},{14,10},{7,3},{... | collective-permute-start | bytes 835592 | tf_op jit(solution)/shard_map/ppermute | solution.py:231

commit v21 on v19

--- a/solution.py
+++ b/solution.py
@@ -98,13 +98,19 @@
                 q_ref[j, rows, :], state, preferred_element_type=jnp.float32
             )
             scaled = n_ref[j] * g_ref[j, rows, :].astype(jnp.float32)
-            o_ref[rows, 0:1] += jnp.sum(raw * raw, axis=1, keepdims=True)
-            o_ref[rows, 1:2] += jnp.sum(scaled * raw, axis=1, keepdims=True)
+            lane = lax.broadcasted_iota(jnp.int32, raw.shape, 1)
+            tile = jnp.where(
+                lane == 0,
+                jnp.sum(raw * raw, axis=1, keepdims=True),
+                jnp.where(lane == 1, jnp.sum(scaled * raw, axis=1, keepdims=True), 0.0),
+            )
+            o_ref[:, rows] += tile.T[0:2, :]
 
 
 def grad_kernel(
     block_len, doc_ref, q_ref, i_ref, s_ref, g_ref, n_ref, c_ref, d_ref, suffix_ref, pay_ref
 ):
+    head_width = q_ref.shape[2]
     for j in range(q_ref.shape[0]):
         count = q_ref.shape[1] // block_len
         width = q_ref.shape[2]
@@ -114,8 +120,12 @@
             q = q_ref[j, rows, :]
             raw = i_ref[j, rows, :] + jnp.dot(q, s_ref[j, n], preferred_element_type=jnp.float32)
             scaled = n_ref[j] * g_ref[j, rows, :].astype(jnp.float32)
-            root_mean = c_ref[rows, 0:1]
-            factor = c_ref[rows, 1:2]
+            row = lax.broadcasted_iota(jnp.int32, (head_width, block_len), 0)
+            table = jnp.where(
+                row == 0, c_ref[0:1, rows], jnp.where(row == 1, c_ref[1:2, rows], 0.0)
+            ).T
+            root_mean = table[:, 0:1]
+            factor = table[:, 1:2]
             d = ((scaled - raw * factor) / root_mean).astype(jnp.bfloat16)
             d_ref[j, rows, :] = d
             parts.append(lax.dot_general(q, d, _ROWS_MAJOR, preferred_element_type=jnp.float32))
@@ -299,14 +309,14 @@
         functools.partial(forward_kernel, block_len),
         [(intra_part, True), (queries, True), (out_grad, True), (gain, True),
          (local_prefix, True), (prior[0], True), (prior[1], True)],
-        [(jax.ShapeDtypeStruct((tok_count, 2), jnp.float32), False),
+        [(jax.ShapeDtypeStruct((2, tok_count), jnp.float32), False),
          (jax.ShapeDtypeStruct(states.shape, jnp.bfloat16), True)],
         pair_flops // 2,
         scalars=doc_ids,
         per_step=4,
     )
     feature_count = head_count * head_width * lax.axis_size(("sub", "head"))
-    total_sums = local_sums.T.reshape(2 * tok_count)
+    total_sums = local_sums
     if lax.axis_size("head") == 2 and lax.axis_size("sub") == 2:
         partners = [
             lax.ppermute(total_sums, ("sub", "head"), [(k, k ^ flip) for k in range(4)])
@@ -315,10 +325,10 @@
         total_sums = (total_sums + partners[0]) + (partners[1] + partners[2])
     else:
         total_sums = lax.psum(total_sums, ("sub", "head"))
-    root_mean = jnp.sqrt(total_sums[:tok_count] / feature_count + 1e-06)
-    inner_mean = total_sums[tok_count:] / feature_count
+    root_mean = jnp.sqrt(total_sums[0] / feature_count + 1e-06)
+    inner_mean = total_sums[1] / feature_count
     factor = inner_mean / (root_mean * root_mean)
-    coefs = jnp.stack([root_mean, factor], axis=1)
+    coefs = jnp.stack([root_mean, factor], axis=0)
     d_attn, local_suffix, qd_payload = per_head_call(
         functools.partial(grad_kernel, block_len),
         [(queries, True), (intra_part, True), (preceding_states, True), (out_grad, True),

time: 109 us -> 109 us (level)
  local copies, waits for them, and re-layouts: 4.08 us -> 1.67 us
  other arithmetic: 0.03 us -> 1.36 us
  Pallas kernels: 61 us -> 62.2 us
    transpose x1 -> x0, local copies, waits for them, and re-layouts: 1.31 us -> none  [on_device(): total_sums = local_sums.T.reshape(2 * tok_count)]
    pallas_call x7, Pallas kernels: 61 us -> 62.2 us  [per_head_call(): pl.pallas_call(body, grid_spec=grid_spec, out_shape=[o for o, _ in output...]
    another operation x3 -> x0, local copies, waits for them, and re-layouts: 1.11 us -> none  [on_device(): coefs = jnp.stack([root_mean, factor], axis=1)]
where the time goes in v21:
time: 109 us
  Pallas kernels  62.2 us (57%)
  waiting for transfers between devices  29.1 us (27%)
  starting transfers between devices  13.9 us (13%)
  local copies, waits for them, and re-layouts  1.67 us (2%)
  other arithmetic  1.36 us (1%)
    pallas_call x7, Pallas kernels, per_head_call(): pl.pallas_call(body, grid_spec=grid_spec, out_shape=[o for o, _ in output...  62.2 us
    ppermute x4, waiting for transfers between devices, shift(): return lax.ppermute(value, axis, pairs)  27 us
    ppermute x4, starting transfers between devices, shift(): return lax.ppermute(value, axis, pairs)  12 us
  transfers between devices with their start and end apart: 7, of which 6 were waited for; matrix products, arithmetic and copies ran while one was open for 0% of the time, Pallas kernels for 25%

profile of v21, /device:TPU:0, one launch (start us, length us, event | category | flops | bytes accessed | tf_op | source)
XLA Modules:
  0.0 108.8 jit_solution(16065794277470165131)
XLA Ops:
  0.6 4.9 %shard_map.85 = (f32[8,5,128,128]{3,2,1,0:T(8,128)}, f32[8,136,128]{2,1,0:T(8,128)}) custom-call(s32[5]{0:T(128)} %refs_0_.13, bf16[8,1280,128]{2,1,0:T(8,128)(2,1)} %refs_3_.3, bf16[8,1280,128]{2,1,0:T(8,128)(2,1)} %refs_4_.3), custom_call_target="tpu_custom_call" | custom-call | flops 335544320 | bytes 8421376 | tf_op jit(solution)/shard_map/pallas_call | solution.py:211
  5.5 5.0 %collective-permute-start = (f32[8,136,128]{2,1,0:T(8,128)}, f32[8,136,128]{2,1,0:T(8,128)S(1)}, u32[]{:S(2)}, u32[]{:S(2)}) collective-permute-start(f32[8,136,128]{2,1,0:T(8,128)} %get-tuple-element.30), channel_id=1, source_target_pairs={{0,4},{4,8},{8,12},{1,5},{5,9},{9,13},{2,6},{6,10},{10,14},{3,7},{... | collective-permute-start | bytes 1671176 | tf_op jit(solution)/shard_map/ppermute | solution.py:242
  10.5 7.2 %shard_map.86.refs_1_.refs_2_ = f32[8,1280,128]{2,1,0:T(8,128)} custom-call(bf16[8,1280,128]{2,1,0:T(8,128)(2,1)} %refs_0_.12, bf16[8,1280,128]{2,1,0:T(8,128)(2,1)} %refs_3_.3, bf16[8,1280,128]{2,1,0:T(8,128)(2,1)} %refs_4_.3), custom_call_target="tpu_custom_call" | custom-call | flops 1342177280 | bytes 13107200 | tf_op jit(solution)/shard_map/pallas_call | solution.py:211
  17.6 5.0 %collective-permute-done.refs_6_ = f32[8,136,128]{2,1,0:T(8,128)S(1)} collective-permute-done((f32[8,136,128]{2,1,0:T(8,128)}, f32[8,136,128]{2,1,0:T(8,128)S(1)}, u32[]{:S(2)}, u32[]{:S(2)}) %collective-permute-start) | collective-permute-done | bytes 557088 | tf_op jit(solution)/shard_map/ppermute | solution.py:242
  22.6 0.0 copy-start.2
  22.6 4.3 %collective-permute-start.1 = (f32[8,136,128]{2,1,0:T(8,128)S(1)}, f32[8,136,128]{2,1,0:T(8,128)S(1)}, u32[]{:S(2)}, u32[]{:S(2)}) collective-permute-start(f32[8,136,128]{2,1,0:T(8,128)S(1)} %collective-permute-done.refs_6_), channel_id=1, source_target_pairs={{0,4},{4,8},{8,12},{1,5},{5,9},{9,13},{2,6},{6,10},{10,14},{3,7},{... | collective-permute-start | bytes 1671176 | tf_op jit(solution)/shard_map/ppermute | solution.py:242
  26.9 11.0 %collective-permute-done.1.refs_7_ = f32[8,136,128]{2,1,0:T(8,128)S(1)} collective-permute-done((f32[8,136,128]{2,1,0:T(8,128)S(1)}, f32[8,136,128]{2,1,0:T(8,128)S(1)}, u32[]{:S(2)}, u32[]{:S(2)}) %collective-permute-start.1) | collective-permute-done | bytes 557088 | tf_op jit(solution)/shard_map/ppermute | solution.py:242
  37.9 0.0 copy-start.3
  37.9 0.0 copy-done.2
  37.9 0.8 copy-done.3
  38.7 8.9 %shard_map.87 = (f32[2,1280]{1,0:T(2,128)}, bf16[8,5,128,128]{3,2,1,0:T(8,128)(2,1)}) custom-call(s32[5]{0:T(128)} %refs_0_.13, f32[8,1280,128]{2,1,0:T(8,128)} %shard_map.86.refs_1_.refs_2_, bf16[8,1280,128]{2,1,0:T(8,128)(2,1)} %refs_0_.12, bf16[8,1280,128]{2,1,0:T(8,128)(2,1)} %refs_4_.2, f32[8,1,128]{2,1,0:T(1,128)} %bitcast.1, ...), custom_call_target="tpu_custom_call" | custom-call | flops 335544320 | bytes 15546368 | tf_op jit(solution)/shard_map/pallas_call | solution.py:211
  47.6 0.0 collective-permute-start.4
  47.6 1.6 %collective-permute-start.3 = (f32[2,1280]{1,0:T(2,128)}, f32[2,1280]{1,0:T(2,128)S(1)}, u32[]{:S(2)}, u32[]{:S(2)}) collective-permute-start(f32[2,1280]{1,0:T(2,128)} %get-tuple-element.37), channel_id=1, source_target_pairs={{0,2},{1,3},{2,0},{3,1},{4,6},{5,7},{6,4},{7,5},{8,10},{9,11},{10,... | collective-permute-start | bytes 30728 | tf_op jit(solution)/shard_map/ppermute | solution.py:322
  49.2 0.3 collective-permute-start.2
  49.5 1.5 %collective-permute-done.4 = f32[2,1280]{1,0:T(2,128)S(1)} collective-permute-done((f32[2,1280]{1,0:T(2,128)}, f32[2,1280]{1,0:T(2,128)S(1)}, u32[]{:S(2)}, u32[]{:S(2)}) %collective-permute-start.4) | collective-permute-done | bytes 10272 | tf_op jit(solution)/shard_map/ppermute | solution.py:322
  51.0 0.6 collective-permute-done.3
  51.6 0.0 collective-permute-done.2
  51.6 0.7 add_add_fusion
  52.4 0.6 pad_maximum_fusion.refs_6_
  53.0 11.2 %shard_map.88 = (bf16[8,1280,128]{2,1,0:T(8,128)(2,1)}, f32[8,5,128,128]{3,2,1,0:T(8,128)}, f32[8,136,128]{2,1,0:T(8,128)}) custom-call(s32[5]{0:T(128)} %refs_0_.13, bf16[8,1280,128]{2,1,0:T(8,128)(2,1)} %refs_0_.12, f32[8,1280,128]{2,1,0:T(8,128)} %shard_map.86.refs_1_.refs_2_, bf16[8,5,128,128]{3,2,1,0:T(8,128)(2,1)} %get-tuple-element.36.refs_3_.refs_4_, ...), custom_call_target="tpu_custom_call" | custom-call | flops 335544320 | bytes 17610752 | tf_op jit(solution)/shard_map/pallas_call | solution.py:211
  64.2 1.3 %collective-permute-start.5 = (f32[8,136,128]{2,1,0:T(8,128)}, f32[8,136,128]{2,1,0:T(8,128)S(1)}, u32[]{:S(2)}, u32[]{:S(2)}) collective-permute-start(f32[8,136,128]{2,1,0:T(8,128)} %get-tuple-element.38), channel_id=1, source_target_pairs={{4,0},{8,4},{12,8},{5,1},{9,5},{13,9},{6,2},{10,6},{14,10},{7,3},{... | collective-permute-start | bytes 1671176 | tf_op jit(solution)/shard_map/ppermute | solution.py:242
  65.5 10.1 %shard_map.89 = (bf16[8,1280,128]{2,1,0:T(8,128)(2,1)}, f32[8,1280,128]{2,1,0:T(8,128)}, f32[8,1280,128]{2,1,0:T(8,128)}) custom-call(bf16[8,1280,128]{2,1,0:T(8,128)(2,1)} %refs_0_.12, bf16[8,1280,128]{2,1,0:T(8,128)(2,1)} %refs_3_.3, bf16[8,1280,128]{2,1,0:T(8,128)(2,1)} %refs_4_.3, bf16[8,1280,128]{2,1,0:T(8,128)(2,1)} %get-tuple-element.39.refs_3_, ...), custom_call_target="tpu_custom_call" | custom-call | flops 1677721600 | bytes 12451840 | tf_op jit(solution)/shard_map/pallas_call | solution.py:211
  75.6 6.4 %collective-permute-done.5.refs_6_ = f32[8,136,128]{2,1,0:T(8,128)S(1)} collective-permute-done((f32[8,136,128]{2,1,0:T(8,128)}, f32[8,136,128]{2,1,0:T(8,128)S(1)}, u32[]{:S(2)}, u32[]{:S(2)}) %collective-permute-start.5) | collective-permute-done | bytes 557088 | tf_op jit(solution)/shard_map/ppermute | solution.py:242
  81.9 0.0 copy-start
  81.9 1.5 %collective-permute-start.6 = (f32[8,136,128]{2,1,0:T(8,128)S(1)}, f32[8,136,128]{2,1,0:T(8,128)S(1)}, u32[]{:S(2)}, u32[]{:S(2)}) collective-permute-start(f32[8,136,128]{2,1,0:T(8,128)S(1)} %collective-permute-done.5.refs_6_), channel_id=1, source_target_pairs={{4,0},{8,4},{12,8},{5,1},{9,5},{13,9},{6,2},{10,6},{14,10},{7,3},{... | collective-permute-start | bytes 1671176 | tf_op jit(solution)/shard_map/ppermute | solution.py:242
  83.4 10.1 %shard_map.90 = (bf16[8,1280,128]{2,1,0:T(8,128)(2,1)}, f32[8,1280,128]{2,1,0:T(8,128)}, f32[8,1280,128]{2,1,0:T(8,128)}) custom-call(bf16[8,1280,128]{2,1,0:T(8,128)(2,1)} %refs_0_.12, bf16[8,1280,128]{2,1,0:T(8,128)(2,1)} %refs_3_.3, bf16[8,1280,128]{2,1,0:T(8,128)(2,1)} %refs_4_.3, ...), custom_call_target="tpu_custom_call", output_to_operand_aliasing={{0}: (5, {}), {1}: (6, {}), {2}: (7, {})} | custom-call | flops 1677721600 | bytes 12451840 | tf_op jit(solution)/shard_map/pallas_call | solution.py:211
  93.5 0.0 copy-done
  93.5 4.7 %collective-permute-done.6.refs_7_ = f32[8,136,128]{2,1,0:T(8,128)S(1)} collective-permute-done((f32[8,136,128]{2,1,0:T(8,128)S(1)}, f32[8,136,128]{2,1,0:T(8,128)S(1)}, u32[]{:S(2)}, u32[]{:S(2)}) %collective-permute-start.6) | collective-permute-done | bytes 557088 | tf_op jit(solution)/shard_map/ppermute | solution.py:242
  98.2 0.0 copy-start.1
  98.2 0.8 copy-done.1
  99.0 9.8 %shard_map.91 = (bf16[8,1280,128]{2,1,0:T(8,128)(2,1)}, bf16[8,1280,128]{2,1,0:T(8,128)(2,1)}) custom-call(s32[5]{0:T(128)} %refs_0_.13, f32[8,1280,128]{2,1,0:T(8,128)} %get-tuple-element.51.refs_1_, f32[8,1280,128]{2,1,0:T(8,128)} %get-tuple-element.52.refs_2_, bf16[8,1280,128]{2,1,0:T(8,128)(2,1)} %refs_3_.3, bf16[8,1280,128]{2,1,0:T(8,128)(2,1)} %refs_4_.3, ...), custom_call_target="tpu_custom_call" | custom-call | flops 671088640 | bytes 24707072 | tf_op jit(solution)/shard_map/pallas_call | solution.py:211
  (1 shorter events, 0.0 us)
Async XLA Ops:
  5.5 17.1 %collective-permute-start = (f32[8,136,128]{2,1,0:T(8,128)}, f32[8,136,128]{2,1,0:T(8,128)S(1)}, u32[]{:S(2)}, u32[]{:S(2)}) collective-permute-start(f32[8,136,128]{2,1,0:T(8,128)} %get-tuple-element.30), channel_id=1, source_target_pairs={{0,4},{4,8},{8,12},{1,5},{5,9},{9,13},{2,6},{6,10},{10,14},{3,7},{... | collective-permute-start | bytes 1671176 | tf_op jit(solution)/shard_map/ppermute | solution.py:242
  22.6 15.3 %copy-start.2 = (f32[8,136,128]{2,1,0:T(8,128)}, f32[8,136,128]{2,1,0:T(8,128)S(1)}, u32[]{:S(2)}) copy-start(f32[8,136,128]{2,1,0:T(8,128)S(1)} %collective-permute-done.refs_6_) | copy-start | bytes 1671172
  22.6 15.3 %collective-permute-start.1 = (f32[8,136,128]{2,1,0:T(8,128)S(1)}, f32[8,136,128]{2,1,0:T(8,128)S(1)}, u32[]{:S(2)}, u32[]{:S(2)}) collective-permute-start(f32[8,136,128]{2,1,0:T(8,128)S(1)} %collective-permute-done.refs_6_), channel_id=1, source_target_pairs={{0,4},{4,8},{8,12},{1,5},{5,9},{9,13},{2,6},{6,10},{10,14},{3,7},{... | collective-permute-start | bytes 1671176 | tf_op jit(solution)/shard_map/ppermute | solution.py:242
  37.9 0.8 copy-start.3
  47.6 3.4 %collective-permute-start.4 = (f32[2,1280]{1,0:T(2,128)}, f32[2,1280]{1,0:T(2,128)S(1)}, u32[]{:S(2)}, u32[]{:S(2)}) collective-permute-start(f32[2,1280]{1,0:T(2,128)} %get-tuple-element.37), channel_id=1, source_target_pairs={{0,3},{1,2},{2,1},{3,0},{4,7},{5,6},{6,5},{7,4},{8,11},{9,10},{10,... | collective-permute-start | bytes 30728 | tf_op jit(solution)/shard_map/ppermute | solution.py:322
  47.6 3.9 %collective-permute-start.3 = (f32[2,1280]{1,0:T(2,128)}, f32[2,1280]{1,0:T(2,128)S(1)}, u32[]{:S(2)}, u32[]{:S(2)}) collective-permute-start(f32[2,1280]{1,0:T(2,128)} %get-tuple-element.37), channel_id=1, source_target_pairs={{0,2},{1,3},{2,0},{3,1},{4,6},{5,7},{6,4},{7,5},{8,10},{9,11},{10,... | collective-permute-start | bytes 30728 | tf_op jit(solution)/shard_map/ppermute | solution.py:322
  49.2 2.4 %collective-permute-start.2 = (f32[2,1280]{1,0:T(2,128)}, f32[2,1280]{1,0:T(2,128)S(1)}, u32[]{:S(2)}, u32[]{:S(2)}) collective-permute-start(f32[2,1280]{1,0:T(2,128)} %get-tuple-element.37), channel_id=1, source_target_pairs={{0,1},{1,0},{2,3},{3,2},{4,5},{5,4},{6,7},{7,6},{8,9},{9,8},{10,11... | collective-permute-start | bytes 30728 | tf_op jit(solution)/shard_map/ppermute | solution.py:322
  64.2 17.8 %collective-permute-start.5 = (f32[8,136,128]{2,1,0:T(8,128)}, f32[8,136,128]{2,1,0:T(8,128)S(1)}, u32[]{:S(2)}, u32[]{:S(2)}) collective-permute-start(f32[8,136,128]{2,1,0:T(8,128)} %get-tuple-element.38), channel_id=1, source_target_pairs={{4,0},{8,4},{12,8},{5,1},{9,5},{13,9},{6,2},{10,6},{14,10},{7,3},{... | collective-permute-start | bytes 1671176 | tf_op jit(solution)/shard_map/ppermute | solution.py:242
  81.9 11.6 %copy-start = (f32[8,136,128]{2,1,0:T(8,128)}, f32[8,136,128]{2,1,0:T(8,128)S(1)}, u32[]{:S(2)}) copy-start(f32[8,136,128]{2,1,0:T(8,128)S(1)} %collective-permute-done.5.refs_6_) | copy-start | bytes 1671172
  81.9 16.2 %collective-permute-start.6 = (f32[8,136,128]{2,1,0:T(8,128)S(1)}, f32[8,136,128]{2,1,0:T(8,128)S(1)}, u32[]{:S(2)}, u32[]{:S(2)}) collective-permute-start(f32[8,136,128]{2,1,0:T(8,128)S(1)} %collective-permute-done.5.refs_6_), channel_id=1, source_target_pairs={{4,0},{8,4},{12,8},{5,1},{9,5},{13,9},{6,2},{10,6},{14,10},{7,3},{... | collective-permute-start | bytes 1671176 | tf_op jit(solution)/shard_map/ppermute | solution.py:242
  98.2 0.8 copy-start.1

commit v22 on v19

--- a/solution.py
+++ b/solution.py
@@ -116,7 +116,8 @@
             scaled = n_ref[j] * g_ref[j, rows, :].astype(jnp.float32)
             root_mean = c_ref[rows, 0:1]
             factor = c_ref[rows, 1:2]
-            d = ((scaled - raw * factor) / root_mean).astype(jnp.bfloat16)
+            inverse = 1.0 / root_mean
+            d = ((scaled - raw * factor) * inverse).astype(jnp.bfloat16)
             d_ref[j, rows, :] = d
             parts.append(lax.dot_general(q, d, _ROWS_MAJOR, preferred_element_type=jnp.float32))
         for b in range(count):

time: 109 us -> 109 us (level)
  no operation moved by 1% of the time
where the time goes in v22:
time: 109 us
  Pallas kernels  61 us (56%)
  waiting for transfers between devices  28.9 us (27%)
  starting transfers between devices  13.9 us (13%)
  local copies, waits for them, and re-layouts  4.08 us (4%)
    pallas_call x7, Pallas kernels, per_head_call(): pl.pallas_call(body, grid_spec=grid_spec, out_shape=[o for o, _ in output...  61 us
    ppermute x4, waiting for transfers between devices, shift(): return lax.ppermute(value, axis, pairs)  27 us
    ppermute x4, starting transfers between devices, shift(): return lax.ppermute(value, axis, pairs)  12 us
  transfers between devices with their start and end apart: 7, of which 6 were waited for; matrix products, arithmetic and copies ran while one was open for 0% of the time, Pallas kernels for 25%

profile of v22, /device:TPU:0, one launch (start us, length us, event | category | flops | bytes accessed | tf_op | source)
XLA Modules:
  0.0 108.6 jit_solution(7927349434156371089)
XLA Ops:
  0.6 4.9 %shard_map.85 = (f32[8,5,128,128]{3,2,1,0:T(8,128)}, f32[8,136,128]{2,1,0:T(8,128)}) custom-call(s32[5]{0:T(128)} %refs_0_.13, bf16[8,1280,128]{2,1,0:T(8,128)(2,1)} %refs_3_.3, bf16[8,1280,128]{2,1,0:T(8,128)(2,1)} %refs_4_.3), custom_call_target="tpu_custom_call" | custom-call | flops 335544320 | bytes 8421376 | tf_op jit(solution)/shard_map/pallas_call | solution.py:202
  5.5 5.0 %collective-permute-start = (f32[8,136,128]{2,1,0:T(8,128)}, f32[8,136,128]{2,1,0:T(8,128)S(1)}, u32[]{:S(2)}, u32[]{:S(2)}) collective-permute-start(f32[8,136,128]{2,1,0:T(8,128)} %get-tuple-element.30), channel_id=1, source_target_pairs={{0,4},{4,8},{8,12},{1,5},{5,9},{9,13},{2,6},{6,10},{10,14},{3,7},{... | collective-permute-start | bytes 1671176 | tf_op jit(solution)/shard_map/ppermute | solution.py:233
  10.5 7.2 %shard_map.86.refs_1_.refs_2_ = f32[8,1280,128]{2,1,0:T(8,128)} custom-call(bf16[8,1280,128]{2,1,0:T(8,128)(2,1)} %refs_0_.12, bf16[8,1280,128]{2,1,0:T(8,128)(2,1)} %refs_3_.3, bf16[8,1280,128]{2,1,0:T(8,128)(2,1)} %refs_4_.3), custom_call_target="tpu_custom_call" | custom-call | flops 1342177280 | bytes 13107200 | tf_op jit(solution)/shard_map/pallas_call | solution.py:202
  17.6 5.0 %collective-permute-done.refs_6_ = f32[8,136,128]{2,1,0:T(8,128)S(1)} collective-permute-done((f32[8,136,128]{2,1,0:T(8,128)}, f32[8,136,128]{2,1,0:T(8,128)S(1)}, u32[]{:S(2)}, u32[]{:S(2)}) %collective-permute-start) | collective-permute-done | bytes 557088 | tf_op jit(solution)/shard_map/ppermute | solution.py:233
  22.6 0.0 copy-start.2
  22.6 4.3 %collective-permute-start.1 = (f32[8,136,128]{2,1,0:T(8,128)S(1)}, f32[8,136,128]{2,1,0:T(8,128)S(1)}, u32[]{:S(2)}, u32[]{:S(2)}) collective-permute-start(f32[8,136,128]{2,1,0:T(8,128)S(1)} %collective-permute-done.refs_6_), channel_id=1, source_target_pairs={{0,4},{4,8},{8,12},{1,5},{5,9},{9,13},{2,6},{6,10},{10,14},{3,7},{... | collective-permute-start | bytes 1671176 | tf_op jit(solution)/shard_map/ppermute | solution.py:233
  26.9 11.0 %collective-permute-done.1.refs_7_ = f32[8,136,128]{2,1,0:T(8,128)S(1)} collective-permute-done((f32[8,136,128]{2,1,0:T(8,128)S(1)}, f32[8,136,128]{2,1,0:T(8,128)S(1)}, u32[]{:S(2)}, u32[]{:S(2)}) %collective-permute-start.1) | collective-permute-done | bytes 557088 | tf_op jit(solution)/shard_map/ppermute | solution.py:233
  37.9 0.0 copy-start.3
  37.9 0.0 copy-done.2
  37.9 0.8 copy-done.3
  38.7 8.4 %shard_map.87 = (f32[1280,2]{1,0:T(8,128)}, bf16[8,5,128,128]{3,2,1,0:T(8,128)(2,1)}) custom-call(s32[5]{0:T(128)} %refs_0_.13, f32[8,1280,128]{2,1,0:T(8,128)} %shard_map.86.refs_1_.refs_2_, bf16[8,1280,128]{2,1,0:T(8,128)(2,1)} %refs_0_.12, bf16[8,1280,128]{2,1,0:T(8,128)(2,1)} %refs_4_.2, f32[8,1,128]{2,1,0:T(1,128)} %bitcast.3, ...), custom_call_target="tpu_custom_call" | custom-call | flops 335544320 | bytes 15546368 | tf_op jit(solution)/shard_map/pallas_call | solution.py:202
  47.1 1.3 %copy.15 = f32[2,1280]{1,0:T(2,128)S(1)} copy(f32[2,1280]{0,1:T(8,128)} %bitcast.2) | data formatting | bytes 20480 | tf_op jit(solution)/shard_map/transpose | solution.py:310
  48.4 0.1 collective-permute-start.4
  48.5 1.6 %collective-permute-start.3 = (f32[2560]{0:T(1024)S(1)}, f32[2560]{0:T(1024)S(1)}, u32[]{:S(2)}, u32[]{:S(2)}) collective-permute-start(f32[2560]{0:T(1024)S(1)} %reshape.13), channel_id=1, source_target_pairs={{0,2},{1,3},{2,0},{3,1},{4,6},{5,7},{6,4},{7,5},{8,10},{9,11},{10,... | collective-permute-start | bytes 30728 | tf_op jit(solution)/shard_map/ppermute | solution.py:313
  50.0 0.3 collective-permute-start.2
  50.3 1.3 %collective-permute-done.4 = f32[2560]{0:T(1024)S(1)} collective-permute-done((f32[2560]{0:T(1024)S(1)}, f32[2560]{0:T(1024)S(1)}, u32[]{:S(2)}, u32[]{:S(2)}) %collective-permute-start.4) | collective-permute-done | bytes 10272 | tf_op jit(solution)/shard_map/ppermute | solution.py:313
  51.7 0.6 collective-permute-done.3
  52.2 0.0 collective-permute-done.2
  52.3 1.1 %copy.16.refs_6_ = f32[1280,2]{1,0:T(8,128)} copy(f32[1280,2]{0,1:T(2,128)S(1)} %pad_maximum_fusion) | data formatting | bytes 20480 | tf_op jit(solution)/shard_map/stack | solution.py:322
  53.4 10.6 %shard_map.88 = (bf16[8,1280,128]{2,1,0:T(8,128)(2,1)}, f32[8,5,128,128]{3,2,1,0:T(8,128)}, f32[8,136,128]{2,1,0:T(8,128)}) custom-call(s32[5]{0:T(128)} %refs_0_.13, bf16[8,1280,128]{2,1,0:T(8,128)(2,1)} %refs_0_.12, f32[8,1280,128]{2,1,0:T(8,128)} %shard_map.86.refs_1_.refs_2_, bf16[8,5,128,128]{3,2,1,0:T(8,128)(2,1)} %get-tuple-element.36.refs_3_.refs_4_, ...), custom_call_target="tpu_custom_call" | custom-call | flops 335544320 | bytes 17610752 | tf_op jit(solution)/shard_map/pallas_call | solution.py:202
  64.0 1.3 %collective-permute-start.5 = (f32[8,136,128]{2,1,0:T(8,128)}, f32[8,136,128]{2,1,0:T(8,128)S(1)}, u32[]{:S(2)}, u32[]{:S(2)}) collective-permute-start(f32[8,136,128]{2,1,0:T(8,128)} %get-tuple-element.38), channel_id=1, source_target_pairs={{4,0},{8,4},{12,8},{5,1},{9,5},{13,9},{6,2},{10,6},{14,10},{7,3},{... | collective-permute-start | bytes 1671176 | tf_op jit(solution)/shard_map/ppermute | solution.py:233
  65.3 10.1 %shard_map.89 = (bf16[8,1280,128]{2,1,0:T(8,128)(2,1)}, f32[8,1280,128]{2,1,0:T(8,128)}, f32[8,1280,128]{2,1,0:T(8,128)}) custom-call(bf16[8,1280,128]{2,1,0:T(8,128)(2,1)} %refs_0_.12, bf16[8,1280,128]{2,1,0:T(8,128)(2,1)} %refs_3_.3, bf16[8,1280,128]{2,1,0:T(8,128)(2,1)} %refs_4_.3, bf16[8,1280,128]{2,1,0:T(8,128)(2,1)} %get-tuple-element.39.refs_3_, ...), custom_call_target="tpu_custom_call" | custom-call | flops 1677721600 | bytes 12451840 | tf_op jit(solution)/shard_map/pallas_call | solution.py:202
  75.3 6.4 %collective-permute-done.5.refs_6_ = f32[8,136,128]{2,1,0:T(8,128)S(1)} collective-permute-done((f32[8,136,128]{2,1,0:T(8,128)}, f32[8,136,128]{2,1,0:T(8,128)S(1)}, u32[]{:S(2)}, u32[]{:S(2)}) %collective-permute-start.5) | collective-permute-done | bytes 557088 | tf_op jit(solution)/shard_map/ppermute | solution.py:233
  81.7 0.0 copy-start
  81.7 1.5 %collective-permute-start.6 = (f32[8,136,128]{2,1,0:T(8,128)S(1)}, f32[8,136,128]{2,1,0:T(8,128)S(1)}, u32[]{:S(2)}, u32[]{:S(2)}) collective-permute-start(f32[8,136,128]{2,1,0:T(8,128)S(1)} %collective-permute-done.5.refs_6_), channel_id=1, source_target_pairs={{4,0},{8,4},{12,8},{5,1},{9,5},{13,9},{6,2},{10,6},{14,10},{7,3},{... | collective-permute-start | bytes 1671176 | tf_op jit(solution)/shard_map/ppermute | solution.py:233
  83.2 10.1 %shard_map.90 = (bf16[8,1280,128]{2,1,0:T(8,128)(2,1)}, f32[8,1280,128]{2,1,0:T(8,128)}, f32[8,1280,128]{2,1,0:T(8,128)}) custom-call(bf16[8,1280,128]{2,1,0:T(8,128)(2,1)} %refs_0_.12, bf16[8,1280,128]{2,1,0:T(8,128)(2,1)} %refs_3_.3, bf16[8,1280,128]{2,1,0:T(8,128)(2,1)} %refs_4_.3, ...), custom_call_target="tpu_custom_call", output_to_operand_aliasing={{0}: (5, {}), {1}: (6, {}), {2}: (7, {})} | custom-call | flops 1677721600 | bytes 12451840 | tf_op jit(solution)/shard_map/pallas_call | solution.py:202
  93.3 0.0 copy-done
  93.3 4.7 %collective-permute-done.6.refs_7_ = f32[8,136,128]{2,1,0:T(8,128)S(1)} collective-permute-done((f32[8,136,128]{2,1,0:T(8,128)S(1)}, f32[8,136,128]{2,1,0:T(8,128)S(1)}, u32[]{:S(2)}, u32[]{:S(2)}) %collective-permute-start.6) | collective-permute-done | bytes 557088 | tf_op jit(solution)/shard_map/ppermute | solution.py:233
  98.0 0.0 copy-start.1
  98.0 0.8 copy-done.1
  98.8 9.8 %shard_map.91 = (bf16[8,1280,128]{2,1,0:T(8,128)(2,1)}, bf16[8,1280,128]{2,1,0:T(8,128)(2,1)}) custom-call(s32[5]{0:T(128)} %refs_0_.13, f32[8,1280,128]{2,1,0:T(8,128)} %get-tuple-element.51.refs_1_, f32[8,1280,128]{2,1,0:T(8,128)} %get-tuple-element.52.refs_2_, bf16[8,1280,128]{2,1,0:T(8,128)(2,1)} %refs_3_.3, bf16[8,1280,128]{2,1,0:T(8,128)(2,1)} %refs_4_.3, ...), custom_call_target="tpu_custom_call" | custom-call | flops 671088640 | bytes 24707072 | tf_op jit(solution)/shard_map/pallas_call | solution.py:202
  (6 shorter events, 0.1 us)
Async XLA Ops:
  5.5 17.1 %collective-permute-start = (f32[8,136,128]{2,1,0:T(8,128)}, f32[8,136,128]{2,1,0:T(8,128)S(1)}, u32[]{:S(2)}, u32[]{:S(2)}) collective-permute-start(f32[8,136,128]{2,1,0:T(8,128)} %get-tuple-element.30), channel_id=1, source_target_pairs={{0,4},{4,8},{8,12},{1,5},{5,9},{9,13},{2,6},{6,10},{10,14},{3,7},{... | collective-permute-start | bytes 1671176 | tf_op jit(solution)/shard_map/ppermute | solution.py:233
  22.6 15.3 %copy-start.2 = (f32[8,136,128]{2,1,0:T(8,128)}, f32[8,136,128]{2,1,0:T(8,128)S(1)}, u32[]{:S(2)}) copy-start(f32[8,136,128]{2,1,0:T(8,128)S(1)} %collective-permute-done.refs_6_) | copy-start | bytes 1671172
  22.6 15.3 %collective-permute-start.1 = (f32[8,136,128]{2,1,0:T(8,128)S(1)}, f32[8,136,128]{2,1,0:T(8,128)S(1)}, u32[]{:S(2)}, u32[]{:S(2)}) collective-permute-start(f32[8,136,128]{2,1,0:T(8,128)S(1)} %collective-permute-done.refs_6_), channel_id=1, source_target_pairs={{0,4},{4,8},{8,12},{1,5},{5,9},{9,13},{2,6},{6,10},{10,14},{3,7},{... | collective-permute-start | bytes 1671176 | tf_op jit(solution)/shard_map/ppermute | solution.py:233
  37.9 0.8 copy-start.3
  48.4 3.3 %collective-permute-start.4 = (f32[2560]{0:T(1024)S(1)}, f32[2560]{0:T(1024)S(1)}, u32[]{:S(2)}, u32[]{:S(2)}) collective-permute-start(f32[2560]{0:T(1024)S(1)} %reshape.13), channel_id=1, source_target_pairs={{0,3},{1,2},{2,1},{3,0},{4,7},{5,6},{6,5},{7,4},{8,11},{9,10},{10,... | collective-permute-start | bytes 30728 | tf_op jit(solution)/shard_map/ppermute | solution.py:313
  48.5 3.8 %collective-permute-start.3 = (f32[2560]{0:T(1024)S(1)}, f32[2560]{0:T(1024)S(1)}, u32[]{:S(2)}, u32[]{:S(2)}) collective-permute-start(f32[2560]{0:T(1024)S(1)} %reshape.13), channel_id=1, source_target_pairs={{0,2},{1,3},{2,0},{3,1},{4,6},{5,7},{6,4},{7,5},{8,10},{9,11},{10,... | collective-permute-start | bytes 30728 | tf_op jit(solution)/shard_map/ppermute | solution.py:313
  50.0 2.2 %collective-permute-start.2 = (f32[2560]{0:T(1024)S(1)}, f32[2560]{0:T(1024)S(1)}, u32[]{:S(2)}, u32[]{:S(2)}) collective-permute-start(f32[2560]{0:T(1024)S(1)} %reshape.13), channel_id=1, source_target_pairs={{0,1},{1,0},{2,3},{3,2},{4,5},{5,4},{6,7},{7,6},{8,9},{9,8},{10,11... | collective-permute-start | bytes 30728 | tf_op jit(solution)/shard_map/ppermute | solution.py:313
  64.0 17.8 %collective-permute-start.5 = (f32[8,136,128]{2,1,0:T(8,128)}, f32[8,136,128]{2,1,0:T(8,128)S(1)}, u32[]{:S(2)}, u32[]{:S(2)}) collective-permute-start(f32[8,136,128]{2,1,0:T(8,128)} %get-tuple-element.38), channel_id=1, source_target_pairs={{4,0},{8,4},{12,8},{5,1},{9,5},{13,9},{6,2},{10,6},{14,10},{7,3},{... | collective-permute-start | bytes 1671176 | tf_op jit(solution)/shard_map/ppermute | solution.py:233
  81.7 11.6 %copy-start = (f32[8,136,128]{2,1,0:T(8,128)}, f32[8,136,128]{2,1,0:T(8,128)S(1)}, u32[]{:S(2)}) copy-start(f32[8,136,128]{2,1,0:T(8,128)S(1)} %collective-permute-done.5.refs_6_) | copy-start | bytes 1671172
  81.7 16.2 %collective-permute-start.6 = (f32[8,136,128]{2,1,0:T(8,128)S(1)}, f32[8,136,128]{2,1,0:T(8,128)S(1)}, u32[]{:S(2)}, u32[]{:S(2)}) collective-permute-start(f32[8,136,128]{2,1,0:T(8,128)S(1)} %collective-permute-done.5.refs_6_), channel_id=1, source_target_pairs={{4,0},{8,4},{12,8},{5,1},{9,5},{13,9},{6,2},{10,6},{14,10},{7,3},{... | collective-permute-start | bytes 1671176 | tf_op jit(solution)/shard_map/ppermute | solution.py:233
  98.0 0.8 copy-start.1

commit v23 on v19

--- a/solution.py
+++ b/solution.py
@@ -277,7 +277,7 @@
         [(states, True), (payload, True)],
         pair_flops // 2,
         scalars=doc_ids,
-        per_step=4,
+        per_step=8,
     )
     prior, intra_part = carry(
         kv_payload,

time: 109 us -> 110 us (level)
  no operation moved by 1% of the time
where the time goes in v23:
time: 110 us; the launch traced here: 109 us
  Pallas kernels  61.8 us (56%)
  waiting for transfers between devices  28.9 us (26%)
  starting transfers between devices  13.9 us (13%)
  local copies, waits for them, and re-layouts  4.08 us (4%)
    pallas_call x7, Pallas kernels, per_head_call(): pl.pallas_call(body, grid_spec=grid_spec, out_shape=[o for o, _ in output...  61.8 us
    ppermute x4, waiting for transfers between devices, shift(): return lax.ppermute(value, axis, pairs)  27 us
    ppermute x4, starting transfers between devices, shift(): return lax.ppermute(value, axis, pairs)  12 us
  transfers between devices with their start and end apart: 7, of which 6 were waited for; matrix products, arithmetic and copies ran while one was open for 0% of the time, Pallas kernels for 25%

profile of v23, /device:TPU:0, one launch (start us, length us, event | category | flops | bytes accessed | tf_op | source)
XLA Modules:
  0.0 109.5 jit_solution(8561928380690020638)
XLA Ops:
  0.6 5.8 %shard_map.85 = (f32[8,5,128,128]{3,2,1,0:T(8,128)}, f32[8,136,128]{2,1,0:T(8,128)}) custom-call(s32[5]{0:T(128)} %refs_0_.13, bf16[8,1280,128]{2,1,0:T(8,128)(2,1)} %refs_3_.3, bf16[8,1280,128]{2,1,0:T(8,128)(2,1)} %refs_4_.3), custom_call_target="tpu_custom_call" | custom-call | flops 335544320 | bytes 8421376 | tf_op jit(solution)/shard_map/pallas_call | solution.py:201
  6.4 4.9 %collective-permute-start = (f32[8,136,128]{2,1,0:T(8,128)}, f32[8,136,128]{2,1,0:T(8,128)S(1)}, u32[]{:S(2)}, u32[]{:S(2)}) collective-permute-start(f32[8,136,128]{2,1,0:T(8,128)} %get-tuple-element.30), channel_id=1, source_target_pairs={{0,4},{4,8},{8,12},{1,5},{5,9},{9,13},{2,6},{6,10},{10,14},{3,7},{... | collective-permute-start | bytes 1671176 | tf_op jit(solution)/shard_map/ppermute | solution.py:232
  11.4 7.2 %shard_map.86.refs_1_.refs_2_ = f32[8,1280,128]{2,1,0:T(8,128)} custom-call(bf16[8,1280,128]{2,1,0:T(8,128)(2,1)} %refs_0_.12, bf16[8,1280,128]{2,1,0:T(8,128)(2,1)} %refs_3_.3, bf16[8,1280,128]{2,1,0:T(8,128)(2,1)} %refs_4_.3), custom_call_target="tpu_custom_call" | custom-call | flops 1342177280 | bytes 13107200 | tf_op jit(solution)/shard_map/pallas_call | solution.py:201
  18.5 5.0 %collective-permute-done.refs_6_ = f32[8,136,128]{2,1,0:T(8,128)S(1)} collective-permute-done((f32[8,136,128]{2,1,0:T(8,128)}, f32[8,136,128]{2,1,0:T(8,128)S(1)}, u32[]{:S(2)}, u32[]{:S(2)}) %collective-permute-start) | collective-permute-done | bytes 557088 | tf_op jit(solution)/shard_map/ppermute | solution.py:232
  23.5 0.0 copy-start.2
  23.5 4.3 %collective-permute-start.1 = (f32[8,136,128]{2,1,0:T(8,128)S(1)}, f32[8,136,128]{2,1,0:T(8,128)S(1)}, u32[]{:S(2)}, u32[]{:S(2)}) collective-permute-start(f32[8,136,128]{2,1,0:T(8,128)S(1)} %collective-permute-done.refs_6_), channel_id=1, source_target_pairs={{0,4},{4,8},{8,12},{1,5},{5,9},{9,13},{2,6},{6,10},{10,14},{3,7},{... | collective-permute-start | bytes 1671176 | tf_op jit(solution)/shard_map/ppermute | solution.py:232
  27.8 11.0 %collective-permute-done.1.refs_7_ = f32[8,136,128]{2,1,0:T(8,128)S(1)} collective-permute-done((f32[8,136,128]{2,1,0:T(8,128)S(1)}, f32[8,136,128]{2,1,0:T(8,128)S(1)}, u32[]{:S(2)}, u32[]{:S(2)}) %collective-permute-start.1) | collective-permute-done | bytes 557088 | tf_op jit(solution)/shard_map/ppermute | solution.py:232
  38.8 0.0 copy-start.3
  38.8 0.0 copy-done.2
  38.8 0.8 copy-done.3
  39.6 8.4 %shard_map.87 = (f32[1280,2]{1,0:T(8,128)}, bf16[8,5,128,128]{3,2,1,0:T(8,128)(2,1)}) custom-call(s32[5]{0:T(128)} %refs_0_.13, f32[8,1280,128]{2,1,0:T(8,128)} %shard_map.86.refs_1_.refs_2_, bf16[8,1280,128]{2,1,0:T(8,128)(2,1)} %refs_0_.12, bf16[8,1280,128]{2,1,0:T(8,128)(2,1)} %refs_4_.2, f32[8,1,128]{2,1,0:T(1,128)} %bitcast.3, ...), custom_call_target="tpu_custom_call" | custom-call | flops 335544320 | bytes 15546368 | tf_op jit(solution)/shard_map/pallas_call | solution.py:201
  48.0 1.3 %copy.15 = f32[2,1280]{1,0:T(2,128)S(1)} copy(f32[2,1280]{0,1:T(8,128)} %bitcast.2) | data formatting | bytes 20480 | tf_op jit(solution)/shard_map/transpose | solution.py:309
  49.3 0.1 collective-permute-start.4
  49.4 1.6 %collective-permute-start.3 = (f32[2560]{0:T(1024)S(1)}, f32[2560]{0:T(1024)S(1)}, u32[]{:S(2)}, u32[]{:S(2)}) collective-permute-start(f32[2560]{0:T(1024)S(1)} %reshape.13), channel_id=1, source_target_pairs={{0,2},{1,3},{2,0},{3,1},{4,6},{5,7},{6,4},{7,5},{8,10},{9,11},{10,... | collective-permute-start | bytes 30728 | tf_op jit(solution)/shard_map/ppermute | solution.py:312
  51.0 0.3 collective-permute-start.2
  51.2 1.3 %collective-permute-done.4 = f32[2560]{0:T(1024)S(1)} collective-permute-done((f32[2560]{0:T(1024)S(1)}, f32[2560]{0:T(1024)S(1)}, u32[]{:S(2)}, u32[]{:S(2)}) %collective-permute-start.4) | collective-permute-done | bytes 10272 | tf_op jit(solution)/shard_map/ppermute | solution.py:312
  52.6 0.6 collective-permute-done.3
  53.2 0.0 collective-permute-done.2
  53.2 1.1 %copy.16.refs_6_ = f32[1280,2]{1,0:T(8,128)} copy(f32[1280,2]{0,1:T(2,128)S(1)} %pad_maximum_fusion) | data formatting | bytes 20480 | tf_op jit(solution)/shard_map/stack | solution.py:321
  54.3 10.5 %shard_map.88 = (bf16[8,1280,128]{2,1,0:T(8,128)(2,1)}, f32[8,5,128,128]{3,2,1,0:T(8,128)}, f32[8,136,128]{2,1,0:T(8,128)}) custom-call(s32[5]{0:T(128)} %refs_0_.13, bf16[8,1280,128]{2,1,0:T(8,128)(2,1)} %refs_0_.12, f32[8,1280,128]{2,1,0:T(8,128)} %shard_map.86.refs_1_.refs_2_, bf16[8,5,128,128]{3,2,1,0:T(8,128)(2,1)} %get-tuple-element.36.refs_3_.refs_4_, ...), custom_call_target="tpu_custom_call" | custom-call | flops 335544320 | bytes 17610752 | tf_op jit(solution)/shard_map/pallas_call | solution.py:201
  64.9 1.3 %collective-permute-start.5 = (f32[8,136,128]{2,1,0:T(8,128)}, f32[8,136,128]{2,1,0:T(8,128)S(1)}, u32[]{:S(2)}, u32[]{:S(2)}) collective-permute-start(f32[8,136,128]{2,1,0:T(8,128)} %get-tuple-element.38), channel_id=1, source_target_pairs={{4,0},{8,4},{12,8},{5,1},{9,5},{13,9},{6,2},{10,6},{14,10},{7,3},{... | collective-permute-start | bytes 1671176 | tf_op jit(solution)/shard_map/ppermute | solution.py:232
  66.1 10.1 %shard_map.89 = (bf16[8,1280,128]{2,1,0:T(8,128)(2,1)}, f32[8,1280,128]{2,1,0:T(8,128)}, f32[8,1280,128]{2,1,0:T(8,128)}) custom-call(bf16[8,1280,128]{2,1,0:T(8,128)(2,1)} %refs_0_.12, bf16[8,1280,128]{2,1,0:T(8,128)(2,1)} %refs_3_.3, bf16[8,1280,128]{2,1,0:T(8,128)(2,1)} %refs_4_.3, bf16[8,1280,128]{2,1,0:T(8,128)(2,1)} %get-tuple-element.39.refs_3_, ...), custom_call_target="tpu_custom_call" | custom-call | flops 1677721600 | bytes 12451840 | tf_op jit(solution)/shard_map/pallas_call | solution.py:201
  76.2 6.4 %collective-permute-done.5.refs_6_ = f32[8,136,128]{2,1,0:T(8,128)S(1)} collective-permute-done((f32[8,136,128]{2,1,0:T(8,128)}, f32[8,136,128]{2,1,0:T(8,128)S(1)}, u32[]{:S(2)}, u32[]{:S(2)}) %collective-permute-start.5) | collective-permute-done | bytes 557088 | tf_op jit(solution)/shard_map/ppermute | solution.py:232
  82.6 0.0 copy-start
  82.6 1.5 %collective-permute-start.6 = (f32[8,136,128]{2,1,0:T(8,128)S(1)}, f32[8,136,128]{2,1,0:T(8,128)S(1)}, u32[]{:S(2)}, u32[]{:S(2)}) collective-permute-start(f32[8,136,128]{2,1,0:T(8,128)S(1)} %collective-permute-done.5.refs_6_), channel_id=1, source_target_pairs={{4,0},{8,4},{12,8},{5,1},{9,5},{13,9},{6,2},{10,6},{14,10},{7,3},{... | collective-permute-start | bytes 1671176 | tf_op jit(solution)/shard_map/ppermute | solution.py:232
  84.1 10.1 %shard_map.90 = (bf16[8,1280,128]{2,1,0:T(8,128)(2,1)}, f32[8,1280,128]{2,1,0:T(8,128)}, f32[8,1280,128]{2,1,0:T(8,128)}) custom-call(bf16[8,1280,128]{2,1,0:T(8,128)(2,1)} %refs_0_.12, bf16[8,1280,128]{2,1,0:T(8,128)(2,1)} %refs_3_.3, bf16[8,1280,128]{2,1,0:T(8,128)(2,1)} %refs_4_.3, ...), custom_call_target="tpu_custom_call", output_to_operand_aliasing={{0}: (5, {}), {1}: (6, {}), {2}: (7, {})} | custom-call | flops 1677721600 | bytes 12451840 | tf_op jit(solution)/shard_map/pallas_call | solution.py:201
  94.2 0.0 copy-done
  94.2 4.7 %collective-permute-done.6.refs_7_ = f32[8,136,128]{2,1,0:T(8,128)S(1)} collective-permute-done((f32[8,136,128]{2,1,0:T(8,128)S(1)}, f32[8,136,128]{2,1,0:T(8,128)S(1)}, u32[]{:S(2)}, u32[]{:S(2)}) %collective-permute-start.6) | collective-permute-done | bytes 557088 | tf_op jit(solution)/shard_map/ppermute | solution.py:232
  98.8 0.0 copy-start.1
  98.8 0.8 copy-done.1
  99.6 9.8 %shard_map.91 = (bf16[8,1280,128]{2,1,0:T(8,128)(2,1)}, bf16[8,1280,128]{2,1,0:T(8,128)(2,1)}) custom-call(s32[5]{0:T(128)} %refs_0_.13, f32[8,1280,128]{2,1,0:T(8,128)} %get-tuple-element.51.refs_1_, f32[8,1280,128]{2,1,0:T(8,128)} %get-tuple-element.52.refs_2_, bf16[8,1280,128]{2,1,0:T(8,128)(2,1)} %refs_3_.3, bf16[8,1280,128]{2,1,0:T(8,128)(2,1)} %refs_4_.3, ...), custom_call_target="tpu_custom_call" | custom-call | flops 671088640 | bytes 24707072 | tf_op jit(solution)/shard_map/pallas_call | solution.py:201
  (6 shorter events, 0.1 us)
Async XLA Ops:
  6.4 17.1 %collective-permute-start = (f32[8,136,128]{2,1,0:T(8,128)}, f32[8,136,128]{2,1,0:T(8,128)S(1)}, u32[]{:S(2)}, u32[]{:S(2)}) collective-permute-start(f32[8,136,128]{2,1,0:T(8,128)} %get-tuple-element.30), channel_id=1, source_target_pairs={{0,4},{4,8},{8,12},{1,5},{5,9},{9,13},{2,6},{6,10},{10,14},{3,7},{... | collective-permute-start | bytes 1671176 | tf_op jit(solution)/shard_map/ppermute | solution.py:232
  23.5 15.3 %copy-start.2 = (f32[8,136,128]{2,1,0:T(8,128)}, f32[8,136,128]{2,1,0:T(8,128)S(1)}, u32[]{:S(2)}) copy-start(f32[8,136,128]{2,1,0:T(8,128)S(1)} %collective-permute-done.refs_6_) | copy-start | bytes 1671172
  23.5 15.3 %collective-permute-start.1 = (f32[8,136,128]{2,1,0:T(8,128)S(1)}, f32[8,136,128]{2,1,0:T(8,128)S(1)}, u32[]{:S(2)}, u32[]{:S(2)}) collective-permute-start(f32[8,136,128]{2,1,0:T(8,128)S(1)} %collective-permute-done.refs_6_), channel_id=1, source_target_pairs={{0,4},{4,8},{8,12},{1,5},{5,9},{9,13},{2,6},{6,10},{10,14},{3,7},{... | collective-permute-start | bytes 1671176 | tf_op jit(solution)/shard_map/ppermute | solution.py:232
  38.8 0.8 copy-start.3
  49.3 3.3 %collective-permute-start.4 = (f32[2560]{0:T(1024)S(1)}, f32[2560]{0:T(1024)S(1)}, u32[]{:S(2)}, u32[]{:S(2)}) collective-permute-start(f32[2560]{0:T(1024)S(1)} %reshape.13), channel_id=1, source_target_pairs={{0,3},{1,2},{2,1},{3,0},{4,7},{5,6},{6,5},{7,4},{8,11},{9,10},{10,... | collective-permute-start | bytes 30728 | tf_op jit(solution)/shard_map/ppermute | solution.py:312
  49.4 3.8 %collective-permute-start.3 = (f32[2560]{0:T(1024)S(1)}, f32[2560]{0:T(1024)S(1)}, u32[]{:S(2)}, u32[]{:S(2)}) collective-permute-start(f32[2560]{0:T(1024)S(1)} %reshape.13), channel_id=1, source_target_pairs={{0,2},{1,3},{2,0},{3,1},{4,6},{5,7},{6,4},{7,5},{8,10},{9,11},{10,... | collective-permute-start | bytes 30728 | tf_op jit(solution)/shard_map/ppermute | solution.py:312
  51.0 2.2 %collective-permute-start.2 = (f32[2560]{0:T(1024)S(1)}, f32[2560]{0:T(1024)S(1)}, u32[]{:S(2)}, u32[]{:S(2)}) collective-permute-start(f32[2560]{0:T(1024)S(1)} %reshape.13), channel_id=1, source_target_pairs={{0,1},{1,0},{2,3},{3,2},{4,5},{5,4},{6,7},{7,6},{8,9},{9,8},{10,11... | collective-permute-start | bytes 30728 | tf_op jit(solution)/shard_map/ppermute | solution.py:312
  64.9 17.8 %collective-permute-start.5 = (f32[8,136,128]{2,1,0:T(8,128)}, f32[8,136,128]{2,1,0:T(8,128)S(1)}, u32[]{:S(2)}, u32[]{:S(2)}) collective-permute-start(f32[8,136,128]{2,1,0:T(8,128)} %get-tuple-element.38), channel_id=1, source_target_pairs={{4,0},{8,4},{12,8},{5,1},{9,5},{13,9},{6,2},{10,6},{14,10},{7,3},{... | collective-permute-start | bytes 1671176 | tf_op jit(solution)/shard_map/ppermute | solution.py:232
  82.6 11.6 %copy-start = (f32[8,136,128]{2,1,0:T(8,128)}, f32[8,136,128]{2,1,0:T(8,128)S(1)}, u32[]{:S(2)}) copy-start(f32[8,136,128]{2,1,0:T(8,128)S(1)} %collective-permute-done.5.refs_6_) | copy-start | bytes 1671172
  82.6 16.2 %collective-permute-start.6 = (f32[8,136,128]{2,1,0:T(8,128)S(1)}, f32[8,136,128]{2,1,0:T(8,128)S(1)}, u32[]{:S(2)}, u32[]{:S(2)}) collective-permute-start(f32[8,136,128]{2,1,0:T(8,128)S(1)} %collective-permute-done.5.refs_6_), channel_id=1, source_target_pairs={{4,0},{8,4},{12,8},{5,1},{9,5},{13,9},{6,2},{10,6},{14,10},{7,3},{... | collective-permute-start | bytes 1671176 | tf_op jit(solution)/shard_map/ppermute | solution.py:232
  98.8 0.8 copy-start.1
